TPU v7x, 32 devices: a whole 2x2x4 slice. The times are simulated.
32 devices in a mesh: expert: 2 (over y), hidden: 16 (over z, x, core).
Axes of the slice: x: 2, y: 2, z: 4, core: 2. Of those that a mesh axis runs over, the one named last changes fastest.
Arguments:
- tokens: bfloat16 [192, 3072], P('expert', 'hidden'), may hold values from -6 to 6
- cotangent: bfloat16 [192, 3072], P('expert', 'hidden'), may hold values from -6 to 6
- w_gate: bfloat16 [2, 3072, 16384], P('expert', None, 'hidden'), may hold values from -0.15625 to 0.15625
- w_up: bfloat16 [2, 3072, 16384], P('expert', None, 'hidden'), may hold values from -0.15625 to 0.15625
- w_down: bfloat16 [2, 16384, 3072], P('expert', 'hidden'), may hold values from -0.046875 to 0.046875
- slot_token: int32 [2, 192], P(None, 'expert'), may hold values from 0 to 95, as said below
- slot_weight: float32 [2, 192], P(None, 'expert'), may hold values from 0.2 to 1
- keep_mask: int32 [2, 192, 16384], P('expert', None, 'hidden'), may hold values 0 or 1
Outputs:
- grad_tokens: bfloat16 [192, 3072], P('expert', 'hidden')
Inputs may be any that keep to these rules, and one draw needn't show every extreme that they name: `slot_token`: slots s of block g = s // 96 of every expert hold tokens of group g (token rows g * 96 to (g + 1) * 96 - 1); within one expert and one block the 96 entries are distinct; every slot is filled.
All inputs are finite; a program needn't handle non-finite values. No bound on the sum of `keep_mask` on one device may be relied on, other than what follows from the above.
Results may differ from a plain program's by a relative error of at most 0.012.
Values may be sent and summed in bfloat16 or wider, within the bound.
No kernel may reach another device: no remote copies, remote signals or barrier semaphores. Data moves between devices by JAX's collectives and lax.ppermute only.
A program may use at most 64 MiB of HBM per device.

v0:
```python
import jax
import jax.numpy as jnp
from jax import lax
from jax.sharding import PartitionSpec as P

keep_rate = 0.9


def gelu_tanh(values):
    return jax.nn.gelu(values, approximate=True)


def fold_slots(slot_values, one_hot):
    high_part = slot_values.astype(jnp.bfloat16)
    low_part = (slot_values - high_part.astype(jnp.float32)).astype(jnp.bfloat16)
    return jnp.dot(high_part, one_hot, preferred_element_type=jnp.float32) + jnp.dot(
        low_part, one_hot, preferred_element_type=jnp.float32
    )


def body(tokens, cotangent, w_gate, w_up, w_down, slot_token, slot_weight, keep_mask):
    gate_mat = w_gate[0]
    up_mat = w_up[0]
    down_mat = w_down[0]
    model_width = gate_mat.shape[0]
    expert_count = lax.axis_size("expert")
    expert_total = slot_token.shape[0]
    per_source = slot_token.shape[1]
    slot_count = expert_count * per_source
    group_tokens = tokens.shape[0]
    slot_list = slot_token.reshape(-1)
    weight_column = slot_weight.reshape(-1, 1)
    inv_keep = 1.0 / keep_rate
    chosen = tokens[slot_list].reshape(expert_total, per_source, -1)
    scaled = (weight_column * cotangent[slot_list].astype(jnp.float32)).astype(jnp.bfloat16)
    sent_cot = scaled.reshape(expert_total, per_source, -1)
    recv_inputs, recv_cot = (
        lax.all_to_all(chosen, "expert", split_axis=0, concat_axis=0, tiled=True),
        lax.all_to_all(sent_cot, "expert", split_axis=0, concat_axis=0, tiled=True),
    )
    slot_inputs = recv_inputs.reshape(slot_count, -1)
    slot_cot = recv_cot.reshape(slot_count, -1)
    part_inputs = lax.all_gather(slot_inputs, "hidden", axis=1, tiled=True)
    part_cot = lax.all_gather(slot_cot, "hidden", axis=1, tiled=True)
    gate_rows = gate_mat
    up_rows = up_mat
    gate_pre = jnp.dot(part_inputs, gate_rows, preferred_element_type=jnp.float32)
    up_pre = jnp.dot(part_inputs, up_rows, preferred_element_type=jnp.float32)
    grad_hidden = lax.dot_general(
        part_cot, down_mat, (((1,), (1,)), ((), ())), preferred_element_type=jnp.float32
    )
    activated, pullback = jax.vjp(gelu_tanh, gate_pre)
    grad_pre = grad_hidden * keep_mask[0].astype(jnp.float32) * inv_keep
    grad_up = (grad_pre * activated).astype(jnp.bfloat16)
    grad_gate = pullback(grad_pre * up_pre)[0].astype(jnp.bfloat16)
    one_hot = (slot_list[:, None] == jnp.arange(group_tokens, dtype=jnp.int32)[None, :]).astype(
        jnp.bfloat16
    )
    local_width = model_width // lax.axis_size("hidden")
    gate_rows = gate_mat
    up_rows = up_mat
    reduced = lax.psum_scatter(
        lax.dot_general(
            gate_rows, grad_gate, (((1,), (1,)), ((), ())), preferred_element_type=jnp.float32
        )
        + lax.dot_general(
            up_rows, grad_up, (((1,), (1,)), ((), ())), preferred_element_type=jnp.float32
        ),
        "hidden",
        scatter_dimension=0,
        tiled=True,
    )
    returned = lax.all_to_all(
        reduced.reshape(local_width, expert_count, per_source),
        "expert",
        split_axis=1,
        concat_axis=1,
        tiled=True,
    )
    token_sum = fold_slots(returned.reshape(local_width, -1), one_hot)
    return token_sum.T.astype(jnp.bfloat16)


def solution(mesh):
    in_specs = (
        P("expert", "hidden"),
        P("expert", "hidden"),
        P("expert", None, "hidden"),
        P("expert", None, "hidden"),
        P("expert", "hidden", None),
        P(None, "expert"),
        P(None, "expert"),
        P("expert", None, "hidden"),
    )
    out_specs = P("expert", "hidden")
    return jax.shard_map(body, mesh=mesh, in_specs=in_specs, out_specs=out_specs, check_vma=False)
```

profile of v0, /device:TPU:0, one launch (start us, length us, event | category | flops | bytes accessed | tf_op | source)
XLA Modules:
  0.0 205.2 jit_solution(17161815436193137995)
XLA Ops:
  6.5 0.0 copy-start
  6.5 0.0 all-gather.5.cloned.1.call-start
  6.5 0.8 reshape.59
  7.3 0.0 copy-done
  7.3 1.0 gather_fusion.1
  8.4 8.3 %all_to_all.15 = bf16[2,96,192]{2,1,0:T(8,128)(2,1)S(1)} all-to-all(bf16[2,96,192]{2,1,0:T(8,128)(2,1)S(1)} %bitcast.53), channel_id=1, replica_groups=mesh['expert'=2,'hidden'=16] {'expert'}, dimensions={0} | all-to-all | bytes 147456 | tf_op jit(solution)/shard_map/all_to_all | solution.py:38
  16.7 0.7 copy.12
  17.4 0.0 all-gather.5.cloned.1.call-update
  17.4 0.0 all-gather.3.cloned.1.call-start
  17.5 1.7 gather_fusion
  19.2 0.8 fusion.48
  19.9 6.7 %all_to_all.16 = bf16[2,96,192]{2,1,0:T(8,128)(2,1)S(1)} all-to-all(bf16[2,96,192]{2,1,0:T(8,128)(2,1)S(1)} %fusion.48), channel_id=1, replica_groups=mesh['expert'=2,'hidden'=16] {'expert'}, dimensions={0} | all-to-all | bytes 147456 | tf_op jit(solution)/shard_map/all_to_all | solution.py:39
  26.6 0.7 copy.11
  27.3 0.0 all-gather.3.cloned.1.call-update
  27.4 0.0 reduce-scatter.4.cloned.1.call-start
  27.4 30.1 %all-gather.5.cloned.1.call-done = bf16[192,3072]{0,1:T(8,128)(2,1)} async-done(((bf16[192,192]{0,1:T(8,128)(2,1)}), bf16[192,3072]{0,1:T(8,128)(2,1)}) %all-gather.5.cloned.1.call-update) | async-done | bytes 1179664 | tf_op jit(solution)/shard_map/all_gather | solution.py:43
  57.6 4.7 %fusion.2 = f32[192,1024]{1,0:T(8,128)S(1)} fusion(bf16[192,3072]{0,1:T(8,128)(2,1)} %all-gather.5.cloned.1.call-done, bf16[1,3072,1024]{2,1,0:T(8,128)(2,1)} %param.10), kind=kOutput, calls=%fused_computation.4 | convolution fusion | flops 1207959552 | bytes 8257536 | tf_op jit(solution)/shard_map/dot_general | solution.py:47
  62.3 0.0 copy-start.2
  62.3 0.0 copy-start.1
  62.3 36.2 %all-gather.3.cloned.1.call-done = bf16[192,3072]{0,1:T(8,128)(2,1)} async-done(((bf16[192,192]{0,1:T(8,128)(2,1)}), bf16[192,3072]{0,1:T(8,128)(2,1)}) %all-gather.3.cloned.1.call-update) | async-done | bytes 1179664 | tf_op jit(solution)/shard_map/all_gather | solution.py:44
  98.4 5.6 %fusion.22 = f32[192,1024]{1,0:T(8,128)S(1)} fusion(bf16[192,3072]{0,1:T(8,128)(2,1)} %all-gather.3.cloned.1.call-done, bf16[1,1024,3072]{2,1,0:T(8,128)(2,1)} %param.12, s32[1,192,1024]{2,1,0:T(8,128)} %param.15), kind=kOutput, calls=%fused_computation.16 | convolution fusion | flops 1208549376 | bytes 9043968 | tf_op jit(solution)/shard_map/dot_general | solution.py:49
  104.1 0.0 copy-done.2
  104.1 0.0 copy-done.1
  104.1 9.9 %fusion = f32[192,3072]{1,0:T(8,128)} fusion(bf16[1,3072,1024]{2,1,0:T(8,128)(2,1)} %param.10, f32[192,1024]{1,0:T(8,128)S(1)} %fusion.2, f32[192,1024]{1,0:T(8,128)S(1)} %fusion.22, bf16[192,3072]{0,1:T(8,128)(2,1)S(1)} %copy-done.1, bf16[1,3072,1024]{2,1,0:T(8,128)(2,1)} %param.11), kind=kOutput, calls=%fused_computation.2 | convolution fusion | flops 2420047872 | bytes 17694720 | tf_op jit(solution)/shard_map/dot_general | solution.py:63
  114.0 5.9 %fusion.13 = f32[3072,192]{0,1:T(8,128)S(1)} fusion(f32[192,3072]{1,0:T(8,128)} %fusion, bf16[1,3072,1024]{2,1,0:T(8,128)(2,1)} %param.11, f32[192,1024]{1,0:T(8,128)S(1)} %fusion.22, f32[192,1024]{1,0:T(8,128)} %copy-done.2), kind=kOutput, calls=%fused_computation.13 | convolution fusion | flops 1210515456 | bytes 12582912 | tf_op jit(solution)/shard_map/dot_general | solution.py:66
  120.0 0.0 copy-start.3
  120.0 2.3 %copy.13 = f32[3072,192]{1,0:T(8,128)} copy(f32[3072,192]{0,1:T(8,128)S(1)} %fusion.13) | data formatting | bytes 4718592
  122.3 0.0 reduce-scatter.4.cloned.1.call-update
  122.3 65.3 %reduce-scatter.4.cloned.1.call-done = f32[192,192]{1,0:T(8,128)} async-done(((f32[3072,192]{1,0:T(8,128)}), f32[192,192]{1,0:T(8,128)}) %reduce-scatter.4.cloned.1.call-update) | async-done | bytes 147472
  187.5 1.7 copy.14
  189.3 3.4 %all-to-all-start.2 = ((f32[192,2,96]{0,2,1:T(8,128)}), f32[192,2,96]{0,2,1:T(8,128)S(1)}, u32[]{:S(2)}, u32[]{:S(2)}) async-start(f32[192,2,96]{0,2,1:T(8,128)} %bitcast.10), calls=%async_computation.2 | async-start | bytes 393216 | tf_op jit(solution)/shard_map/all_to_all | solution.py:73
  192.7 0.0 copy-done.3
  192.7 0.1 eq.15
  192.8 4.7 %all-to-all-done.2 = f32[192,2,96]{0,2,1:T(8,128)S(1)} async-done(((f32[192,2,96]{0,2,1:T(8,128)}), f32[192,2,96]{0,2,1:T(8,128)S(1)}, u32[]{:S(2)}, u32[]{:S(2)}) %all-to-all-start.2) | async-done | bytes 147488 | tf_op jit(solution)/shard_map/all_to_all | solution.py:73
  197.5 0.3 fusion.50
  197.8 0.9 fusion.25
  (3 shorter events, 0.0 us)
Async XLA Ops:
  6.5 0.8 copy-start
  6.5 51.0 %all-gather.5.cloned.1.call-start = ((), (), s32[]{:S(2)}) async-start(), calls=%async_computation.5 | async-start | bytes 1671168 | tf_op jit(solution)/shard_map/all_gather | solution.py:43
  17.4 81.0 %all-gather.3.cloned.1.call-start = ((), (), s32[]{:S(2)}) async-start(), calls=%async_computation.4 | async-start | bytes 1671168 | tf_op jit(solution)/shard_map/all_gather | solution.py:44
  27.4 160.2 %reduce-scatter.4.cloned.1.call-start = ((), (), s32[]{:S(2)}) async-start(), calls=%async_computation.6 | async-start | bytes 3342336
  62.3 41.9 %copy-start.2 = (f32[192,1024]{1,0:T(8,128)}, f32[192,1024]{1,0:T(8,128)S(1)}, u32[]{:S(2)}) copy-start(f32[192,1024]{1,0:T(8,128)S(1)} %fusion.2) | copy-start | bytes 2359300
  62.3 41.9 %copy-start.1 = (bf16[192,3072]{0,1:T(8,128)(2,1)S(1)}, bf16[192,3072]{0,1:T(8,128)(2,1)}, u32[]{:S(2)}) copy-start(bf16[192,3072]{0,1:T(8,128)(2,1)} %all-gather.5.cloned.1.call-done) | copy-start | bytes 3538948
  120.0 72.7 %copy-start.3 = (s32[2,96]{1,0:T(2,128)S(1)}, s32[2,96]{1,0:T(2,128)}, u32[]{:S(2)}) copy-start(s32[2,96]{1,0:T(2,128)} %param.13) | copy-start | bytes 2308
  189.3 8.2 %all-to-all-start.2 = ((f32[192,2,96]{0,2,1:T(8,128)}), f32[192,2,96]{0,2,1:T(8,128)S(1)}, u32[]{:S(2)}, u32[]{:S(2)}) async-start(f32[192,2,96]{0,2,1:T(8,128)} %bitcast.10), calls=%async_computation.2 | async-start | bytes 393216 | tf_op jit(solution)/shard_map/all_to_all | solution.py:73
Sparse Core Ops, SparseCore 0:
  17.6 39.9 all-gather.4
  59.8 38.5 all-gather.2
  122.4 65.0 reduce-scatter.3
where the time goes:
time: 206 us; the launch traced here: 205 us
  waiting for transfers between devices  136 us (66%)
  matrix products  27.3 us (13%)
  blocking collectives  15 us (7%)
  between operations  13.2 us (6%)
  local copies, waits for them, and re-layouts  9.05 us (4%)
  starting transfers between devices  3.52 us (2%)
    unnamed x4, waiting for transfers between devices  65.3 us
    all_gather x1, waiting for transfers between devices, body(): part_cot = lax.all_gather(slot_cot, 'hidden', axis=1, tiled=True)  36.2 us
    all_gather x1, waiting for transfers between devices, body(): part_inputs = lax.all_gather(slot_inputs, 'hidden', axis=1, tiled=True)  30.1 us
    dot_general x1, matrix products, body(): lax.dot_general(gate_rows, grad_gate, (((1,), (1,)), ((), ())), preferred...  9.91 us
    all_to_all x1, blocking collectives, body(): lax.all_to_all(chosen, 'expert', split_axis=0, concat_axis=0, tiled=True)  8.33 us
    all_to_all x1, blocking collectives, body(): lax.all_to_all(sent_cot, 'expert', split_axis=0, concat_axis=0, tiled=True)  6.65 us
    dot_general x1, matrix products, body(): lax.dot_general(up_rows, grad_up, (((1,), (1,)), ((), ())), preferred_ele...  5.93 us
    dot_general x1, matrix products, body(): lax.dot_general(part_cot, down_mat, (((1,), (1,)), ((), ())), preferred_e...  5.65 us
  transfers between devices with their start and end apart: 4, of which 4 were waited for; matrix products, arithmetic and copies ran while one was open for 4% of the time, Pallas kernels for 0%

commit v1 on v0

v1 whole, which is shorter than its diff:
```python
import jax
import jax.numpy as jnp
from jax import lax
from jax.sharding import PartitionSpec as P

keep_rate = 0.9


def gelu_tanh(values):
    return jax.nn.gelu(values, approximate=True)


def fold_slots(one_hot, slot_values):
    high_part = slot_values.astype(jnp.bfloat16)
    low_part = (slot_values - high_part.astype(jnp.float32)).astype(jnp.bfloat16)
    dims = (((0,), (0,)), ((), ()))
    return lax.dot_general(one_hot, high_part, dims, preferred_element_type=jnp.float32) + lax.dot_general(
        one_hot, low_part, dims, preferred_element_type=jnp.float32
    )


def body(tokens, cotangent, w_gate, w_up, w_down, slot_token, slot_weight, keep_mask):
    gate_mat = w_gate[0]
    up_mat = w_up[0]
    down_mat = w_down[0]
    model_width, local_ff = gate_mat.shape
    hidden_count = lax.axis_size("hidden")
    expert_count = lax.axis_size("expert")
    expert_total, per_source = slot_token.shape
    slot_count = expert_count * per_source
    group_tokens, local_width = tokens.shape
    slot_list = slot_token.reshape(-1)
    weight_column = slot_weight.reshape(-1, 1)
    inv_keep = 1.0 / keep_rate

    chosen = tokens[slot_list]
    scaled = (weight_column * cotangent[slot_list].astype(jnp.float32)).astype(jnp.bfloat16)
    slab = jnp.concatenate([chosen, scaled], axis=1).reshape(expert_total, per_source, 2 * local_width)
    recv = lax.all_to_all(slab, "expert", split_axis=0, concat_axis=0, tiled=True)
    slab_slots = recv.reshape(slot_count, 2 * local_width)
    gathered = lax.all_gather(slab_slots, "hidden", axis=0, tiled=False)
    part_inputs = gathered[:, :, :local_width]
    part_cot = gathered[:, :, local_width:]

    gate_rows = gate_mat.reshape(hidden_count, local_width, local_ff)
    up_rows = up_mat.reshape(hidden_count, local_width, local_ff)
    down_cols = down_mat.reshape(local_ff, hidden_count, local_width)
    fwd_dims = (((0, 2), (0, 1)), ((), ()))
    gate_pre = lax.dot_general(part_inputs, gate_rows, fwd_dims, preferred_element_type=jnp.float32)
    up_pre = lax.dot_general(part_inputs, up_rows, fwd_dims, preferred_element_type=jnp.float32)
    grad_hidden = lax.dot_general(
        part_cot, down_cols, (((0, 2), (1, 2)), ((), ())), preferred_element_type=jnp.float32
    )
    activated, pullback = jax.vjp(gelu_tanh, gate_pre)
    grad_pre = grad_hidden * keep_mask[0].astype(jnp.float32) * inv_keep
    grad_up = (grad_pre * activated).astype(jnp.bfloat16)
    grad_gate = pullback(grad_pre * up_pre)[0].astype(jnp.bfloat16)

    back_dims = (((1,), (1,)), ((), ()))
    partial = lax.dot_general(
        grad_gate, gate_mat, back_dims, preferred_element_type=jnp.float32
    ) + lax.dot_general(grad_up, up_mat, back_dims, preferred_element_type=jnp.float32)
    blocks = partial.reshape(expert_count, per_source, hidden_count, local_width).transpose(0, 2, 1, 3)
    blocks = blocks.astype(jnp.bfloat16).reshape(expert_count * hidden_count, per_source, local_width)
    returned = lax.all_to_all(blocks, ("expert", "hidden"), split_axis=0, concat_axis=0, tiled=True)
    per_expert = returned.reshape(expert_total, hidden_count, per_source, local_width).astype(jnp.float32).sum(1)
    one_hot = (slot_list[:, None] == jnp.arange(group_tokens, dtype=jnp.int32)[None, :]).astype(jnp.bfloat16)
    token_sum = fold_slots(one_hot, per_expert.reshape(expert_total * per_source, local_width))
    return token_sum.astype(jnp.bfloat16)


def solution(mesh):
    in_specs = (
        P("expert", "hidden"),
        P("expert", "hidden"),
        P("expert", None, "hidden"),
        P("expert", None, "hidden"),
        P("expert", "hidden", None),
        P(None, "expert"),
        P(None, "expert"),
        P("expert", None, "hidden"),
    )
    out_specs = P("expert", "hidden")
    return jax.shard_map(body, mesh=mesh, in_specs=in_specs, out_specs=out_specs, check_vma=False)
```

time: 206 us -> 139 us (0.67)
  waiting for transfers between devices: 136 us -> 72.7 us
  local copies, waits for them, and re-layouts: 9.05 us -> 17.1 us
  blocking collectives: 15 us -> 8.7 us
  matrix products: 27.3 us -> 22.1 us
    unnamed x4 -> x1, waiting for transfers between devices: 65.3 us -> 0.02 us
    all_to_all x1, waiting for transfers between devices: 4.72 us -> 38.3 us  [body(): lax.all_to_all(blocks, ('expert', 'hidden'), split_axis=0, concat_axis=0,...]
    all_gather x2 -> x1, waiting for transfers between devices: 66.3 us -> 34.3 us  [body(): gathered = lax.all_gather(slab_slots, 'hidden', axis=0, tiled=False)]
    all_to_all x2 -> x1, blocking collectives: 15 us -> 8.7 us  [body(): lax.all_to_all(slab, 'expert', split_axis=0, concat_axis=0, tiled=True)]
    unnamed x10 -> x19, local copies, waits for them, and re-layouts: 4.04 us -> 10.1 us
    dot_general x6, matrix products: 27.3 us -> 22.1 us  [the longest x1 10.1 us: body(): lax.dot_general(grad_gate, gate_mat, back_dims, preferred_element_type=jn...]
    convert_element_type x0 -> x2, local copies, waits for them, and re-layouts: none -> 3.48 us  [body(): blocks.astype(jnp.bfloat16)]
  transfers between devices with their start and end apart: 4 -> 2, of which waited for: 4 -> 2; matrix products, arithmetic and copies ran while one was open for 4% -> 6% of each run, Pallas kernels for 0% -> 0%
where the time goes in v1:
time: 139 us
  waiting for transfers between devices  72.7 us (52%)
  matrix products  22.1 us (16%)
  local copies, waits for them, and re-layouts  17.1 us (12%)
  between operations  13.5 us (10%)
  blocking collectives  8.7 us (6%)
  starting transfers between devices  3.4 us (2%)
    all_to_all x1, waiting for transfers between devices, body(): lax.all_to_all(blocks, ('expert', 'hidden'), split_axis=0, concat_axis=0,...  38.3 us
    all_gather x1, waiting for transfers between devices, body(): gathered = lax.all_gather(slab_slots, 'hidden', axis=0, tiled=False)  34.3 us
    unnamed x19, local copies, waits for them, and re-layouts  10.1 us
    dot_general x1, matrix products, body(): lax.dot_general(grad_gate, gate_mat, back_dims, preferred_element_type=jn...  10.1 us
    all_to_all x1, blocking collectives, body(): lax.all_to_all(slab, 'expert', split_axis=0, concat_axis=0, tiled=True)  8.7 us
    dot_general x1, matrix products, body(): lax.dot_general(part_inputs, gate_rows, fwd_dims, preferred_element_type=...  4.83 us
    dot_general x1, matrix products, body(): lax.dot_general(grad_up, up_mat, back_dims, preferred_element_type=jnp.fl...  3.71 us
    convert_element_type x2, local copies, waits for them, and re-layouts, body(): blocks.astype(jnp.bfloat16)  3.48 us
  transfers between devices with their start and end apart: 2, of which 2 were waited for; matrix products, arithmetic and copies ran while one was open for 6% of the time, Pallas kernels for 0%

profile of v1, /device:TPU:0, one launch (start us, length us, event | category | flops | bytes accessed | tf_op | source)
XLA Modules:
  0.0 138.7 jit_solution(2172089514542743153)
XLA Ops:
  6.5 0.0 copy-start
  6.5 0.0 all-gather.2.cloned.1.call-start
  6.5 0.8 reshape.57
  7.3 0.0 copy-done
  7.3 1.0 gather_fusion.1
  8.4 1.7 %gather_fusion = bf16[192,192]{1,0:T(8,128)(2,1)S(1)} fusion(bf16[96,192]{1,0:T(8,128)(2,1)} %param.8, s32[1024]{0:T(1024)S(1)} %pad_clamp_fusion), kind=kCustom, calls=%fused_computation | custom fusion | bytes 148224 | tf_op jit(solution)/shard_map/gather | solution.py:36
  10.0 0.8 fusion.57
  10.8 0.1 pad_maximum_fusion
  10.9 8.7 %all_to_all.10 = bf16[2,96,384]{2,1,0:T(8,128)(2,1)} all-to-all(bf16[2,96,384]{2,1,0:T(8,128)(2,1)S(1)} %pad_maximum_fusion), channel_id=1, replica_groups=mesh['expert'=2,'hidden'=16] {'expert'}, dimensions={0} | all-to-all | bytes 294912 | tf_op jit(solution)/shard_map/all_to_all | solution.py:39
  19.6 0.0 all-gather.2.cloned.1.call-update
  19.6 0.0 slice-start
  19.6 8.8 %copy.12 = bf16[1,1024,3072]{1,2,0:T(8,128)(2,1)} copy(bf16[1,1024,3072]{2,1,0:T(8,128)(2,1)} %param.12) | data formatting | bytes 12582912 | tf_op args[4]
  28.4 34.3 %all-gather.2.cloned.1.call-done = bf16[16,192,384]{2,1,0:T(8,128)(2,1)} async-done(((bf16[1,192,384]{2,1,0:T(8,128)(2,1)}), bf16[16,192,384]{2,1,0:T(8,128)(2,1)}) %all-gather.2.cloned.1.call-update) | async-done | bytes 2359312 | tf_op jit(solution)/shard_map/all_gather | solution.py:41
  62.8 0.0 copy-start.1
  62.8 0.0 copy-start.5
  62.8 0.0 copy-start.6
  62.8 0.0 slice-start.1
  62.8 4.8 %fusion.22 = f32[192,1024]{1,0:T(8,128)S(1)} fusion(bf16[16,192,1024]{2,1,0:T(8,128)(2,1)} %bitcast.61, bf16[16,192,384]{2,1,0:T(8,128)(2,1)} %all-gather.2.cloned.1.call-done), kind=kOutput, calls=%fused_computation.17 | convolution fusion | flops 1207959552 | bytes 8650752 | tf_op jit(solution)/shard_map/dot_general | solution.py:49
  67.6 0.0 copy-start.2
  67.6 0.2 copy-done.1
  67.8 0.7 copy-done.5
  68.5 0.4 copy-done.6
  68.9 2.3 %fusion.31 = f32[192,1024]{1,0:T(8,128)S(1)} fusion(bf16[1024,16,192]{0,2,1:T(8,128)(2,1)S(1)} %bitcast.56, bf16[16,192,384]{2,1,0:T(8,128)(2,1)S(1)} %copy-done.5, s32[1,192,1024]{2,1,0:T(8,128)S(1)} %copy-done.6), kind=kOutput, calls=%fused_computation.20 | convolution fusion | flops 1208549376 | bytes 9437184 | tf_op jit(solution)/shard_map/dot_general | solution.py:51
  71.2 0.0 copy-done.2
  71.2 0.0 slice-done
  71.2 0.0 slice-done.1
  71.2 0.0 copy-start.3
  71.2 3.7 %fusion = f32[192,3072]{1,0:T(8,128)} fusion(bf16[1,3072,1024]{2,1,0:T(8,128)(2,1)S(1)} %bitcast.55, f32[192,1024]{1,0:T(8,128)S(1)} %fusion.31, f32[192,1024]{1,0:T(8,128)S(1)} %fusion.22), kind=kOutput, calls=%fused_computation.2 | convolution fusion | flops 1209925632 | bytes 10223616 | tf_op jit(solution)/shard_map/dot_general | solution.py:62
  74.9 0.0 copy-done.3
  74.9 10.1 %fusion.7 = bf16[192,3072]{1,0:T(8,128)(2,1)S(1)} fusion(f32[192,3072]{1,0:T(8,128)} %fusion, bf16[1,3072,1024]{2,1,0:T(8,128)(2,1)} %param.10, f32[192,1024]{1,0:T(8,128)} %copy-done.2, f32[192,1024]{1,0:T(8,128)} %copy-done.3, bf16[16,192,1024]{2,1,0:T(8,128)(2,1)} %bitcast.53, bf16[16,192,384]{2,1,0:T(8,128)(2,1)} %all-gather.2.cloned.1.call-done), kind=kOutput, calls=%fused_computation.7 | convolution fusion | flops 2421227520 | bytes 19267584 | tf_op jit(solution)/shard_map/dot_general | solution.py:60
  85.0 1.7 %convert_element_type.59 = bf16[2,96,16,192]{3,2,1,0:T(8,128)(2,1)S(1)} reshape(bf16[192,3072]{1,0:T(8,128)(2,1)S(1)} %fusion.7) | data formatting | bytes 2359296 | tf_op jit(solution)/shard_map/convert_element_type | solution.py:64
  86.8 1.7 %copy.13 = bf16[2,96,16,192]{3,1,2,0:T(8,128)(2,1)} copy(bf16[2,96,16,192]{3,2,1,0:T(8,128)(2,1)S(1)} %convert_element_type.59) | data formatting | bytes 2359296 | tf_op jit(solution)/shard_map/convert_element_type | solution.py:64
  88.5 0.0 copy-start.4
  88.5 3.4 %all-to-all-start.1 = ((bf16[32,96,192]{2,1,0:T(8,128)(2,1)}), bf16[32,96,192]{2,1,0:T(8,128)(2,1)S(1)}, u32[]{:S(2)}, u32[]{:S(2)}) async-start(bf16[32,96,192]{2,1,0:T(8,128)(2,1)} %bitcast.14), calls=%async_computation.1 | async-start | bytes 3145728 | tf_op jit(solution)/shard_map/all_to_all | solution.py:65
  91.9 0.0 copy-done.4
  91.9 0.1 eq.15
  92.0 38.3 %all-to-all-done.1 = bf16[32,96,192]{2,1,0:T(8,128)(2,1)S(1)} async-done(((bf16[32,96,192]{2,1,0:T(8,128)(2,1)}), bf16[32,96,192]{2,1,0:T(8,128)(2,1)S(1)}, u32[]{:S(2)}, u32[]{:S(2)}) %all-to-all-start.1) | async-done | bytes 1179680 | tf_op jit(solution)/shard_map/all_to_all | solution.py:65
  130.3 0.3 convert_reduce_fusion
  130.6 0.3 fusion.59
  130.9 0.9 fusion.34
  (4 shorter events, 0.0 us)
Async XLA Ops:
  6.5 0.8 copy-start
  6.5 56.2 %all-gather.2.cloned.1.call-start = ((), (), s32[]{:S(2)}) async-start(), calls=%async_computation.2 | async-start | bytes 2506752 | tf_op jit(solution)/shard_map/all_gather | solution.py:41
  19.6 51.6 %slice-start = ((s8[6291456]{0:T(1024)(128)(4,1)}), s8[2097152]{0:T(1024)(128)(4,1)S(1)}, s32[]{:S(2)}) async-start(s8[6291456]{0:T(1024)(128)(4,1)} %bitcast.54), calls=%async_computation.3 | async-start | bytes 4194304
  62.8 5.0 %copy-start.1 = (bf16[1,1024,3072]{1,2,0:T(8,128)(2,1)S(1)}, bf16[1,1024,3072]{1,2,0:T(8,128)(2,1)}, u32[]{:S(2)}) copy-start(bf16[1,1024,3072]{1,2,0:T(8,128)(2,1)} %copy.12) | copy-start | bytes 18874372
  62.8 5.7 %copy-start.5 = (bf16[16,192,384]{2,1,0:T(8,128)(2,1)S(1)}, bf16[16,192,384]{2,1,0:T(8,128)(2,1)}, u32[]{:S(2)}) copy-start(bf16[16,192,384]{2,1,0:T(8,128)(2,1)} %all-gather.2.cloned.1.call-done) | copy-start | bytes 7077892
  62.8 6.1 %copy-start.6 = (s32[1,192,1024]{2,1,0:T(8,128)S(1)}, s32[1,192,1024]{2,1,0:T(8,128)}, u32[]{:S(2)}) copy-start(s32[1,192,1024]{2,1,0:T(8,128)} %param.15) | copy-start | bytes 2359300
  62.8 8.4 %slice-start.1 = ((s8[6291456]{0:T(1024)(128)(4,1)}), s8[4194304]{0:T(1024)(128)(4,1)S(1)}, s32[]{:S(2)}) async-start(s8[6291456]{0:T(1024)(128)(4,1)} %bitcast.54), calls=%async_computation.4 | async-start | bytes 8388608
  67.6 3.6 %copy-start.2 = (f32[192,1024]{1,0:T(8,128)}, f32[192,1024]{1,0:T(8,128)S(1)}, u32[]{:S(2)}) copy-start(f32[192,1024]{1,0:T(8,128)S(1)} %fusion.22) | copy-start | bytes 2359300
  71.2 3.7 %copy-start.3 = (f32[192,1024]{1,0:T(8,128)}, f32[192,1024]{1,0:T(8,128)S(1)}, u32[]{:S(2)}) copy-start(f32[192,1024]{1,0:T(8,128)S(1)} %fusion.31) | copy-start | bytes 2359300
  88.5 3.4 %copy-start.4 = (s32[2,96]{1,0:T(2,128)S(1)}, s32[2,96]{1,0:T(2,128)}, u32[]{:S(2)}) copy-start(s32[2,96]{1,0:T(2,128)} %param.13) | copy-start | bytes 2308
  88.5 41.8 %all-to-all-start.1 = ((bf16[32,96,192]{2,1,0:T(8,128)(2,1)}), bf16[32,96,192]{2,1,0:T(8,128)(2,1)S(1)}, u32[]{:S(2)}, u32[]{:S(2)}) async-start(bf16[32,96,192]{2,1,0:T(8,128)(2,1)} %bitcast.14), calls=%async_computation.1 | async-start | bytes 3145728 | tf_op jit(solution)/shard_map/all_to_all | solution.py:65
Sparse Core Ops, SparseCore 0:
  19.8 42.9 all-gather.1

commit v2 on v1

--- a/solution.py
+++ b/solution.py
@@ -55,6 +55,7 @@
     grad_pre = grad_hidden * keep_mask[0].astype(jnp.float32) * inv_keep
     grad_up = (grad_pre * activated).astype(jnp.bfloat16)
     grad_gate = pullback(grad_pre * up_pre)[0].astype(jnp.bfloat16)
+    grad_gate, grad_up = lax.optimization_barrier((grad_gate, grad_up))
 
     back_dims = (((1,), (1,)), ((), ()))
     partial = lax.dot_general(

time: 139 us -> 132 us (0.950)
  matrix products: 22.1 us -> 14.9 us
    dot_general x1, matrix products: 10.1 us -> 2.23 us  [body(): lax.dot_general(grad_gate, gate_mat, back_dims, preferred_element_type=jn...]
    dot_general x0 -> x1, matrix products: none -> 1.99 us  [body(): lax.dot_general(part_inputs, up_rows, fwd_dims, preferred_element_type=jn...]
    dot_general x1, matrix products: 3.71 us -> 2.21 us  [body(): lax.dot_general(grad_up, up_mat, back_dims, preferred_element_type=jnp.fl...]
  transfers between devices with their start and end apart: 2 -> 2, of which waited for: 2 -> 2; matrix products, arithmetic and copies ran while one was open for 6% -> 7% of each run, Pallas kernels for 0% -> 0%
where the time goes in v2:
time: 132 us; the launch traced here: 131 us
  waiting for transfers between devices  72.7 us (55%)
  local copies, waits for them, and re-layouts  16.9 us (13%)
  matrix products  14.9 us (11%)
  between operations  13.5 us (10%)
  blocking collectives  8.7 us (7%)
  starting transfers between devices  3.39 us (3%)
    all_to_all x1, waiting for transfers between devices, body(): lax.all_to_all(blocks, ('expert', 'hidden'), split_axis=0, concat_axis=0,...  38.3 us
    all_gather x1, waiting for transfers between devices, body(): gathered = lax.all_gather(slab_slots, 'hidden', axis=0, tiled=False)  34.3 us
    unnamed x19, local copies, waits for them, and re-layouts  9.89 us
    all_to_all x1, blocking collectives, body(): lax.all_to_all(slab, 'expert', split_axis=0, concat_axis=0, tiled=True)  8.7 us
    dot_general x1, matrix products, body(): lax.dot_general(part_inputs, gate_rows, fwd_dims, preferred_element_type=...  4.83 us
    convert_element_type x2, local copies, waits for them, and re-layouts, body(): blocks.astype(jnp.bfloat16)  3.48 us
    all_to_all x1, starting transfers between devices, body(): lax.all_to_all(blocks, ('expert', 'hidden'), split_axis=0, concat_axis=0,...  3.38 us
  transfers between devices with their start and end apart: 2, of which 2 were waited for; matrix products, arithmetic and copies ran while one was open for 7% of the time, Pallas kernels for 0%

profile of v2, /device:TPU:0, one launch (start us, length us, event | category | flops | bytes accessed | tf_op | source)
XLA Modules:
  0.0 131.2 jit_solution(3988856731334238211)
XLA Ops:
  6.5 0.0 copy-start
  6.5 0.0 all-gather.2.cloned.1.call-start
  6.5 0.8 reshape.57
  7.3 0.0 copy-done
  7.3 1.0 gather_fusion.1
  8.4 1.7 %gather_fusion = bf16[192,192]{1,0:T(8,128)(2,1)S(1)} fusion(bf16[96,192]{1,0:T(8,128)(2,1)} %param.8, s32[1024]{0:T(1024)S(1)} %pad_clamp_fusion), kind=kCustom, calls=%fused_computation | custom fusion | bytes 148224 | tf_op jit(solution)/shard_map/gather | solution.py:36
  10.0 0.8 fusion.44
  10.8 0.1 pad_maximum_fusion
  10.9 8.7 %all_to_all.10 = bf16[2,96,384]{2,1,0:T(8,128)(2,1)} all-to-all(bf16[2,96,384]{2,1,0:T(8,128)(2,1)S(1)} %pad_maximum_fusion), channel_id=1, replica_groups=mesh['expert'=2,'hidden'=16] {'expert'}, dimensions={0} | all-to-all | bytes 294912 | tf_op jit(solution)/shard_map/all_to_all | solution.py:39
  19.6 0.0 all-gather.2.cloned.1.call-update
  19.6 0.0 slice-start
  19.6 8.8 %copy.12 = bf16[1,1024,3072]{1,2,0:T(8,128)(2,1)} copy(bf16[1,1024,3072]{2,1,0:T(8,128)(2,1)} %param.12) | data formatting | bytes 12582912 | tf_op args[4]
  28.4 34.3 %all-gather.2.cloned.1.call-done = bf16[16,192,384]{2,1,0:T(8,128)(2,1)} async-done(((bf16[1,192,384]{2,1,0:T(8,128)(2,1)}), bf16[16,192,384]{2,1,0:T(8,128)(2,1)}) %all-gather.2.cloned.1.call-update) | async-done | bytes 2359312 | tf_op jit(solution)/shard_map/all_gather | solution.py:41
  62.8 0.0 copy-start.1
  62.8 0.0 copy-start.3
  62.8 0.0 copy-start.4
  62.8 0.0 slice-start.1
  62.8 4.8 %fusion.22 = f32[192,1024]{1,0:T(8,128)S(1)} fusion(bf16[16,192,1024]{2,1,0:T(8,128)(2,1)} %bitcast.56, bf16[16,192,384]{2,1,0:T(8,128)(2,1)} %all-gather.2.cloned.1.call-done), kind=kOutput, calls=%fused_computation.17 | convolution fusion | flops 1207959552 | bytes 8650752 | tf_op jit(solution)/shard_map/dot_general | solution.py:49
  67.6 0.2 copy-done.1
  67.8 0.7 copy-done.3
  68.5 0.1 copy-done.4
  68.7 0.0 slice-start.2
  68.7 2.4 %multiply_convert_fusion = (bf16[192,1024]{1,0:T(8,128)(2,1)S(1)}, f32[192,1024]{1,0:T(8,128)S(1)}) fusion(f32[192,1024]{1,0:T(8,128)S(1)} %fusion.22, s32[1,192,1024]{2,1,0:T(8,128)S(1)} %copy-done.4, bf16[1024,16,192]{0,2,1:T(8,128)(2,1)S(1)} %bitcast.59, bf16[16,192,384]{2,1,0:T(8,128)(2,1)S(1)} %copy-done.3), kind=kOutput, calls=%fused_computation.32 | convolution fusion | flops 1210515456 | bytes 10616832 | tf_op jit(solution)/shard_map/dot_general | solution.py:51
  71.1 0.0 slice-done
  71.1 0.0 slice-done.1
  71.1 0.0 slice-start.3
  71.1 2.0 %fusion.41 = bf16[192,1024]{1,0:T(8,128)(2,1)S(1)} fusion(f32[192,1024]{1,0:T(8,128)S(1)} %fusion.22, f32[192,1024]{1,0:T(8,128)S(1)} %get-tuple-element.12, bf16[16,192,1024]{2,1,0:T(8,128)(2,1)S(1)} %bitcast.55, bf16[16,192,384]{2,1,0:T(8,128)(2,1)S(1)} %copy-done.3), kind=kOutput, calls=%fused_computation.31 | convolution fusion | flops 1212088320 | bytes 9830400 | tf_op jit(solution)/shard_map/dot_general | solution.py:50
  73.1 2.2 %fusion = f32[192,3072]{1,0:T(8,128)S(1)} fusion(bf16[192,1024]{1,0:T(8,128)(2,1)S(1)} %get-tuple-element.8, bf16[1,3072,1024]{2,1,0:T(8,128)(2,1)S(1)} %bitcast.54), kind=kOutput, calls=%fused_computation.2 | convolution fusion | flops 1207959552 | bytes 9043968 | tf_op jit(solution)/shard_map/dot_general | solution.py:63
  75.4 0.0 slice-done.2
  75.4 0.0 slice-done.3
  75.4 2.2 %fusion.7 = bf16[192,3072]{1,0:T(8,128)(2,1)S(1)} fusion(f32[192,3072]{1,0:T(8,128)S(1)} %fusion, bf16[192,1024]{1,0:T(8,128)(2,1)S(1)} %fusion.41, bf16[1,3072,1024]{2,1,0:T(8,128)(2,1)S(1)} %bitcast.58), kind=kOutput, calls=%fused_computation.7 | convolution fusion | flops 1209139200 | bytes 10223616 | tf_op jit(solution)/shard_map/dot_general | solution.py:61
  77.6 1.7 %convert_element_type.59 = bf16[2,96,16,192]{3,2,1,0:T(8,128)(2,1)S(1)} reshape(bf16[192,3072]{1,0:T(8,128)(2,1)S(1)} %fusion.7) | data formatting | bytes 2359296 | tf_op jit(solution)/shard_map/convert_element_type | solution.py:65
  79.4 1.7 %copy.13 = bf16[2,96,16,192]{3,1,2,0:T(8,128)(2,1)} copy(bf16[2,96,16,192]{3,2,1,0:T(8,128)(2,1)S(1)} %convert_element_type.59) | data formatting | bytes 2359296 | tf_op jit(solution)/shard_map/convert_element_type | solution.py:65
  81.1 0.0 copy-start.2
  81.1 3.4 %all-to-all-start.1 = ((bf16[32,96,192]{2,1,0:T(8,128)(2,1)}), bf16[32,96,192]{2,1,0:T(8,128)(2,1)S(1)}, u32[]{:S(2)}, u32[]{:S(2)}) async-start(bf16[32,96,192]{2,1,0:T(8,128)(2,1)} %bitcast.14), calls=%async_computation.1 | async-start | bytes 3145728 | tf_op jit(solution)/shard_map/all_to_all | solution.py:66
  84.5 0.0 copy-done.2
  84.5 0.1 eq.15
  84.6 38.3 %all-to-all-done.1 = bf16[32,96,192]{2,1,0:T(8,128)(2,1)S(1)} async-done(((bf16[32,96,192]{2,1,0:T(8,128)(2,1)}), bf16[32,96,192]{2,1,0:T(8,128)(2,1)S(1)}, u32[]{:S(2)}, u32[]{:S(2)}) %all-to-all-start.1) | async-done | bytes 1179680 | tf_op jit(solution)/shard_map/all_to_all | solution.py:66
  122.9 0.3 convert_reduce_fusion
  123.2 0.3 fusion.46
  123.5 0.9 fusion.34
  (5 shorter events, 0.0 us)
Async XLA Ops:
  6.5 0.8 copy-start
  6.5 56.2 %all-gather.2.cloned.1.call-start = ((), (), s32[]{:S(2)}) async-start(), calls=%async_computation.2 | async-start | bytes 2506752 | tf_op jit(solution)/shard_map/all_gather | solution.py:41
  19.6 51.5 %slice-start = ((s8[6291456]{0:T(1024)(128)(4,1)}), s8[2097152]{0:T(1024)(128)(4,1)S(1)}, s32[]{:S(2)}) async-start(s8[6291456]{0:T(1024)(128)(4,1)} %bitcast.53), calls=%async_computation.3 | async-start | bytes 4194304
  62.8 5.0 %copy-start.1 = (bf16[1,1024,3072]{1,2,0:T(8,128)(2,1)S(1)}, bf16[1,1024,3072]{1,2,0:T(8,128)(2,1)}, u32[]{:S(2)}) copy-start(bf16[1,1024,3072]{1,2,0:T(8,128)(2,1)} %copy.12) | copy-start | bytes 18874372
  62.8 5.7 %copy-start.3 = (bf16[16,192,384]{2,1,0:T(8,128)(2,1)S(1)}, bf16[16,192,384]{2,1,0:T(8,128)(2,1)}, u32[]{:S(2)}) copy-start(bf16[16,192,384]{2,1,0:T(8,128)(2,1)} %all-gather.2.cloned.1.call-done) | copy-start | bytes 7077892
  62.8 5.9 %copy-start.4 = (s32[1,192,1024]{2,1,0:T(8,128)S(1)}, s32[1,192,1024]{2,1,0:T(8,128)}, u32[]{:S(2)}) copy-start(s32[1,192,1024]{2,1,0:T(8,128)} %param.15) | copy-start | bytes 2359300
  62.8 8.3 %slice-start.1 = ((s8[6291456]{0:T(1024)(128)(4,1)}), s8[4194304]{0:T(1024)(128)(4,1)S(1)}, s32[]{:S(2)}) async-start(s8[6291456]{0:T(1024)(128)(4,1)} %bitcast.53), calls=%async_computation.4 | async-start | bytes 8388608
  68.7 6.7 %slice-start.2 = ((s8[6291456]{0:T(1024)(128)(4,1)}), s8[4194304]{0:T(1024)(128)(4,1)S(1)}, s32[]{:S(2)}) async-start(s8[6291456]{0:T(1024)(128)(4,1)} %bitcast.57), calls=%async_computation.5 | async-start | bytes 8388608
  71.1 4.2 %slice-start.3 = ((s8[6291456]{0:T(1024)(128)(4,1)}), s8[2097152]{0:T(1024)(128)(4,1)S(1)}, s32[]{:S(2)}) async-start(s8[6291456]{0:T(1024)(128)(4,1)} %bitcast.57), calls=%async_computation.6 | async-start | bytes 4194304
  81.1 3.4 %copy-start.2 = (s32[2,96]{1,0:T(2,128)S(1)}, s32[2,96]{1,0:T(2,128)}, u32[]{:S(2)}) copy-start(s32[2,96]{1,0:T(2,128)} %param.13) | copy-start | bytes 2308
  81.1 41.8 %all-to-all-start.1 = ((bf16[32,96,192]{2,1,0:T(8,128)(2,1)}), bf16[32,96,192]{2,1,0:T(8,128)(2,1)S(1)}, u32[]{:S(2)}, u32[]{:S(2)}) async-start(bf16[32,96,192]{2,1,0:T(8,128)(2,1)} %bitcast.14), calls=%async_computation.1 | async-start | bytes 3145728 | tf_op jit(solution)/shard_map/all_to_all | solution.py:66
Sparse Core Ops, SparseCore 0:
  19.8 42.9 all-gather.1

commit v3 on v2

v3 whole, which is shorter than its diff:
```python
import jax
import jax.numpy as jnp
from jax import lax
from jax.sharding import Mesh
from jax.sharding import PartitionSpec as P

keep_rate = 0.9
CROSS = ("expert", "chip")
HIDDEN = ("chip", "core")


def gelu_tanh(values):
    return jax.nn.gelu(values, approximate=True)


def fold_slots(one_hot, slot_values):
    high_part = slot_values.astype(jnp.bfloat16)
    low_part = (slot_values - high_part.astype(jnp.float32)).astype(jnp.bfloat16)
    dims = (((0,), (0,)), ((), ()))
    return lax.dot_general(one_hot, high_part, dims, preferred_element_type=jnp.float32) + lax.dot_general(
        one_hot, low_part, dims, preferred_element_type=jnp.float32
    )


def order_by_core(own, other, axis):
    first = lax.axis_index("core") == 0
    low = jnp.where(first, own, other)
    high = jnp.where(first, other, own)
    return jnp.stack([low, high], axis=axis)


def swap_cores(values):
    return lax.ppermute(values, "core", [(0, 1), (1, 0)])


def body(tokens, cotangent, w_gate, w_up, w_down, slot_token, slot_weight, keep_mask):
    gate_mat = w_gate[0]
    up_mat = w_up[0]
    down_mat = w_down[0]
    model_width, local_ff = gate_mat.shape
    chip_count = lax.axis_size("chip")
    expert_count = lax.axis_size("expert")
    expert_total, per_source = slot_token.shape
    slot_count = expert_count * per_source
    group_tokens, local_width = tokens.shape
    slot_list = slot_token.reshape(-1)
    weight_column = slot_weight.reshape(-1, 1)
    inv_keep = 1.0 / keep_rate

    chosen = tokens[slot_list]
    scaled = (weight_column * cotangent[slot_list].astype(jnp.float32)).astype(jnp.bfloat16)
    slab = jnp.concatenate([chosen, scaled], axis=1).reshape(expert_total, 1, per_source, 2 * local_width)
    outgoing = jnp.broadcast_to(slab, (expert_total, chip_count, per_source, 2 * local_width))
    outgoing = outgoing.reshape(expert_total * chip_count, per_source, 2 * local_width)
    own = lax.all_to_all(outgoing, CROSS, split_axis=0, concat_axis=0, tiled=True)
    own = own.reshape(expert_count, chip_count, per_source, 2 * local_width)
    other = swap_cores(own)
    full = order_by_core(own, other, axis=2)
    part_inputs = full[..., :local_width]
    part_cot = full[..., local_width:]

    gate_rows = gate_mat.reshape(chip_count, 2, local_width, local_ff)
    up_rows = up_mat.reshape(chip_count, 2, local_width, local_ff)
    down_cols = down_mat.reshape(local_ff, chip_count, 2, local_width)
    fwd_dims = (((1, 2, 4), (0, 1, 2)), ((), ()))
    gate_pre = lax.dot_general(part_inputs, gate_rows, fwd_dims, preferred_element_type=jnp.float32)
    up_pre = lax.dot_general(part_inputs, up_rows, fwd_dims, preferred_element_type=jnp.float32)
    grad_hidden = lax.dot_general(
        part_cot, down_cols, (((1, 2, 4), (1, 2, 3)), ((), ())), preferred_element_type=jnp.float32
    )
    gate_pre = gate_pre.reshape(slot_count, local_ff)
    up_pre = up_pre.reshape(slot_count, local_ff)
    grad_hidden = grad_hidden.reshape(slot_count, local_ff)
    activated, pullback = jax.vjp(gelu_tanh, gate_pre)
    grad_pre = grad_hidden * keep_mask[0].astype(jnp.float32) * inv_keep
    grad_up = (grad_pre * activated).astype(jnp.bfloat16)
    grad_gate = pullback(grad_pre * up_pre)[0].astype(jnp.bfloat16)
    grad_gate, grad_up = lax.optimization_barrier((grad_gate, grad_up))

    back_dims = (((1,), (1,)), ((), ()))
    partial = lax.dot_general(
        grad_gate, gate_mat, back_dims, preferred_element_type=jnp.float32
    ) + lax.dot_general(grad_up, up_mat, back_dims, preferred_element_type=jnp.float32)
    partial = partial.reshape(expert_count, per_source, chip_count, 2, local_width)
    first = lax.axis_index("core") == 0
    keep_half = jnp.where(first, partial[:, :, :, 0], partial[:, :, :, 1])
    send_half = jnp.where(first, partial[:, :, :, 1], partial[:, :, :, 0]).astype(jnp.bfloat16)
    chip_sum = keep_half + swap_cores(send_half).astype(jnp.float32)
    blocks = chip_sum.astype(jnp.bfloat16).transpose(0, 2, 1, 3)
    blocks = blocks.reshape(expert_count * chip_count, per_source, local_width)
    returned = lax.all_to_all(blocks, CROSS, split_axis=0, concat_axis=0, tiled=True)
    per_expert = returned.reshape(expert_total, chip_count, per_source, local_width).astype(jnp.float32).sum(1)
    one_hot = (slot_list[:, None] == jnp.arange(group_tokens, dtype=jnp.int32)[None, :]).astype(jnp.bfloat16)
    token_sum = fold_slots(one_hot, per_expert.reshape(expert_total * per_source, local_width))
    return token_sum.astype(jnp.bfloat16)


def solution(mesh):
    expert_count, hidden_count = mesh.devices.shape
    split_mesh = Mesh(mesh.devices.reshape(expert_count, hidden_count // 2, 2), ("expert", "chip", "core"))
    in_specs = (
        P("expert", HIDDEN),
        P("expert", HIDDEN),
        P("expert", None, HIDDEN),
        P("expert", None, HIDDEN),
        P("expert", HIDDEN, None),
        P(None, "expert"),
        P(None, "expert"),
        P("expert", None, HIDDEN),
    )
    out_specs = P("expert", HIDDEN)
    return jax.shard_map(body, mesh=split_mesh, in_specs=in_specs, out_specs=out_specs, check_vma=False)
```

time: 132 us -> 104 us (0.79)
  waiting for transfers between devices: 72.7 us -> 23.4 us
  blocking collectives: 8.7 us -> 38.1 us
  between operations: 13.5 us -> 0.19 us
  local copies, waits for them, and re-layouts: 16.9 us -> 23.2 us
  matrix products: 14.9 us -> 12.1 us
    all_gather x1 -> x0, waiting for transfers between devices: 34.3 us -> none  [body(): gathered = lax.all_gather(slab_slots, 'hidden', axis=0, tiled=False)]
    all_to_all x1, blocking collectives: 8.7 us -> 38.1 us  [body(): lax.all_to_all(outgoing, CROSS, split_axis=0, concat_axis=0, tiled=True)]
    all_to_all x1, waiting for transfers between devices: 38.3 us -> 21.5 us  [body(): lax.all_to_all(blocks, CROSS, split_axis=0, concat_axis=0, tiled=True)]
    reshape x0 -> x1, local copies, waits for them, and re-layouts: none -> 4.81 us  [body(): partial.reshape(expert_count, per_source, chip_count, 2, local_width)]
    convert_element_type x2 -> x0, local copies, waits for them, and re-layouts: 3.48 us -> none  [body(): blocks.astype(jnp.bfloat16)]
    dot_general x1, matrix products: 4.83 us -> 1.45 us  [body(): lax.dot_general(part_inputs, gate_rows, fwd_dims, preferred_element_type=...]
    slice x0 -> x1, local copies, waits for them, and re-layouts: none -> 2.43 us  [body(): keep_half = jnp.where(first, partial[:, :, :, 0], partial[:, :, :, 1])]
    ppermute x0 -> x2, waiting for transfers between devices: none -> 1.91 us  [swap_cores(): return lax.ppermute(values, 'core', [(0, 1), (1, 0)])]
  transfers between devices with their start and end apart: 2 -> 3, of which waited for: 2 -> 2; matrix products, arithmetic and copies ran while one was open for 7% -> 8% of each run, Pallas kernels for 0% -> 0%
where the time goes in v3:
time: 104 us; the launch traced here: 103 us
  blocking collectives  38.1 us (37%)
  waiting for transfers between devices  23.4 us (22%)
  local copies, waits for them, and re-layouts  23.2 us (22%)
  matrix products  12.1 us (12%)
  starting transfers between devices  4.19 us (4%)
  other arithmetic  1.99 us (2%)
    all_to_all x1, blocking collectives, body(): lax.all_to_all(outgoing, CROSS, split_axis=0, concat_axis=0, tiled=True)  38.1 us
    all_to_all x1, waiting for transfers between devices, body(): lax.all_to_all(blocks, CROSS, split_axis=0, concat_axis=0, tiled=True)  21.5 us
    unnamed x21, local copies, waits for them, and re-layouts  11 us
    reshape x1, local copies, waits for them, and re-layouts, body(): partial.reshape(expert_count, per_source, chip_count, 2, local_width)  4.81 us
    dot_general x1, matrix products, body(): lax.dot_general(grad_gate, gate_mat, back_dims, preferred_element_type=jn...  3.67 us
    all_to_all x1, starting transfers between devices, body(): lax.all_to_all(blocks, CROSS, split_axis=0, concat_axis=0, tiled=True)  3.61 us
    slice x1, local copies, waits for them, and re-layouts, body(): keep_half = jnp.where(first, partial[:, :, :, 0], partial[:, :, :, 1])  2.43 us
    dot_general x1, matrix products, body(): lax.dot_general(grad_up, up_mat, back_dims, preferred_element_type=jnp.fl...  2.2 us
  transfers between devices with their start and end apart: 3, of which 2 were waited for; matrix products, arithmetic and copies ran while one was open for 8% of the time, Pallas kernels for 0%

profile of v3, /device:TPU:0, one launch (start us, length us, event | category | flops | bytes accessed | tf_op | source)
XLA Modules:
  0.0 103.2 jit_solution(3256341461267227192)
XLA Ops:
  0.0 0.0 copy-start
  0.0 0.0 copy-start.2
  0.0 0.8 reshape.90
  0.8 0.0 copy-done
  0.8 1.0 gather_fusion.1
  1.8 1.7 %gather_fusion = bf16[192,192]{1,0:T(8,128)(2,1)S(1)} fusion(bf16[96,192]{1,0:T(8,128)(2,1)} %param.8, s32[1024]{0:T(1024)S(1)} %pad_clamp_fusion), kind=kCustom, calls=%fused_computation | custom fusion | bytes 148224 | tf_op jit(solution)/shard_map/gather | solution.py:50
  3.5 0.0 copy-done.2
  3.5 0.1 fusion.24
  3.6 0.1 maximum_bitcast_fusion
  3.7 0.1 broadcast_in_dim.5
  3.8 38.1 %all_to_all.10 = bf16[16,96,384]{2,1,0:T(8,128)(2,1)S(1)} all-to-all(bf16[16,96,384]{2,1,0:T(8,128)(2,1)S(1)} %bitcast.92), channel_id=1, replica_groups=mesh['expert'=2,'chip'=8,'core'=2] {'expert','chip'}, dimensions={0} | all-to-all | bytes 2359296 | tf_op jit(solution)/shard_map/all_to_all | solution.py:55
  41.9 0.0 collective-permute-start
  41.9 8.6 %copy.16 = bf16[1,1024,3072]{1,2,0:T(8,128)(2,1)} copy(bf16[1,1024,3072]{2,1,0:T(8,128)(2,1)} %param.12) | data formatting | bytes 12582912 | tf_op args[4]
  50.5 0.0 collective-permute-done
  50.5 0.0 slice-start.4
  50.5 0.2 select_bitcast_fusion.1
  50.8 0.0 slice-start.5
  50.8 0.9 fusion.8
  51.6 0.0 slice-start.2
  51.7 0.1 copy.17
  51.8 0.1 copy.15
  51.9 0.8 slice-done.4
  52.7 0.7 slice-done.5
  53.5 1.5 %convolution_bitcast_fusion = f32[192,1024]{1,0:T(8,128)S(1)} fusion(bf16[192,8,2,192]{3,0,2,1:T(8,128)(2,1)S(1)} %bitcast.93, bf16[8,2,192,1024]{3,2,1,0:T(8,128)(2,1)S(1)} %bitcast.89), kind=kOutput, calls=%fused_computation.17 | convolution fusion | flops 1207959552 | bytes 8257536 | tf_op jit(solution)/shard_map/dot_general | solution.py:66
  54.9 0.0 slice-done.2
  54.9 0.5 slice-done.3
  55.4 0.1 copy-done.3
  55.5 1.7 %multiply_convert_fusion = (bf16[192,1024]{1,0:T(8,128)(2,1)S(1)}, f32[192,1024]{1,0:T(8,128)S(1)}) fusion(f32[192,1024]{1,0:T(8,128)S(1)} %convolution_bitcast_fusion, s32[1,192,1024]{2,1,0:T(8,128)S(1)} %copy-done.3, bf16[192,8,2,192]{3,0,2,1:T(8,128)(2,1)S(1)} %bitcast.95, bf16[1024,8,2,192]{0,3,2,1:T(8,128)(2,1)S(1)} %bitcast.86), kind=kOutput, calls=%fused_computation.38 | convolution fusion | flops 1210515456 | bytes 10223616 | tf_op jit(solution)/shard_map/dot_general | solution.py:68
  57.2 0.0 slice-done
  57.3 0.2 slice-done.1
  57.4 1.9 %fusion.21 = bf16[192,1024]{1,0:T(8,128)(2,1)S(1)} fusion(f32[192,1024]{1,0:T(8,128)S(1)} %convolution_bitcast_fusion, f32[192,1024]{1,0:T(8,128)S(1)} %get-tuple-element.18, bf16[192,8,2,192]{3,0,2,1:T(8,128)(2,1)S(1)} %bitcast.94, bf16[8,2,192,1024]{3,2,1,0:T(8,128)(2,1)S(1)} %bitcast.83), kind=kOutput, calls=%fused_computation.35 | convolution fusion | flops 1212088320 | bytes 9437184 | tf_op jit(solution)/shard_map/dot_general | solution.py:67
  59.4 2.2 %fusion = f32[192,3072]{1,0:T(8,128)S(1)} fusion(bf16[192,1024]{1,0:T(8,128)(2,1)S(1)} %get-tuple-element.8, bf16[1,3072,1024]{2,1,0:T(8,128)(2,1)S(1)} %bitcast.82), kind=kOutput, calls=%fused_computation.2 | convolution fusion | flops 1207959552 | bytes 9043968 | tf_op jit(solution)/shard_map/dot_general | solution.py:83
  61.6 3.7 %fusion.4 = f32[192,3072]{1,0:T(8,128)} fusion(f32[192,3072]{1,0:T(8,128)S(1)} %fusion, bf16[192,1024]{1,0:T(8,128)(2,1)S(1)} %fusion.21, bf16[1,3072,1024]{2,1,0:T(8,128)(2,1)S(1)} %bitcast.88), kind=kOutput, calls=%fused_computation.6 | convolution fusion | flops 1208549376 | bytes 11403264 | tf_op jit(solution)/shard_map/dot_general | solution.py:81
  65.2 4.8 %reshape.93 = f32[2,96,8,2,192]{4,3,2,1,0:T(2,128)S(1)} reshape(f32[192,3072]{1,0:T(8,128)} %fusion.4) | data formatting | bytes 4718592 | tf_op jit(solution)/shard_map/reshape | solution.py:84
  70.0 2.4 %fusion.29 = (f32[2,96,8,1,192]{4,3,2,1,0:T(1,128)S(1)}, f32[2,96,8,1,192]{4,3,2,1,0:T(1,128)S(1)}) fusion(f32[2,96,8,2,192]{4,3,2,1,0:T(2,128)S(1)} %reshape.93), kind=kLoop, calls=%fused_computation.51 | loop fusion | bytes 4718592 | tf_op jit(solution)/shard_map/slice | solution.py:86
  72.5 0.2 fusion.22
  72.7 0.6 collective-permute-start.1
  73.2 1.9 %collective-permute-done.1 = bf16[2,96,8,192]{3,2,1,0:T(8,128)(2,1)S(1)} collective-permute-done((bf16[2,96,8,192]{3,2,1,0:T(8,128)(2,1)S(1)}, bf16[2,96,8,192]{3,2,1,0:T(8,128)(2,1)S(1)}, u32[]{:S(2)}, u32[]{:S(2)}) %collective-permute-start.1) | collective-permute-done | bytes 589856 | tf_op jit(solution)/shard_map/ppermute | solution.py:33
  75.2 0.4 fusion.23
  75.5 0.0 copy-start.1
  75.6 1.1 %copy.20 = bf16[2,8,96,192]{3,2,1,0:T(8,128)(2,1)} copy(bf16[2,8,96,192]{3,1,2,0:T(8,128)(2,1)S(1)} %fusion.23) | data formatting | bytes 1179648 | tf_op jit(solution)/shard_map/transpose | solution.py:89
  76.6 3.6 %all-to-all-start.1 = ((bf16[16,96,192]{2,1,0:T(8,128)(2,1)}), bf16[16,96,192]{2,1,0:T(8,128)(2,1)S(1)}, u32[]{:S(2)}, u32[]{:S(2)}) async-start(bf16[16,96,192]{2,1,0:T(8,128)(2,1)} %bitcast.28), calls=%async_computation.1 | async-start | bytes 1572864 | tf_op jit(solution)/shard_map/all_to_all | solution.py:91
  80.2 0.0 copy-done.1
  80.3 0.1 eq.19
  80.3 21.5 %all-to-all-done.1 = bf16[16,96,192]{2,1,0:T(8,128)(2,1)S(1)} async-done(((bf16[16,96,192]{2,1,0:T(8,128)(2,1)}), bf16[16,96,192]{2,1,0:T(8,128)(2,1)S(1)}, u32[]{:S(2)}, u32[]{:S(2)}) %all-to-all-start.1) | async-done | bytes 589856 | tf_op jit(solution)/shard_map/all_to_all | solution.py:91
  101.8 0.1 convert_reduce_fusion
  102.0 0.3 fusion.26
  102.3 0.9 fusion.14
  (10 shorter events, 0.0 us)
Async XLA Ops:
  0.0 0.8 copy-start
  0.0 3.5 %copy-start.2 = (f32[2,96]{1,0:T(2,128)S(1)}, f32[2,96]{1,0:T(2,128)}, u32[]{:S(2)}) copy-start(f32[2,96]{1,0:T(2,128)} %param.14) | copy-start | bytes 2308
  41.9 8.6 %collective-permute-start = (bf16[2,8,96,384]{3,2,1,0:T(8,128)(2,1)S(1)}, bf16[2,8,96,384]{3,2,1,0:T(8,128)(2,1)S(1)}, u32[]{:S(2)}, u32[]{:S(2)}) collective-permute-start(bf16[2,8,96,384]{3,2,1,0:T(8,128)(2,1)S(1)} %bitcast.90), channel_id=1, source_target_pairs={{0,1},{1,0},{2,3},{3,2},{4,5},{5,4},{6,7},{7,6},{8,9},{9,8},{10,11... | collective-permute-start | bytes 3538952 | tf_op jit(solution)/shard_map/ppermute | solution.py:33
  50.5 2.2 %slice-start.4 = ((s8[6291456]{0:T(1024)(128)(4,1)}), s8[4194304]{0:T(1024)(128)(4,1)S(1)}, s32[]{:S(2)}) async-start(s8[6291456]{0:T(1024)(128)(4,1)} %bitcast.87), calls=%async_computation.6 | async-start | bytes 8388608
  50.8 2.7 %slice-start.5 = ((s8[6291456]{0:T(1024)(128)(4,1)}), s8[2097152]{0:T(1024)(128)(4,1)S(1)}, s32[]{:S(2)}) async-start(s8[6291456]{0:T(1024)(128)(4,1)} %bitcast.87), calls=%async_computation.7 | async-start | bytes 4194304
  51.6 3.3 %slice-start.2 = ((s8[6291456]{0:T(1024)(128)(4,1)}), s8[4194304]{0:T(1024)(128)(4,1)S(1)}, s32[]{:S(2)}) async-start(s8[6291456]{0:T(1024)(128)(4,1)} %bitcast.84), calls=%async_computation.4 | async-start | bytes 8388608
  53.5 1.9 %slice-start.3 = ((s8[6291456]{0:T(1024)(128)(4,1)}), s8[2097152]{0:T(1024)(128)(4,1)S(1)}, s32[]{:S(2)}) async-start(s8[6291456]{0:T(1024)(128)(4,1)} %bitcast.84), calls=%async_computation.5 | async-start | bytes 4194304
  53.5 2.1 %copy-start.3 = (s32[1,192,1024]{2,1,0:T(8,128)S(1)}, s32[1,192,1024]{2,1,0:T(8,128)}, u32[]{:S(2)}) copy-start(s32[1,192,1024]{2,1,0:T(8,128)} %param.15) | copy-start | bytes 2359300
  53.5 3.8 %slice-start = ((s8[6291456]{0:T(1024)(128)(4,1)}), s8[4194304]{0:T(1024)(128)(4,1)S(1)}, s32[]{:S(2)}) async-start(s8[6291456]{0:T(1024)(128)(4,1)} %bitcast.81), calls=%async_computation.2 | async-start | bytes 8388608
  55.5 1.9 %slice-start.1 = ((s8[6291456]{0:T(1024)(128)(4,1)}), s8[2097152]{0:T(1024)(128)(4,1)S(1)}, s32[]{:S(2)}) async-start(s8[6291456]{0:T(1024)(128)(4,1)} %bitcast.81), calls=%async_computation.3 | async-start | bytes 4194304
  72.7 2.5 %collective-permute-start.1 = (bf16[2,96,8,192]{3,2,1,0:T(8,128)(2,1)S(1)}, bf16[2,96,8,192]{3,2,1,0:T(8,128)(2,1)S(1)}, u32[]{:S(2)}, u32[]{:S(2)}) collective-permute-start(bf16[2,96,8,192]{3,2,1,0:T(8,128)(2,1)S(1)} %fusion.22), channel_id=1, source_target_pairs={{0,1},{1,0},{2,3},{3,2},{4,5},{5,4},{6,7},{7,6},{8,9},{9,8},{10,11... | collective-permute-start | bytes 1769480 | tf_op jit(solution)/shard_map/ppermute | solution.py:33
  75.5 4.7 %copy-start.1 = (s32[2,96]{1,0:T(2,128)S(1)}, s32[2,96]{1,0:T(2,128)}, u32[]{:S(2)}) copy-start(s32[2,96]{1,0:T(2,128)} %param.13) | copy-start | bytes 2308
  76.6 25.2 %all-to-all-start.1 = ((bf16[16,96,192]{2,1,0:T(8,128)(2,1)}), bf16[16,96,192]{2,1,0:T(8,128)(2,1)S(1)}, u32[]{:S(2)}, u32[]{:S(2)}) async-start(bf16[16,96,192]{2,1,0:T(8,128)(2,1)} %bitcast.28), calls=%async_computation.1 | async-start | bytes 1572864 | tf_op jit(solution)/shard_map/all_to_all | solution.py:91

commit v4 on v3

--- a/solution.py
+++ b/solution.py
@@ -57,20 +57,17 @@
     other = swap_cores(own)
     full = order_by_core(own, other, axis=2)
     part_inputs = full[..., :local_width]
-    part_cot = full[..., local_width:]
+    cot_t = full[..., local_width:].transpose(1, 2, 4, 0, 3).reshape(model_width, slot_count)
 
     gate_rows = gate_mat.reshape(chip_count, 2, local_width, local_ff)
     up_rows = up_mat.reshape(chip_count, 2, local_width, local_ff)
-    down_cols = down_mat.reshape(local_ff, chip_count, 2, local_width)
     fwd_dims = (((1, 2, 4), (0, 1, 2)), ((), ()))
     gate_pre = lax.dot_general(part_inputs, gate_rows, fwd_dims, preferred_element_type=jnp.float32)
     up_pre = lax.dot_general(part_inputs, up_rows, fwd_dims, preferred_element_type=jnp.float32)
-    grad_hidden = lax.dot_general(
-        part_cot, down_cols, (((1, 2, 4), (1, 2, 3)), ((), ())), preferred_element_type=jnp.float32
-    )
+    hidden_t = jnp.dot(down_mat, cot_t, preferred_element_type=jnp.float32)
     gate_pre = gate_pre.reshape(slot_count, local_ff)
     up_pre = up_pre.reshape(slot_count, local_ff)
-    grad_hidden = grad_hidden.reshape(slot_count, local_ff)
+    grad_hidden = hidden_t.reshape(local_ff, slot_count).T
     activated, pullback = jax.vjp(gelu_tanh, gate_pre)
     grad_pre = grad_hidden * keep_mask[0].astype(jnp.float32) * inv_keep
     grad_up = (grad_pre * activated).astype(jnp.bfloat16)
@@ -79,19 +76,20 @@
 
     back_dims = (((1,), (1,)), ((), ()))
     partial = lax.dot_general(
-        grad_gate, gate_mat, back_dims, preferred_element_type=jnp.float32
-    ) + lax.dot_general(grad_up, up_mat, back_dims, preferred_element_type=jnp.float32)
-    partial = partial.reshape(expert_count, per_source, chip_count, 2, local_width)
+        gate_mat, grad_gate, back_dims, preferred_element_type=jnp.float32
+    ) + lax.dot_general(up_mat, grad_up, back_dims, preferred_element_type=jnp.float32)
+    partial = partial.reshape(chip_count, 2, local_width, slot_count)
     first = lax.axis_index("core") == 0
-    keep_half = jnp.where(first, partial[:, :, :, 0], partial[:, :, :, 1])
-    send_half = jnp.where(first, partial[:, :, :, 1], partial[:, :, :, 0]).astype(jnp.bfloat16)
+    keep_half = jnp.where(first, partial[:, 0], partial[:, 1])
+    send_half = jnp.where(first, partial[:, 1], partial[:, 0]).astype(jnp.bfloat16)
     chip_sum = keep_half + swap_cores(send_half).astype(jnp.float32)
-    blocks = chip_sum.astype(jnp.bfloat16).transpose(0, 2, 1, 3)
-    blocks = blocks.reshape(expert_count * chip_count, per_source, local_width)
+    blocks = chip_sum.astype(jnp.bfloat16).reshape(chip_count, local_width, expert_count, per_source)
+    blocks = blocks.transpose(2, 0, 1, 3).reshape(expert_count * chip_count, local_width, per_source)
     returned = lax.all_to_all(blocks, CROSS, split_axis=0, concat_axis=0, tiled=True)
-    per_expert = returned.reshape(expert_total, chip_count, per_source, local_width).astype(jnp.float32).sum(1)
+    per_expert = returned.reshape(expert_total, chip_count, local_width, per_source).astype(jnp.float32).sum(1)
+    per_expert = per_expert.transpose(0, 2, 1).reshape(expert_total * per_source, local_width)
     one_hot = (slot_list[:, None] == jnp.arange(group_tokens, dtype=jnp.int32)[None, :]).astype(jnp.bfloat16)
-    token_sum = fold_slots(one_hot, per_expert.reshape(expert_total * per_source, local_width))
+    token_sum = fold_slots(one_hot, per_expert)
     return token_sum.astype(jnp.bfloat16)
 
 

time: 104 us -> 123 us (1.18)
  local copies, waits for them, and re-layouts: 23.2 us -> 32.8 us
  matrix products: 12.1 us -> 19.2 us
  waiting for transfers between devices: 23.4 us -> 25.8 us
    reshape x1 -> x4, local copies, waits for them, and re-layouts: 4.81 us -> 12.6 us  [the longest x1 4.85 us: body(): partial = partial.reshape(chip_count, 2, local_width, slot_count)]
    dot_general x3, matrix products: 7.58 us -> 11.2 us  [the longest x1 5.35 us: body(): hidden_t = jnp.dot(down_mat, cot_t, preferred_element_type=jnp.float32)]
    dot_general x1, matrix products: 1.45 us -> 4.83 us  [body(): lax.dot_general(part_inputs, gate_rows, fwd_dims, preferred_element_type=...]
    ppermute x2, waiting for transfers between devices: 1.91 us -> 5 us  [swap_cores(): return lax.ppermute(values, 'core', [(0, 1), (1, 0)])]
    unnamed x21 -> x20, local copies, waits for them, and re-layouts: 11 us -> 8.34 us
    transpose x1 -> x2, local copies, waits for them, and re-layouts: 1.06 us -> 2.87 us  [the longest x1 2.75 us: body(): full[..., local_width:].transpose(1, 2, 4, 0, 3)]
    slice x1, local copies, waits for them, and re-layouts: 2.43 us -> 4.07 us  [body(): keep_half = jnp.where(first, partial[:, 0], partial[:, 1])]
    convert_element_type x1 -> x2, other arithmetic: 0.17 us -> 1.54 us  [the longest x1 1.26 us: body(): chip_sum.astype(jnp.bfloat16)]
  transfers between devices with their start and end apart: 3 -> 3, of which waited for: 2 -> 3; matrix products, arithmetic and copies ran while one was open for 8% -> 0% of each run, Pallas kernels for 0% -> 0%
where the time goes in v4:
time: 123 us
  blocking collectives  38.1 us (31%)
  local copies, waits for them, and re-layouts  32.8 us (27%)
  waiting for transfers between devices  25.8 us (21%)
  matrix products  19.2 us (16%)
  starting transfers between devices  3.81 us (3%)
  other arithmetic  2.99 us (2%)
    all_to_all x1, blocking collectives, body(): lax.all_to_all(outgoing, CROSS, split_axis=0, concat_axis=0, tiled=True)  38.1 us
    all_to_all x1, waiting for transfers between devices, body(): lax.all_to_all(blocks, CROSS, split_axis=0, concat_axis=0, tiled=True)  20.8 us
    unnamed x20, local copies, waits for them, and re-layouts  8.34 us
    dot_general x1, matrix products, body(): hidden_t = jnp.dot(down_mat, cot_t, preferred_element_type=jnp.float32)  5.35 us
    ppermute x2, waiting for transfers between devices, swap_cores(): return lax.ppermute(values, 'core', [(0, 1), (1, 0)])  5 us
    reshape x1, local copies, waits for them, and re-layouts, body(): partial = partial.reshape(chip_count, 2, local_width, slot_count)  4.85 us
    dot_general x1, matrix products, body(): lax.dot_general(part_inputs, gate_rows, fwd_dims, preferred_element_type=...  4.83 us
    reshape x1, local copies, waits for them, and re-layouts, body(): full[..., local_width:].transpose(1, 2, 4, 0, 3)  4.33 us
  transfers between devices with their start and end apart: 3, of which 3 were waited for; matrix products, arithmetic and copies ran while one was open for 0% of the time, Pallas kernels for 0%

profile of v4, /device:TPU:0, one launch (start us, length us, event | category | flops | bytes accessed | tf_op | source)
XLA Modules:
  0.0 122.9 jit_solution(10168134561109364208)
XLA Ops:
  0.0 0.0 copy-start
  0.0 0.8 reshape.94
  0.8 0.0 copy-done
  0.8 1.0 gather_fusion.1
  1.8 1.7 %gather_fusion = bf16[192,192]{1,0:T(8,128)(2,1)S(1)} fusion(bf16[96,192]{1,0:T(8,128)(2,1)} %param.8, s32[1024]{0:T(1024)S(1)} %pad_clamp_fusion), kind=kCustom, calls=%fused_computation | custom fusion | bytes 148224 | tf_op jit(solution)/shard_map/gather | solution.py:50
  3.5 0.0 copy-done.3
  3.5 0.1 fusion.32
  3.6 0.1 maximum_bitcast_fusion
  3.7 0.1 broadcast_in_dim.5
  3.8 38.1 %all_to_all.10 = bf16[16,96,384]{2,1,0:T(8,128)(2,1)S(1)} all-to-all(bf16[16,96,384]{2,1,0:T(8,128)(2,1)S(1)} %bitcast.94), channel_id=1, replica_groups=mesh['expert'=2,'chip'=8,'core'=2] {'expert','chip'}, dimensions={0} | all-to-all | bytes 2359296 | tf_op jit(solution)/shard_map/all_to_all | solution.py:55
  41.9 0.0 collective-permute-start
  41.9 2.8 %collective-permute-done = bf16[2,8,96,384]{3,2,1,0:T(8,128)(2,1)S(1)} collective-permute-done((bf16[2,8,96,384]{3,2,1,0:T(8,128)(2,1)S(1)}, bf16[2,8,96,384]{3,2,1,0:T(8,128)(2,1)S(1)}, u32[]{:S(2)}, u32[]{:S(2)}) %collective-permute-start) | collective-permute-done | bytes 1179680 | tf_op jit(solution)/shard_map/ppermute | solution.py:33
  44.7 0.2 select_bitcast_fusion.1
  45.0 0.8 fusion.13
  45.8 1.3 %copy.20 = bf16[2,96,8,2,192]{4,1,0,3,2:T(8,128)(2,1)} copy(bf16[2,96,8,2,192]{4,1,2,0,3:T(8,128)(2,1)S(1)} %get-tuple-element.14) | data formatting | bytes 2359296 | tf_op jit(solution)/shard_map/dot_general | solution.py:66
  47.1 2.7 %copy.19 = bf16[8,2,192,2,96]{2,1,0,4,3:T(2,128)(2,1)} copy(bf16[8,2,192,2,96]{2,4,0,3,1:T(8,128)(2,1)S(1)} %get-tuple-element.13) | data formatting | bytes 2359296 | tf_op jit(solution)/shard_map/transpose | solution.py:60
  49.9 4.3 %reshape.97 = bf16[3072,192]{0,1:T(8,128)(2,1)S(1)} reshape(bf16[8,2,192,2,96]{2,1,0,4,3:T(2,128)(2,1)} %copy.19) | data formatting | bytes 2359296 | tf_op jit(solution)/shard_map/reshape | solution.py:60
  54.2 0.0 copy-start.4
  54.2 0.0 slice-start.1
  54.2 4.8 %convolution_bitcast_fusion = f32[192,1024]{1,0:T(8,128)S(1)} fusion(bf16[192,8,2,192]{3,0,2,1:T(8,128)(2,1)} %bitcast.95, bf16[8,2,192,1024]{3,2,1,0:T(8,128)(2,1)} %bitcast.89), kind=kOutput, calls=%fused_computation.21 | convolution fusion | flops 1207959552 | bytes 8257536 | tf_op jit(solution)/shard_map/dot_general | solution.py:65
  59.1 0.0 copy-done.4
  59.1 0.0 copy-start.1
  59.1 0.0 slice-start.2
  59.1 5.4 %multiply_convert_fusion = (bf16[192,1024]{1,0:T(8,128)(2,1)S(1)}, f32[192,1024]{1,0:T(8,128)S(1)}) fusion(f32[192,1024]{1,0:T(8,128)S(1)} %convolution_bitcast_fusion, s32[1,192,1024]{2,1,0:T(8,128)S(1)} %copy-done.4, bf16[3072,192]{0,1:T(8,128)(2,1)S(1)} %reshape.97, bf16[1,1024,3072]{2,1,0:T(8,128)(2,1)} %param.12), kind=kOutput, calls=%fused_computation.39 | convolution fusion | flops 1210515456 | bytes 10223616 | tf_op jit(solution)/shard_map/dot_general | solution.py:67
  64.5 0.0 slice-done
  64.5 0.0 slice-done.1
  64.5 0.0 slice-start.3
  64.5 1.9 %fusion.30 = bf16[192,1024]{1,0:T(8,128)(2,1)S(1)} fusion(f32[192,1024]{1,0:T(8,128)S(1)} %convolution_bitcast_fusion, f32[192,1024]{1,0:T(8,128)S(1)} %get-tuple-element.18, bf16[192,8,2,192]{3,0,2,1:T(8,128)(2,1)S(1)} %bitcast.96, bf16[8,2,192,1024]{3,2,1,0:T(8,128)(2,1)S(1)} %bitcast.88), kind=kOutput, calls=%fused_computation.37 | convolution fusion | flops 1212088320 | bytes 9437184 | tf_op jit(solution)/shard_map/dot_general | solution.py:66
  66.5 2.2 %fusion = f32[192,3072]{1,0:T(8,128)S(1)} fusion(bf16[192,1024]{1,0:T(8,128)(2,1)S(1)} %get-tuple-element.8, bf16[1,3072,1024]{2,1,0:T(8,128)(2,1)S(1)} %bitcast.87), kind=kOutput, calls=%fused_computation.2 | convolution fusion | flops 1207959552 | bytes 9043968 | tf_op jit(solution)/shard_map/dot_general | solution.py:80
  68.7 3.7 %fusion.9 = f32[3072,192]{0,1:T(8,128)} fusion(f32[192,3072]{1,0:T(8,128)S(1)} %fusion, bf16[192,1024]{1,0:T(8,128)(2,1)S(1)} %fusion.30, bf16[1,3072,1024]{2,1,0:T(8,128)(2,1)S(1)} %bitcast.91), kind=kOutput, calls=%fused_computation.9 | convolution fusion | flops 1208549376 | bytes 11403264 | tf_op jit(solution)/shard_map/dot_general | solution.py:78
  72.4 4.8 %reshape.98 = f32[8,2,192,192]{2,1,0,3:T(2,128)S(1)} reshape(f32[3072,192]{0,1:T(8,128)} %fusion.9) | data formatting | bytes 4718592 | tf_op jit(solution)/shard_map/reshape | solution.py:81
  77.2 4.1 %fusion.37 = (f32[8,1,192,192]{2,1,0,3:T(1,128)}, f32[8,1,192,192]{2,1,0,3:T(1,128)}) fusion(f32[8,2,192,192]{2,1,0,3:T(2,128)S(1)} %reshape.98), kind=kLoop, calls=%fused_computation.52 | loop fusion | bytes 4718592 | tf_op jit(solution)/shard_map/slice | solution.py:83
  81.3 4.1 %copy.27 = f32[8,1,192,192]{3,2,0,1:T(8,128)S(1)} copy(f32[8,1,192,192]{2,1,0,3:T(1,128)} %get-tuple-element.11) | data formatting | bytes 2359296
  85.4 4.1 %copy.28 = f32[8,1,192,192]{3,2,0,1:T(8,128)S(1)} copy(f32[8,1,192,192]{2,1,0,3:T(1,128)} %get-tuple-element.12) | data formatting | bytes 2359296
  89.5 0.3 fusion.31
  89.8 0.2 collective-permute-start.1
  90.0 2.2 %collective-permute-done.1 = bf16[8,192,192]{2,1,0:T(8,128)(2,1)S(1)} collective-permute-done((bf16[8,192,192]{2,1,0:T(8,128)(2,1)S(1)}, bf16[8,192,192]{2,1,0:T(8,128)(2,1)S(1)}, u32[]{:S(2)}, u32[]{:S(2)}) %collective-permute-start.1) | collective-permute-done | bytes 589856 | tf_op jit(solution)/shard_map/ppermute | solution.py:33
  92.2 1.3 %fusion.15 = bf16[8,192,192]{2,1,0:T(8,128)(2,1)} fusion(bf16[8,192,192]{2,1,0:T(8,128)(2,1)S(1)} %collective-permute-done.1, f32[8,1,192,192]{3,2,0,1:T(8,128)S(1)} %copy.27, f32[8,1,192,192]{3,2,0,1:T(8,128)S(1)} %copy.28, pred[]{:T(512)S(6)} %eq.23), kind=kLoop, calls=%fused_computation.18 | loop fusion | flops 1179648 | bytes 3538945 | tf_op jit(solution)/shard_map/convert_element_type | solution.py:86
  93.4 2.4 %reshape.99 = bf16[8,192,2,96]{3,2,1,0:T(2,128)(2,1)S(1)} reshape(bf16[8,192,192]{2,1,0:T(8,128)(2,1)} %fusion.15) | data formatting | bytes 1179648 | tf_op jit(solution)/shard_map/reshape | solution.py:86
  95.9 0.0 copy-start.2
  95.9 1.0 copy.23
  96.9 3.6 %all-to-all-start.1 = ((bf16[16,192,96]{2,1,0:T(8,128)(2,1)}), bf16[16,192,96]{2,1,0:T(8,128)(2,1)S(1)}, u32[]{:S(2)}, u32[]{:S(2)}) async-start(bf16[16,192,96]{2,1,0:T(8,128)(2,1)} %bitcast.26), calls=%async_computation.1 | async-start | bytes 1572864 | tf_op jit(solution)/shard_map/all_to_all | solution.py:88
  100.6 0.1 eq.19
  100.6 20.8 %all-to-all-done.1 = bf16[16,192,96]{2,1,0:T(8,128)(2,1)S(1)} async-done(((bf16[16,192,96]{2,1,0:T(8,128)(2,1)}), bf16[16,192,96]{2,1,0:T(8,128)(2,1)S(1)}, u32[]{:S(2)}, u32[]{:S(2)}) %all-to-all-start.1) | async-done | bytes 589856 | tf_op jit(solution)/shard_map/all_to_all | solution.py:88
  121.4 0.2 convert_reduce_fusion
  121.6 0.1 copy.24
  121.7 0.3 fusion.34
  122.0 0.9 fusion.23
  (11 shorter events, 0.0 us)
Async XLA Ops:
  0.0 0.8 copy-start
  0.0 3.5 %copy-start.3 = (f32[2,96]{1,0:T(2,128)S(1)}, f32[2,96]{1,0:T(2,128)}, u32[]{:S(2)}) copy-start(f32[2,96]{1,0:T(2,128)} %param.14) | copy-start | bytes 2308
  41.9 2.8 %collective-permute-start = (bf16[2,8,96,384]{3,2,1,0:T(8,128)(2,1)S(1)}, bf16[2,8,96,384]{3,2,1,0:T(8,128)(2,1)S(1)}, u32[]{:S(2)}, u32[]{:S(2)}) collective-permute-start(bf16[2,8,96,384]{3,2,1,0:T(8,128)(2,1)S(1)} %bitcast.92), channel_id=1, source_target_pairs={{0,1},{1,0},{2,3},{3,2},{4,5},{5,4},{6,7},{7,6},{8,9},{9,8},{10,11... | collective-permute-start | bytes 3538952 | tf_op jit(solution)/shard_map/ppermute | solution.py:33
  49.9 14.6 %slice-start = ((s8[6291456]{0:T(1024)(128)(4,1)}), s8[2097152]{0:T(1024)(128)(4,1)S(1)}, s32[]{:S(2)}) async-start(s8[6291456]{0:T(1024)(128)(4,1)} %bitcast.86), calls=%async_computation.2 | async-start | bytes 4194304
  54.2 4.9 %copy-start.4 = (s32[1,192,1024]{2,1,0:T(8,128)S(1)}, s32[1,192,1024]{2,1,0:T(8,128)}, u32[]{:S(2)}) copy-start(s32[1,192,1024]{2,1,0:T(8,128)} %param.15) | copy-start | bytes 2359300
  54.2 10.3 %slice-start.1 = ((s8[6291456]{0:T(1024)(128)(4,1)}), s8[4194304]{0:T(1024)(128)(4,1)S(1)}, s32[]{:S(2)}) async-start(s8[6291456]{0:T(1024)(128)(4,1)} %bitcast.86), calls=%async_computation.3 | async-start | bytes 8388608
  59.1 5.4 %copy-start.1 = (bf16[2,96,8,2,192]{4,1,0,3,2:T(8,128)(2,1)S(1)}, bf16[2,96,8,2,192]{4,1,0,3,2:T(8,128)(2,1)}, u32[]{:S(2)}) copy-start(bf16[2,96,8,2,192]{4,1,0,3,2:T(8,128)(2,1)} %copy.20) | copy-start | bytes 3538948
  59.1 9.6 %slice-start.2 = ((s8[6291456]{0:T(1024)(128)(4,1)}), s8[4194304]{0:T(1024)(128)(4,1)S(1)}, s32[]{:S(2)}) async-start(s8[6291456]{0:T(1024)(128)(4,1)} %bitcast.90), calls=%async_computation.4 | async-start | bytes 8388608
  64.5 4.2 %slice-start.3 = ((s8[6291456]{0:T(1024)(128)(4,1)}), s8[2097152]{0:T(1024)(128)(4,1)S(1)}, s32[]{:S(2)}) async-start(s8[6291456]{0:T(1024)(128)(4,1)} %bitcast.90), calls=%async_computation.5 | async-start | bytes 4194304
  89.8 2.4 %collective-permute-start.1 = (bf16[8,192,192]{2,1,0:T(8,128)(2,1)S(1)}, bf16[8,192,192]{2,1,0:T(8,128)(2,1)S(1)}, u32[]{:S(2)}, u32[]{:S(2)}) collective-permute-start(bf16[8,192,192]{2,1,0:T(8,128)(2,1)S(1)} %fusion.31), channel_id=1, source_target_pairs={{0,1},{1,0},{2,3},{3,2},{4,5},{5,4},{6,7},{7,6},{8,9},{9,8},{10,11... | collective-permute-start | bytes 1769480 | tf_op jit(solution)/shard_map/ppermute | solution.py:33
  95.9 4.7 %copy-start.2 = (s32[2,96]{1,0:T(2,128)S(1)}, s32[2,96]{1,0:T(2,128)}, u32[]{:S(2)}) copy-start(s32[2,96]{1,0:T(2,128)} %param.13) | copy-start | bytes 2308
  96.9 24.5 %all-to-all-start.1 = ((bf16[16,192,96]{2,1,0:T(8,128)(2,1)}), bf16[16,192,96]{2,1,0:T(8,128)(2,1)S(1)}, u32[]{:S(2)}, u32[]{:S(2)}) async-start(bf16[16,192,96]{2,1,0:T(8,128)(2,1)} %bitcast.26), calls=%async_computation.1 | async-start | bytes 1572864 | tf_op jit(solution)/shard_map/all_to_all | solution.py:88

commit v5 on v3

--- a/solution.py
+++ b/solution.py
@@ -1,16 +1,67 @@
+import math
+
 import jax
 import jax.numpy as jnp
 from jax import lax
+from jax.experimental import pallas as pl
+from jax.experimental.pallas import tpu as pltpu
 from jax.sharding import Mesh
 from jax.sharding import PartitionSpec as P
 
 keep_rate = 0.9
 CROSS = ("expert", "chip")
 HIDDEN = ("chip", "core")
+GELU_C = math.sqrt(2.0 / math.pi)
+GELU_A = 0.044715
 
 
 def gelu_tanh(values):
     return jax.nn.gelu(values, approximate=True)
+
+
+def expert_kernel(x_ref, dy_ref, wg_ref, wu_ref, wd_ref, mask_ref, out_ref):
+    @pl.when(pl.program_id(0) == 0)
+    def _():
+        out_ref[...] = jnp.zeros_like(out_ref)
+
+    x = x_ref[...]
+    wg = wg_ref[...]
+    wu = wu_ref[...]
+    gate_pre = jnp.dot(x, wg, preferred_element_type=jnp.float32)
+    up_pre = jnp.dot(x, wu, preferred_element_type=jnp.float32)
+    nt = (((1,), (1,)), ((), ()))
+    grad_hidden = lax.dot_general(dy_ref[...], wd_ref[...], nt, preferred_element_type=jnp.float32)
+    grad_pre = grad_hidden * mask_ref[...].astype(jnp.float32) * (1.0 / keep_rate)
+    inner = GELU_C * (gate_pre + GELU_A * gate_pre * gate_pre * gate_pre)
+    t = jnp.tanh(inner)
+    activated = 0.5 * gate_pre * (1.0 + t)
+    slope = 0.5 * (1.0 + t) + 0.5 * gate_pre * (1.0 - t * t) * GELU_C * (1.0 + 3.0 * GELU_A * gate_pre * gate_pre)
+    grad_up = (grad_pre * activated).astype(jnp.bfloat16)
+    grad_gate = (grad_pre * up_pre * slope).astype(jnp.bfloat16)
+    out_ref[...] += lax.dot_general(grad_gate, wg, nt, preferred_element_type=jnp.float32) + lax.dot_general(
+        grad_up, wu, nt, preferred_element_type=jnp.float32
+    )
+
+
+def expert_grad(x, dy, wg, wu, wd, mask, tile=256):
+    slots, width = x.shape
+    ff = wg.shape[1]
+    tile = min(tile, ff)
+    return pl.pallas_call(
+        expert_kernel,
+        grid=(ff // tile,),
+        in_specs=[
+            pl.BlockSpec((slots, width), lambda f: (0, 0)),
+            pl.BlockSpec((slots, width), lambda f: (0, 0)),
+            pl.BlockSpec((width, tile), lambda f: (0, f)),
+            pl.BlockSpec((width, tile), lambda f: (0, f)),
+            pl.BlockSpec((tile, width), lambda f: (f, 0)),
+            pl.BlockSpec((slots, tile), lambda f: (0, f)),
+        ],
+        out_specs=pl.BlockSpec((slots, width), lambda f: (0, 0)),
+        out_shape=jax.ShapeDtypeStruct((slots, width), jnp.float32),
+        compiler_params=pltpu.CompilerParams(dimension_semantics=("arbitrary",), vmem_limit_bytes=48 * 1024 * 1024),
+    )(x, dy, wg, wu, wd, mask)
 
 
 def fold_slots(one_hot, slot_values):
@@ -56,31 +107,9 @@
     own = own.reshape(expert_count, chip_count, per_source, 2 * local_width)
     other = swap_cores(own)
     full = order_by_core(own, other, axis=2)
-    part_inputs = full[..., :local_width]
-    part_cot = full[..., local_width:]
-
-    gate_rows = gate_mat.reshape(chip_count, 2, local_width, local_ff)
-    up_rows = up_mat.reshape(chip_count, 2, local_width, local_ff)
-    down_cols = down_mat.reshape(local_ff, chip_count, 2, local_width)
-    fwd_dims = (((1, 2, 4), (0, 1, 2)), ((), ()))
-    gate_pre = lax.dot_general(part_inputs, gate_rows, fwd_dims, preferred_element_type=jnp.float32)
-    up_pre = lax.dot_general(part_inputs, up_rows, fwd_dims, preferred_element_type=jnp.float32)
-    grad_hidden = lax.dot_general(
-        part_cot, down_cols, (((1, 2, 4), (1, 2, 3)), ((), ())), preferred_element_type=jnp.float32
-    )
-    gate_pre = gate_pre.reshape(slot_count, local_ff)
-    up_pre = up_pre.reshape(slot_count, local_ff)
-    grad_hidden = grad_hidden.reshape(slot_count, local_ff)
-    activated, pullback = jax.vjp(gelu_tanh, gate_pre)
-    grad_pre = grad_hidden * keep_mask[0].astype(jnp.float32) * inv_keep
-    grad_up = (grad_pre * activated).astype(jnp.bfloat16)
-    grad_gate = pullback(grad_pre * up_pre)[0].astype(jnp.bfloat16)
-    grad_gate, grad_up = lax.optimization_barrier((grad_gate, grad_up))
-
-    back_dims = (((1,), (1,)), ((), ()))
-    partial = lax.dot_general(
-        grad_gate, gate_mat, back_dims, preferred_element_type=jnp.float32
-    ) + lax.dot_general(grad_up, up_mat, back_dims, preferred_element_type=jnp.float32)
+    part_inputs = full[..., :local_width].transpose(0, 3, 1, 2, 4).reshape(slot_count, model_width)
+    part_cot = full[..., local_width:].transpose(0, 3, 1, 2, 4).reshape(slot_count, model_width)
+    partial = expert_grad(part_inputs, part_cot, gate_mat, up_mat, down_mat, keep_mask[0])
     partial = partial.reshape(expert_count, per_source, chip_count, 2, local_width)
     first = lax.axis_index("core") == 0
     keep_half = jnp.where(first, partial[:, :, :, 0], partial[:, :, :, 1])

time: 104 us -> 112 us (1.077)
  Pallas kernels: 0 us -> 14.8 us
  matrix products: 12.1 us -> 1.18 us
  waiting for transfers between devices: 23.4 us -> 25.8 us
  local copies, waits for them, and re-layouts: 23.2 us -> 25.5 us
    pallas_call x0 -> x1, Pallas kernels: none -> 14.8 us  [expert_grad(): pl.pallas_call(expert_kernel, grid=(ff // tile,), in_specs=[pl.BlockSpec(...]
    dot_general x5 -> x0, matrix products: 10.9 us -> none  [the longest x1 3.67 us: body(): lax.dot_general(grad_gate, gate_mat, back_dims, preferred_element_type=jn...]
    unnamed x21 -> x12, local copies, waits for them, and re-layouts: 11 us -> 2.59 us
    reshape x0 -> x2, local copies, waits for them, and re-layouts: none -> 4.8 us  [the longest x1 2.41 us: body(): full[..., :local_width].transpose(0, 3, 1, 2, 4)]
    slice x1, local copies, waits for them, and re-layouts: 2.43 us -> 6.07 us  [body(): keep_half = jnp.where(first, partial[:, :, :, 0], partial[:, :, :, 1])]
    transpose x0 -> x2, local copies, waits for them, and re-layouts: none -> 3.24 us  [the longest x1 1.62 us: body(): full[..., :local_width].transpose(0, 3, 1, 2, 4)]
    ppermute x2, waiting for transfers between devices: 1.91 us -> 4.99 us  [swap_cores(): return lax.ppermute(values, 'core', [(0, 1), (1, 0)])]
  transfers between devices with their start and end apart: 3 -> 3, of which waited for: 2 -> 3; matrix products, arithmetic and copies ran while one was open for 8% -> 0% of each run, Pallas kernels for 0% -> 0%
where the time goes in v5:
time: 112 us; the launch traced here: 111 us
  blocking collectives  38.1 us (34%)
  waiting for transfers between devices  25.8 us (23%)
  local copies, waits for them, and re-layouts  25.5 us (23%)
  Pallas kernels  14.8 us (13%)
  starting transfers between devices  3.82 us (3%)
  other arithmetic  1.98 us (2%)
  matrix products  1.18 us (1%)
    all_to_all x1, blocking collectives, body(): lax.all_to_all(outgoing, CROSS, split_axis=0, concat_axis=0, tiled=True)  38.1 us
    all_to_all x1, waiting for transfers between devices, body(): lax.all_to_all(blocks, CROSS, split_axis=0, concat_axis=0, tiled=True)  20.8 us
    pallas_call x1, Pallas kernels, expert_grad(): pl.pallas_call(expert_kernel, grid=(ff // tile,), in_specs=[pl.BlockSpec(...  14.8 us
    slice x1, local copies, waits for them, and re-layouts, body(): keep_half = jnp.where(first, partial[:, :, :, 0], partial[:, :, :, 1])  6.07 us
    ppermute x2, waiting for transfers between devices, swap_cores(): return lax.ppermute(values, 'core', [(0, 1), (1, 0)])  4.99 us
    reshape x1, local copies, waits for them, and re-layouts, body(): partial.reshape(expert_count, per_source, chip_count, 2, local_width)  4.07 us
    all_to_all x1, starting transfers between devices, body(): lax.all_to_all(blocks, CROSS, split_axis=0, concat_axis=0, tiled=True)  3.61 us
    unnamed x12, local copies, waits for them, and re-layouts  2.59 us
  transfers between devices with their start and end apart: 3, of which 3 were waited for; matrix products, arithmetic and copies ran while one was open for 0% of the time, Pallas kernels for 0%

profile of v5, /device:TPU:0, one launch (start us, length us, event | category | flops | bytes accessed | tf_op | source)
XLA Modules:
  0.0 111.2 jit_solution(9367019338445997302)
XLA Ops:
  0.0 0.0 copy-start
  0.0 0.0 copy-start.5
  0.0 0.8 reshape.89
  0.8 0.0 copy-done
  0.8 1.0 gather_fusion.1
  1.8 1.7 %gather_fusion = bf16[192,192]{1,0:T(8,128)(2,1)S(1)} fusion(bf16[96,192]{1,0:T(8,128)(2,1)} %param.8, s32[1024]{0:T(1024)S(1)} %pad_clamp_fusion), kind=kCustom, calls=%fused_computation | custom fusion | bytes 148224 | tf_op jit(solution)/shard_map/gather | solution.py:101
  3.5 0.0 copy-done.5
  3.5 0.1 fusion.7
  3.6 0.1 maximum_bitcast_fusion
  3.7 0.1 broadcast_in_dim.5
  3.8 38.1 %all_to_all.10 = bf16[16,96,384]{2,1,0:T(8,128)(2,1)S(1)} all-to-all(bf16[16,96,384]{2,1,0:T(8,128)(2,1)S(1)} %bitcast.48), channel_id=1, replica_groups=mesh['expert'=2,'chip'=8,'core'=2] {'expert','chip'}, dimensions={0} | all-to-all | bytes 2359296 | tf_op jit(solution)/shard_map/all_to_all | solution.py:106
  41.9 0.0 collective-permute-start
  41.9 2.8 %collective-permute-done = bf16[2,8,96,384]{3,2,1,0:T(8,128)(2,1)S(1)} collective-permute-done((bf16[2,8,96,384]{3,2,1,0:T(8,128)(2,1)S(1)}, bf16[2,8,96,384]{3,2,1,0:T(8,128)(2,1)S(1)}, u32[]{:S(2)}, u32[]{:S(2)}) %collective-permute-start) | collective-permute-done | bytes 1179680 | tf_op jit(solution)/shard_map/ppermute | solution.py:84
  44.7 0.2 select_bitcast_fusion
  45.0 0.8 fusion.2
  45.8 1.6 %copy.14 = bf16[2,96,8,2,192]{4,3,2,1,0:T(2,128)(2,1)S(1)} copy(bf16[2,96,8,2,192]{4,1,2,0,3:T(8,128)(2,1)S(1)} %get-tuple-element.10) | data formatting | bytes 2359296 | tf_op jit(solution)/shard_map/transpose | solution.py:110
  47.5 2.4 %reshape.92.x_ref = bf16[192,3072]{1,0:T(8,128)(2,1)} reshape(bf16[2,96,8,2,192]{4,3,2,1,0:T(2,128)(2,1)S(1)} %copy.14) | data formatting | bytes 2359296 | tf_op jit(solution)/shard_map/reshape | solution.py:110
  49.9 1.6 %copy.15 = bf16[2,96,8,2,192]{4,3,2,1,0:T(2,128)(2,1)S(1)} copy(bf16[2,96,8,2,192]{4,1,2,0,3:T(8,128)(2,1)S(1)} %get-tuple-element.9) | data formatting | bytes 2359296 | tf_op jit(solution)/shard_map/transpose | solution.py:111
  51.5 0.0 copy-start.3
  51.5 2.4 %reshape.93.dy_ref = bf16[192,3072]{1,0:T(8,128)(2,1)} reshape(bf16[2,96,8,2,192]{4,3,2,1,0:T(2,128)(2,1)S(1)} %copy.15) | data formatting | bytes 2359296 | tf_op jit(solution)/shard_map/reshape | solution.py:111
  53.9 0.0 copy-done.3
  53.9 0.0 copy-start.1
  53.9 1.3 %copy-done.1 = bf16[192,3072]{1,0:T(8,128)(2,1)S(1)} copy-done((bf16[192,3072]{1,0:T(8,128)(2,1)S(1)}, bf16[192,3072]{1,0:T(8,128)(2,1)}, u32[]{:S(2)}) %copy-start.1) | copy-done | bytes 1179672
  55.2 0.0 copy-start.2
  55.2 1.3 %copy-done.2 = bf16[192,3072]{1,0:T(8,128)(2,1)S(1)} copy-done((bf16[192,3072]{1,0:T(8,128)(2,1)S(1)}, bf16[192,3072]{1,0:T(8,128)(2,1)}, u32[]{:S(2)}) %copy-start.2) | copy-done | bytes 1179672
  56.4 14.8 %shard_map.82 = f32[192,3072]{1,0:T(8,128)S(1)} custom-call(bf16[192,3072]{1,0:T(8,128)(2,1)S(1)} %copy-done.1, bf16[192,3072]{1,0:T(8,128)(2,1)S(1)} %copy-done.2, bf16[3072,1024]{1,0:T(8,128)(2,1)} %bitcast.43, bf16[3072,1024]{1,0:T(8,128)(2,1)} %bitcast.44, bf16[1024,3072]{1,0:T(8,128)(2,1)} %bitcast.45, s32[192,1024]{1,0:T(8,128)S(1)} %bitcast.42), custom_call_target="tpu_custom_call" | custom-call | tf_op jit(solution)/shard_map/pallas_call | solution.py:50
  71.2 4.1 %reshape.94 = f32[2,96,8,2,192]{4,3,2,1,0:T(2,128)} reshape(f32[192,3072]{1,0:T(8,128)S(1)} %shard_map.82) | data formatting | bytes 4718592 | tf_op jit(solution)/shard_map/reshape | solution.py:113
  75.3 6.1 %fusion.12 = (f32[2,96,8,1,192]{4,3,2,1,0:T(1,128)S(1)}, f32[2,96,8,1,192]{4,3,2,1,0:T(1,128)S(1)}) fusion(f32[2,96,8,2,192]{4,3,2,1,0:T(2,128)} %reshape.94), kind=kLoop, calls=%fused_computation.30 | loop fusion | bytes 4718592 | tf_op jit(solution)/shard_map/slice | solution.py:115
  81.4 0.2 fusion.5
  81.6 0.2 collective-permute-start.1
  81.8 2.1 %collective-permute-done.1 = bf16[2,96,8,192]{3,2,1,0:T(8,128)(2,1)S(1)} collective-permute-done((bf16[2,96,8,192]{3,2,1,0:T(8,128)(2,1)S(1)}, bf16[2,96,8,192]{3,2,1,0:T(8,128)(2,1)S(1)}, u32[]{:S(2)}, u32[]{:S(2)}) %collective-permute-start.1) | collective-permute-done | bytes 589856 | tf_op jit(solution)/shard_map/ppermute | solution.py:84
  83.9 0.4 fusion.6
  84.3 0.0 copy-start.4
  84.3 1.1 copy.18
  85.4 3.6 %all-to-all-start.1 = ((bf16[16,96,192]{2,1,0:T(8,128)(2,1)}), bf16[16,96,192]{2,1,0:T(8,128)(2,1)S(1)}, u32[]{:S(2)}, u32[]{:S(2)}) async-start(bf16[16,96,192]{2,1,0:T(8,128)(2,1)} %bitcast.17), calls=%async_computation.1 | async-start | bytes 1572864 | tf_op jit(solution)/shard_map/all_to_all | solution.py:120
  89.0 0.0 copy-done.4
  89.0 0.1 eq.19
  89.1 20.8 %all-to-all-done.1 = bf16[16,96,192]{2,1,0:T(8,128)(2,1)S(1)} async-done(((bf16[16,96,192]{2,1,0:T(8,128)(2,1)}), bf16[16,96,192]{2,1,0:T(8,128)(2,1)S(1)}, u32[]{:S(2)}, u32[]{:S(2)}) %all-to-all-start.1) | async-done | bytes 589856 | tf_op jit(solution)/shard_map/all_to_all | solution.py:120
  109.9 0.1 convert_reduce_fusion
  110.0 0.3 fusion.9
  110.3 0.9 fusion.4
  (3 shorter events, 0.0 us)
Async XLA Ops:
  0.0 0.8 copy-start
  0.0 3.5 %copy-start.5 = (f32[2,96]{1,0:T(2,128)S(1)}, f32[2,96]{1,0:T(2,128)}, u32[]{:S(2)}) copy-start(f32[2,96]{1,0:T(2,128)} %param.14) | copy-start | bytes 2308
  41.9 2.8 %collective-permute-start = (bf16[2,8,96,384]{3,2,1,0:T(8,128)(2,1)S(1)}, bf16[2,8,96,384]{3,2,1,0:T(8,128)(2,1)S(1)}, u32[]{:S(2)}, u32[]{:S(2)}) collective-permute-start(bf16[2,8,96,384]{3,2,1,0:T(8,128)(2,1)S(1)} %bitcast.46), channel_id=1, source_target_pairs={{0,1},{1,0},{2,3},{3,2},{4,5},{5,4},{6,7},{7,6},{8,9},{9,8},{10,11... | collective-permute-start | bytes 3538952 | tf_op jit(solution)/shard_map/ppermute | solution.py:84
  51.5 2.4 %copy-start.3 = (s32[1,192,1024]{2,1,0:T(8,128)S(1)}, s32[1,192,1024]{2,1,0:T(8,128)}, u32[]{:S(2)}) copy-start(s32[1,192,1024]{2,1,0:T(8,128)} %param.15) | copy-start | bytes 2359300
  53.9 1.3 %copy-start.1 = (bf16[192,3072]{1,0:T(8,128)(2,1)S(1)}, bf16[192,3072]{1,0:T(8,128)(2,1)}, u32[]{:S(2)}) copy-start(bf16[192,3072]{1,0:T(8,128)(2,1)} %reshape.92.x_ref) | copy-start | bytes 3538948
  55.2 1.3 %copy-start.2 = (bf16[192,3072]{1,0:T(8,128)(2,1)S(1)}, bf16[192,3072]{1,0:T(8,128)(2,1)}, u32[]{:S(2)}) copy-start(bf16[192,3072]{1,0:T(8,128)(2,1)} %reshape.93.dy_ref) | copy-start | bytes 3538948
  81.6 2.4 %collective-permute-start.1 = (bf16[2,96,8,192]{3,2,1,0:T(8,128)(2,1)S(1)}, bf16[2,96,8,192]{3,2,1,0:T(8,128)(2,1)S(1)}, u32[]{:S(2)}, u32[]{:S(2)}) collective-permute-start(bf16[2,96,8,192]{3,2,1,0:T(8,128)(2,1)S(1)} %fusion.5), channel_id=1, source_target_pairs={{0,1},{1,0},{2,3},{3,2},{4,5},{5,4},{6,7},{7,6},{8,9},{9,8},{10,11... | collective-permute-start | bytes 1769480 | tf_op jit(solution)/shard_map/ppermute | solution.py:84
  84.3 4.7 %copy-start.4 = (s32[2,96]{1,0:T(2,128)S(1)}, s32[2,96]{1,0:T(2,128)}, u32[]{:S(2)}) copy-start(s32[2,96]{1,0:T(2,128)} %param.13) | copy-start | bytes 2308
  85.4 24.5 %all-to-all-start.1 = ((bf16[16,96,192]{2,1,0:T(8,128)(2,1)}), bf16[16,96,192]{2,1,0:T(8,128)(2,1)S(1)}, u32[]{:S(2)}, u32[]{:S(2)}) async-start(bf16[16,96,192]{2,1,0:T(8,128)(2,1)} %bitcast.17), calls=%async_computation.1 | async-start | bytes 1572864 | tf_op jit(solution)/shard_map/all_to_all | solution.py:120

commit v6 on v5

--- a/solution.py
+++ b/solution.py
@@ -19,7 +19,7 @@
     return jax.nn.gelu(values, approximate=True)
 
 
-def expert_kernel(x_ref, dy_ref, wg_ref, wu_ref, wd_ref, mask_ref, out_ref):
+def expert_kernel(x_ref, dyt_ref, wg_ref, wu_ref, wd_ref, mask_ref, out_ref):
     @pl.when(pl.program_id(0) == 0)
     def _():
         out_ref[...] = jnp.zeros_like(out_ref)
@@ -29,8 +29,7 @@
     wu = wu_ref[...]
     gate_pre = jnp.dot(x, wg, preferred_element_type=jnp.float32)
     up_pre = jnp.dot(x, wu, preferred_element_type=jnp.float32)
-    nt = (((1,), (1,)), ((), ()))
-    grad_hidden = lax.dot_general(dy_ref[...], wd_ref[...], nt, preferred_element_type=jnp.float32)
+    grad_hidden = jnp.dot(wd_ref[...], dyt_ref[...], preferred_element_type=jnp.float32).T
     grad_pre = grad_hidden * mask_ref[...].astype(jnp.float32) * (1.0 / keep_rate)
     inner = GELU_C * (gate_pre + GELU_A * gate_pre * gate_pre * gate_pre)
     t = jnp.tanh(inner)
@@ -38,12 +37,13 @@
     slope = 0.5 * (1.0 + t) + 0.5 * gate_pre * (1.0 - t * t) * GELU_C * (1.0 + 3.0 * GELU_A * gate_pre * gate_pre)
     grad_up = (grad_pre * activated).astype(jnp.bfloat16)
     grad_gate = (grad_pre * up_pre * slope).astype(jnp.bfloat16)
-    out_ref[...] += lax.dot_general(grad_gate, wg, nt, preferred_element_type=jnp.float32) + lax.dot_general(
-        grad_up, wu, nt, preferred_element_type=jnp.float32
+    nt = (((1,), (1,)), ((), ()))
+    out_ref[...] += lax.dot_general(wg, grad_gate, nt, preferred_element_type=jnp.float32) + lax.dot_general(
+        wu, grad_up, nt, preferred_element_type=jnp.float32
     )
 
 
-def expert_grad(x, dy, wg, wu, wd, mask, tile=256):
+def expert_grad(x, dyt, wg, wu, wd, mask, tile=256):
     slots, width = x.shape
     ff = wg.shape[1]
     tile = min(tile, ff)
@@ -52,22 +52,22 @@
         grid=(ff // tile,),
         in_specs=[
             pl.BlockSpec((slots, width), lambda f: (0, 0)),
-            pl.BlockSpec((slots, width), lambda f: (0, 0)),
+            pl.BlockSpec((width, slots), lambda f: (0, 0)),
             pl.BlockSpec((width, tile), lambda f: (0, f)),
             pl.BlockSpec((width, tile), lambda f: (0, f)),
             pl.BlockSpec((tile, width), lambda f: (f, 0)),
             pl.BlockSpec((slots, tile), lambda f: (0, f)),
         ],
-        out_specs=pl.BlockSpec((slots, width), lambda f: (0, 0)),
-        out_shape=jax.ShapeDtypeStruct((slots, width), jnp.float32),
+        out_specs=pl.BlockSpec((width, slots), lambda f: (0, 0)),
+        out_shape=jax.ShapeDtypeStruct((width, slots), jnp.float32),
         compiler_params=pltpu.CompilerParams(dimension_semantics=("arbitrary",), vmem_limit_bytes=48 * 1024 * 1024),
-    )(x, dy, wg, wu, wd, mask)
+    )(x, dyt, wg, wu, wd, mask)
 
 
 def fold_slots(one_hot, slot_values):
     high_part = slot_values.astype(jnp.bfloat16)
     low_part = (slot_values - high_part.astype(jnp.float32)).astype(jnp.bfloat16)
-    dims = (((0,), (0,)), ((), ()))
+    dims = (((0, 1), (0, 2)), ((), ()))
     return lax.dot_general(one_hot, high_part, dims, preferred_element_type=jnp.float32) + lax.dot_general(
         one_hot, low_part, dims, preferred_element_type=jnp.float32
     )
@@ -108,19 +108,20 @@
     other = swap_cores(own)
     full = order_by_core(own, other, axis=2)
     part_inputs = full[..., :local_width].transpose(0, 3, 1, 2, 4).reshape(slot_count, model_width)
-    part_cot = full[..., local_width:].transpose(0, 3, 1, 2, 4).reshape(slot_count, model_width)
-    partial = expert_grad(part_inputs, part_cot, gate_mat, up_mat, down_mat, keep_mask[0])
-    partial = partial.reshape(expert_count, per_source, chip_count, 2, local_width)
+    cot_t = full[..., local_width:].transpose(1, 2, 4, 0, 3).reshape(model_width, slot_count)
+    partial = expert_grad(part_inputs, cot_t, gate_mat, up_mat, down_mat, keep_mask[0])
+    partial = partial.reshape(chip_count, 2, local_width, slot_count)
     first = lax.axis_index("core") == 0
-    keep_half = jnp.where(first, partial[:, :, :, 0], partial[:, :, :, 1])
-    send_half = jnp.where(first, partial[:, :, :, 1], partial[:, :, :, 0]).astype(jnp.bfloat16)
+    keep_half = jnp.where(first, partial[:, 0], partial[:, 1])
+    send_half = jnp.where(first, partial[:, 1], partial[:, 0]).astype(jnp.bfloat16)
     chip_sum = keep_half + swap_cores(send_half).astype(jnp.float32)
-    blocks = chip_sum.astype(jnp.bfloat16).transpose(0, 2, 1, 3)
-    blocks = blocks.reshape(expert_count * chip_count, per_source, local_width)
+    blocks = chip_sum.astype(jnp.bfloat16).reshape(chip_count, local_width, expert_count, per_source)
+    blocks = blocks.transpose(2, 0, 1, 3).reshape(expert_count * chip_count, local_width, per_source)
     returned = lax.all_to_all(blocks, CROSS, split_axis=0, concat_axis=0, tiled=True)
-    per_expert = returned.reshape(expert_total, chip_count, per_source, local_width).astype(jnp.float32).sum(1)
+    per_expert = returned.reshape(expert_total, chip_count, local_width, per_source).astype(jnp.float32).sum(1)
     one_hot = (slot_list[:, None] == jnp.arange(group_tokens, dtype=jnp.int32)[None, :]).astype(jnp.bfloat16)
-    token_sum = fold_slots(one_hot, per_expert.reshape(expert_total * per_source, local_width))
+    one_hot = one_hot.reshape(expert_total, per_source, group_tokens)
+    token_sum = fold_slots(one_hot, per_expert)
     return token_sum.astype(jnp.bfloat16)
 
 

time: 112 us -> 113 us (level)
  blocking collectives: 38.1 us -> 62.5 us
  waiting for transfers between devices: 25.8 us -> 5 us
  starting transfers between devices: 3.82 us -> 0.19 us
  local copies, waits for them, and re-layouts: 25.5 us -> 23.2 us
  other arithmetic: 1.98 us -> 4.14 us
  Pallas kernels: 14.8 us -> 16.5 us
    all_to_all x0 -> x1, blocking collectives: none -> 24.5 us  [body(): lax.all_to_all(blocks, CROSS, split_axis=0, concat_axis=0, tiled=True)]
    all_to_all x1 -> x0, waiting for transfers between devices: 20.8 us -> none  [body(): lax.all_to_all(blocks, CROSS, split_axis=0, concat_axis=0, tiled=True)]
    all_to_all x1 -> x0, starting transfers between devices: 3.61 us -> none  [body(): lax.all_to_all(blocks, CROSS, split_axis=0, concat_axis=0, tiled=True)]
    reshape x2, local copies, waits for them, and re-layouts: 6.46 us -> 2.91 us  [body(): full[..., local_width:].transpose(1, 2, 4, 0, 3)]
    slice x1, local copies, waits for them, and re-layouts: 6.07 us -> 3.32 us  [body(): keep_half = jnp.where(first, partial[:, 0], partial[:, 1])]
    transpose x1, local copies, waits for them, and re-layouts: 1.62 us -> 4.19 us  [body(): full[..., :local_width].transpose(0, 3, 1, 2, 4)]
    pallas_call x1, Pallas kernels: 14.8 us -> 16.5 us  [expert_grad(): pl.pallas_call(expert_kernel, grid=(ff // tile,), in_specs=[pl.BlockSpec(...]
    reshape x1, local copies, waits for them, and re-layouts: 2.41 us -> 4 us  [body(): full[..., :local_width].transpose(0, 3, 1, 2, 4)]
  transfers between devices with their start and end apart: 3 -> 2, of which waited for: 3 -> 2; matrix products, arithmetic and copies ran while one was open for 0% -> 0% of each run, Pallas kernels for 0% -> 0%
where the time goes in v6:
time: 113 us
  blocking collectives  62.5 us (55%)
  local copies, waits for them, and re-layouts  23.2 us (21%)
  Pallas kernels  16.5 us (15%)
  waiting for transfers between devices  5 us (4%)
  other arithmetic  4.14 us (4%)
    all_to_all x1, blocking collectives, body(): lax.all_to_all(outgoing, CROSS, split_axis=0, concat_axis=0, tiled=True)  38.1 us
    all_to_all x1, blocking collectives, body(): lax.all_to_all(blocks, CROSS, split_axis=0, concat_axis=0, tiled=True)  24.5 us
    pallas_call x1, Pallas kernels, expert_grad(): pl.pallas_call(expert_kernel, grid=(ff // tile,), in_specs=[pl.BlockSpec(...  16.5 us
    ppermute x2, waiting for transfers between devices, swap_cores(): return lax.ppermute(values, 'core', [(0, 1), (1, 0)])  5 us
    transpose x1, local copies, waits for them, and re-layouts, body(): full[..., :local_width].transpose(0, 3, 1, 2, 4)  4.19 us
    reshape x1, local copies, waits for them, and re-layouts, body(): full[..., :local_width].transpose(0, 3, 1, 2, 4)  4 us
    unnamed x10, local copies, waits for them, and re-layouts  3.74 us
    slice x1, local copies, waits for them, and re-layouts, body(): keep_half = jnp.where(first, partial[:, 0], partial[:, 1])  3.32 us
  transfers between devices with their start and end apart: 2, of which 2 were waited for; matrix products, arithmetic and copies ran while one was open for 0% of the time, Pallas kernels for 0%

profile of v6, /device:TPU:0, one launch (start us, length us, event | category | flops | bytes accessed | tf_op | source)
XLA Modules:
  0.0 112.7 jit_solution(2431094805718516515)
XLA Ops:
  0.0 0.0 copy-start
  0.0 0.0 copy-start.3
  0.0 0.8 reshape.98
  0.8 0.0 copy-done
  0.8 1.0 gather_fusion.1
  1.8 1.7 %gather_fusion = bf16[192,192]{1,0:T(8,128)(2,1)S(1)} fusion(bf16[96,192]{1,0:T(8,128)(2,1)} %param.8, s32[1024]{0:T(1024)S(1)} %pad_clamp_fusion), kind=kCustom, calls=%fused_computation | custom fusion | bytes 148224 | tf_op jit(solution)/shard_map/gather | solution.py:101
  3.5 0.0 copy-done.3
  3.5 0.1 fusion.7
  3.6 0.1 maximum_bitcast_fusion
  3.7 0.1 broadcast_in_dim.5
  3.8 38.1 %all_to_all.10 = bf16[16,96,384]{2,1,0:T(8,128)(2,1)S(1)} all-to-all(bf16[16,96,384]{2,1,0:T(8,128)(2,1)S(1)} %bitcast.49), channel_id=1, replica_groups=mesh['expert'=2,'chip'=8,'core'=2] {'expert','chip'}, dimensions={0} | all-to-all | bytes 2359296 | tf_op jit(solution)/shard_map/all_to_all | solution.py:106
  41.9 0.0 collective-permute-start
  41.9 2.8 %collective-permute-done = bf16[2,8,96,384]{3,2,1,0:T(8,128)(2,1)S(1)} collective-permute-done((bf16[2,8,96,384]{3,2,1,0:T(8,128)(2,1)S(1)}, bf16[2,8,96,384]{3,2,1,0:T(8,128)(2,1)S(1)}, u32[]{:S(2)}, u32[]{:S(2)}) %collective-permute-start) | collective-permute-done | bytes 1179680 | tf_op jit(solution)/shard_map/ppermute | solution.py:84
  44.7 0.2 select_bitcast_fusion
  45.0 2.0 %fusion.2 = (bf16[8,2,192,2,96]{2,4,0,3,1:T(8,128)(2,1)S(1)}, bf16[2,96,8,2,192]{4,1,2,0,3:T(8,128)(2,1)}) fusion(bf16[2,8,1,96,384]{4,3,1,0,2:T(8,128)(2,1)S(1)} %get-tuple-element.9, bf16[2,8,1,96,384]{4,3,1,0,2:T(8,128)(2,1)S(1)} %get-tuple-element.10), kind=kLoop, calls=%fused_computation.7 | loop fusion | flops 4718592 | bytes 4718592 | tf_op jit(solution)/shard_map/transpose | solution.py:111
  47.0 1.9 %copy.28 = bf16[8,2,192,2,96]{4,3,2,1,0:T(2,128)(2,1)S(1)} copy(bf16[8,2,192,2,96]{2,4,0,3,1:T(8,128)(2,1)S(1)} %get-tuple-element.7) | data formatting | bytes 2359296 | tf_op jit(solution)/shard_map/reshape | solution.py:111
  48.9 1.0 reshape.126.dyt_ref
  49.9 4.2 %copy.22 = bf16[2,96,8,2,192]{4,3,2,1,0:T(2,128)(2,1)} copy(bf16[2,96,8,2,192]{4,1,2,0,3:T(8,128)(2,1)} %get-tuple-element.8) | data formatting | bytes 2359296 | tf_op jit(solution)/shard_map/transpose | solution.py:110
  54.1 4.0 %reshape.101.x_ref = bf16[192,3072]{1,0:T(8,128)(2,1)S(1)} reshape(bf16[2,96,8,2,192]{4,3,2,1,0:T(2,128)(2,1)} %copy.22) | data formatting | bytes 2359296 | tf_op jit(solution)/shard_map/reshape | solution.py:110
  58.1 0.0 copy-start.1
  58.1 1.1 copy-done.1
  59.2 16.5 %shard_map.82 = f32[3072,192]{1,0:T(8,128)} custom-call(bf16[192,3072]{1,0:T(8,128)(2,1)S(1)} %reshape.101.x_ref, bf16[3072,192]{1,0:T(8,128)(2,1)S(1)} %reshape.126.dyt_ref, bf16[3072,1024]{1,0:T(8,128)(2,1)} %bitcast.44, bf16[3072,1024]{1,0:T(8,128)(2,1)} %bitcast.45, bf16[1024,3072]{1,0:T(8,128)(2,1)} %bitcast.46, s32[192,1024]{1,0:T(8,128)S(1)} %bitcast.42), custom_call_target="tpu_custom_call" | custom-call | tf_op jit(solution)/shard_map/pallas_call | solution.py:50
  75.7 3.3 %fusion.12 = (f32[8,1,192,192]{3,2,1,0:T(8,128)S(1)}, f32[8,1,192,192]{3,2,1,0:T(8,128)}) fusion(f32[8,2,192,192]{3,2,1,0:T(8,128)} %bitcast.43), kind=kLoop, calls=%fused_computation.30 | loop fusion | bytes 4718592 | tf_op jit(solution)/shard_map/slice | solution.py:115
  79.0 0.6 copy.30
  79.6 2.0 %copy.31 = f32[8,1,192,192]{2,3,0,1:T(8,128)S(1)} copy(f32[8,1,192,192]{3,2,1,0:T(8,128)} %get-tuple-element.6) | data formatting | bytes 2359296
  81.6 0.3 fusion.6
  81.9 0.2 collective-permute-start.1
  82.1 2.2 %collective-permute-done.1 = bf16[8,192,192]{1,2,0:T(8,128)(2,1)S(1)} collective-permute-done((bf16[8,192,192]{1,2,0:T(8,128)(2,1)S(1)}, bf16[8,192,192]{1,2,0:T(8,128)(2,1)S(1)}, u32[]{:S(2)}, u32[]{:S(2)}) %collective-permute-start.1) | collective-permute-done | bytes 589856 | tf_op jit(solution)/shard_map/ppermute | solution.py:84
  84.3 1.3 %fusion.3 = bf16[8,192,192]{1,2,0:T(8,128)(2,1)} fusion(bf16[8,192,192]{1,2,0:T(8,128)(2,1)S(1)} %collective-permute-done.1, f32[8,1,192,192]{2,3,0,1:T(8,128)S(1)} %copy.30, f32[8,1,192,192]{2,3,0,1:T(8,128)S(1)} %copy.31, pred[]{:T(512)S(6)} %eq.21), kind=kLoop, calls=%fused_computation.10 | loop fusion | flops 1179648 | bytes 3538945 | tf_op jit(solution)/shard_map/convert_element_type | solution.py:118
  85.5 1.5 %copy.27 = bf16[2,8,192,96]{3,2,1,0:T(8,128)(2,1)S(1)} copy(bf16[2,8,192,96]{2,3,0,1:T(8,128)(2,1)} %bitcast.50) | data formatting | bytes 1179648 | tf_op jit(solution)/shard_map/transpose | solution.py:119
  87.1 0.0 copy-start.2
  87.1 24.5 %all_to_all.11 = bf16[16,192,96]{2,1,0:T(8,128)(2,1)S(1)} all-to-all(bf16[16,192,96]{2,1,0:T(8,128)(2,1)S(1)} %bitcast.51), channel_id=1, replica_groups=mesh['expert'=2,'chip'=8,'core'=2] {'expert','chip'}, dimensions={0} | all-to-all | bytes 1179648 | tf_op jit(solution)/shard_map/all_to_all | solution.py:120
  111.5 0.2 convert_reduce_fusion
  111.7 0.0 copy-done.2
  111.7 0.2 convolution_bitcast_fusion
  111.9 0.8 fusion.5
  (2 shorter events, 0.0 us)
Async XLA Ops:
  0.0 0.8 copy-start
  0.0 3.5 %copy-start.3 = (f32[2,96]{1,0:T(2,128)S(1)}, f32[2,96]{1,0:T(2,128)}, u32[]{:S(2)}) copy-start(f32[2,96]{1,0:T(2,128)} %param.14) | copy-start | bytes 2308
  41.9 2.8 %collective-permute-start = (bf16[2,8,96,384]{3,2,1,0:T(8,128)(2,1)S(1)}, bf16[2,8,96,384]{3,2,1,0:T(8,128)(2,1)S(1)}, u32[]{:S(2)}, u32[]{:S(2)}) collective-permute-start(bf16[2,8,96,384]{3,2,1,0:T(8,128)(2,1)S(1)} %bitcast.47), channel_id=1, source_target_pairs={{0,1},{1,0},{2,3},{3,2},{4,5},{5,4},{6,7},{7,6},{8,9},{9,8},{10,11... | collective-permute-start | bytes 3538952 | tf_op jit(solution)/shard_map/ppermute | solution.py:84
  58.1 1.1 %copy-start.1 = (s32[1,192,1024]{2,1,0:T(8,128)S(1)}, s32[1,192,1024]{2,1,0:T(8,128)}, u32[]{:S(2)}) copy-start(s32[1,192,1024]{2,1,0:T(8,128)} %param.15) | copy-start | bytes 2359300
  81.9 2.4 %collective-permute-start.1 = (bf16[8,192,192]{1,2,0:T(8,128)(2,1)S(1)}, bf16[8,192,192]{1,2,0:T(8,128)(2,1)S(1)}, u32[]{:S(2)}, u32[]{:S(2)}) collective-permute-start(bf16[8,192,192]{1,2,0:T(8,128)(2,1)S(1)} %fusion.6), channel_id=1, source_target_pairs={{0,1},{1,0},{2,3},{3,2},{4,5},{5,4},{6,7},{7,6},{8,9},{9,8},{10,11... | collective-permute-start | bytes 1769480 | tf_op jit(solution)/shard_map/ppermute | solution.py:84
  87.1 24.6 %copy-start.2 = (s32[2,96]{1,0:T(2,128)S(1)}, s32[2,96]{1,0:T(2,128)}, u32[]{:S(2)}) copy-start(s32[2,96]{1,0:T(2,128)} %param.13) | copy-start | bytes 2308

commit v7 on v3

--- a/solution.py
+++ b/solution.py
@@ -57,20 +57,17 @@
     other = swap_cores(own)
     full = order_by_core(own, other, axis=2)
     part_inputs = full[..., :local_width]
-    part_cot = full[..., local_width:]
+    cot_t = full[..., local_width:].transpose(1, 2, 4, 0, 3).reshape(model_width, slot_count)
 
     gate_rows = gate_mat.reshape(chip_count, 2, local_width, local_ff)
     up_rows = up_mat.reshape(chip_count, 2, local_width, local_ff)
-    down_cols = down_mat.reshape(local_ff, chip_count, 2, local_width)
     fwd_dims = (((1, 2, 4), (0, 1, 2)), ((), ()))
     gate_pre = lax.dot_general(part_inputs, gate_rows, fwd_dims, preferred_element_type=jnp.float32)
     up_pre = lax.dot_general(part_inputs, up_rows, fwd_dims, preferred_element_type=jnp.float32)
-    grad_hidden = lax.dot_general(
-        part_cot, down_cols, (((1, 2, 4), (1, 2, 3)), ((), ())), preferred_element_type=jnp.float32
-    )
+    hidden_t = jnp.dot(down_mat, cot_t, preferred_element_type=jnp.float32)
     gate_pre = gate_pre.reshape(slot_count, local_ff)
     up_pre = up_pre.reshape(slot_count, local_ff)
-    grad_hidden = grad_hidden.reshape(slot_count, local_ff)
+    grad_hidden = hidden_t.T
     activated, pullback = jax.vjp(gelu_tanh, gate_pre)
     grad_pre = grad_hidden * keep_mask[0].astype(jnp.float32) * inv_keep
     grad_up = (grad_pre * activated).astype(jnp.bfloat16)

time: 104 us -> 110 us (1.058)
  matrix products: 12.1 us -> 19.1 us
  local copies, waits for them, and re-layouts: 23.2 us -> 20.4 us
  waiting for transfers between devices: 23.4 us -> 25.8 us
    unnamed x21 -> x18, local copies, waits for them, and re-layouts: 11 us -> 0.08 us
    reshape x0 -> x1, local copies, waits for them, and re-layouts: none -> 4.33 us  [body(): full[..., local_width:].transpose(1, 2, 4, 0, 3)]
    dot_general x1, matrix products: 1.71 us -> 5.35 us  [body(): hidden_t = jnp.dot(down_mat, cot_t, preferred_element_type=jnp.float32)]
    dot_general x1, matrix products: 1.45 us -> 4.83 us  [body(): lax.dot_general(part_inputs, gate_rows, fwd_dims, preferred_element_type=...]
    ppermute x2, waiting for transfers between devices: 1.91 us -> 4.99 us  [swap_cores(): return lax.ppermute(values, 'core', [(0, 1), (1, 0)])]
    transpose x0 -> x1, local copies, waits for them, and re-layouts: none -> 2.75 us  [body(): full[..., local_width:].transpose(1, 2, 4, 0, 3)]
    dot_general x1, local copies, waits for them, and re-layouts: 0.12 us -> 1.31 us  [body(): lax.dot_general(part_inputs, up_rows, fwd_dims, preferred_element_type=jn...]
  transfers between devices with their start and end apart: 3 -> 3, of which waited for: 2 -> 3; matrix products, arithmetic and copies ran while one was open for 8% -> 0% of each run, Pallas kernels for 0% -> 0%
where the time goes in v7:
time: 110 us; the launch traced here: 109 us
  blocking collectives  38.1 us (35%)
  waiting for transfers between devices  25.8 us (23%)
  local copies, waits for them, and re-layouts  20.4 us (19%)
  matrix products  19.1 us (17%)
  starting transfers between devices  3.82 us (3%)
  other arithmetic  1.99 us (2%)
    all_to_all x1, blocking collectives, body(): lax.all_to_all(outgoing, CROSS, split_axis=0, concat_axis=0, tiled=True)  38.1 us
    all_to_all x1, waiting for transfers between devices, body(): lax.all_to_all(blocks, CROSS, split_axis=0, concat_axis=0, tiled=True)  20.8 us
    dot_general x1, matrix products, body(): hidden_t = jnp.dot(down_mat, cot_t, preferred_element_type=jnp.float32)  5.35 us
    ppermute x2, waiting for transfers between devices, swap_cores(): return lax.ppermute(values, 'core', [(0, 1), (1, 0)])  4.99 us
    reshape x1, local copies, waits for them, and re-layouts, body(): partial.reshape(expert_count, per_source, chip_count, 2, local_width)  4.85 us
    dot_general x1, matrix products, body(): lax.dot_general(part_inputs, gate_rows, fwd_dims, preferred_element_type=...  4.83 us
    reshape x1, local copies, waits for them, and re-layouts, body(): full[..., local_width:].transpose(1, 2, 4, 0, 3)  4.33 us
    dot_general x1, matrix products, body(): lax.dot_general(grad_gate, gate_mat, back_dims, preferred_element_type=jn...  3.65 us
  transfers between devices with their start and end apart: 3, of which 3 were waited for; matrix products, arithmetic and copies ran while one was open for 0% of the time, Pallas kernels for 0%

profile of v7, /device:TPU:0, one launch (start us, length us, event | category | flops | bytes accessed | tf_op | source)
XLA Modules:
  0.0 109.5 jit_solution(2296268074847544449)
XLA Ops:
  0.0 0.0 copy-start
  0.0 0.8 reshape.91
  0.8 0.0 copy-done
  0.8 1.0 gather_fusion.1
  1.8 1.7 %gather_fusion = bf16[192,192]{1,0:T(8,128)(2,1)S(1)} fusion(bf16[96,192]{1,0:T(8,128)(2,1)} %param.8, s32[1024]{0:T(1024)S(1)} %pad_clamp_fusion), kind=kCustom, calls=%fused_computation | custom fusion | bytes 148224 | tf_op jit(solution)/shard_map/gather | solution.py:50
  3.5 0.0 copy-done.3
  3.5 0.1 fusion.30
  3.6 0.1 maximum_bitcast_fusion
  3.7 0.1 broadcast_in_dim.5
  3.8 38.1 %all_to_all.10 = bf16[16,96,384]{2,1,0:T(8,128)(2,1)S(1)} all-to-all(bf16[16,96,384]{2,1,0:T(8,128)(2,1)S(1)} %bitcast.89), channel_id=1, replica_groups=mesh['expert'=2,'chip'=8,'core'=2] {'expert','chip'}, dimensions={0} | all-to-all | bytes 2359296 | tf_op jit(solution)/shard_map/all_to_all | solution.py:55
  41.9 0.0 collective-permute-start
  41.9 2.8 %collective-permute-done = bf16[2,8,96,384]{3,2,1,0:T(8,128)(2,1)S(1)} collective-permute-done((bf16[2,8,96,384]{3,2,1,0:T(8,128)(2,1)S(1)}, bf16[2,8,96,384]{3,2,1,0:T(8,128)(2,1)S(1)}, u32[]{:S(2)}, u32[]{:S(2)}) %collective-permute-start) | collective-permute-done | bytes 1179680 | tf_op jit(solution)/shard_map/ppermute | solution.py:33
  44.7 0.2 select_bitcast_fusion.1
  45.0 0.8 fusion.10
  45.8 1.3 %copy.15 = bf16[2,96,8,2,192]{4,1,0,3,2:T(8,128)(2,1)} copy(bf16[2,96,8,2,192]{4,1,2,0,3:T(8,128)(2,1)S(1)} %get-tuple-element.14) | data formatting | bytes 2359296 | tf_op jit(solution)/shard_map/dot_general | solution.py:66
  47.1 2.7 %copy.14 = bf16[8,2,192,2,96]{2,1,0,4,3:T(2,128)(2,1)} copy(bf16[8,2,192,2,96]{2,4,0,3,1:T(8,128)(2,1)S(1)} %get-tuple-element.13) | data formatting | bytes 2359296 | tf_op jit(solution)/shard_map/transpose | solution.py:60
  49.9 4.3 %reshape.94 = bf16[3072,192]{0,1:T(8,128)(2,1)S(1)} reshape(bf16[8,2,192,2,96]{2,1,0,4,3:T(2,128)(2,1)} %copy.14) | data formatting | bytes 2359296 | tf_op jit(solution)/shard_map/reshape | solution.py:60
  54.2 0.0 copy-start.4
  54.2 0.0 slice-start.1
  54.3 4.8 %convolution_bitcast_fusion = f32[192,1024]{1,0:T(8,128)S(1)} fusion(bf16[192,8,2,192]{3,0,2,1:T(8,128)(2,1)} %bitcast.90, bf16[8,2,192,1024]{3,2,1,0:T(8,128)(2,1)} %bitcast.84), kind=kOutput, calls=%fused_computation.20 | convolution fusion | flops 1207959552 | bytes 8257536 | tf_op jit(solution)/shard_map/dot_general | solution.py:65
  59.1 0.0 copy-done.4
  59.1 0.0 copy-start.1
  59.1 0.0 slice-start.2
  59.1 5.3 %multiply_convert_fusion = (bf16[192,1024]{1,0:T(8,128)(2,1)S(1)}, f32[192,1024]{1,0:T(8,128)S(1)}) fusion(f32[192,1024]{1,0:T(8,128)S(1)} %convolution_bitcast_fusion, s32[1,192,1024]{2,1,0:T(8,128)S(1)} %copy-done.4, bf16[3072,192]{0,1:T(8,128)(2,1)S(1)} %reshape.94, bf16[1,1024,3072]{2,1,0:T(8,128)(2,1)} %param.12), kind=kOutput, calls=%fused_computation.39 | convolution fusion | flops 1210515456 | bytes 10223616 | tf_op jit(solution)/shard_map/dot_general | solution.py:67
  64.5 0.0 slice-done
  64.5 0.0 slice-done.1
  64.5 0.0 copy-done.1
  64.5 0.0 slice-start.3
  64.5 1.9 %fusion.27 = bf16[192,1024]{1,0:T(8,128)(2,1)S(1)} fusion(f32[192,1024]{1,0:T(8,128)S(1)} %convolution_bitcast_fusion, f32[192,1024]{1,0:T(8,128)S(1)} %get-tuple-element.18, bf16[192,8,2,192]{3,0,2,1:T(8,128)(2,1)S(1)} %bitcast.91, bf16[8,2,192,1024]{3,2,1,0:T(8,128)(2,1)S(1)} %bitcast.83), kind=kOutput, calls=%fused_computation.36 | convolution fusion | flops 1212088320 | bytes 9437184 | tf_op jit(solution)/shard_map/dot_general | solution.py:66
  66.5 2.2 %fusion = f32[192,3072]{1,0:T(8,128)S(1)} fusion(bf16[192,1024]{1,0:T(8,128)(2,1)S(1)} %get-tuple-element.8, bf16[1,3072,1024]{2,1,0:T(8,128)(2,1)S(1)} %bitcast.82), kind=kOutput, calls=%fused_computation.2 | convolution fusion | flops 1207959552 | bytes 9043968 | tf_op jit(solution)/shard_map/dot_general | solution.py:80
  68.7 0.0 slice-done.2
  68.7 0.0 slice-done.3
  68.7 3.7 %fusion.6 = f32[192,3072]{1,0:T(8,128)} fusion(f32[192,3072]{1,0:T(8,128)S(1)} %fusion, bf16[192,1024]{1,0:T(8,128)(2,1)S(1)} %fusion.27, bf16[1,3072,1024]{2,1,0:T(8,128)(2,1)S(1)} %bitcast.86), kind=kOutput, calls=%fused_computation.8 | convolution fusion | flops 1208549376 | bytes 11403264 | tf_op jit(solution)/shard_map/dot_general | solution.py:78
  72.4 4.8 %reshape.95 = f32[2,96,8,2,192]{4,3,2,1,0:T(2,128)S(1)} reshape(f32[192,3072]{1,0:T(8,128)} %fusion.6) | data formatting | bytes 4718592 | tf_op jit(solution)/shard_map/reshape | solution.py:81
  77.2 2.4 %fusion.35 = (f32[2,96,8,1,192]{4,3,2,1,0:T(1,128)S(1)}, f32[2,96,8,1,192]{4,3,2,1,0:T(1,128)S(1)}) fusion(f32[2,96,8,2,192]{4,3,2,1,0:T(2,128)S(1)} %reshape.95), kind=kLoop, calls=%fused_computation.52 | loop fusion | bytes 4718592 | tf_op jit(solution)/shard_map/slice | solution.py:83
  79.7 0.2 fusion.28
  79.8 0.2 collective-permute-start.1
  80.0 2.1 %collective-permute-done.1 = bf16[2,96,8,192]{3,2,1,0:T(8,128)(2,1)S(1)} collective-permute-done((bf16[2,96,8,192]{3,2,1,0:T(8,128)(2,1)S(1)}, bf16[2,96,8,192]{3,2,1,0:T(8,128)(2,1)S(1)}, u32[]{:S(2)}, u32[]{:S(2)}) %collective-permute-start.1) | collective-permute-done | bytes 589856 | tf_op jit(solution)/shard_map/ppermute | solution.py:33
  82.2 0.4 fusion.29
  82.6 0.0 copy-start.2
  82.6 1.1 copy.18
  83.6 3.6 %all-to-all-start.1 = ((bf16[16,96,192]{2,1,0:T(8,128)(2,1)}), bf16[16,96,192]{2,1,0:T(8,128)(2,1)S(1)}, u32[]{:S(2)}, u32[]{:S(2)}) async-start(bf16[16,96,192]{2,1,0:T(8,128)(2,1)} %bitcast.25), calls=%async_computation.1 | async-start | bytes 1572864 | tf_op jit(solution)/shard_map/all_to_all | solution.py:88
  87.3 0.0 copy-done.2
  87.3 0.1 eq.19
  87.4 20.8 %all-to-all-done.1 = bf16[16,96,192]{2,1,0:T(8,128)(2,1)S(1)} async-done(((bf16[16,96,192]{2,1,0:T(8,128)(2,1)}), bf16[16,96,192]{2,1,0:T(8,128)(2,1)S(1)}, u32[]{:S(2)}, u32[]{:S(2)}) %all-to-all-start.1) | async-done | bytes 589856 | tf_op jit(solution)/shard_map/all_to_all | solution.py:88
  108.1 0.1 convert_reduce_fusion
  108.3 0.3 fusion.32
  108.6 0.9 fusion.20
  (7 shorter events, 0.0 us)
Async XLA Ops:
  0.0 0.8 copy-start
  0.0 3.5 %copy-start.3 = (f32[2,96]{1,0:T(2,128)S(1)}, f32[2,96]{1,0:T(2,128)}, u32[]{:S(2)}) copy-start(f32[2,96]{1,0:T(2,128)} %param.14) | copy-start | bytes 2308
  41.9 2.8 %collective-permute-start = (bf16[2,8,96,384]{3,2,1,0:T(8,128)(2,1)S(1)}, bf16[2,8,96,384]{3,2,1,0:T(8,128)(2,1)S(1)}, u32[]{:S(2)}, u32[]{:S(2)}) collective-permute-start(bf16[2,8,96,384]{3,2,1,0:T(8,128)(2,1)S(1)} %bitcast.87), channel_id=1, source_target_pairs={{0,1},{1,0},{2,3},{3,2},{4,5},{5,4},{6,7},{7,6},{8,9},{9,8},{10,11... | collective-permute-start | bytes 3538952 | tf_op jit(solution)/shard_map/ppermute | solution.py:33
  49.9 14.6 %slice-start = ((s8[6291456]{0:T(1024)(128)(4,1)}), s8[2097152]{0:T(1024)(128)(4,1)S(1)}, s32[]{:S(2)}) async-start(s8[6291456]{0:T(1024)(128)(4,1)} %bitcast.81), calls=%async_computation.2 | async-start | bytes 4194304
  54.2 4.9 %copy-start.4 = (s32[1,192,1024]{2,1,0:T(8,128)S(1)}, s32[1,192,1024]{2,1,0:T(8,128)}, u32[]{:S(2)}) copy-start(s32[1,192,1024]{2,1,0:T(8,128)} %param.15) | copy-start | bytes 2359300
  54.2 10.2 %slice-start.1 = ((s8[6291456]{0:T(1024)(128)(4,1)}), s8[4194304]{0:T(1024)(128)(4,1)S(1)}, s32[]{:S(2)}) async-start(s8[6291456]{0:T(1024)(128)(4,1)} %bitcast.81), calls=%async_computation.3 | async-start | bytes 8388608
  59.1 5.4 %copy-start.1 = (bf16[2,96,8,2,192]{4,1,0,3,2:T(8,128)(2,1)S(1)}, bf16[2,96,8,2,192]{4,1,0,3,2:T(8,128)(2,1)}, u32[]{:S(2)}) copy-start(bf16[2,96,8,2,192]{4,1,0,3,2:T(8,128)(2,1)} %copy.15) | copy-start | bytes 3538948
  59.1 9.6 %slice-start.2 = ((s8[6291456]{0:T(1024)(128)(4,1)}), s8[4194304]{0:T(1024)(128)(4,1)S(1)}, s32[]{:S(2)}) async-start(s8[6291456]{0:T(1024)(128)(4,1)} %bitcast.85), calls=%async_computation.4 | async-start | bytes 8388608
  64.5 4.2 %slice-start.3 = ((s8[6291456]{0:T(1024)(128)(4,1)}), s8[2097152]{0:T(1024)(128)(4,1)S(1)}, s32[]{:S(2)}) async-start(s8[6291456]{0:T(1024)(128)(4,1)} %bitcast.85), calls=%async_computation.5 | async-start | bytes 4194304
  79.8 2.4 %collective-permute-start.1 = (bf16[2,96,8,192]{3,2,1,0:T(8,128)(2,1)S(1)}, bf16[2,96,8,192]{3,2,1,0:T(8,128)(2,1)S(1)}, u32[]{:S(2)}, u32[]{:S(2)}) collective-permute-start(bf16[2,96,8,192]{3,2,1,0:T(8,128)(2,1)S(1)} %fusion.28), channel_id=1, source_target_pairs={{0,1},{1,0},{2,3},{3,2},{4,5},{5,4},{6,7},{7,6},{8,9},{9,8},{10,11... | collective-permute-start | bytes 1769480 | tf_op jit(solution)/shard_map/ppermute | solution.py:33
  82.6 4.7 %copy-start.2 = (s32[2,96]{1,0:T(2,128)S(1)}, s32[2,96]{1,0:T(2,128)}, u32[]{:S(2)}) copy-start(s32[2,96]{1,0:T(2,128)} %param.13) | copy-start | bytes 2308
  83.6 24.5 %all-to-all-start.1 = ((bf16[16,96,192]{2,1,0:T(8,128)(2,1)}), bf16[16,96,192]{2,1,0:T(8,128)(2,1)S(1)}, u32[]{:S(2)}, u32[]{:S(2)}) async-start(bf16[16,96,192]{2,1,0:T(8,128)(2,1)} %bitcast.25), calls=%async_computation.1 | async-start | bytes 1572864 | tf_op jit(solution)/shard_map/all_to_all | solution.py:88

commit v8 on v3

--- a/solution.py
+++ b/solution.py
@@ -81,11 +81,11 @@
     partial = lax.dot_general(
         grad_gate, gate_mat, back_dims, preferred_element_type=jnp.float32
     ) + lax.dot_general(grad_up, up_mat, back_dims, preferred_element_type=jnp.float32)
-    partial = partial.reshape(expert_count, per_source, chip_count, 2, local_width)
+    partial = partial.astype(jnp.bfloat16).reshape(expert_count, per_source, chip_count, 2, local_width)
     first = lax.axis_index("core") == 0
     keep_half = jnp.where(first, partial[:, :, :, 0], partial[:, :, :, 1])
-    send_half = jnp.where(first, partial[:, :, :, 1], partial[:, :, :, 0]).astype(jnp.bfloat16)
-    chip_sum = keep_half + swap_cores(send_half).astype(jnp.float32)
+    send_half = jnp.where(first, partial[:, :, :, 1], partial[:, :, :, 0])
+    chip_sum = keep_half.astype(jnp.float32) + swap_cores(send_half).astype(jnp.float32)
     blocks = chip_sum.astype(jnp.bfloat16).transpose(0, 2, 1, 3)
     blocks = blocks.reshape(expert_count * chip_count, per_source, local_width)
     returned = lax.all_to_all(blocks, CROSS, split_axis=0, concat_axis=0, tiled=True)

time: 104 us -> 99.2 us (0.954)
  local copies, waits for them, and re-layouts: 23.2 us -> 20.1 us
  matrix products: 12.1 us -> 10.7 us
    reshape x1, local copies, waits for them, and re-layouts: 4.81 us -> 1.94 us  [body(): partial.astype(jnp.bfloat16)]
    dot_general x1, matrix products: 3.67 us -> 2.22 us  [body(): lax.dot_general(grad_gate, gate_mat, back_dims, preferred_element_type=jn...]
  transfers between devices with their start and end apart: 3 -> 3, of which waited for: 2 -> 2; matrix products, arithmetic and copies ran while one was open for 8% -> 9% of each run, Pallas kernels for 0% -> 0%
where the time goes in v8:
time: 99.2 us; the launch traced here: 98.6 us
  blocking collectives  38.1 us (38%)
  waiting for transfers between devices  23.4 us (24%)
  local copies, waits for them, and re-layouts  20.1 us (20%)
  matrix products  10.7 us (11%)
  starting transfers between devices  4.18 us (4%)
  other arithmetic  1.94 us (2%)
    all_to_all x1, blocking collectives, body(): lax.all_to_all(outgoing, CROSS, split_axis=0, concat_axis=0, tiled=True)  38.1 us
    all_to_all x1, waiting for transfers between devices, body(): lax.all_to_all(blocks, CROSS, split_axis=0, concat_axis=0, tiled=True)  21.5 us
    unnamed x21, local copies, waits for them, and re-layouts  11 us
    all_to_all x1, starting transfers between devices, body(): lax.all_to_all(blocks, CROSS, split_axis=0, concat_axis=0, tiled=True)  3.61 us
    slice x1, local copies, waits for them, and re-layouts, body(): keep_half = jnp.where(first, partial[:, :, :, 0], partial[:, :, :, 1])  2.24 us
    dot_general x1, matrix products, body(): lax.dot_general(grad_gate, gate_mat, back_dims, preferred_element_type=jn...  2.22 us
    dot_general x1, matrix products, body(): lax.dot_general(grad_up, up_mat, back_dims, preferred_element_type=jnp.fl...  2.2 us
  transfers between devices with their start and end apart: 3, of which 2 were waited for; matrix products, arithmetic and copies ran while one was open for 9% of the time, Pallas kernels for 0%

profile of v8, /device:TPU:0, one launch (start us, length us, event | category | flops | bytes accessed | tf_op | source)
XLA Modules:
  0.0 98.6 jit_solution(9132037279740551624)
XLA Ops:
  0.0 0.0 copy-start
  0.0 0.0 copy-start.2
  0.0 0.8 reshape.91
  0.8 0.0 copy-done
  0.8 1.0 %gather_fusion.1 = bf16[192,192]{1,0:T(8,128)(2,1)S(1)} fusion(bf16[96,192]{1,0:T(8,128)(2,1)S(1)} %copy-done, s32[1024]{0:T(1024)S(1)} %pad_clamp_fusion), kind=kCustom, calls=%fused_computation.1 | custom fusion | bytes 148224 | tf_op jit(solution)/shard_map/gather | solution.py:51
  1.8 1.7 %gather_fusion = bf16[192,192]{1,0:T(8,128)(2,1)S(1)} fusion(bf16[96,192]{1,0:T(8,128)(2,1)} %param.8, s32[1024]{0:T(1024)S(1)} %pad_clamp_fusion), kind=kCustom, calls=%fused_computation | custom fusion | bytes 148224 | tf_op jit(solution)/shard_map/gather | solution.py:50
  3.5 0.0 copy-done.2
  3.5 0.1 fusion.26
  3.6 0.1 maximum_bitcast_fusion
  3.7 0.1 broadcast_in_dim.5
  3.8 38.1 %all_to_all.10 = bf16[16,96,384]{2,1,0:T(8,128)(2,1)S(1)} all-to-all(bf16[16,96,384]{2,1,0:T(8,128)(2,1)S(1)} %bitcast.91), channel_id=1, replica_groups=mesh['expert'=2,'chip'=8,'core'=2] {'expert','chip'}, dimensions={0} | all-to-all | bytes 2359296 | tf_op jit(solution)/shard_map/all_to_all | solution.py:55
  41.9 0.0 collective-permute-start
  41.9 8.6 %copy.16 = bf16[1,1024,3072]{1,2,0:T(8,128)(2,1)} copy(bf16[1,1024,3072]{2,1,0:T(8,128)(2,1)} %param.12) | data formatting | bytes 12582912 | tf_op args[4]
  50.5 0.0 collective-permute-done
  50.5 0.0 slice-start.2
  50.5 0.2 select_bitcast_fusion.1
  50.8 0.0 slice-start.3
  50.8 0.9 fusion.11
  51.6 0.0 slice-start.4
  51.7 0.1 copy.17
  51.8 0.1 copy.15
  51.9 0.8 slice-done.2
  52.7 0.7 slice-done.3
  53.5 1.5 %convolution_bitcast_fusion = f32[192,1024]{1,0:T(8,128)S(1)} fusion(bf16[192,8,2,192]{3,0,2,1:T(8,128)(2,1)S(1)} %bitcast.92, bf16[8,2,192,1024]{3,2,1,0:T(8,128)(2,1)S(1)} %bitcast.85), kind=kOutput, calls=%fused_computation.17 | convolution fusion | flops 1207959552 | bytes 8257536 | tf_op jit(solution)/shard_map/dot_general | solution.py:66
  54.9 0.0 slice-done.4
  54.9 0.4 slice-done.5
  55.4 0.1 copy-done.3
  55.5 1.7 %multiply_convert_fusion = (bf16[192,1024]{1,0:T(8,128)(2,1)S(1)}, f32[192,1024]{1,0:T(8,128)S(1)}) fusion(f32[192,1024]{1,0:T(8,128)S(1)} %convolution_bitcast_fusion, s32[1,192,1024]{2,1,0:T(8,128)S(1)} %copy-done.3, bf16[192,8,2,192]{3,0,2,1:T(8,128)(2,1)S(1)} %bitcast.94, bf16[1024,8,2,192]{0,3,2,1:T(8,128)(2,1)S(1)} %bitcast.88), kind=kOutput, calls=%fused_computation.38 | convolution fusion | flops 1210515456 | bytes 10223616 | tf_op jit(solution)/shard_map/dot_general | solution.py:68
  57.2 0.0 slice-done
  57.2 0.2 slice-done.1
  57.4 1.9 %fusion.24 = bf16[192,1024]{1,0:T(8,128)(2,1)S(1)} fusion(f32[192,1024]{1,0:T(8,128)S(1)} %convolution_bitcast_fusion, f32[192,1024]{1,0:T(8,128)S(1)} %get-tuple-element.18, bf16[192,8,2,192]{3,0,2,1:T(8,128)(2,1)S(1)} %bitcast.93, bf16[8,2,192,1024]{3,2,1,0:T(8,128)(2,1)S(1)} %bitcast.82), kind=kOutput, calls=%fused_computation.35 | convolution fusion | flops 1212088320 | bytes 9437184 | tf_op jit(solution)/shard_map/dot_general | solution.py:67
  59.4 2.2 %fusion = f32[192,3072]{1,0:T(8,128)S(1)} fusion(bf16[192,1024]{1,0:T(8,128)(2,1)S(1)} %get-tuple-element.8, bf16[1,3072,1024]{2,1,0:T(8,128)(2,1)S(1)} %bitcast.81), kind=kOutput, calls=%fused_computation.2 | convolution fusion | flops 1207959552 | bytes 9043968 | tf_op jit(solution)/shard_map/dot_general | solution.py:83
  61.6 2.2 %fusion.7 = bf16[192,3072]{1,0:T(8,128)(2,1)S(1)} fusion(f32[192,3072]{1,0:T(8,128)S(1)} %fusion, bf16[192,1024]{1,0:T(8,128)(2,1)S(1)} %fusion.24, bf16[1,3072,1024]{2,1,0:T(8,128)(2,1)S(1)} %bitcast.84), kind=kOutput, calls=%fused_computation.7 | convolution fusion | flops 1209139200 | bytes 10223616 | tf_op jit(solution)/shard_map/dot_general | solution.py:81
  63.8 1.9 %reshape.94 = bf16[2,96,8,2,192]{4,3,2,1,0:T(2,128)(2,1)S(1)} reshape(bf16[192,3072]{1,0:T(8,128)(2,1)S(1)} %fusion.7) | data formatting | bytes 2359296 | tf_op jit(solution)/shard_map/reshape | solution.py:84
  65.7 2.2 %fusion.31 = (bf16[2,96,8,1,192]{4,3,2,1,0:T(2,128)(2,1)S(1)}, bf16[2,96,8,1,192]{4,3,2,1,0:T(2,128)(2,1)S(1)}) fusion(bf16[2,96,8,2,192]{4,3,2,1,0:T(2,128)(2,1)S(1)} %reshape.94), kind=kLoop, calls=%fused_computation.51 | loop fusion | bytes 2359296 | tf_op jit(solution)/shard_map/slice | solution.py:86
  68.0 0.2 select_bitcast_fusion.2
  68.2 0.6 collective-permute-start.1
  68.8 1.9 %collective-permute-done.1 = bf16[2,96,8,192]{3,2,1,0:T(8,128)(2,1)S(1)} collective-permute-done((bf16[2,96,8,192]{3,2,1,0:T(8,128)(2,1)S(1)}, bf16[2,96,8,192]{3,2,1,0:T(8,128)(2,1)S(1)}, u32[]{:S(2)}, u32[]{:S(2)}) %collective-permute-start.1) | collective-permute-done | bytes 589856 | tf_op jit(solution)/shard_map/ppermute | solution.py:33
  70.7 0.3 fusion.25
  71.0 0.0 copy-start.1
  71.0 1.1 %copy.20 = bf16[2,8,96,192]{3,2,1,0:T(8,128)(2,1)} copy(bf16[2,8,96,192]{3,1,2,0:T(8,128)(2,1)S(1)} %fusion.25) | data formatting | bytes 1179648 | tf_op jit(solution)/shard_map/transpose | solution.py:89
  72.1 3.6 %all-to-all-start.1 = ((bf16[16,96,192]{2,1,0:T(8,128)(2,1)}), bf16[16,96,192]{2,1,0:T(8,128)(2,1)S(1)}, u32[]{:S(2)}, u32[]{:S(2)}) async-start(bf16[16,96,192]{2,1,0:T(8,128)(2,1)} %bitcast.28), calls=%async_computation.1 | async-start | bytes 1572864 | tf_op jit(solution)/shard_map/all_to_all | solution.py:91
  75.7 0.0 copy-done.1
  75.7 0.1 eq.19
  75.8 21.5 %all-to-all-done.1 = bf16[16,96,192]{2,1,0:T(8,128)(2,1)S(1)} async-done(((bf16[16,96,192]{2,1,0:T(8,128)(2,1)}), bf16[16,96,192]{2,1,0:T(8,128)(2,1)S(1)}, u32[]{:S(2)}, u32[]{:S(2)}) %all-to-all-start.1) | async-done | bytes 589856 | tf_op jit(solution)/shard_map/all_to_all | solution.py:91
  97.3 0.1 convert_reduce_fusion
  97.4 0.3 fusion.28
  97.7 0.9 fusion.17
  (10 shorter events, 0.0 us)
Async XLA Ops:
  0.0 0.8 copy-start
  0.0 3.5 %copy-start.2 = (f32[2,96]{1,0:T(2,128)S(1)}, f32[2,96]{1,0:T(2,128)}, u32[]{:S(2)}) copy-start(f32[2,96]{1,0:T(2,128)} %param.14) | copy-start | bytes 2308
  41.9 8.6 %collective-permute-start = (bf16[2,8,96,384]{3,2,1,0:T(8,128)(2,1)S(1)}, bf16[2,8,96,384]{3,2,1,0:T(8,128)(2,1)S(1)}, u32[]{:S(2)}, u32[]{:S(2)}) collective-permute-start(bf16[2,8,96,384]{3,2,1,0:T(8,128)(2,1)S(1)} %bitcast.89), channel_id=1, source_target_pairs={{0,1},{1,0},{2,3},{3,2},{4,5},{5,4},{6,7},{7,6},{8,9},{9,8},{10,11... | collective-permute-start | bytes 3538952 | tf_op jit(solution)/shard_map/ppermute | solution.py:33
  50.5 2.2 %slice-start.2 = ((s8[6291456]{0:T(1024)(128)(4,1)}), s8[4194304]{0:T(1024)(128)(4,1)S(1)}, s32[]{:S(2)}) async-start(s8[6291456]{0:T(1024)(128)(4,1)} %bitcast.83), calls=%async_computation.4 | async-start | bytes 8388608
  50.8 2.7 %slice-start.3 = ((s8[6291456]{0:T(1024)(128)(4,1)}), s8[2097152]{0:T(1024)(128)(4,1)S(1)}, s32[]{:S(2)}) async-start(s8[6291456]{0:T(1024)(128)(4,1)} %bitcast.83), calls=%async_computation.5 | async-start | bytes 4194304
  51.6 3.3 %slice-start.4 = ((s8[6291456]{0:T(1024)(128)(4,1)}), s8[4194304]{0:T(1024)(128)(4,1)S(1)}, s32[]{:S(2)}) async-start(s8[6291456]{0:T(1024)(128)(4,1)} %bitcast.86), calls=%async_computation.6 | async-start | bytes 8388608
  53.5 1.9 %slice-start.5 = ((s8[6291456]{0:T(1024)(128)(4,1)}), s8[2097152]{0:T(1024)(128)(4,1)S(1)}, s32[]{:S(2)}) async-start(s8[6291456]{0:T(1024)(128)(4,1)} %bitcast.86), calls=%async_computation.7 | async-start | bytes 4194304
  53.5 2.1 %copy-start.3 = (s32[1,192,1024]{2,1,0:T(8,128)S(1)}, s32[1,192,1024]{2,1,0:T(8,128)}, u32[]{:S(2)}) copy-start(s32[1,192,1024]{2,1,0:T(8,128)} %param.15) | copy-start | bytes 2359300
  53.5 3.8 %slice-start = ((s8[6291456]{0:T(1024)(128)(4,1)}), s8[4194304]{0:T(1024)(128)(4,1)S(1)}, s32[]{:S(2)}) async-start(s8[6291456]{0:T(1024)(128)(4,1)} %bitcast.80), calls=%async_computation.2 | async-start | bytes 8388608
  55.5 1.9 %slice-start.1 = ((s8[6291456]{0:T(1024)(128)(4,1)}), s8[2097152]{0:T(1024)(128)(4,1)S(1)}, s32[]{:S(2)}) async-start(s8[6291456]{0:T(1024)(128)(4,1)} %bitcast.80), calls=%async_computation.3 | async-start | bytes 4194304
  68.2 2.5 %collective-permute-start.1 = (bf16[2,96,8,192]{3,2,1,0:T(8,128)(2,1)S(1)}, bf16[2,96,8,192]{3,2,1,0:T(8,128)(2,1)S(1)}, u32[]{:S(2)}, u32[]{:S(2)}) collective-permute-start(bf16[2,96,8,192]{3,2,1,0:T(8,128)(2,1)S(1)} %select_bitcast_fusion.2), channel_id=1, source_target_pairs={{0,1},{1,0},{2,3},{3,2},{4,5},{5,4},{6,7},{7,6},{8,9},{9,8},{10,11... | collective-permute-start | bytes 1769480 | tf_op jit(solution)/shard_map/ppermute | solution.py:33
  71.0 4.7 %copy-start.1 = (s32[2,96]{1,0:T(2,128)S(1)}, s32[2,96]{1,0:T(2,128)}, u32[]{:S(2)}) copy-start(s32[2,96]{1,0:T(2,128)} %param.13) | copy-start | bytes 2308
  72.1 25.2 %all-to-all-start.1 = ((bf16[16,96,192]{2,1,0:T(8,128)(2,1)}), bf16[16,96,192]{2,1,0:T(8,128)(2,1)S(1)}, u32[]{:S(2)}, u32[]{:S(2)}) async-start(bf16[16,96,192]{2,1,0:T(8,128)(2,1)} %bitcast.28), calls=%async_computation.1 | async-start | bytes 1572864 | tf_op jit(solution)/shard_map/all_to_all | solution.py:91

commit v9 on v8

--- a/solution.py
+++ b/solution.py
@@ -1,6 +1,8 @@
 import jax
 import jax.numpy as jnp
 from jax import lax
+from jax.experimental import pallas as pl
+from jax.experimental.pallas import tpu as pltpu
 from jax.sharding import Mesh
 from jax.sharding import PartitionSpec as P
 
@@ -11,6 +13,27 @@
 
 def gelu_tanh(values):
     return jax.nn.gelu(values, approximate=True)
+
+
+def hidden_kernel(wd_ref, dyt_ref, out_ref):
+    out_ref[...] = jnp.dot(wd_ref[...], dyt_ref[...], preferred_element_type=jnp.float32).T
+
+
+def hidden_grad(wd, dyt, tile=256):
+    ff, width = wd.shape
+    slots = dyt.shape[1]
+    tile = min(tile, ff)
+    return pl.pallas_call(
+        hidden_kernel,
+        grid=(ff // tile,),
+        in_specs=[
+            pl.BlockSpec((tile, width), lambda f: (f, 0)),
+            pl.BlockSpec((width, slots), lambda f: (0, 0)),
+        ],
+        out_specs=pl.BlockSpec((slots, tile), lambda f: (0, f)),
+        out_shape=jax.ShapeDtypeStruct((slots, ff), jnp.float32),
+        compiler_params=pltpu.CompilerParams(dimension_semantics=("arbitrary",)),
+    )(wd, dyt)
 
 
 def fold_slots(one_hot, slot_values):
@@ -57,20 +80,16 @@
     other = swap_cores(own)
     full = order_by_core(own, other, axis=2)
     part_inputs = full[..., :local_width]
-    part_cot = full[..., local_width:]
+    cot_t = full[..., local_width:].transpose(1, 2, 4, 0, 3).reshape(model_width, slot_count)
 
     gate_rows = gate_mat.reshape(chip_count, 2, local_width, local_ff)
     up_rows = up_mat.reshape(chip_count, 2, local_width, local_ff)
-    down_cols = down_mat.reshape(local_ff, chip_count, 2, local_width)
     fwd_dims = (((1, 2, 4), (0, 1, 2)), ((), ()))
     gate_pre = lax.dot_general(part_inputs, gate_rows, fwd_dims, preferred_element_type=jnp.float32)
     up_pre = lax.dot_general(part_inputs, up_rows, fwd_dims, preferred_element_type=jnp.float32)
-    grad_hidden = lax.dot_general(
-        part_cot, down_cols, (((1, 2, 4), (1, 2, 3)), ((), ())), preferred_element_type=jnp.float32
-    )
+    grad_hidden = hidden_grad(down_mat, cot_t)
     gate_pre = gate_pre.reshape(slot_count, local_ff)
     up_pre = up_pre.reshape(slot_count, local_ff)
-    grad_hidden = grad_hidden.reshape(slot_count, local_ff)
     activated, pullback = jax.vjp(gelu_tanh, gate_pre)
     grad_pre = grad_hidden * keep_mask[0].astype(jnp.float32) * inv_keep
     grad_up = (grad_pre * activated).astype(jnp.bfloat16)

time: 99.2 us -> 107 us (1.079)
  Pallas kernels: 0 us -> 6.32 us
  local copies, waits for them, and re-layouts: 20.1 us -> 16.3 us
  waiting for transfers between devices: 23.4 us -> 25.8 us
  matrix products: 10.7 us -> 12.9 us
  other arithmetic: 1.94 us -> 3.1 us
    unnamed x21 -> x20, local copies, waits for them, and re-layouts: 11 us -> 0.09 us
    pallas_call x0 -> x1, Pallas kernels: none -> 6.32 us  [hidden_grad(): pl.pallas_call(hidden_kernel, grid=(ff // tile,), in_specs=[pl.BlockSpec(...]
    reshape x0 -> x2, local copies, waits for them, and re-layouts: none -> 6.13 us  [body(): full[..., local_width:].transpose(1, 2, 4, 0, 3)]
    dot_general x1, matrix products: 1.45 us -> 5.25 us  [body(): lax.dot_general(part_inputs, gate_rows, fwd_dims, preferred_element_type=...]
    ppermute x2, waiting for transfers between devices: 1.91 us -> 5 us  [swap_cores(): return lax.ppermute(values, 'core', [(0, 1), (1, 0)])]
    transpose x0 -> x1, other arithmetic: none -> 2.02 us  [body(): full[..., local_width:].transpose(1, 2, 4, 0, 3)]
    dot_general x1 -> x0, matrix products: 1.7 us -> none  [body(): lax.dot_general(part_cot, down_cols, (((1, 2, 4), (1, 2, 3)), ((), ())),...]
    dot_general x1, local copies, waits for them, and re-layouts: 0.12 us -> 1.26 us  [body(): lax.dot_general(part_inputs, up_rows, fwd_dims, preferred_element_type=jn...]
  transfers between devices with their start and end apart: 3 -> 3, of which waited for: 2 -> 3; matrix products, arithmetic and copies ran while one was open for 9% -> 0% of each run, Pallas kernels for 0% -> 0%
where the time goes in v9:
time: 107 us
  blocking collectives  38.1 us (36%)
  waiting for transfers between devices  25.8 us (24%)
  local copies, waits for them, and re-layouts  16.3 us (15%)
  matrix products  12.9 us (12%)
  Pallas kernels  6.32 us (6%)
  starting transfers between devices  3.81 us (4%)
  other arithmetic  3.1 us (3%)
    all_to_all x1, blocking collectives, body(): lax.all_to_all(outgoing, CROSS, split_axis=0, concat_axis=0, tiled=True)  38.1 us
    all_to_all x1, waiting for transfers between devices, body(): lax.all_to_all(blocks, CROSS, split_axis=0, concat_axis=0, tiled=True)  20.8 us
    pallas_call x1, Pallas kernels, hidden_grad(): pl.pallas_call(hidden_kernel, grid=(ff // tile,), in_specs=[pl.BlockSpec(...  6.32 us
    reshape x2, local copies, waits for them, and re-layouts, body(): full[..., local_width:].transpose(1, 2, 4, 0, 3)  6.13 us
    dot_general x1, matrix products, body(): lax.dot_general(part_inputs, gate_rows, fwd_dims, preferred_element_type=...  5.25 us
    ppermute x2, waiting for transfers between devices, swap_cores(): return lax.ppermute(values, 'core', [(0, 1), (1, 0)])  5 us
    all_to_all x1, starting transfers between devices, body(): lax.all_to_all(blocks, CROSS, split_axis=0, concat_axis=0, tiled=True)  3.61 us
    slice x1, local copies, waits for them, and re-layouts, body(): keep_half = jnp.where(first, partial[:, :, :, 0], partial[:, :, :, 1])  2.24 us
  transfers between devices with their start and end apart: 3, of which 3 were waited for; matrix products, arithmetic and copies ran while one was open for 0% of the time, Pallas kernels for 0%

profile of v9, /device:TPU:0, one launch (start us, length us, event | category | flops | bytes accessed | tf_op | source)
XLA Modules:
  0.0 106.5 jit_solution(289275617229243799)
XLA Ops:
  0.0 0.0 copy-start
  0.0 0.0 copy-start.4
  0.0 0.8 reshape.92
  0.8 0.0 copy-done
  0.8 1.0 gather_fusion.1
  1.8 1.7 %gather_fusion = bf16[192,192]{1,0:T(8,128)(2,1)S(1)} fusion(bf16[96,192]{1,0:T(8,128)(2,1)} %param.8, s32[1024]{0:T(1024)S(1)} %pad_clamp_fusion), kind=kCustom, calls=%fused_computation | custom fusion | bytes 148224 | tf_op jit(solution)/shard_map/gather | solution.py:73
  3.5 0.0 copy-done.4
  3.5 0.1 fusion.25
  3.6 0.1 maximum_bitcast_fusion
  3.7 0.1 broadcast_in_dim.5
  3.8 38.1 %all_to_all.10 = bf16[16,96,384]{2,1,0:T(8,128)(2,1)S(1)} all-to-all(bf16[16,96,384]{2,1,0:T(8,128)(2,1)S(1)} %bitcast.84), channel_id=1, replica_groups=mesh['expert'=2,'chip'=8,'core'=2] {'expert','chip'}, dimensions={0} | all-to-all | bytes 2359296 | tf_op jit(solution)/shard_map/all_to_all | solution.py:78
  41.9 0.0 collective-permute-start
  41.9 2.8 %collective-permute-done = bf16[2,8,96,384]{3,2,1,0:T(8,128)(2,1)S(1)} collective-permute-done((bf16[2,8,96,384]{3,2,1,0:T(8,128)(2,1)S(1)}, bf16[2,8,96,384]{3,2,1,0:T(8,128)(2,1)S(1)}, u32[]{:S(2)}, u32[]{:S(2)}) %collective-permute-start) | collective-permute-done | bytes 1179680 | tf_op jit(solution)/shard_map/ppermute | solution.py:56
  44.7 0.2 select_bitcast_fusion.1
  45.0 2.0 %fusion.11 = (bf16[8,2,192,2,96]{2,4,0,3,1:T(8,128)(2,1)}, bf16[2,96,8,2,192]{4,1,2,0,3:T(8,128)(2,1)S(1)}) fusion(bf16[2,8,1,96,384]{4,3,1,0,2:T(8,128)(2,1)S(1)} %get-tuple-element.13, bf16[2,8,1,96,384]{4,3,1,0,2:T(8,128)(2,1)S(1)} %get-tuple-element.14), kind=kLoop, calls=%fused_computation.11 | loop fusion | flops 4718592 | bytes 4718592 | tf_op jit(solution)/shard_map/transpose | solution.py:83
  47.0 3.9 %copy.23 = bf16[8,2,192,2,96]{4,3,2,1,0:T(2,128)(2,1)S(1)} copy(bf16[8,2,192,2,96]{2,4,0,3,1:T(8,128)(2,1)} %get-tuple-element.11) | data formatting | bytes 2359296 | tf_op jit(solution)/shard_map/reshape | solution.py:83
  50.9 2.3 %reshape.120.dyt_ref = bf16[3072,192]{1,0:T(8,128)(2,1)} reshape(bf16[8,2,192,2,96]{4,3,2,1,0:T(2,128)(2,1)S(1)} %copy.23) | data formatting | bytes 2359296 | tf_op jit(solution)/shard_map/reshape | solution.py:83
  53.1 1.3 %copy.17 = bf16[2,96,8,2,192]{4,1,0,3,2:T(8,128)(2,1)} copy(bf16[2,96,8,2,192]{4,1,2,0,3:T(8,128)(2,1)S(1)} %get-tuple-element.12) | data formatting | bytes 2359296 | tf_op jit(solution)/shard_map/dot_general | solution.py:89
  54.4 0.0 slice-start
  54.4 6.3 %shard_map.82 = f32[192,1024]{1,0:T(8,128)} custom-call(bf16[1024,3072]{1,0:T(8,128)(2,1)} %bitcast.81, bf16[3072,192]{1,0:T(8,128)(2,1)} %reshape.120.dyt_ref), custom_call_target="tpu_custom_call" | custom-call | tf_op jit(solution)/shard_map/pallas_call | solution.py:26
  60.7 0.0 copy-done.5
  60.7 0.0 copy-start.2
  60.7 0.0 slice-start.2
  60.8 5.2 %multiply_convert_fusion = (bf16[192,1024]{1,0:T(8,128)(2,1)S(1)}, f32[192,1024]{1,0:T(8,128)S(1)}) fusion(f32[192,1024]{1,0:T(8,128)} %shard_map.82, s32[1,192,1024]{2,1,0:T(8,128)S(1)} %copy-done.5, bf16[192,8,2,192]{3,0,2,1:T(8,128)(2,1)} %bitcast.85, bf16[8,2,192,1024]{3,2,1,0:T(8,128)(2,1)} %bitcast.78), kind=kOutput, calls=%fused_computation.37 | convolution fusion | flops 1210515456 | bytes 10223616 | tf_op jit(solution)/shard_map/dot_general | solution.py:88
  66.0 0.0 slice-done
  66.0 0.0 slice-done.1
  66.0 0.0 copy-done.1
  66.0 0.0 copy-done.2
  66.1 2.0 %fusion.22 = bf16[192,1024]{1,0:T(8,128)(2,1)S(1)} fusion(f32[192,1024]{1,0:T(8,128)S(1)} %get-tuple-element.18, bf16[192,8,2,192]{3,0,2,1:T(8,128)(2,1)S(1)} %bitcast.86, bf16[8,2,192,1024]{3,2,1,0:T(8,128)(2,1)S(1)} %bitcast.77, f32[192,1024]{1,0:T(8,128)S(1)} %copy-done.2, s32[1,192,1024]{2,1,0:T(8,128)S(1)} %copy-done.5), kind=kOutput, calls=%fused_computation.32 | convolution fusion | flops 1212678144 | bytes 10223616 | tf_op jit(solution)/shard_map/dot_general | solution.py:89
  68.1 2.2 %fusion = f32[192,3072]{1,0:T(8,128)S(1)} fusion(bf16[192,1024]{1,0:T(8,128)(2,1)S(1)} %get-tuple-element.8, bf16[1,3072,1024]{2,1,0:T(8,128)(2,1)S(1)} %bitcast.76), kind=kOutput, calls=%fused_computation.2 | convolution fusion | flops 1207959552 | bytes 9043968 | tf_op jit(solution)/shard_map/dot_general | solution.py:102
  70.3 0.0 slice-done.2
  70.3 0.0 slice-done.3
  70.3 2.2 %fusion.7 = bf16[192,3072]{1,0:T(8,128)(2,1)S(1)} fusion(f32[192,3072]{1,0:T(8,128)S(1)} %fusion, bf16[192,1024]{1,0:T(8,128)(2,1)S(1)} %fusion.22, bf16[1,3072,1024]{2,1,0:T(8,128)(2,1)S(1)} %bitcast.80), kind=kOutput, calls=%fused_computation.7 | convolution fusion | flops 1209139200 | bytes 10223616 | tf_op jit(solution)/shard_map/dot_general | solution.py:100
  72.5 1.9 %reshape.96 = bf16[2,96,8,2,192]{4,3,2,1,0:T(2,128)(2,1)S(1)} reshape(bf16[192,3072]{1,0:T(8,128)(2,1)S(1)} %fusion.7) | data formatting | bytes 2359296 | tf_op jit(solution)/shard_map/reshape | solution.py:103
  74.5 2.2 %fusion.30 = (bf16[2,96,8,1,192]{4,3,2,1,0:T(2,128)(2,1)S(1)}, bf16[2,96,8,1,192]{4,3,2,1,0:T(2,128)(2,1)S(1)}) fusion(bf16[2,96,8,2,192]{4,3,2,1,0:T(2,128)(2,1)S(1)} %reshape.96), kind=kLoop, calls=%fused_computation.50 | loop fusion | bytes 2359296 | tf_op jit(solution)/shard_map/slice | solution.py:105
  76.7 0.2 select_bitcast_fusion.2
  76.9 0.2 collective-permute-start.1
  77.1 2.2 %collective-permute-done.1 = bf16[2,96,8,192]{3,2,1,0:T(8,128)(2,1)S(1)} collective-permute-done((bf16[2,96,8,192]{3,2,1,0:T(8,128)(2,1)S(1)}, bf16[2,96,8,192]{3,2,1,0:T(8,128)(2,1)S(1)}, u32[]{:S(2)}, u32[]{:S(2)}) %collective-permute-start.1) | collective-permute-done | bytes 589856 | tf_op jit(solution)/shard_map/ppermute | solution.py:56
  79.3 0.3 fusion.23
  79.6 0.0 copy-start.3
  79.6 1.1 copy.20
  80.7 3.6 %all-to-all-start.1 = ((bf16[16,96,192]{2,1,0:T(8,128)(2,1)}), bf16[16,96,192]{2,1,0:T(8,128)(2,1)S(1)}, u32[]{:S(2)}, u32[]{:S(2)}) async-start(bf16[16,96,192]{2,1,0:T(8,128)(2,1)} %bitcast.25), calls=%async_computation.1 | async-start | bytes 1572864 | tf_op jit(solution)/shard_map/all_to_all | solution.py:110
  84.3 0.0 copy-done.3
  84.3 0.1 eq.19
  84.4 20.8 %all-to-all-done.1 = bf16[16,96,192]{2,1,0:T(8,128)(2,1)S(1)} async-done(((bf16[16,96,192]{2,1,0:T(8,128)(2,1)}), bf16[16,96,192]{2,1,0:T(8,128)(2,1)S(1)}, u32[]{:S(2)}, u32[]{:S(2)}) %all-to-all-start.1) | async-done | bytes 589856 | tf_op jit(solution)/shard_map/all_to_all | solution.py:110
  105.2 0.1 convert_reduce_fusion
  105.3 0.3 fusion.27
  105.6 0.9 fusion.15
  (9 shorter events, 0.0 us)
Async XLA Ops:
  0.0 0.8 copy-start
  0.0 3.5 %copy-start.4 = (f32[2,96]{1,0:T(2,128)S(1)}, f32[2,96]{1,0:T(2,128)}, u32[]{:S(2)}) copy-start(f32[2,96]{1,0:T(2,128)} %param.14) | copy-start | bytes 2308
  41.9 2.8 %collective-permute-start = (bf16[2,8,96,384]{3,2,1,0:T(8,128)(2,1)S(1)}, bf16[2,8,96,384]{3,2,1,0:T(8,128)(2,1)S(1)}, u32[]{:S(2)}, u32[]{:S(2)}) collective-permute-start(bf16[2,8,96,384]{3,2,1,0:T(8,128)(2,1)S(1)} %bitcast.82), channel_id=1, source_target_pairs={{0,1},{1,0},{2,3},{3,2},{4,5},{5,4},{6,7},{7,6},{8,9},{9,8},{10,11... | collective-permute-start | bytes 3538952 | tf_op jit(solution)/shard_map/ppermute | solution.py:56
  54.4 6.3 %copy-start.5 = (s32[1,192,1024]{2,1,0:T(8,128)S(1)}, s32[1,192,1024]{2,1,0:T(8,128)}, u32[]{:S(2)}) copy-start(s32[1,192,1024]{2,1,0:T(8,128)} %param.15) | copy-start | bytes 2359300
  54.4 11.6 %slice-start = ((s8[6291456]{0:T(1024)(128)(4,1)}), s8[2097152]{0:T(1024)(128)(4,1)S(1)}, s32[]{:S(2)}) async-start(s8[6291456]{0:T(1024)(128)(4,1)} %bitcast.75), calls=%async_computation.2 | async-start | bytes 4194304
  60.7 5.3 %slice-start.1 = ((s8[6291456]{0:T(1024)(128)(4,1)}), s8[4194304]{0:T(1024)(128)(4,1)S(1)}, s32[]{:S(2)}) async-start(s8[6291456]{0:T(1024)(128)(4,1)} %bitcast.75), calls=%async_computation.3 | async-start | bytes 8388608
  60.7 5.3 %copy-start.1 = (bf16[2,96,8,2,192]{4,1,0,3,2:T(8,128)(2,1)S(1)}, bf16[2,96,8,2,192]{4,1,0,3,2:T(8,128)(2,1)}, u32[]{:S(2)}) copy-start(bf16[2,96,8,2,192]{4,1,0,3,2:T(8,128)(2,1)} %copy.17) | copy-start | bytes 3538948
  60.7 5.3 %copy-start.2 = (f32[192,1024]{1,0:T(8,128)S(1)}, f32[192,1024]{1,0:T(8,128)}, u32[]{:S(2)}) copy-start(f32[192,1024]{1,0:T(8,128)} %shard_map.82) | copy-start | bytes 2359300
  60.7 9.6 %slice-start.2 = ((s8[6291456]{0:T(1024)(128)(4,1)}), s8[4194304]{0:T(1024)(128)(4,1)S(1)}, s32[]{:S(2)}) async-start(s8[6291456]{0:T(1024)(128)(4,1)} %bitcast.79), calls=%async_computation.4 | async-start | bytes 8388608
  66.1 4.2 %slice-start.3 = ((s8[6291456]{0:T(1024)(128)(4,1)}), s8[2097152]{0:T(1024)(128)(4,1)S(1)}, s32[]{:S(2)}) async-start(s8[6291456]{0:T(1024)(128)(4,1)} %bitcast.79), calls=%async_computation.5 | async-start | bytes 4194304
  76.9 2.4 %collective-permute-start.1 = (bf16[2,96,8,192]{3,2,1,0:T(8,128)(2,1)S(1)}, bf16[2,96,8,192]{3,2,1,0:T(8,128)(2,1)S(1)}, u32[]{:S(2)}, u32[]{:S(2)}) collective-permute-start(bf16[2,96,8,192]{3,2,1,0:T(8,128)(2,1)S(1)} %select_bitcast_fusion.2), channel_id=1, source_target_pairs={{0,1},{1,0},{2,3},{3,2},{4,5},{5,4},{6,7},{7,6},{8,9},{9,8},{10,11... | collective-permute-start | bytes 1769480 | tf_op jit(solution)/shard_map/ppermute | solution.py:56
  79.6 4.7 %copy-start.3 = (s32[2,96]{1,0:T(2,128)S(1)}, s32[2,96]{1,0:T(2,128)}, u32[]{:S(2)}) copy-start(s32[2,96]{1,0:T(2,128)} %param.13) | copy-start | bytes 2308
  80.7 24.5 %all-to-all-start.1 = ((bf16[16,96,192]{2,1,0:T(8,128)(2,1)}), bf16[16,96,192]{2,1,0:T(8,128)(2,1)S(1)}, u32[]{:S(2)}, u32[]{:S(2)}) async-start(bf16[16,96,192]{2,1,0:T(8,128)(2,1)} %bitcast.25), calls=%async_computation.1 | async-start | bytes 1572864 | tf_op jit(solution)/shard_map/all_to_all | solution.py:110

commit v10 on v8

--- a/solution.py
+++ b/solution.py
@@ -57,20 +57,18 @@
     other = swap_cores(own)
     full = order_by_core(own, other, axis=2)
     part_inputs = full[..., :local_width]
-    part_cot = full[..., local_width:]
+    part_cot = full[..., local_width:].transpose(0, 3, 1, 2, 4).reshape(slot_count, model_width)
 
     gate_rows = gate_mat.reshape(chip_count, 2, local_width, local_ff)
     up_rows = up_mat.reshape(chip_count, 2, local_width, local_ff)
-    down_cols = down_mat.reshape(local_ff, chip_count, 2, local_width)
     fwd_dims = (((1, 2, 4), (0, 1, 2)), ((), ()))
     gate_pre = lax.dot_general(part_inputs, gate_rows, fwd_dims, preferred_element_type=jnp.float32)
     up_pre = lax.dot_general(part_inputs, up_rows, fwd_dims, preferred_element_type=jnp.float32)
     grad_hidden = lax.dot_general(
-        part_cot, down_cols, (((1, 2, 4), (1, 2, 3)), ((), ())), preferred_element_type=jnp.float32
+        part_cot, down_mat, (((1,), (1,)), ((), ())), preferred_element_type=jnp.float32
     )
     gate_pre = gate_pre.reshape(slot_count, local_ff)
     up_pre = up_pre.reshape(slot_count, local_ff)
-    grad_hidden = grad_hidden.reshape(slot_count, local_ff)
     activated, pullback = jax.vjp(gelu_tanh, gate_pre)
     grad_pre = grad_hidden * keep_mask[0].astype(jnp.float32) * inv_keep
     grad_up = (grad_pre * activated).astype(jnp.bfloat16)

time: 99.2 us -> 105 us (1.058)
  matrix products: 10.7 us -> 17.7 us
  local copies, waits for them, and re-layouts: 20.1 us -> 17.3 us
  waiting for transfers between devices: 23.4 us -> 25.8 us
    unnamed x21 -> x18, local copies, waits for them, and re-layouts: 11 us -> 0.08 us
    reshape x0 -> x1, local copies, waits for them, and re-layouts: none -> 4.33 us  [body(): full[..., local_width:].transpose(0, 3, 1, 2, 4)]
    dot_general x1, matrix products: 1.7 us -> 5.35 us  [body(): lax.dot_general(part_cot, down_mat, (((1,), (1,)), ((), ())), preferred_e...]
    dot_general x1, matrix products: 1.45 us -> 4.83 us  [body(): lax.dot_general(part_inputs, gate_rows, fwd_dims, preferred_element_type=...]
    ppermute x2, waiting for transfers between devices: 1.91 us -> 4.99 us  [swap_cores(): return lax.ppermute(values, 'core', [(0, 1), (1, 0)])]
    transpose x0 -> x1, local copies, waits for them, and re-layouts: none -> 2.75 us  [body(): full[..., local_width:].transpose(0, 3, 1, 2, 4)]
    dot_general x1, local copies, waits for them, and re-layouts: 0.12 us -> 1.31 us  [body(): lax.dot_general(part_inputs, up_rows, fwd_dims, preferred_element_type=jn...]
  transfers between devices with their start and end apart: 3 -> 3, of which waited for: 2 -> 3; matrix products, arithmetic and copies ran while one was open for 9% -> 0% of each run, Pallas kernels for 0% -> 0%
where the time goes in v10:
time: 105 us
  blocking collectives  38.1 us (36%)
  waiting for transfers between devices  25.8 us (25%)
  matrix products  17.7 us (17%)
  local copies, waits for them, and re-layouts  17.3 us (16%)
  starting transfers between devices  3.82 us (4%)
  other arithmetic  1.93 us (2%)
    all_to_all x1, blocking collectives, body(): lax.all_to_all(outgoing, CROSS, split_axis=0, concat_axis=0, tiled=True)  38.1 us
    all_to_all x1, waiting for transfers between devices, body(): lax.all_to_all(blocks, CROSS, split_axis=0, concat_axis=0, tiled=True)  20.8 us
    dot_general x1, matrix products, body(): lax.dot_general(part_cot, down_mat, (((1,), (1,)), ((), ())), preferred_e...  5.35 us
    ppermute x2, waiting for transfers between devices, swap_cores(): return lax.ppermute(values, 'core', [(0, 1), (1, 0)])  4.99 us
    dot_general x1, matrix products, body(): lax.dot_general(part_inputs, gate_rows, fwd_dims, preferred_element_type=...  4.83 us
    reshape x1, local copies, waits for them, and re-layouts, body(): full[..., local_width:].transpose(0, 3, 1, 2, 4)  4.33 us
    all_to_all x1, starting transfers between devices, body(): lax.all_to_all(blocks, CROSS, split_axis=0, concat_axis=0, tiled=True)  3.61 us
    transpose x1, local copies, waits for them, and re-layouts, body(): full[..., local_width:].transpose(0, 3, 1, 2, 4)  2.75 us
  transfers between devices with their start and end apart: 3, of which 3 were waited for; matrix products, arithmetic and copies ran while one was open for 0% of the time, Pallas kernels for 0%

profile of v10, /device:TPU:0, one launch (start us, length us, event | category | flops | bytes accessed | tf_op | source)
XLA Modules:
  0.0 104.9 jit_solution(4794385933651617091)
XLA Ops:
  0.0 0.0 copy-start
  0.0 0.8 reshape.92
  0.8 0.0 copy-done
  0.8 1.0 gather_fusion.1
  1.8 1.7 %gather_fusion = bf16[192,192]{1,0:T(8,128)(2,1)S(1)} fusion(bf16[96,192]{1,0:T(8,128)(2,1)} %param.8, s32[1024]{0:T(1024)S(1)} %pad_clamp_fusion), kind=kCustom, calls=%fused_computation | custom fusion | bytes 148224 | tf_op jit(solution)/shard_map/gather | solution.py:50
  3.5 0.0 copy-done.3
  3.5 0.1 fusion.32
  3.6 0.1 maximum_bitcast_fusion
  3.7 0.1 broadcast_in_dim.5
  3.8 38.1 %all_to_all.10 = bf16[16,96,384]{2,1,0:T(8,128)(2,1)S(1)} all-to-all(bf16[16,96,384]{2,1,0:T(8,128)(2,1)S(1)} %bitcast.86), channel_id=1, replica_groups=mesh['expert'=2,'chip'=8,'core'=2] {'expert','chip'}, dimensions={0} | all-to-all | bytes 2359296 | tf_op jit(solution)/shard_map/all_to_all | solution.py:55
  41.9 0.0 collective-permute-start
  41.9 2.8 %collective-permute-done = bf16[2,8,96,384]{3,2,1,0:T(8,128)(2,1)S(1)} collective-permute-done((bf16[2,8,96,384]{3,2,1,0:T(8,128)(2,1)S(1)}, bf16[2,8,96,384]{3,2,1,0:T(8,128)(2,1)S(1)}, u32[]{:S(2)}, u32[]{:S(2)}) %collective-permute-start) | collective-permute-done | bytes 1179680 | tf_op jit(solution)/shard_map/ppermute | solution.py:33
  44.7 0.2 select_bitcast_fusion.1
  45.0 0.8 fusion.13
  45.8 1.3 %copy.15 = bf16[2,96,8,2,192]{4,1,0,3,2:T(8,128)(2,1)} copy(bf16[2,96,8,2,192]{4,1,2,0,3:T(8,128)(2,1)S(1)} %get-tuple-element.12) | data formatting | bytes 2359296 | tf_op jit(solution)/shard_map/dot_general | solution.py:66
  47.1 2.7 %copy.14 = bf16[2,96,8,2,192]{4,3,2,1,0:T(2,128)(2,1)} copy(bf16[2,96,8,2,192]{4,1,2,0,3:T(8,128)(2,1)S(1)} %get-tuple-element.11) | data formatting | bytes 2359296 | tf_op jit(solution)/shard_map/transpose | solution.py:60
  49.9 4.3 %reshape.95 = bf16[192,3072]{1,0:T(8,128)(2,1)S(1)} reshape(bf16[2,96,8,2,192]{4,3,2,1,0:T(2,128)(2,1)} %copy.14) | data formatting | bytes 2359296 | tf_op jit(solution)/shard_map/reshape | solution.py:60
  54.2 0.0 copy-start.4
  54.2 0.0 slice-start.1
  54.3 4.8 %convolution_bitcast_fusion = f32[192,1024]{1,0:T(8,128)S(1)} fusion(bf16[192,8,2,192]{3,0,2,1:T(8,128)(2,1)} %bitcast.87, bf16[8,2,192,1024]{3,2,1,0:T(8,128)(2,1)} %bitcast.81), kind=kOutput, calls=%fused_computation.20 | convolution fusion | flops 1207959552 | bytes 8257536 | tf_op jit(solution)/shard_map/dot_general | solution.py:65
  59.1 0.0 copy-done.4
  59.1 0.0 copy-start.1
  59.1 0.0 slice-start.2
  59.1 5.3 %multiply_convert_fusion = (bf16[192,1024]{1,0:T(8,128)(2,1)S(1)}, f32[192,1024]{1,0:T(8,128)S(1)}) fusion(f32[192,1024]{1,0:T(8,128)S(1)} %convolution_bitcast_fusion, s32[1,192,1024]{2,1,0:T(8,128)S(1)} %copy-done.4, bf16[192,3072]{1,0:T(8,128)(2,1)S(1)} %reshape.95, bf16[1,1024,3072]{2,1,0:T(8,128)(2,1)} %param.12), kind=kOutput, calls=%fused_computation.39 | convolution fusion | flops 1210515456 | bytes 10223616 | tf_op jit(solution)/shard_map/dot_general | solution.py:67
  64.5 0.0 slice-done
  64.5 0.0 slice-done.1
  64.5 0.0 copy-done.1
  64.5 0.0 slice-start.3
  64.5 1.9 %fusion.30 = bf16[192,1024]{1,0:T(8,128)(2,1)S(1)} fusion(f32[192,1024]{1,0:T(8,128)S(1)} %convolution_bitcast_fusion, f32[192,1024]{1,0:T(8,128)S(1)} %get-tuple-element.18, bf16[192,8,2,192]{3,0,2,1:T(8,128)(2,1)S(1)} %bitcast.88, bf16[8,2,192,1024]{3,2,1,0:T(8,128)(2,1)S(1)} %bitcast.80), kind=kOutput, calls=%fused_computation.36 | convolution fusion | flops 1212088320 | bytes 9437184 | tf_op jit(solution)/shard_map/dot_general | solution.py:66
  66.5 2.2 %fusion = f32[192,3072]{1,0:T(8,128)S(1)} fusion(bf16[192,1024]{1,0:T(8,128)(2,1)S(1)} %get-tuple-element.8, bf16[1,3072,1024]{2,1,0:T(8,128)(2,1)S(1)} %bitcast.79), kind=kOutput, calls=%fused_computation.2 | convolution fusion | flops 1207959552 | bytes 9043968 | tf_op jit(solution)/shard_map/dot_general | solution.py:81
  68.7 0.0 slice-done.2
  68.7 0.0 slice-done.3
  68.7 2.2 %fusion.9 = bf16[192,3072]{1,0:T(8,128)(2,1)S(1)} fusion(f32[192,3072]{1,0:T(8,128)S(1)} %fusion, bf16[192,1024]{1,0:T(8,128)(2,1)S(1)} %fusion.30, bf16[1,3072,1024]{2,1,0:T(8,128)(2,1)S(1)} %bitcast.83), kind=kOutput, calls=%fused_computation.9 | convolution fusion | flops 1209139200 | bytes 10223616 | tf_op jit(solution)/shard_map/dot_general | solution.py:79
  70.9 1.9 %reshape.96 = bf16[2,96,8,2,192]{4,3,2,1,0:T(2,128)(2,1)S(1)} reshape(bf16[192,3072]{1,0:T(8,128)(2,1)S(1)} %fusion.9) | data formatting | bytes 2359296 | tf_op jit(solution)/shard_map/reshape | solution.py:82
  72.9 2.2 %fusion.37 = (bf16[2,96,8,1,192]{4,3,2,1,0:T(2,128)(2,1)S(1)}, bf16[2,96,8,1,192]{4,3,2,1,0:T(2,128)(2,1)S(1)}) fusion(bf16[2,96,8,2,192]{4,3,2,1,0:T(2,128)(2,1)S(1)} %reshape.96), kind=kLoop, calls=%fused_computation.52 | loop fusion | bytes 2359296 | tf_op jit(solution)/shard_map/slice | solution.py:84
  75.1 0.2 select_bitcast_fusion.2
  75.3 0.2 collective-permute-start.1
  75.5 2.1 %collective-permute-done.1 = bf16[2,96,8,192]{3,2,1,0:T(8,128)(2,1)S(1)} collective-permute-done((bf16[2,96,8,192]{3,2,1,0:T(8,128)(2,1)S(1)}, bf16[2,96,8,192]{3,2,1,0:T(8,128)(2,1)S(1)}, u32[]{:S(2)}, u32[]{:S(2)}) %collective-permute-start.1) | collective-permute-done | bytes 589856 | tf_op jit(solution)/shard_map/ppermute | solution.py:33
  77.7 0.3 fusion.31
  78.0 0.0 copy-start.2
  78.0 1.1 %copy.18 = bf16[2,8,96,192]{3,2,1,0:T(8,128)(2,1)} copy(bf16[2,8,96,192]{3,1,2,0:T(8,128)(2,1)S(1)} %fusion.31) | data formatting | bytes 1179648 | tf_op jit(solution)/shard_map/transpose | solution.py:87
  79.1 3.6 %all-to-all-start.1 = ((bf16[16,96,192]{2,1,0:T(8,128)(2,1)}), bf16[16,96,192]{2,1,0:T(8,128)(2,1)S(1)}, u32[]{:S(2)}, u32[]{:S(2)}) async-start(bf16[16,96,192]{2,1,0:T(8,128)(2,1)} %bitcast.25), calls=%async_computation.1 | async-start | bytes 1572864 | tf_op jit(solution)/shard_map/all_to_all | solution.py:89
  82.7 0.0 copy-done.2
  82.7 0.1 eq.19
  82.8 20.8 %all-to-all-done.1 = bf16[16,96,192]{2,1,0:T(8,128)(2,1)S(1)} async-done(((bf16[16,96,192]{2,1,0:T(8,128)(2,1)}), bf16[16,96,192]{2,1,0:T(8,128)(2,1)S(1)}, u32[]{:S(2)}, u32[]{:S(2)}) %all-to-all-start.1) | async-done | bytes 589856 | tf_op jit(solution)/shard_map/all_to_all | solution.py:89
  103.6 0.1 convert_reduce_fusion
  103.7 0.3 fusion.34
  104.0 0.9 fusion.23
  (7 shorter events, 0.0 us)
Async XLA Ops:
  0.0 0.8 copy-start
  0.0 3.5 %copy-start.3 = (f32[2,96]{1,0:T(2,128)S(1)}, f32[2,96]{1,0:T(2,128)}, u32[]{:S(2)}) copy-start(f32[2,96]{1,0:T(2,128)} %param.14) | copy-start | bytes 2308
  41.9 2.8 %collective-permute-start = (bf16[2,8,96,384]{3,2,1,0:T(8,128)(2,1)S(1)}, bf16[2,8,96,384]{3,2,1,0:T(8,128)(2,1)S(1)}, u32[]{:S(2)}, u32[]{:S(2)}) collective-permute-start(bf16[2,8,96,384]{3,2,1,0:T(8,128)(2,1)S(1)} %bitcast.84), channel_id=1, source_target_pairs={{0,1},{1,0},{2,3},{3,2},{4,5},{5,4},{6,7},{7,6},{8,9},{9,8},{10,11... | collective-permute-start | bytes 3538952 | tf_op jit(solution)/shard_map/ppermute | solution.py:33
  49.9 14.6 %slice-start = ((s8[6291456]{0:T(1024)(128)(4,1)}), s8[2097152]{0:T(1024)(128)(4,1)S(1)}, s32[]{:S(2)}) async-start(s8[6291456]{0:T(1024)(128)(4,1)} %bitcast.78), calls=%async_computation.2 | async-start | bytes 4194304
  54.2 4.9 %copy-start.4 = (s32[1,192,1024]{2,1,0:T(8,128)S(1)}, s32[1,192,1024]{2,1,0:T(8,128)}, u32[]{:S(2)}) copy-start(s32[1,192,1024]{2,1,0:T(8,128)} %param.15) | copy-start | bytes 2359300
  54.2 10.2 %slice-start.1 = ((s8[6291456]{0:T(1024)(128)(4,1)}), s8[4194304]{0:T(1024)(128)(4,1)S(1)}, s32[]{:S(2)}) async-start(s8[6291456]{0:T(1024)(128)(4,1)} %bitcast.78), calls=%async_computation.3 | async-start | bytes 8388608
  59.1 5.4 %copy-start.1 = (bf16[2,96,8,2,192]{4,1,0,3,2:T(8,128)(2,1)S(1)}, bf16[2,96,8,2,192]{4,1,0,3,2:T(8,128)(2,1)}, u32[]{:S(2)}) copy-start(bf16[2,96,8,2,192]{4,1,0,3,2:T(8,128)(2,1)} %copy.15) | copy-start | bytes 3538948
  59.1 9.6 %slice-start.2 = ((s8[6291456]{0:T(1024)(128)(4,1)}), s8[4194304]{0:T(1024)(128)(4,1)S(1)}, s32[]{:S(2)}) async-start(s8[6291456]{0:T(1024)(128)(4,1)} %bitcast.82), calls=%async_computation.4 | async-start | bytes 8388608
  64.5 4.2 %slice-start.3 = ((s8[6291456]{0:T(1024)(128)(4,1)}), s8[2097152]{0:T(1024)(128)(4,1)S(1)}, s32[]{:S(2)}) async-start(s8[6291456]{0:T(1024)(128)(4,1)} %bitcast.82), calls=%async_computation.5 | async-start | bytes 4194304
  75.3 2.4 %collective-permute-start.1 = (bf16[2,96,8,192]{3,2,1,0:T(8,128)(2,1)S(1)}, bf16[2,96,8,192]{3,2,1,0:T(8,128)(2,1)S(1)}, u32[]{:S(2)}, u32[]{:S(2)}) collective-permute-start(bf16[2,96,8,192]{3,2,1,0:T(8,128)(2,1)S(1)} %select_bitcast_fusion.2), channel_id=1, source_target_pairs={{0,1},{1,0},{2,3},{3,2},{4,5},{5,4},{6,7},{7,6},{8,9},{9,8},{10,11... | collective-permute-start | bytes 1769480 | tf_op jit(solution)/shard_map/ppermute | solution.py:33
  78.0 4.7 %copy-start.2 = (s32[2,96]{1,0:T(2,128)S(1)}, s32[2,96]{1,0:T(2,128)}, u32[]{:S(2)}) copy-start(s32[2,96]{1,0:T(2,128)} %param.13) | copy-start | bytes 2308
  79.1 24.5 %all-to-all-start.1 = ((bf16[16,96,192]{2,1,0:T(8,128)(2,1)}), bf16[16,96,192]{2,1,0:T(8,128)(2,1)S(1)}, u32[]{:S(2)}, u32[]{:S(2)}) async-start(bf16[16,96,192]{2,1,0:T(8,128)(2,1)} %bitcast.25), calls=%async_computation.1 | async-start | bytes 1572864 | tf_op jit(solution)/shard_map/all_to_all | solution.py:89

commit v11 on v8

--- a/solution.py
+++ b/solution.py
@@ -47,8 +47,12 @@
     weight_column = slot_weight.reshape(-1, 1)
     inv_keep = 1.0 / keep_rate
 
-    chosen = tokens[slot_list]
-    scaled = (weight_column * cotangent[slot_list].astype(jnp.float32)).astype(jnp.bfloat16)
+    one_hot = (slot_list[:, None] == jnp.arange(group_tokens, dtype=jnp.int32)[None, :]).astype(jnp.bfloat16)
+    rows = jnp.dot(
+        one_hot, jnp.concatenate([tokens, cotangent], axis=1), preferred_element_type=jnp.float32
+    )
+    chosen = rows[:, :local_width].astype(jnp.bfloat16)
+    scaled = (weight_column * rows[:, local_width:]).astype(jnp.bfloat16)
     slab = jnp.concatenate([chosen, scaled], axis=1).reshape(expert_total, 1, per_source, 2 * local_width)
     outgoing = jnp.broadcast_to(slab, (expert_total, chip_count, per_source, 2 * local_width))
     outgoing = outgoing.reshape(expert_total * chip_count, per_source, 2 * local_width)
@@ -90,7 +94,6 @@
     blocks = blocks.reshape(expert_count * chip_count, per_source, local_width)
     returned = lax.all_to_all(blocks, CROSS, split_axis=0, concat_axis=0, tiled=True)
     per_expert = returned.reshape(expert_total, chip_count, per_source, local_width).astype(jnp.float32).sum(1)
-    one_hot = (slot_list[:, None] == jnp.arange(group_tokens, dtype=jnp.int32)[None, :]).astype(jnp.bfloat16)
     token_sum = fold_slots(one_hot, per_expert.reshape(expert_total * per_source, local_width))
     return token_sum.astype(jnp.bfloat16)
 

time: 99.2 us -> 96.8 us (0.976)
  blocking collectives: 38.1 us -> 62.8 us
  waiting for transfers between devices: 23.4 us -> 1.91 us
  starting transfers between devices: 4.18 us -> 0.57 us
  local copies, waits for them, and re-layouts: 20.1 us -> 17.2 us
  matrix products: 10.7 us -> 11.7 us
    all_to_all x0 -> x1, blocking collectives: none -> 24.7 us  [body(): lax.all_to_all(blocks, CROSS, split_axis=0, concat_axis=0, tiled=True)]
    all_to_all x1 -> x0, waiting for transfers between devices: 21.5 us -> none  [body(): lax.all_to_all(blocks, CROSS, split_axis=0, concat_axis=0, tiled=True)]
    all_to_all x1 -> x0, starting transfers between devices: 3.61 us -> none  [body(): lax.all_to_all(blocks, CROSS, split_axis=0, concat_axis=0, tiled=True)]
    gather x2 -> x0, local copies, waits for them, and re-layouts: 2.67 us -> none  [the longest x1 1.67 us: body(): chosen = tokens[slot_list]]
    dot_general x0 -> x1, matrix products: none -> 1.07 us  [body(): jnp.dot(one_hot, jnp.concatenate([tokens, cotangent], axis=1), preferred_...]
    unnamed x21 -> x15, local copies, waits for them, and re-layouts: 11 us -> 11 us
  transfers between devices with their start and end apart: 3 -> 2, of which waited for: 2 -> 1; matrix products, arithmetic and copies ran while one was open for 9% -> 9% of each run, Pallas kernels for 0% -> 0%
where the time goes in v11:
time: 96.8 us; the launch traced here: 96.4 us
  blocking collectives  62.8 us (65%)
  local copies, waits for them, and re-layouts  17.2 us (18%)
  matrix products  11.7 us (12%)
  other arithmetic  1.97 us (2%)
  waiting for transfers between devices  1.91 us (2%)
    all_to_all x1, blocking collectives, body(): lax.all_to_all(outgoing, CROSS, split_axis=0, concat_axis=0, tiled=True)  38.1 us
    all_to_all x1, blocking collectives, body(): lax.all_to_all(blocks, CROSS, split_axis=0, concat_axis=0, tiled=True)  24.7 us
    unnamed x15, local copies, waits for them, and re-layouts  11 us
    slice x1, local copies, waits for them, and re-layouts, body(): keep_half = jnp.where(first, partial[:, :, :, 0], partial[:, :, :, 1])  2.24 us
    dot_general x1, matrix products, body(): lax.dot_general(grad_gate, gate_mat, back_dims, preferred_element_type=jn...  2.22 us
    dot_general x1, matrix products, body(): lax.dot_general(grad_up, up_mat, back_dims, preferred_element_type=jnp.fl...  2.2 us
    reshape x1, local copies, waits for them, and re-layouts, body(): partial.astype(jnp.bfloat16)  1.94 us
  transfers between devices with their start and end apart: 2, of which 1 were waited for; matrix products, arithmetic and copies ran while one was open for 9% of the time, Pallas kernels for 0%

profile of v11, /device:TPU:0, one launch (start us, length us, event | category | flops | bytes accessed | tf_op | source)
XLA Modules:
  0.0 96.4 jit_solution(9106462701775704339)
XLA Ops:
  0.0 0.8 eq.19
  0.8 0.8 mul.69
  1.5 1.1 %fusion.29 = f32[192,384]{1,0:T(8,128)S(1)} fusion(bf16[96,192]{1,0:T(8,128)(2,1)} %param.9, bf16[96,192]{1,0:T(8,128)(2,1)} %param.8, s32[192]{0:T(256)S(1)} %eq.19), kind=kOutput, calls=%fused_computation.46 | convolution fusion | flops 14321664 | bytes 369408 | tf_op jit(solution)/shard_map/dot_general | solution.py:51
  2.6 0.1 fusion.26
  2.8 0.1 pad_maximum_fusion.1
  2.9 0.1 broadcast_in_dim.9
  3.0 38.1 %all_to_all.10 = bf16[16,96,384]{2,1,0:T(8,128)(2,1)S(1)} all-to-all(bf16[16,96,384]{2,1,0:T(8,128)(2,1)S(1)} %bitcast.86), channel_id=1, replica_groups=mesh['expert'=2,'chip'=8,'core'=2] {'expert','chip'}, dimensions={0} | all-to-all | bytes 2359296 | tf_op jit(solution)/shard_map/all_to_all | solution.py:59
  41.1 0.0 collective-permute-start
  41.1 8.7 %copy.16 = bf16[1,1024,3072]{1,2,0:T(8,128)(2,1)} copy(bf16[1,1024,3072]{2,1,0:T(8,128)(2,1)} %param.12) | data formatting | bytes 12582912 | tf_op args[4]
  49.7 0.0 collective-permute-done
  49.7 0.0 slice-start.2
  49.7 0.2 select_bitcast_fusion.1
  49.9 0.0 slice-start.3
  50.0 0.9 fusion.11
  50.8 0.0 slice-start.4
  50.8 0.1 copy.15
  51.0 0.1 copy.17
  51.1 0.8 slice-done.2
  51.9 0.7 slice-done.3
  52.6 0.0 slice-start.5
  52.6 0.0 copy-start
  52.6 0.0 slice-start
  52.7 1.4 %convolution_bitcast_fusion = f32[192,1024]{1,0:T(8,128)S(1)} fusion(bf16[192,8,2,192]{3,0,2,1:T(8,128)(2,1)S(1)} %bitcast.89, bf16[8,2,192,1024]{3,2,1,0:T(8,128)(2,1)S(1)} %bitcast.80), kind=kOutput, calls=%fused_computation.15 | convolution fusion | flops 1207959552 | bytes 8257536 | tf_op jit(solution)/shard_map/dot_general | solution.py:70
  54.1 0.0 slice-done.4
  54.1 0.5 slice-done.5
  54.6 0.1 copy-done
  54.7 0.0 slice-start.1
  54.7 1.7 %multiply_convert_fusion = (bf16[192,1024]{1,0:T(8,128)(2,1)S(1)}, f32[192,1024]{1,0:T(8,128)S(1)}) fusion(f32[192,1024]{1,0:T(8,128)S(1)} %convolution_bitcast_fusion, s32[1,192,1024]{2,1,0:T(8,128)S(1)} %copy-done, bf16[192,8,2,192]{3,0,2,1:T(8,128)(2,1)S(1)} %bitcast.88, bf16[1024,8,2,192]{0,3,2,1:T(8,128)(2,1)S(1)} %bitcast.83), kind=kOutput, calls=%fused_computation.36 | convolution fusion | flops 1210515456 | bytes 10223616 | tf_op jit(solution)/shard_map/dot_general | solution.py:72
  56.4 0.0 slice-done
  56.4 0.2 slice-done.1
  56.6 1.9 %fusion.24 = bf16[192,1024]{1,0:T(8,128)(2,1)S(1)} fusion(f32[192,1024]{1,0:T(8,128)S(1)} %convolution_bitcast_fusion, f32[192,1024]{1,0:T(8,128)S(1)} %get-tuple-element.18, bf16[192,8,2,192]{3,0,2,1:T(8,128)(2,1)S(1)} %bitcast.90, bf16[8,2,192,1024]{3,2,1,0:T(8,128)(2,1)S(1)} %bitcast.77), kind=kOutput, calls=%fused_computation.33 | convolution fusion | flops 1212088320 | bytes 9437184 | tf_op jit(solution)/shard_map/dot_general | solution.py:71
  58.5 2.2 %fusion = f32[192,3072]{1,0:T(8,128)S(1)} fusion(bf16[192,1024]{1,0:T(8,128)(2,1)S(1)} %get-tuple-element.8, bf16[1,3072,1024]{2,1,0:T(8,128)(2,1)S(1)} %bitcast.76), kind=kOutput, calls=%fused_computation | convolution fusion | flops 1207959552 | bytes 9043968 | tf_op jit(solution)/shard_map/dot_general | solution.py:87
  60.7 2.2 %fusion.7 = bf16[192,3072]{1,0:T(8,128)(2,1)S(1)} fusion(f32[192,3072]{1,0:T(8,128)S(1)} %fusion, bf16[192,1024]{1,0:T(8,128)(2,1)S(1)} %fusion.24, bf16[1,3072,1024]{2,1,0:T(8,128)(2,1)S(1)} %bitcast.79), kind=kOutput, calls=%fused_computation.5 | convolution fusion | flops 1209139200 | bytes 10223616 | tf_op jit(solution)/shard_map/dot_general | solution.py:85
  63.0 1.9 %reshape.38 = bf16[2,96,8,2,192]{4,3,2,1,0:T(2,128)(2,1)S(1)} reshape(bf16[192,3072]{1,0:T(8,128)(2,1)S(1)} %fusion.7) | data formatting | bytes 2359296 | tf_op jit(solution)/shard_map/reshape | solution.py:88
  64.9 2.2 %fusion.37 = (bf16[2,96,8,1,192]{4,3,2,1,0:T(2,128)(2,1)S(1)}, bf16[2,96,8,1,192]{4,3,2,1,0:T(2,128)(2,1)S(1)}) fusion(bf16[2,96,8,2,192]{4,3,2,1,0:T(2,128)(2,1)S(1)} %reshape.38), kind=kLoop, calls=%fused_computation.54 | loop fusion | bytes 2359296 | tf_op jit(solution)/shard_map/slice | solution.py:90
  67.2 0.2 select_bitcast_fusion.2
  67.3 0.6 collective-permute-start.1
  67.9 1.9 %collective-permute-done.1 = bf16[2,96,8,192]{3,2,1,0:T(8,128)(2,1)S(1)} collective-permute-done((bf16[2,96,8,192]{3,2,1,0:T(8,128)(2,1)S(1)}, bf16[2,96,8,192]{3,2,1,0:T(8,128)(2,1)S(1)}, u32[]{:S(2)}, u32[]{:S(2)}) %collective-permute-start.1) | collective-permute-done | bytes 589856 | tf_op jit(solution)/shard_map/ppermute | solution.py:33
  69.8 0.3 fusion.25
  70.2 0.2 copy.20
  70.3 24.7 %all_to_all.11 = bf16[16,96,192]{2,1,0:T(8,128)(2,1)S(1)} all-to-all(bf16[16,96,192]{2,1,0:T(8,128)(2,1)S(1)} %bitcast.87), channel_id=1, replica_groups=mesh['expert'=2,'chip'=8,'core'=2] {'expert','chip'}, dimensions={0} | all-to-all | bytes 1179648 | tf_op jit(solution)/shard_map/all_to_all | solution.py:95
  95.0 0.1 convert_reduce_fusion
  95.2 0.3 fusion.28
  95.5 0.9 fusion.17
  (5 shorter events, 0.0 us)
Async XLA Ops:
  41.1 8.7 %collective-permute-start = (bf16[2,8,96,384]{3,2,1,0:T(8,128)(2,1)S(1)}, bf16[2,8,96,384]{3,2,1,0:T(8,128)(2,1)S(1)}, u32[]{:S(2)}, u32[]{:S(2)}) collective-permute-start(bf16[2,8,96,384]{3,2,1,0:T(8,128)(2,1)S(1)} %bitcast.84), channel_id=1, source_target_pairs={{0,1},{1,0},{2,3},{3,2},{4,5},{5,4},{6,7},{7,6},{8,9},{9,8},{10,11... | collective-permute-start | bytes 3538952 | tf_op jit(solution)/shard_map/ppermute | solution.py:33
  49.7 2.2 %slice-start.2 = ((s8[6291456]{0:T(1024)(128)(4,1)}), s8[4194304]{0:T(1024)(128)(4,1)S(1)}, s32[]{:S(2)}) async-start(s8[6291456]{0:T(1024)(128)(4,1)} %bitcast.78), calls=%async_computation.4 | async-start | bytes 8388608
  49.9 2.7 %slice-start.3 = ((s8[6291456]{0:T(1024)(128)(4,1)}), s8[2097152]{0:T(1024)(128)(4,1)S(1)}, s32[]{:S(2)}) async-start(s8[6291456]{0:T(1024)(128)(4,1)} %bitcast.78), calls=%async_computation.5 | async-start | bytes 4194304
  50.8 3.3 %slice-start.4 = ((s8[6291456]{0:T(1024)(128)(4,1)}), s8[4194304]{0:T(1024)(128)(4,1)S(1)}, s32[]{:S(2)}) async-start(s8[6291456]{0:T(1024)(128)(4,1)} %bitcast.81), calls=%async_computation.6 | async-start | bytes 8388608
  52.6 1.9 %slice-start.5 = ((s8[6291456]{0:T(1024)(128)(4,1)}), s8[2097152]{0:T(1024)(128)(4,1)S(1)}, s32[]{:S(2)}) async-start(s8[6291456]{0:T(1024)(128)(4,1)} %bitcast.81), calls=%async_computation.7 | async-start | bytes 4194304
  52.6 2.1 %copy-start = (s32[1,192,1024]{2,1,0:T(8,128)S(1)}, s32[1,192,1024]{2,1,0:T(8,128)}, u32[]{:S(2)}) copy-start(s32[1,192,1024]{2,1,0:T(8,128)} %param.15) | copy-start | bytes 2359300
  52.6 3.8 %slice-start = ((s8[6291456]{0:T(1024)(128)(4,1)}), s8[4194304]{0:T(1024)(128)(4,1)S(1)}, s32[]{:S(2)}) async-start(s8[6291456]{0:T(1024)(128)(4,1)} %bitcast.75), calls=%async_computation.2 | async-start | bytes 8388608
  54.7 1.9 %slice-start.1 = ((s8[6291456]{0:T(1024)(128)(4,1)}), s8[2097152]{0:T(1024)(128)(4,1)S(1)}, s32[]{:S(2)}) async-start(s8[6291456]{0:T(1024)(128)(4,1)} %bitcast.75), calls=%async_computation.3 | async-start | bytes 4194304
  67.3 2.5 %collective-permute-start.1 = (bf16[2,96,8,192]{3,2,1,0:T(8,128)(2,1)S(1)}, bf16[2,96,8,192]{3,2,1,0:T(8,128)(2,1)S(1)}, u32[]{:S(2)}, u32[]{:S(2)}) collective-permute-start(bf16[2,96,8,192]{3,2,1,0:T(8,128)(2,1)S(1)} %select_bitcast_fusion.2), channel_id=1, source_target_pairs={{0,1},{1,0},{2,3},{3,2},{4,5},{5,4},{6,7},{7,6},{8,9},{9,8},{10,11... | collective-permute-start | bytes 1769480 | tf_op jit(solution)/shard_map/ppermute | solution.py:33

commit v12 on v11

--- a/solution.py
+++ b/solution.py
@@ -61,20 +61,25 @@
     other = swap_cores(own)
     full = order_by_core(own, other, axis=2)
     part_inputs = full[..., :local_width]
-    part_cot = full[..., local_width:]
+    part_cot = full[..., local_width:].transpose(0, 3, 1, 2, 4).reshape(slot_count, model_width)
 
     gate_rows = gate_mat.reshape(chip_count, 2, local_width, local_ff)
     up_rows = up_mat.reshape(chip_count, 2, local_width, local_ff)
-    down_cols = down_mat.reshape(local_ff, chip_count, 2, local_width)
     fwd_dims = (((1, 2, 4), (0, 1, 2)), ((), ()))
     gate_pre = lax.dot_general(part_inputs, gate_rows, fwd_dims, preferred_element_type=jnp.float32)
     up_pre = lax.dot_general(part_inputs, up_rows, fwd_dims, preferred_element_type=jnp.float32)
-    grad_hidden = lax.dot_general(
-        part_cot, down_cols, (((1, 2, 4), (1, 2, 3)), ((), ())), preferred_element_type=jnp.float32
-    )
+    chunk = 1024 if model_width % 1024 == 0 else model_width
+    grad_hidden = None
+    for start in range(0, model_width, chunk):
+        piece = lax.dot_general(
+            part_cot[:, start:start + chunk],
+            down_mat[:, start:start + chunk],
+            (((1,), (1,)), ((), ())),
+            preferred_element_type=jnp.float32,
+        )
+        grad_hidden = piece if grad_hidden is None else grad_hidden + piece
     gate_pre = gate_pre.reshape(slot_count, local_ff)
     up_pre = up_pre.reshape(slot_count, local_ff)
-    grad_hidden = grad_hidden.reshape(slot_count, local_ff)
     activated, pullback = jax.vjp(gelu_tanh, gate_pre)
     grad_pre = grad_hidden * keep_mask[0].astype(jnp.float32) * inv_keep
     grad_up = (grad_pre * activated).astype(jnp.bfloat16)

time: 96.8 us -> 103 us (1.064)
  matrix products: 11.7 us -> 18.4 us
  local copies, waits for them, and re-layouts: 17.2 us -> 13.1 us
  waiting for transfers between devices: 1.91 us -> 5 us
  other arithmetic: 1.97 us -> 3.13 us
    unnamed x15 -> x12, local copies, waits for them, and re-layouts: 11 us -> 0.04 us
    dot_general x1 -> x3, matrix products: 1.7 us -> 8.28 us  [body(): lax.dot_general(part_cot[:, start:start + chunk], down_mat[:, start:start...]
    reshape x0 -> x1, local copies, waits for them, and re-layouts: none -> 4.18 us  [body(): full[..., local_width:].transpose(0, 3, 1, 2, 4)]
    ppermute x2, waiting for transfers between devices: 1.91 us -> 5 us  [swap_cores(): return lax.ppermute(values, 'core', [(0, 1), (1, 0)])]
    transpose x0 -> x1, local copies, waits for them, and re-layouts: none -> 2.76 us  [body(): full[..., local_width:].transpose(0, 3, 1, 2, 4)]
    transpose x0 -> x1, other arithmetic: none -> 2.01 us  [body(): full[..., local_width:].transpose(0, 3, 1, 2, 4)]
  transfers between devices with their start and end apart: 2 -> 2, of which waited for: 1 -> 2; matrix products, arithmetic and copies ran while one was open for 9% -> 0% of each run, Pallas kernels for 0% -> 0%
where the time goes in v12:
time: 103 us
  blocking collectives  62.5 us (61%)
  matrix products  18.4 us (18%)
  local copies, waits for them, and re-layouts  13.1 us (13%)
  waiting for transfers between devices  5 us (5%)
  other arithmetic  3.13 us (3%)
    all_to_all x1, blocking collectives, body(): lax.all_to_all(outgoing, CROSS, split_axis=0, concat_axis=0, tiled=True)  38.1 us
    all_to_all x1, blocking collectives, body(): lax.all_to_all(blocks, CROSS, split_axis=0, concat_axis=0, tiled=True)  24.5 us
    dot_general x3, matrix products, body(): lax.dot_general(part_cot[:, start:start + chunk], down_mat[:, start:start...  8.28 us
    ppermute x2, waiting for transfers between devices, swap_cores(): return lax.ppermute(values, 'core', [(0, 1), (1, 0)])  5 us
    reshape x1, local copies, waits for them, and re-layouts, body(): full[..., local_width:].transpose(0, 3, 1, 2, 4)  4.18 us
    transpose x1, local copies, waits for them, and re-layouts, body(): full[..., local_width:].transpose(0, 3, 1, 2, 4)  2.76 us
    dot_general x1, matrix products, body(): lax.dot_general(grad_gate, gate_mat, back_dims, preferred_element_type=jn...  2.26 us
    slice x1, local copies, waits for them, and re-layouts, body(): keep_half = jnp.where(first, partial[:, :, :, 0], partial[:, :, :, 1])  2.24 us
  transfers between devices with their start and end apart: 2, of which 2 were waited for; matrix products, arithmetic and copies ran while one was open for 0% of the time, Pallas kernels for 0%

profile of v12, /device:TPU:0, one launch (start us, length us, event | category | flops | bytes accessed | tf_op | source)
XLA Modules:
  0.0 102.6 jit_solution(12783958360164066774)
XLA Ops:
  0.0 0.8 eq.19
  0.8 0.8 mul.69
  1.5 1.1 %fusion.48 = f32[192,384]{1,0:T(8,128)S(1)} fusion(bf16[96,192]{1,0:T(8,128)(2,1)} %param.9, bf16[96,192]{1,0:T(8,128)(2,1)} %param.8, s32[192]{0:T(256)S(1)} %eq.19), kind=kOutput, calls=%fused_computation.56 | convolution fusion | flops 14321664 | bytes 369408 | tf_op jit(solution)/shard_map/dot_general | solution.py:51
  2.6 0.1 fusion.45
  2.8 0.1 pad_maximum_fusion.1
  2.9 0.1 broadcast_in_dim.9
  3.0 38.1 %all_to_all.10 = bf16[16,96,384]{2,1,0:T(8,128)(2,1)S(1)} all-to-all(bf16[16,96,384]{2,1,0:T(8,128)(2,1)S(1)} %bitcast.72), channel_id=1, replica_groups=mesh['expert'=2,'chip'=8,'core'=2] {'expert','chip'}, dimensions={0} | all-to-all | bytes 2359296 | tf_op jit(solution)/shard_map/all_to_all | solution.py:59
  41.1 0.0 collective-permute-start
  41.1 2.8 %collective-permute-done = bf16[2,8,96,384]{3,2,1,0:T(8,128)(2,1)S(1)} collective-permute-done((bf16[2,8,96,384]{3,2,1,0:T(8,128)(2,1)S(1)}, bf16[2,8,96,384]{3,2,1,0:T(8,128)(2,1)S(1)}, u32[]{:S(2)}, u32[]{:S(2)}) %collective-permute-start) | collective-permute-done | bytes 1179680 | tf_op jit(solution)/shard_map/ppermute | solution.py:33
  43.9 0.2 select_bitcast_fusion.1
  44.1 2.0 %fusion.17 = (bf16[2,96,8,2,192]{4,1,2,0,3:T(8,128)(2,1)S(1)}, bf16[2,96,8,2,192]{4,1,2,0,3:T(8,128)(2,1)}) fusion(bf16[2,8,1,96,384]{4,3,1,0,2:T(8,128)(2,1)S(1)} %get-tuple-element.13, bf16[2,8,1,96,384]{4,3,1,0,2:T(8,128)(2,1)S(1)} %get-tuple-element.14), kind=kLoop, calls=%fused_computation.15 | loop fusion | flops 4718592 | bytes 4718592 | tf_op jit(solution)/shard_map/transpose | solution.py:64
  46.1 0.0 slice-start.2
  46.1 2.8 %copy.14 = bf16[2,96,8,2,192]{4,3,2,1,0:T(2,128)(2,1)} copy(bf16[2,96,8,2,192]{4,1,2,0,3:T(8,128)(2,1)S(1)} %get-tuple-element.11) | data formatting | bytes 2359296 | tf_op jit(solution)/shard_map/transpose | solution.py:64
  48.9 4.2 %reshape.39 = bf16[192,3072]{1,0:T(8,128)(2,1)S(1)} reshape(bf16[2,96,8,2,192]{4,3,2,1,0:T(2,128)(2,1)} %copy.14) | data formatting | bytes 2359296 | tf_op jit(solution)/shard_map/reshape | solution.py:64
  53.1 0.0 slice-start.3
  53.1 2.6 %fusion.10 = f32[192,1024]{1,0:T(8,128)S(1)} fusion(bf16[1024,3072]{1,0:T(8,128)(2,1)} %bitcast.76, bf16[192,3072]{1,0:T(8,128)(2,1)S(1)} %reshape.39), kind=kOutput, calls=%fused_computation.8 | convolution fusion | flops 402653184 | bytes 3276800 | tf_op jit(solution)/shard_map/dot_general | solution.py:74
  55.7 0.0 copy-start
  55.7 2.6 %fusion.12 = f32[192,1024]{1,0:T(8,128)S(1)} fusion(bf16[1024,3072]{1,0:T(8,128)(2,1)} %bitcast.77, bf16[192,3072]{1,0:T(8,128)(2,1)S(1)} %reshape.39), kind=kOutput, calls=%fused_computation.10 | convolution fusion | flops 402653184 | bytes 3276800 | tf_op jit(solution)/shard_map/dot_general | solution.py:74
  58.3 0.0 copy-done
  58.3 0.0 slice-start
  58.3 0.1 copy.15
  58.4 0.0 slice-done.2
  58.4 0.0 slice-done.3
  58.4 0.0 copy-start.1
  58.5 0.0 slice-start.1
  58.5 1.5 %convolution_bitcast_fusion = f32[192,1024]{1,0:T(8,128)S(1)} fusion(bf16[192,8,2,192]{3,0,2,1:T(8,128)(2,1)S(1)} %bitcast.74, bf16[8,2,192,1024]{3,2,1,0:T(8,128)(2,1)S(1)} %bitcast.69), kind=kOutput, calls=%fused_computation.21 | convolution fusion | flops 1207959552 | bytes 8257536 | tf_op jit(solution)/shard_map/dot_general | solution.py:69
  59.9 0.0 copy-done.1
  59.9 3.1 %multiply_convert_fusion = (bf16[192,1024]{1,0:T(8,128)(2,1)S(1)}, f32[192,1024]{1,0:T(8,128)S(1)}) fusion(f32[192,1024]{1,0:T(8,128)S(1)} %convolution_bitcast_fusion, s32[1,192,1024]{2,1,0:T(8,128)S(1)} %copy-done.1, f32[192,1024]{1,0:T(8,128)S(1)} %fusion.10, f32[192,1024]{1,0:T(8,128)S(1)} %fusion.12, bf16[1024,3072]{1,0:T(8,128)(2,1)} %bitcast.78, ...), kind=kOutput, calls=%fused_computation.43 | convolution fusion | flops 405602304 | bytes 6815744 | tf_op jit(solution)/shard_map/dot_general | solution.py:74
  63.1 0.0 slice-done
  63.1 0.0 slice-done.1
  63.1 2.0 %fusion.40 = bf16[192,1024]{1,0:T(8,128)(2,1)S(1)} fusion(f32[192,1024]{1,0:T(8,128)S(1)} %convolution_bitcast_fusion, f32[192,1024]{1,0:T(8,128)S(1)} %get-tuple-element.18, bf16[192,8,2,192]{3,0,2,1:T(8,128)(2,1)S(1)} %bitcast.75, bf16[8,2,192,1024]{3,2,1,0:T(8,128)(2,1)S(1)} %bitcast.66), kind=kOutput, calls=%fused_computation.40 | convolution fusion | flops 1212088320 | bytes 9437184 | tf_op jit(solution)/shard_map/dot_general | solution.py:70
  65.1 2.2 %fusion = f32[192,3072]{1,0:T(8,128)S(1)} fusion(bf16[192,1024]{1,0:T(8,128)(2,1)S(1)} %get-tuple-element.8, bf16[1,3072,1024]{2,1,0:T(8,128)(2,1)S(1)} %bitcast.65), kind=kOutput, calls=%fused_computation | convolution fusion | flops 1207959552 | bytes 9043968 | tf_op jit(solution)/shard_map/dot_general | solution.py:92
  67.3 2.3 %fusion.7 = bf16[192,3072]{1,0:T(8,128)(2,1)S(1)} fusion(f32[192,3072]{1,0:T(8,128)S(1)} %fusion, bf16[192,1024]{1,0:T(8,128)(2,1)S(1)} %fusion.40, bf16[1,3072,1024]{2,1,0:T(8,128)(2,1)S(1)} %bitcast.68), kind=kOutput, calls=%fused_computation.5 | convolution fusion | flops 1209139200 | bytes 10223616 | tf_op jit(solution)/shard_map/dot_general | solution.py:90
  69.6 1.9 %reshape.40 = bf16[2,96,8,2,192]{4,3,2,1,0:T(2,128)(2,1)S(1)} reshape(bf16[192,3072]{1,0:T(8,128)(2,1)S(1)} %fusion.7) | data formatting | bytes 2359296 | tf_op jit(solution)/shard_map/reshape | solution.py:93
  71.5 2.2 %fusion.56 = (bf16[2,96,8,1,192]{4,3,2,1,0:T(2,128)(2,1)S(1)}, bf16[2,96,8,1,192]{4,3,2,1,0:T(2,128)(2,1)S(1)}) fusion(bf16[2,96,8,2,192]{4,3,2,1,0:T(2,128)(2,1)S(1)} %reshape.40), kind=kLoop, calls=%fused_computation.64 | loop fusion | bytes 2359296 | tf_op jit(solution)/shard_map/slice | solution.py:95
  73.8 0.2 select_bitcast_fusion.2
  73.9 0.2 collective-permute-start.1
  74.1 2.2 %collective-permute-done.1 = bf16[2,96,8,192]{3,2,1,0:T(8,128)(2,1)S(1)} collective-permute-done((bf16[2,96,8,192]{3,2,1,0:T(8,128)(2,1)S(1)}, bf16[2,96,8,192]{3,2,1,0:T(8,128)(2,1)S(1)}, u32[]{:S(2)}, u32[]{:S(2)}) %collective-permute-start.1) | collective-permute-done | bytes 589856 | tf_op jit(solution)/shard_map/ppermute | solution.py:33
  76.3 0.3 fusion.41
  76.6 0.2 copy.18
  76.8 24.5 %all_to_all.11 = bf16[16,96,192]{2,1,0:T(8,128)(2,1)S(1)} all-to-all(bf16[16,96,192]{2,1,0:T(8,128)(2,1)S(1)} %bitcast.73), channel_id=1, replica_groups=mesh['expert'=2,'chip'=8,'core'=2] {'expert','chip'}, dimensions={0} | all-to-all | bytes 1179648 | tf_op jit(solution)/shard_map/all_to_all | solution.py:100
  101.2 0.1 convert_reduce_fusion
  101.4 0.3 fusion.47
  101.7 0.9 fusion.33
  (4 shorter events, 0.0 us)
Async XLA Ops:
  41.1 2.8 %collective-permute-start = (bf16[2,8,96,384]{3,2,1,0:T(8,128)(2,1)S(1)}, bf16[2,8,96,384]{3,2,1,0:T(8,128)(2,1)S(1)}, u32[]{:S(2)}, u32[]{:S(2)}) collective-permute-start(bf16[2,8,96,384]{3,2,1,0:T(8,128)(2,1)S(1)} %bitcast.70), channel_id=1, source_target_pairs={{0,1},{1,0},{2,3},{3,2},{4,5},{5,4},{6,7},{7,6},{8,9},{9,8},{10,11... | collective-permute-start | bytes 3538952 | tf_op jit(solution)/shard_map/ppermute | solution.py:33
  46.1 12.3 %slice-start.2 = ((s8[6291456]{0:T(1024)(128)(4,1)}), s8[2097152]{0:T(1024)(128)(4,1)S(1)}, s32[]{:S(2)}) async-start(s8[6291456]{0:T(1024)(128)(4,1)} %bitcast.67), calls=%async_computation.4 | async-start | bytes 4194304
  53.1 5.3 %slice-start.3 = ((s8[6291456]{0:T(1024)(128)(4,1)}), s8[4194304]{0:T(1024)(128)(4,1)S(1)}, s32[]{:S(2)}) async-start(s8[6291456]{0:T(1024)(128)(4,1)} %bitcast.67), calls=%async_computation.5 | async-start | bytes 8388608
  55.7 2.6 %copy-start = (bf16[2,96,8,2,192]{4,1,2,0,3:T(8,128)(2,1)S(1)}, bf16[2,96,8,2,192]{4,1,2,0,3:T(8,128)(2,1)}, u32[]{:S(2)}) copy-start(bf16[2,96,8,2,192]{4,1,2,0,3:T(8,128)(2,1)} %get-tuple-element.12) | copy-start | bytes 3538948
  58.3 4.8 %slice-start = ((s8[6291456]{0:T(1024)(128)(4,1)}), s8[4194304]{0:T(1024)(128)(4,1)S(1)}, s32[]{:S(2)}) async-start(s8[6291456]{0:T(1024)(128)(4,1)} %bitcast.64), calls=%async_computation.2 | async-start | bytes 8388608
  58.4 1.5 %copy-start.1 = (s32[1,192,1024]{2,1,0:T(8,128)S(1)}, s32[1,192,1024]{2,1,0:T(8,128)}, u32[]{:S(2)}) copy-start(s32[1,192,1024]{2,1,0:T(8,128)} %param.15) | copy-start | bytes 2359300
  58.5 4.6 %slice-start.1 = ((s8[6291456]{0:T(1024)(128)(4,1)}), s8[2097152]{0:T(1024)(128)(4,1)S(1)}, s32[]{:S(2)}) async-start(s8[6291456]{0:T(1024)(128)(4,1)} %bitcast.64), calls=%async_computation.3 | async-start | bytes 4194304
  73.9 2.4 %collective-permute-start.1 = (bf16[2,96,8,192]{3,2,1,0:T(8,128)(2,1)S(1)}, bf16[2,96,8,192]{3,2,1,0:T(8,128)(2,1)S(1)}, u32[]{:S(2)}, u32[]{:S(2)}) collective-permute-start(bf16[2,96,8,192]{3,2,1,0:T(8,128)(2,1)S(1)} %select_bitcast_fusion.2), channel_id=1, source_target_pairs={{0,1},{1,0},{2,3},{3,2},{4,5},{5,4},{6,7},{7,6},{8,9},{9,8},{10,11... | collective-permute-start | bytes 1769480 | tf_op jit(solution)/shard_map/ppermute | solution.py:33

commit v13 on v11

--- a/solution.py
+++ b/solution.py
@@ -16,7 +16,7 @@
 def fold_slots(one_hot, slot_values):
     high_part = slot_values.astype(jnp.bfloat16)
     low_part = (slot_values - high_part.astype(jnp.float32)).astype(jnp.bfloat16)
-    dims = (((0,), (0,)), ((), ()))
+    dims = (((0, 1), (0, 1)), ((), ()))
     return lax.dot_general(one_hot, high_part, dims, preferred_element_type=jnp.float32) + lax.dot_general(
         one_hot, low_part, dims, preferred_element_type=jnp.float32
     )
@@ -85,16 +85,22 @@
     partial = lax.dot_general(
         grad_gate, gate_mat, back_dims, preferred_element_type=jnp.float32
     ) + lax.dot_general(grad_up, up_mat, back_dims, preferred_element_type=jnp.float32)
-    partial = partial.astype(jnp.bfloat16).reshape(expert_count, per_source, chip_count, 2, local_width)
+    half = per_source // 2
+    partial = partial.astype(jnp.bfloat16).reshape(expert_count, 2, half, model_width)
     first = lax.axis_index("core") == 0
-    keep_half = jnp.where(first, partial[:, :, :, 0], partial[:, :, :, 1])
-    send_half = jnp.where(first, partial[:, :, :, 1], partial[:, :, :, 0])
-    chip_sum = keep_half.astype(jnp.float32) + swap_cores(send_half).astype(jnp.float32)
-    blocks = chip_sum.astype(jnp.bfloat16).transpose(0, 2, 1, 3)
-    blocks = blocks.reshape(expert_count * chip_count, per_source, local_width)
+    keep_rows = jnp.where(first, partial[:, 0], partial[:, 1])
+    send_rows = jnp.where(first, partial[:, 1], partial[:, 0])
+    chip_sum = keep_rows.astype(jnp.float32) + swap_cores(send_rows).astype(jnp.float32)
+    blocks = chip_sum.astype(jnp.bfloat16).reshape(expert_count, half, chip_count, 2 * local_width)
+    blocks = blocks.transpose(0, 2, 1, 3).reshape(expert_count * chip_count, half, 2 * local_width)
     returned = lax.all_to_all(blocks, CROSS, split_axis=0, concat_axis=0, tiled=True)
-    per_expert = returned.reshape(expert_total, chip_count, per_source, local_width).astype(jnp.float32).sum(1)
-    token_sum = fold_slots(one_hot, per_expert.reshape(expert_total * per_source, local_width))
+    per_expert = returned.reshape(expert_total, chip_count, half, 2 * local_width).astype(jnp.float32).sum(1)
+    row_hot = one_hot.reshape(expert_total, 2, half, group_tokens)
+    own_hot = jnp.where(first, row_hot[:, 0], row_hot[:, 1])
+    chip_tokens = fold_slots(own_hot, per_expert)
+    keep_cols = jnp.where(first, chip_tokens[:, :local_width], chip_tokens[:, local_width:])
+    send_cols = jnp.where(first, chip_tokens[:, local_width:], chip_tokens[:, :local_width])
+    token_sum = keep_cols + swap_cores(send_cols)
     return token_sum.astype(jnp.bfloat16)
 
 

time: 96.8 us -> 90.4 us (0.934)
  blocking collectives: 62.8 us -> 38.1 us
  waiting for transfers between devices: 1.91 us -> 19.7 us
  starting transfers between devices: 0.57 us -> 4.22 us
  local copies, waits for them, and re-layouts: 17.2 us -> 14 us
    all_to_all x1 -> x0, blocking collectives: 24.7 us -> none  [body(): lax.all_to_all(blocks, CROSS, split_axis=0, concat_axis=0, tiled=True)]
    all_to_all x0 -> x1, waiting for transfers between devices: none -> 16.8 us  [body(): lax.all_to_all(blocks, CROSS, split_axis=0, concat_axis=0, tiled=True)]
    all_to_all x0 -> x1, starting transfers between devices: none -> 3.58 us  [body(): lax.all_to_all(blocks, CROSS, split_axis=0, concat_axis=0, tiled=True)]
    slice x1 -> x0, local copies, waits for them, and re-layouts: 2.24 us -> none  [body(): keep_half = jnp.where(first, partial[:, :, :, 0], partial[:, :, :, 1])]
    reshape x1 -> x0, local copies, waits for them, and re-layouts: 1.94 us -> none  [body(): partial.astype(jnp.bfloat16)]
    convert_element_type x1 -> x3, other arithmetic: 0.02 us -> 1.03 us  [the longest x1 0.72 us: body(): return token_sum.astype(jnp.bfloat16)]
    ppermute x2 -> x3, waiting for transfers between devices: 1.91 us -> 2.92 us  [swap_cores(): return lax.ppermute(values, 'core', [(0, 1), (1, 0)])]
    unnamed x15 -> x18, local copies, waits for them, and re-layouts: 11 us -> 11.1 us
  transfers between devices with their start and end apart: 2 -> 4, of which waited for: 1 -> 3; matrix products, arithmetic and copies ran while one was open for 9% -> 10% of each run, Pallas kernels for 0% -> 0%
where the time goes in v13:
time: 90.4 us; the launch traced here: 89.8 us
  blocking collectives  38.1 us (42%)
  waiting for transfers between devices  19.7 us (22%)
  local copies, waits for them, and re-layouts  14 us (15%)
  matrix products  11 us (12%)
  starting transfers between devices  4.22 us (5%)
  other arithmetic  2.58 us (3%)
    all_to_all x1, blocking collectives, body(): lax.all_to_all(outgoing, CROSS, split_axis=0, concat_axis=0, tiled=True)  38.1 us
    all_to_all x1, waiting for transfers between devices, body(): lax.all_to_all(blocks, CROSS, split_axis=0, concat_axis=0, tiled=True)  16.8 us
    unnamed x18, local copies, waits for them, and re-layouts  11.1 us
    all_to_all x1, starting transfers between devices, body(): lax.all_to_all(blocks, CROSS, split_axis=0, concat_axis=0, tiled=True)  3.58 us
    ppermute x3, waiting for transfers between devices, swap_cores(): return lax.ppermute(values, 'core', [(0, 1), (1, 0)])  2.92 us
    dot_general x1, matrix products, body(): lax.dot_general(grad_gate, gate_mat, back_dims, preferred_element_type=jn...  2.22 us
    dot_general x1, matrix products, body(): lax.dot_general(grad_up, up_mat, back_dims, preferred_element_type=jnp.fl...  2.2 us
    dot_general x1, matrix products, body(): lax.dot_general(part_inputs, up_rows, fwd_dims, preferred_element_type=jn...  1.92 us
  transfers between devices with their start and end apart: 4, of which 3 were waited for; matrix products, arithmetic and copies ran while one was open for 10% of the time, Pallas kernels for 0%

profile of v13, /device:TPU:0, one launch (start us, length us, event | category | flops | bytes accessed | tf_op | source)
XLA Modules:
  0.0 89.8 jit_solution(9495602629253608091)
XLA Ops:
  0.0 0.8 eq.33
  0.8 0.8 mul.69
  1.5 1.1 %fusion.27 = f32[192,384]{1,0:T(8,128)S(1)} fusion(bf16[96,192]{1,0:T(8,128)(2,1)} %param.9, bf16[96,192]{1,0:T(8,128)(2,1)} %param.8, s32[192]{0:T(256)S(1)} %eq.33), kind=kOutput, calls=%fused_computation.49 | convolution fusion | flops 14321664 | bytes 369408 | tf_op jit(solution)/shard_map/dot_general | solution.py:51
  2.6 0.1 fusion.25
  2.8 0.1 pad_maximum_fusion.1
  2.9 0.1 broadcast_in_dim.9
  3.0 38.1 %all_to_all.10 = bf16[16,96,384]{2,1,0:T(8,128)(2,1)S(1)} all-to-all(bf16[16,96,384]{2,1,0:T(8,128)(2,1)S(1)} %bitcast.109), channel_id=1, replica_groups=mesh['expert'=2,'chip'=8,'core'=2] {'expert','chip'}, dimensions={0} | all-to-all | bytes 2359296 | tf_op jit(solution)/shard_map/all_to_all | solution.py:59
  41.1 0.0 collective-permute-start
  41.1 8.7 %copy.26 = bf16[1,1024,3072]{1,2,0:T(8,128)(2,1)} copy(bf16[1,1024,3072]{2,1,0:T(8,128)(2,1)} %param.12) | data formatting | bytes 12582912 | tf_op args[4]
  49.7 0.0 collective-permute-done
  49.7 0.2 select_bitcast_fusion.1
  50.0 0.0 slice-start.3
  50.0 0.9 fusion.11
  50.8 0.0 slice-start.4
  50.8 0.1 copy.27
  51.0 0.1 copy.25
  51.1 0.8 slice-done.2
  51.9 0.7 slice-done.3
  52.7 1.5 %convolution_bitcast_fusion = f32[192,1024]{1,0:T(8,128)S(1)} fusion(bf16[192,8,2,192]{3,0,2,1:T(8,128)(2,1)S(1)} %bitcast.112, bf16[8,2,192,1024]{3,2,1,0:T(8,128)(2,1)S(1)} %bitcast.103), kind=kOutput, calls=%fused_computation.12 | convolution fusion | flops 1207959552 | bytes 8257536 | tf_op jit(solution)/shard_map/dot_general | solution.py:70
  54.1 0.0 slice-done.4
  54.1 0.5 slice-done.5
  54.6 0.1 copy-done.1
  54.7 1.7 %multiply_convert_fusion = (bf16[192,1024]{1,0:T(8,128)(2,1)S(1)}, f32[192,1024]{1,0:T(8,128)S(1)}) fusion(f32[192,1024]{1,0:T(8,128)S(1)} %convolution_bitcast_fusion, s32[1,192,1024]{2,1,0:T(8,128)S(1)} %copy-done.1, bf16[192,8,2,192]{3,0,2,1:T(8,128)(2,1)S(1)} %bitcast.114, bf16[1024,8,2,192]{0,3,2,1:T(8,128)(2,1)S(1)} %bitcast.106), kind=kOutput, calls=%fused_computation.35 | convolution fusion | flops 1210515456 | bytes 10223616 | tf_op jit(solution)/shard_map/dot_general | solution.py:72
  56.4 0.0 slice-done
  56.4 0.2 slice-done.1
  56.6 1.9 %fusion.24 = bf16[192,1024]{1,0:T(8,128)(2,1)S(1)} fusion(f32[192,1024]{1,0:T(8,128)S(1)} %convolution_bitcast_fusion, f32[192,1024]{1,0:T(8,128)S(1)} %get-tuple-element.14, bf16[192,8,2,192]{3,0,2,1:T(8,128)(2,1)S(1)} %bitcast.113, bf16[8,2,192,1024]{3,2,1,0:T(8,128)(2,1)S(1)} %bitcast.100), kind=kOutput, calls=%fused_computation.34 | convolution fusion | flops 1212088320 | bytes 9437184 | tf_op jit(solution)/shard_map/dot_general | solution.py:71
  58.5 2.2 %fusion = f32[192,3072]{1,0:T(8,128)S(1)} fusion(bf16[192,1024]{1,0:T(8,128)(2,1)S(1)} %get-tuple-element.8, bf16[1,3072,1024]{2,1,0:T(8,128)(2,1)S(1)} %bitcast.99), kind=kOutput, calls=%fused_computation | convolution fusion | flops 1207959552 | bytes 9043968 | tf_op jit(solution)/shard_map/dot_general | solution.py:87
  60.8 2.2 %fusion.7 = bf16[192,3072]{1,0:T(8,128)(2,1)S(1)} fusion(f32[192,3072]{1,0:T(8,128)S(1)} %fusion, bf16[192,1024]{1,0:T(8,128)(2,1)S(1)} %fusion.24, bf16[1,3072,1024]{2,1,0:T(8,128)(2,1)S(1)} %bitcast.102), kind=kOutput, calls=%fused_computation.5 | convolution fusion | flops 1209139200 | bytes 10223616 | tf_op jit(solution)/shard_map/dot_general | solution.py:85
  63.0 0.1 select_bitcast_fusion.2
  63.0 0.6 collective-permute-start.1
  63.6 1.6 %collective-permute-done.1 = bf16[2,48,3072]{2,1,0:T(8,128)(2,1)S(1)} collective-permute-done((bf16[2,48,3072]{2,1,0:T(8,128)(2,1)S(1)}, bf16[2,48,3072]{2,1,0:T(8,128)(2,1)S(1)}, u32[]{:S(2)}, u32[]{:S(2)}) %collective-permute-start.1) | collective-permute-done | bytes 589856 | tf_op jit(solution)/shard_map/ppermute | solution.py:33
  65.2 0.2 fusion.16
  65.5 0.1 copy.36
  65.6 0.0 copy-start
  65.6 0.1 bitcast_bitcast_fusion
  65.6 0.9 copy.30
  66.5 3.6 %all-to-all-start.1 = ((bf16[16,48,384]{2,1,0:T(8,128)(2,1)}), bf16[16,48,384]{2,1,0:T(8,128)(2,1)S(1)}, u32[]{:S(2)}, u32[]{:S(2)}) async-start(bf16[16,48,384]{2,1,0:T(8,128)(2,1)} %bitcast.27), calls=%async_computation.1 | async-start | bytes 1179648 | tf_op jit(solution)/shard_map/all_to_all | solution.py:96
  70.1 0.0 copy-done
  70.1 0.1 eq.29
  70.2 0.1 fusion.26
  70.3 16.8 %all-to-all-done.1 = bf16[16,48,384]{2,1,0:T(8,128)(2,1)S(1)} async-done(((bf16[16,48,384]{2,1,0:T(8,128)(2,1)}), bf16[16,48,384]{2,1,0:T(8,128)(2,1)S(1)}, u32[]{:S(2)}, u32[]{:S(2)}) %all-to-all-start.1) | async-done | bytes 589856 | tf_op jit(solution)/shard_map/all_to_all | solution.py:96
  87.1 0.1 convert_reduce_fusion
  87.2 0.2 convolution_bitcast_fusion.3
  87.4 0.2 fusion.17
  87.6 0.1 slice_select_fusion
  87.7 0.1 collective-permute-start.2
  87.8 1.3 %collective-permute-done.2 = f32[96,192]{1,0:T(8,128)S(1)} collective-permute-done((f32[96,192]{1,0:T(8,128)S(1)}, f32[96,192]{1,0:T(8,128)S(1)}, u32[]{:S(2)}, u32[]{:S(2)}) %collective-permute-start.2) | collective-permute-done | bytes 73760 | tf_op jit(solution)/shard_map/ppermute | solution.py:33
  89.1 0.7 add_convert_fusion
  (10 shorter events, 0.0 us)
Async XLA Ops:
  41.1 8.7 %collective-permute-start = (bf16[2,8,96,384]{3,2,1,0:T(8,128)(2,1)S(1)}, bf16[2,8,96,384]{3,2,1,0:T(8,128)(2,1)S(1)}, u32[]{:S(2)}, u32[]{:S(2)}) collective-permute-start(bf16[2,8,96,384]{3,2,1,0:T(8,128)(2,1)S(1)} %bitcast.107), channel_id=1, source_target_pairs={{0,1},{1,0},{2,3},{3,2},{4,5},{5,4},{6,7},{7,6},{8,9},{9,8},{10,11... | collective-permute-start | bytes 3538952 | tf_op jit(solution)/shard_map/ppermute | solution.py:33
  49.7 2.2 %slice-start.2 = ((s8[6291456]{0:T(1024)(128)(4,1)}), s8[4194304]{0:T(1024)(128)(4,1)S(1)}, s32[]{:S(2)}) async-start(s8[6291456]{0:T(1024)(128)(4,1)} %bitcast.101), calls=%async_computation.4 | async-start | bytes 8388608
  50.0 2.7 %slice-start.3 = ((s8[6291456]{0:T(1024)(128)(4,1)}), s8[2097152]{0:T(1024)(128)(4,1)S(1)}, s32[]{:S(2)}) async-start(s8[6291456]{0:T(1024)(128)(4,1)} %bitcast.101), calls=%async_computation.5 | async-start | bytes 4194304
  50.8 3.3 %slice-start.4 = ((s8[6291456]{0:T(1024)(128)(4,1)}), s8[4194304]{0:T(1024)(128)(4,1)S(1)}, s32[]{:S(2)}) async-start(s8[6291456]{0:T(1024)(128)(4,1)} %bitcast.104), calls=%async_computation.6 | async-start | bytes 8388608
  52.7 1.9 %slice-start.5 = ((s8[6291456]{0:T(1024)(128)(4,1)}), s8[2097152]{0:T(1024)(128)(4,1)S(1)}, s32[]{:S(2)}) async-start(s8[6291456]{0:T(1024)(128)(4,1)} %bitcast.104), calls=%async_computation.7 | async-start | bytes 4194304
  52.7 2.1 %copy-start.1 = (s32[1,192,1024]{2,1,0:T(8,128)S(1)}, s32[1,192,1024]{2,1,0:T(8,128)}, u32[]{:S(2)}) copy-start(s32[1,192,1024]{2,1,0:T(8,128)} %param.15) | copy-start | bytes 2359300
  52.7 3.8 %slice-start = ((s8[6291456]{0:T(1024)(128)(4,1)}), s8[4194304]{0:T(1024)(128)(4,1)S(1)}, s32[]{:S(2)}) async-start(s8[6291456]{0:T(1024)(128)(4,1)} %bitcast.98), calls=%async_computation.2 | async-start | bytes 8388608
  54.7 1.9 %slice-start.1 = ((s8[6291456]{0:T(1024)(128)(4,1)}), s8[2097152]{0:T(1024)(128)(4,1)S(1)}, s32[]{:S(2)}) async-start(s8[6291456]{0:T(1024)(128)(4,1)} %bitcast.98), calls=%async_computation.3 | async-start | bytes 4194304
  63.0 2.2 %collective-permute-start.1 = (bf16[2,48,3072]{2,1,0:T(8,128)(2,1)S(1)}, bf16[2,48,3072]{2,1,0:T(8,128)(2,1)S(1)}, u32[]{:S(2)}, u32[]{:S(2)}) collective-permute-start(bf16[2,48,3072]{2,1,0:T(8,128)(2,1)S(1)} %select_bitcast_fusion.2), channel_id=1, source_target_pairs={{0,1},{1,0},{2,3},{3,2},{4,5},{5,4},{6,7},{7,6},{8,9},{9,8},{10,11... | collective-permute-start | bytes 1769480 | tf_op jit(solution)/shard_map/ppermute | solution.py:33
  65.6 4.6 %copy-start = (s32[2,96]{1,0:T(2,128)S(1)}, s32[2,96]{1,0:T(2,128)}, u32[]{:S(2)}) copy-start(s32[2,96]{1,0:T(2,128)} %param.13) | copy-start | bytes 2308
  66.5 20.6 %all-to-all-start.1 = ((bf16[16,48,384]{2,1,0:T(8,128)(2,1)}), bf16[16,48,384]{2,1,0:T(8,128)(2,1)S(1)}, u32[]{:S(2)}, u32[]{:S(2)}) async-start(bf16[16,48,384]{2,1,0:T(8,128)(2,1)} %bitcast.27), calls=%async_computation.1 | async-start | bytes 1179648 | tf_op jit(solution)/shard_map/all_to_all | solution.py:96
  87.7 1.4 %collective-permute-start.2 = (f32[96,192]{1,0:T(8,128)S(1)}, f32[96,192]{1,0:T(8,128)S(1)}, u32[]{:S(2)}, u32[]{:S(2)}) collective-permute-start(f32[96,192]{1,0:T(8,128)S(1)} %slice_select_fusion), channel_id=1, source_target_pairs={{0,1},{1,0},{2,3},{3,2},{4,5},{5,4},{6,7},{7,6},{8,9},{9,8},{10,11... | collective-permute-start | bytes 221192 | tf_op jit(solution)/shard_map/ppermute | solution.py:33

commit v14 on v13

--- a/solution.py
+++ b/solution.py
@@ -47,30 +47,44 @@
     weight_column = slot_weight.reshape(-1, 1)
     inv_keep = 1.0 / keep_rate
 
-    one_hot = (slot_list[:, None] == jnp.arange(group_tokens, dtype=jnp.int32)[None, :]).astype(jnp.bfloat16)
-    rows = jnp.dot(
-        one_hot, jnp.concatenate([tokens, cotangent], axis=1), preferred_element_type=jnp.float32
-    )
-    chosen = rows[:, :local_width].astype(jnp.bfloat16)
-    scaled = (weight_column * rows[:, local_width:]).astype(jnp.bfloat16)
-    slab = jnp.concatenate([chosen, scaled], axis=1).reshape(expert_total, 1, per_source, 2 * local_width)
-    outgoing = jnp.broadcast_to(slab, (expert_total, chip_count, per_source, 2 * local_width))
-    outgoing = outgoing.reshape(expert_total * chip_count, per_source, 2 * local_width)
-    own = lax.all_to_all(outgoing, CROSS, split_axis=0, concat_axis=0, tiled=True)
-    own = own.reshape(expert_count, chip_count, per_source, 2 * local_width)
+    group = lax.axis_index("expert")
+    shifts = range(1, expert_count)
+
+    def from_groups(local, pick):
+        pieces = [pick(local, group)]
+        for shift in shifts:
+            moved = pick(local, (group + shift) % expert_count)
+            pieces.append(lax.ppermute(moved, "expert", [(i, (i + shift) % expert_count) for i in range(expert_count)]))
+        return jnp.stack(pieces)
+
+    info = jnp.stack([slot_token.astype(jnp.float32), slot_weight], axis=1)
+    info_rel = from_groups(info, lambda values, row: values[row])
+    info_abs = info_rel[(group - jnp.arange(expert_count)) % expert_count]
+    mine_tokens = info_abs[:, 0].astype(jnp.int32)
+    mine_weights = info_abs[:, 1].reshape(slot_count, 1, 1, 1)
+
+    raw = jnp.concatenate([tokens, cotangent], axis=1)
+    outgoing = jnp.broadcast_to(raw[None], (chip_count, group_tokens, 2 * local_width))
+    in_plane = lax.all_to_all(outgoing, "chip", split_axis=0, concat_axis=0, tiled=True)
+    own = from_groups(in_plane, lambda values, row: values)
     other = swap_cores(own)
     full = order_by_core(own, other, axis=2)
-    part_inputs = full[..., :local_width]
-    part_cot = full[..., local_width:]
+    block_rel = (group - jnp.arange(expert_count)) % expert_count
+    column = (block_rel[:, None] * group_tokens + mine_tokens).reshape(-1)
+    pick = (column[:, None] == jnp.arange(expert_count * group_tokens)[None, :]).astype(jnp.bfloat16)
+    pick = pick.reshape(slot_count, expert_count, group_tokens)
+    rows = lax.dot_general(pick, full, (((1, 2), (0, 3)), ((), ())), preferred_element_type=jnp.float32)
+    part_inputs = rows[..., :local_width].astype(jnp.bfloat16)
+    part_cot = (mine_weights * rows[..., local_width:]).astype(jnp.bfloat16)
 
     gate_rows = gate_mat.reshape(chip_count, 2, local_width, local_ff)
     up_rows = up_mat.reshape(chip_count, 2, local_width, local_ff)
     down_cols = down_mat.reshape(local_ff, chip_count, 2, local_width)
-    fwd_dims = (((1, 2, 4), (0, 1, 2)), ((), ()))
+    fwd_dims = (((1, 2, 3), (0, 1, 2)), ((), ()))
     gate_pre = lax.dot_general(part_inputs, gate_rows, fwd_dims, preferred_element_type=jnp.float32)
     up_pre = lax.dot_general(part_inputs, up_rows, fwd_dims, preferred_element_type=jnp.float32)
     grad_hidden = lax.dot_general(
-        part_cot, down_cols, (((1, 2, 4), (1, 2, 3)), ((), ())), preferred_element_type=jnp.float32
+        part_cot, down_cols, (((1, 2, 3), (1, 2, 3)), ((), ())), preferred_element_type=jnp.float32
     )
     gate_pre = gate_pre.reshape(slot_count, local_ff)
     up_pre = up_pre.reshape(slot_count, local_ff)
@@ -95,6 +109,7 @@
     blocks = blocks.transpose(0, 2, 1, 3).reshape(expert_count * chip_count, half, 2 * local_width)
     returned = lax.all_to_all(blocks, CROSS, split_axis=0, concat_axis=0, tiled=True)
     per_expert = returned.reshape(expert_total, chip_count, half, 2 * local_width).astype(jnp.float32).sum(1)
+    one_hot = (slot_list[:, None] == jnp.arange(group_tokens, dtype=jnp.int32)[None, :]).astype(jnp.bfloat16)
     row_hot = one_hot.reshape(expert_total, 2, half, group_tokens)
     own_hot = jnp.where(first, row_hot[:, 0], row_hot[:, 1])
     chip_tokens = fold_slots(own_hot, per_expert)

time: 90.4 us -> 96.2 us (1.064)
  blocking collectives: 38.1 us -> 23.6 us
  waiting for transfers between devices: 19.7 us -> 32 us
  matrix products: 11 us -> 14.5 us
  starting transfers between devices: 4.22 us -> 7.44 us
  other arithmetic: 2.58 us -> 5.57 us
  local copies, waits for them, and re-layouts: 14 us -> 12.3 us
    all_to_all x1, blocking collectives: 38.1 us -> 23.6 us  [body(): lax.all_to_all(outgoing, 'chip', split_axis=0, concat_axis=0, tiled=True)]
    ppermute x0 -> x2, waiting for transfers between devices: none -> 12.4 us  [from_groups(): lax.ppermute(moved, 'expert', [(i, (i + shift) % expert_count) for i in r...]
    dot_general x1, matrix products: 1.45 us -> 4.53 us  [body(): lax.dot_general(part_inputs, gate_rows, fwd_dims, preferred_element_type=...]
    ppermute x0 -> x2, starting transfers between devices: none -> 3.04 us  [from_groups(): lax.ppermute(moved, 'expert', [(i, (i + shift) % expert_count) for i in r...]
    unnamed x18 -> x22, local copies, waits for them, and re-layouts: 11.1 us -> 9.18 us
    another operation x0 -> x3, other arithmetic: none -> 1.34 us  [the longest x2 0.76 us: from_groups(): return jnp.stack(pieces)]
    add x0 -> x2, local copies, waits for them, and re-layouts: none -> 1.29 us  [body(): column = (block_rel[:, None] * group_tokens + mine_tokens).reshape(-1)]
  transfers between devices with their start and end apart: 4 -> 6, of which waited for: 3 -> 4; matrix products, arithmetic and copies ran while one was open for 10% -> 14% of each run, Pallas kernels for 0% -> 0%
where the time goes in v14:
time: 96.2 us; the launch traced here: 95.7 us
  waiting for transfers between devices  32 us (33%)
  blocking collectives  23.6 us (25%)
  matrix products  14.5 us (15%)
  local copies, waits for them, and re-layouts  12.3 us (13%)
  starting transfers between devices  7.44 us (8%)
  other arithmetic  5.57 us (6%)
    all_to_all x1, blocking collectives, body(): lax.all_to_all(outgoing, 'chip', split_axis=0, concat_axis=0, tiled=True)  23.6 us
    all_to_all x1, waiting for transfers between devices, body(): lax.all_to_all(blocks, CROSS, split_axis=0, concat_axis=0, tiled=True)  16.5 us
    ppermute x2, waiting for transfers between devices, from_groups(): lax.ppermute(moved, 'expert', [(i, (i + shift) % expert_count) for i in r...  12.4 us
    unnamed x22, local copies, waits for them, and re-layouts  9.18 us
    dot_general x1, matrix products, body(): lax.dot_general(part_inputs, gate_rows, fwd_dims, preferred_element_type=...  4.53 us
    all_to_all x1, starting transfers between devices, body(): lax.all_to_all(blocks, CROSS, split_axis=0, concat_axis=0, tiled=True)  4.02 us
    ppermute x3, waiting for transfers between devices, swap_cores(): return lax.ppermute(values, 'core', [(0, 1), (1, 0)])  3.13 us
    ppermute x2, starting transfers between devices, from_groups(): lax.ppermute(moved, 'expert', [(i, (i + shift) % expert_count) for i in r...  3.04 us
  transfers between devices with their start and end apart: 6, of which 4 were waited for; matrix products, arithmetic and copies ran while one was open for 14% of the time, Pallas kernels for 0%

profile of v14, /device:TPU:0, one launch (start us, length us, event | category | flops | bytes accessed | tf_op | source)
XLA Modules:
  0.0 95.7 jit_solution(12027815471044776621)
XLA Ops:
  0.0 0.9 pad_maximum_fusion.1
  0.9 0.1 broadcast_in_dim.2
  1.0 23.6 %all_to_all.10 = bf16[8,96,384]{2,1,0:T(8,128)(2,1)S(1)} all-to-all(bf16[8,96,384]{2,1,0:T(8,128)(2,1)S(1)} %broadcast_in_dim.2), channel_id=1, replica_groups=mesh['expert'=2,'chip'=8,'core'=2] {'chip'}, dimensions={0} | all-to-all | bytes 1179648 | tf_op jit(solution)/shard_map/all_to_all | solution.py:68
  24.6 1.5 %collective-permute-start.1 = (bf16[8,96,384]{2,1,0:T(8,128)(2,1)S(1)}, bf16[8,96,384]{2,1,0:T(8,128)(2,1)S(1)}, u32[]{:S(2)}, u32[]{:S(2)}) collective-permute-start(bf16[8,96,384]{2,1,0:T(8,128)(2,1)S(1)} %all_to_all.10), channel_id=1, source_target_pairs={{0,16},{16,0},{1,17},{17,1},{2,18},{18,2},{3,19},{19,3},{4,20},{20... | collective-permute-start | bytes 1769480 | tf_op jit(solution)/shard_map/ppermute | solution.py:57
  26.1 12.4 %collective-permute-done.1 = bf16[8,96,384]{2,1,0:T(8,128)(2,1)S(1)} collective-permute-done((bf16[8,96,384]{2,1,0:T(8,128)(2,1)S(1)}, bf16[8,96,384]{2,1,0:T(8,128)(2,1)S(1)}, u32[]{:S(2)}, u32[]{:S(2)}) %collective-permute-start.1) | collective-permute-done | bytes 589856 | tf_op jit(solution)/shard_map/ppermute | solution.py:57
  38.5 0.1 pad_maximum_fusion
  38.7 0.1 collective-permute-start.2
  38.8 0.6 fusion.52
  39.4 1.5 %collective-permute-start = (f32[2,96]{1,0:T(2,128)}, f32[2,96]{1,0:T(2,128)}, u32[]{:S(2)}, u32[]{:S(2)}) collective-permute-start(f32[2,96]{1,0:T(2,128)} %get-tuple-element.12), channel_id=1, source_target_pairs={{0,16},{16,0},{1,17},{17,1},{2,18},{18,2},{3,19},{19,3},{4,20},{20... | collective-permute-start | bytes 2312 | tf_op jit(solution)/shard_map/ppermute | solution.py:57
  40.9 0.6 multiply_add_fusion
  41.5 0.5 fusion.54
  42.0 0.6 add.87
  42.6 0.6 add.88
  43.3 8.6 %copy.28 = bf16[1,1024,3072]{1,2,0:T(8,128)(2,1)} copy(bf16[1,1024,3072]{2,1,0:T(8,128)(2,1)} %param.12) | data formatting | bytes 12582912 | tf_op args[4]
  51.9 0.6 pad_maximum_fusion.2
  52.6 0.6 gather_fusion
  53.1 0.1 convert_element_type.70
  53.3 0.1 mul.77
  53.3 0.7 add.89
  54.0 0.3 select_bitcast_fusion.1
  54.3 0.4 copy-done.1
  54.7 0.9 fusion.15
  55.6 4.5 %convolution_bitcast_fusion = f32[192,1024]{1,0:T(8,128)S(1)} fusion(bf16[8,2,192,1024]{3,2,1,0:T(8,128)(2,1)} %bitcast.110, f32[192,8,2,384]{3,0,2,1:T(8,128)S(1)} %fusion.15), kind=kOutput, calls=%fused_computation.17 | convolution fusion | flops 1207959552 | bytes 8650752 | tf_op jit(solution)/shard_map/dot_general | solution.py:84
  60.2 0.0 slice-start.1
  60.2 0.0 slice-start.2
  60.2 2.3 %multiply_convert_fusion = (bf16[192,1024]{1,0:T(8,128)(2,1)S(1)}, f32[192,1024]{1,0:T(8,128)S(1)}) fusion(f32[192,1024]{1,0:T(8,128)S(1)} %convolution_bitcast_fusion, s32[1,192,1024]{2,1,0:T(8,128)S(1)} %copy-done.3, bf16[1024,8,2,192]{0,3,2,1:T(8,128)(2,1)S(1)} %bitcast.115, f32[192,8,2,384]{3,0,2,1:T(8,128)S(1)} %fusion.15, f32[192]{0:T(256)S(1)} %mul.77), kind=kOutput, calls=%fused_computation.41 | convolution fusion | flops 1211695104 | bytes 12190720 | tf_op jit(solution)/shard_map/dot_general | solution.py:86
  62.6 0.0 slice-start.3
  62.6 1.9 %fusion.39 = bf16[192,1024]{1,0:T(8,128)(2,1)S(1)} fusion(f32[192,1024]{1,0:T(8,128)S(1)} %convolution_bitcast_fusion, f32[192,1024]{1,0:T(8,128)S(1)} %get-tuple-element.14, bf16[8,2,192,1024]{3,2,1,0:T(8,128)(2,1)S(1)} %bitcast.109, f32[192,8,2,384]{3,0,2,1:T(8,128)S(1)} %fusion.15), kind=kOutput, calls=%fused_computation.40 | convolution fusion | flops 1212088320 | bytes 9830400 | tf_op jit(solution)/shard_map/dot_general | solution.py:85
  64.5 2.2 %fusion = f32[192,3072]{1,0:T(8,128)S(1)} fusion(bf16[192,1024]{1,0:T(8,128)(2,1)S(1)} %get-tuple-element.8, bf16[1,3072,1024]{2,1,0:T(8,128)(2,1)S(1)} %bitcast.108), kind=kOutput, calls=%fused_computation.1 | convolution fusion | flops 1207959552 | bytes 9043968 | tf_op jit(solution)/shard_map/dot_general | solution.py:101
  66.7 2.2 %fusion.7 = bf16[192,3072]{1,0:T(8,128)(2,1)S(1)} fusion(f32[192,3072]{1,0:T(8,128)S(1)} %fusion, bf16[192,1024]{1,0:T(8,128)(2,1)S(1)} %fusion.39, bf16[1,3072,1024]{2,1,0:T(8,128)(2,1)S(1)} %bitcast.112), kind=kOutput, calls=%fused_computation.6 | convolution fusion | flops 1209139200 | bytes 10223616 | tf_op jit(solution)/shard_map/dot_general | solution.py:99
  68.9 0.1 select_bitcast_fusion.2
  69.0 0.2 collective-permute-start.3
  69.2 1.8 %collective-permute-done.3 = bf16[2,48,3072]{2,1,0:T(8,128)(2,1)S(1)} collective-permute-done((bf16[2,48,3072]{2,1,0:T(8,128)(2,1)S(1)}, bf16[2,48,3072]{2,1,0:T(8,128)(2,1)S(1)}, u32[]{:S(2)}, u32[]{:S(2)}) %collective-permute-start.3) | collective-permute-done | bytes 589856 | tf_op jit(solution)/shard_map/ppermute | solution.py:33
  71.1 0.2 fusion.31
  71.3 0.1 copy.39
  71.4 0.1 bitcast_bitcast_fusion
  71.5 0.9 copy.31
  72.4 4.0 %all-to-all-start.1 = ((bf16[16,48,384]{2,1,0:T(8,128)(2,1)}), bf16[16,48,384]{2,1,0:T(8,128)(2,1)S(1)}, u32[]{:S(2)}, u32[]{:S(2)}) async-start(bf16[16,48,384]{2,1,0:T(8,128)(2,1)} %bitcast.33), calls=%async_computation.1 | async-start | bytes 1179648 | tf_op jit(solution)/shard_map/all_to_all | solution.py:110
  76.4 0.1 eq.46
  76.5 0.1 fusion.44
  76.6 16.5 %all-to-all-done.1 = bf16[16,48,384]{2,1,0:T(8,128)(2,1)S(1)} async-done(((bf16[16,48,384]{2,1,0:T(8,128)(2,1)}), bf16[16,48,384]{2,1,0:T(8,128)(2,1)S(1)}, u32[]{:S(2)}, u32[]{:S(2)}) %all-to-all-start.1) | async-done | bytes 589856 | tf_op jit(solution)/shard_map/all_to_all | solution.py:110
  93.0 0.1 convert_reduce_fusion
  93.1 0.2 convolution_bitcast_fusion.2
  93.3 0.2 fusion.32
  93.5 0.1 slice_select_fusion
  93.6 0.1 collective-permute-start.4
  93.7 1.3 %collective-permute-done.4 = f32[96,192]{1,0:T(8,128)S(1)} collective-permute-done((f32[96,192]{1,0:T(8,128)S(1)}, f32[96,192]{1,0:T(8,128)S(1)}, u32[]{:S(2)}, u32[]{:S(2)}) %collective-permute-start.4) | collective-permute-done | bytes 73760 | tf_op jit(solution)/shard_map/ppermute | solution.py:33
  95.0 0.7 add_convert_fusion
  (27 shorter events, 0.1 us)
Async XLA Ops:
  0.0 38.8 %copy-start = (s32[2,96]{1,0:T(2,128)S(1)}, s32[2,96]{1,0:T(2,128)}, u32[]{:S(2)}) copy-start(s32[2,96]{1,0:T(2,128)} %param.13) | copy-start | bytes 2308
  0.0 38.8 %copy-start.2 = (f32[2,96]{1,0:T(2,128)S(1)}, f32[2,96]{1,0:T(2,128)}, u32[]{:S(2)}) copy-start(f32[2,96]{1,0:T(2,128)} %param.14) | copy-start | bytes 2308
  24.6 13.9 %collective-permute-start.1 = (bf16[8,96,384]{2,1,0:T(8,128)(2,1)S(1)}, bf16[8,96,384]{2,1,0:T(8,128)(2,1)S(1)}, u32[]{:S(2)}, u32[]{:S(2)}) collective-permute-start(bf16[8,96,384]{2,1,0:T(8,128)(2,1)S(1)} %all_to_all.10), channel_id=1, source_target_pairs={{0,16},{16,0},{1,17},{17,1},{2,18},{18,2},{3,19},{19,3},{4,20},{20... | collective-permute-start | bytes 1769480 | tf_op jit(solution)/shard_map/ppermute | solution.py:57
  38.7 15.3 %collective-permute-start.2 = (bf16[2,8,96,384]{3,2,0,1:T(8,128)(2,1)S(1)}, bf16[2,8,96,384]{3,2,0,1:T(8,128)(2,1)S(1)}, u32[]{:S(2)}, u32[]{:S(2)}) collective-permute-start(bf16[2,8,96,384]{3,2,0,1:T(8,128)(2,1)S(1)} %pad_maximum_fusion), channel_id=1, source_target_pairs={{0,1},{1,0},{2,3},{3,2},{4,5},{5,4},{6,7},{7,6},{8,9},{9,8},{10,11... | collective-permute-start | bytes 3538952 | tf_op jit(solution)/shard_map/ppermute | solution.py:33
  39.4 12.5 %collective-permute-start = (f32[2,96]{1,0:T(2,128)}, f32[2,96]{1,0:T(2,128)}, u32[]{:S(2)}, u32[]{:S(2)}) collective-permute-start(f32[2,96]{1,0:T(2,128)} %get-tuple-element.12), channel_id=1, source_target_pairs={{0,16},{16,0},{1,17},{17,1},{2,18},{18,2},{3,19},{19,3},{4,20},{20... | collective-permute-start | bytes 2312 | tf_op jit(solution)/shard_map/ppermute | solution.py:57
  54.0 0.7 copy-start.1
  54.0 6.1 %slice-start.4 = ((s8[6291456]{0:T(1024)(128)(4,1)}), s8[4194304]{0:T(1024)(128)(4,1)S(1)}, s32[]{:S(2)}) async-start(s8[6291456]{0:T(1024)(128)(4,1)} %bitcast.113), calls=%async_computation.6 | async-start | bytes 8388608
  54.7 5.5 %slice-start.5 = ((s8[6291456]{0:T(1024)(128)(4,1)}), s8[2097152]{0:T(1024)(128)(4,1)S(1)}, s32[]{:S(2)}) async-start(s8[6291456]{0:T(1024)(128)(4,1)} %bitcast.113), calls=%async_computation.7 | async-start | bytes 4194304
  55.6 4.6 %copy-start.3 = (s32[1,192,1024]{2,1,0:T(8,128)S(1)}, s32[1,192,1024]{2,1,0:T(8,128)}, u32[]{:S(2)}) copy-start(s32[1,192,1024]{2,1,0:T(8,128)} %param.15) | copy-start | bytes 2359300
  55.6 7.0 %slice-start = ((s8[6291456]{0:T(1024)(128)(4,1)}), s8[4194304]{0:T(1024)(128)(4,1)S(1)}, s32[]{:S(2)}) async-start(s8[6291456]{0:T(1024)(128)(4,1)} %bitcast.107), calls=%async_computation.2 | async-start | bytes 8388608
  60.2 2.4 %slice-start.1 = ((s8[6291456]{0:T(1024)(128)(4,1)}), s8[2097152]{0:T(1024)(128)(4,1)S(1)}, s32[]{:S(2)}) async-start(s8[6291456]{0:T(1024)(128)(4,1)} %bitcast.107), calls=%async_computation.3 | async-start | bytes 4194304
  60.2 6.5 %slice-start.2 = ((s8[6291456]{0:T(1024)(128)(4,1)}), s8[4194304]{0:T(1024)(128)(4,1)S(1)}, s32[]{:S(2)}) async-start(s8[6291456]{0:T(1024)(128)(4,1)} %bitcast.111), calls=%async_computation.4 | async-start | bytes 8388608
  62.6 4.1 %slice-start.3 = ((s8[6291456]{0:T(1024)(128)(4,1)}), s8[2097152]{0:T(1024)(128)(4,1)S(1)}, s32[]{:S(2)}) async-start(s8[6291456]{0:T(1024)(128)(4,1)} %bitcast.111), calls=%async_computation.5 | async-start | bytes 4194304
  69.0 2.1 %collective-permute-start.3 = (bf16[2,48,3072]{2,1,0:T(8,128)(2,1)S(1)}, bf16[2,48,3072]{2,1,0:T(8,128)(2,1)S(1)}, u32[]{:S(2)}, u32[]{:S(2)}) collective-permute-start(bf16[2,48,3072]{2,1,0:T(8,128)(2,1)S(1)} %select_bitcast_fusion.2), channel_id=1, source_target_pairs={{0,1},{1,0},{2,3},{3,2},{4,5},{5,4},{6,7},{7,6},{8,9},{9,8},{10,11... | collective-permute-start | bytes 1769480 | tf_op jit(solution)/shard_map/ppermute | solution.py:33
  72.4 20.7 %all-to-all-start.1 = ((bf16[16,48,384]{2,1,0:T(8,128)(2,1)}), bf16[16,48,384]{2,1,0:T(8,128)(2,1)S(1)}, u32[]{:S(2)}, u32[]{:S(2)}) async-start(bf16[16,48,384]{2,1,0:T(8,128)(2,1)} %bitcast.33), calls=%async_computation.1 | async-start | bytes 1179648 | tf_op jit(solution)/shard_map/all_to_all | solution.py:110
  93.6 1.4 %collective-permute-start.4 = (f32[96,192]{1,0:T(8,128)S(1)}, f32[96,192]{1,0:T(8,128)S(1)}, u32[]{:S(2)}, u32[]{:S(2)}) collective-permute-start(f32[96,192]{1,0:T(8,128)S(1)} %slice_select_fusion), channel_id=1, source_target_pairs={{0,1},{1,0},{2,3},{3,2},{4,5},{5,4},{6,7},{7,6},{8,9},{9,8},{10,11... | collective-permute-start | bytes 221192 | tf_op jit(solution)/shard_map/ppermute | solution.py:33

commit v15 on v14

--- a/solution.py
+++ b/solution.py
@@ -67,6 +67,7 @@
     outgoing = jnp.broadcast_to(raw[None], (chip_count, group_tokens, 2 * local_width))
     in_plane = lax.all_to_all(outgoing, "chip", split_axis=0, concat_axis=0, tiled=True)
     own = from_groups(in_plane, lambda values, row: values)
+    down_t, own = lax.optimization_barrier((jnp.transpose(down_mat), own))
     other = swap_cores(own)
     full = order_by_core(own, other, axis=2)
     block_rel = (group - jnp.arange(expert_count)) % expert_count
@@ -79,13 +80,11 @@
 
     gate_rows = gate_mat.reshape(chip_count, 2, local_width, local_ff)
     up_rows = up_mat.reshape(chip_count, 2, local_width, local_ff)
-    down_cols = down_mat.reshape(local_ff, chip_count, 2, local_width)
+    down_rows = down_t.reshape(chip_count, 2, local_width, local_ff)
     fwd_dims = (((1, 2, 3), (0, 1, 2)), ((), ()))
     gate_pre = lax.dot_general(part_inputs, gate_rows, fwd_dims, preferred_element_type=jnp.float32)
     up_pre = lax.dot_general(part_inputs, up_rows, fwd_dims, preferred_element_type=jnp.float32)
-    grad_hidden = lax.dot_general(
-        part_cot, down_cols, (((1, 2, 3), (1, 2, 3)), ((), ())), preferred_element_type=jnp.float32
-    )
+    grad_hidden = lax.dot_general(part_cot, down_rows, fwd_dims, preferred_element_type=jnp.float32)
     gate_pre = gate_pre.reshape(slot_count, local_ff)
     up_pre = up_pre.reshape(slot_count, local_ff)
     grad_hidden = grad_hidden.reshape(slot_count, local_ff)

time: 96.2 us -> 86.5 us (0.90)
  waiting for transfers between devices: 32 us -> 25.4 us
  matrix products: 14.5 us -> 11.5 us
    ppermute x2, waiting for transfers between devices: 12.4 us -> 5.69 us  [from_groups(): lax.ppermute(moved, 'expert', [(i, (i + shift) % expert_count) for i in r...]
    dot_general x1, matrix products: 4.53 us -> 1.5 us  [body(): lax.dot_general(part_inputs, gate_rows, fwd_dims, preferred_element_type=...]
    another operation x1, other arithmetic: 0.27 us -> 1.64 us  [order_by_core(): return jnp.stack([low, high], axis=axis)]
    add x2, local copies, waits for them, and re-layouts: 1.29 us -> 0.15 us  [body(): column = (block_rel[:, None] * group_tokens + mine_tokens).reshape(-1)]
    all_to_all x1, starting transfers between devices: 4.02 us -> 5 us  [body(): lax.all_to_all(blocks, CROSS, split_axis=0, concat_axis=0, tiled=True)]
  transfers between devices with their start and end apart: 6 -> 6, of which waited for: 4 -> 5; matrix products, arithmetic and copies ran while one was open for 14% -> 11% of each run, Pallas kernels for 0% -> 0%
where the time goes in v15:
time: 86.5 us; the launch traced here: 86 us
  waiting for transfers between devices  25.4 us (29%)
  blocking collectives  23.6 us (27%)
  matrix products  11.5 us (13%)
  local copies, waits for them, and re-layouts  11.4 us (13%)
  starting transfers between devices  8.31 us (10%)
  other arithmetic  5.42 us (6%)
    all_to_all x1, blocking collectives, body(): lax.all_to_all(outgoing, 'chip', split_axis=0, concat_axis=0, tiled=True)  23.6 us
    all_to_all x1, waiting for transfers between devices, body(): lax.all_to_all(blocks, CROSS, split_axis=0, concat_axis=0, tiled=True)  16.4 us
    unnamed x22, local copies, waits for them, and re-layouts  9.41 us
    ppermute x2, waiting for transfers between devices, from_groups(): lax.ppermute(moved, 'expert', [(i, (i + shift) % expert_count) for i in r...  5.69 us
    all_to_all x1, starting transfers between devices, body(): lax.all_to_all(blocks, CROSS, split_axis=0, concat_axis=0, tiled=True)  5 us
    ppermute x3, waiting for transfers between devices, swap_cores(): return lax.ppermute(values, 'core', [(0, 1), (1, 0)])  3.28 us
    ppermute x2, starting transfers between devices, from_groups(): lax.ppermute(moved, 'expert', [(i, (i + shift) % expert_count) for i in r...  3.1 us
    dot_general x1, matrix products, body(): lax.dot_general(part_cot, down_rows, fwd_dims, preferred_element_type=jnp...  2.3 us
  transfers between devices with their start and end apart: 6, of which 5 were waited for; matrix products, arithmetic and copies ran while one was open for 11% of the time, Pallas kernels for 0%

profile of v15, /device:TPU:0, one launch (start us, length us, event | category | flops | bytes accessed | tf_op | source)
XLA Modules:
  0.0 86.0 jit_solution(16384995991726642394)
XLA Ops:
  0.0 0.9 %pad_maximum_fusion.1 = bf16[96,384]{1,0:T(8,128)(2,1)S(1)} fusion(bf16[96,192]{1,0:T(8,128)(2,1)} %param.9, bf16[96,192]{1,0:T(8,128)(2,1)} %param.8), kind=kLoop, calls=%fused_computation.55 | loop fusion | flops 147456 | bytes 147456 | tf_op jit(solution)/shard_map/concatenate | solution.py:66
  0.9 0.1 broadcast_in_dim.2
  1.0 23.6 %all_to_all.10 = bf16[8,96,384]{2,1,0:T(8,128)(2,1)S(1)} all-to-all(bf16[8,96,384]{2,1,0:T(8,128)(2,1)S(1)} %broadcast_in_dim.2), channel_id=1, replica_groups=mesh['expert'=2,'chip'=8,'core'=2] {'chip'}, dimensions={0} | all-to-all | bytes 1179648 | tf_op jit(solution)/shard_map/all_to_all | solution.py:68
  24.6 1.5 %collective-permute-start.1 = (bf16[8,96,384]{2,1,0:T(8,128)(2,1)S(1)}, bf16[8,96,384]{2,1,0:T(8,128)(2,1)}, u32[]{:S(2)}, u32[]{:S(2)}) collective-permute-start(bf16[8,96,384]{2,1,0:T(8,128)(2,1)S(1)} %all_to_all.10), channel_id=1, source_target_pairs={{0,16},{16,0},{1,17},{17,1},{2,18},{18,2},{3,19},{19,3},{4,20},{20... | collective-permute-start | bytes 1769480 | tf_op jit(solution)/shard_map/ppermute | solution.py:57
  26.1 8.6 %copy.26 = bf16[1,1024,3072]{1,2,0:T(8,128)(2,1)} copy(bf16[1,1024,3072]{2,1,0:T(8,128)(2,1)} %param.12) | data formatting | bytes 12582912 | tf_op args[4]
  34.8 3.8 %collective-permute-done.1 = bf16[8,96,384]{2,1,0:T(8,128)(2,1)} collective-permute-done((bf16[8,96,384]{2,1,0:T(8,128)(2,1)S(1)}, bf16[8,96,384]{2,1,0:T(8,128)(2,1)}, u32[]{:S(2)}, u32[]{:S(2)}) %collective-permute-start.1) | collective-permute-done | bytes 589856 | tf_op jit(solution)/shard_map/ppermute | solution.py:57
  38.6 1.5 %pad_maximum_fusion = bf16[2,8,96,384]{3,2,0,1:T(8,128)(2,1)S(1)} fusion(bf16[1,8,96,384]{3,2,0,1:T(8,128)(2,1)} %bitcast.12, bf16[1,8,96,384]{3,2,0,1:T(8,128)(2,1)} %bitcast.121), kind=kLoop, calls=%fused_computation.23 | loop fusion | flops 589824 | bytes 2359296 | tf_op jit(solution)/shard_map/stack | solution.py:58
  40.1 0.1 collective-permute-start.2
  40.2 0.0 copy-done.1
  40.3 1.6 %collective-permute-start = (f32[2,96]{1,0:T(2,128)S(1)}, f32[2,96]{1,0:T(2,128)S(1)}, u32[]{:S(2)}, u32[]{:S(2)}) collective-permute-start(f32[2,96]{1,0:T(2,128)S(1)} %get-tuple-element.16), channel_id=1, source_target_pairs={{0,16},{16,0},{1,17},{17,1},{2,18},{18,2},{3,19},{19,3},{4,20},{20... | collective-permute-start | bytes 2312 | tf_op jit(solution)/shard_map/ppermute | solution.py:57
  41.9 0.1 add.87
  42.0 0.1 add.88
  42.1 1.8 %collective-permute-done = f32[2,96]{1,0:T(2,128)S(1)} collective-permute-done((f32[2,96]{1,0:T(2,128)S(1)}, f32[2,96]{1,0:T(2,128)S(1)}, u32[]{:S(2)}, u32[]{:S(2)}) %collective-permute-start) | collective-permute-done | bytes 800 | tf_op jit(solution)/shard_map/ppermute | solution.py:57
  43.9 0.6 gather_fusion
  44.5 0.1 convert_element_type.70
  44.6 0.1 mul.77
  44.7 0.0 collective-permute-done.2
  44.7 1.6 %select_bitcast_fusion.1 = (bf16[2,8,1,96,384]{4,3,0,2,1:T(8,128)(2,1)S(1)}, bf16[2,8,1,96,384]{4,3,0,2,1:T(8,128)(2,1)S(1)}) fusion(bf16[2,8,96,384]{3,2,0,1:T(8,128)(2,1)S(1)} %pad_maximum_fusion, bf16[2,8,96,384]{3,2,0,1:T(8,128)(2,1)} %collective-permute-done.2, pred[]{:T(512)S(6)} %eq.45), kind=kLoop, calls=%fused_computation.28 | loop fusion | flops 1179648 | bytes 4718593 | tf_op jit(solution)/shard_map/stack | solution.py:29
  46.4 0.0 slice-start.5
  46.4 0.9 %fusion.15 = f32[192,8,2,384]{3,0,2,1:T(8,128)S(1)} fusion(bf16[2,8,1,96,384]{4,3,0,2,1:T(8,128)(2,1)S(1)} %get-tuple-element.14, bf16[2,8,1,96,384]{4,3,0,2,1:T(8,128)(2,1)S(1)} %get-tuple-element.13, s32[2,96]{1,0:T(2,128)S(1)} %multiply_add_fusion, s32[192]{0:T(256)S(1)} %add.89), kind=kOutput, calls=%fused_computation.14 | convolution fusion | flops 457740288 | bytes 7079424 | tf_op jit(solution)/shard_map/dot_general | solution.py:77
  47.3 0.0 copy-start.3
  47.3 0.0 slice-start
  47.3 1.5 %convolution_bitcast_fusion = f32[192,1024]{1,0:T(8,128)S(1)} fusion(bf16[8,2,192,1024]{3,2,1,0:T(8,128)(2,1)S(1)} %bitcast.115, f32[192,8,2,384]{3,0,2,1:T(8,128)S(1)} %fusion.15), kind=kOutput, calls=%fused_computation.17 | convolution fusion | flops 1207959552 | bytes 8650752 | tf_op jit(solution)/shard_map/dot_general | solution.py:85
  48.8 0.0 slice-done.4
  48.9 0.5 slice-done.5
  49.4 0.1 copy-done.3
  49.5 2.3 %multiply_convert_fusion = (bf16[192,1024]{1,0:T(8,128)(2,1)S(1)}, f32[192,1024]{1,0:T(8,128)S(1)}) fusion(f32[192,1024]{1,0:T(8,128)S(1)} %convolution_bitcast_fusion, s32[1,192,1024]{2,1,0:T(8,128)S(1)} %copy-done.3, bf16[8,2,192,1024]{3,2,1,0:T(8,128)(2,1)S(1)} %bitcast.118, f32[192,8,2,384]{3,0,2,1:T(8,128)S(1)} %fusion.15, f32[192]{0:T(256)S(1)} %mul.77), kind=kOutput, calls=%fused_computation.41 | convolution fusion | flops 1211695104 | bytes 12190720 | tf_op jit(solution)/shard_map/dot_general | solution.py:87
  51.8 2.0 %fusion.39 = bf16[192,1024]{1,0:T(8,128)(2,1)S(1)} fusion(f32[192,1024]{1,0:T(8,128)S(1)} %convolution_bitcast_fusion, f32[192,1024]{1,0:T(8,128)S(1)} %get-tuple-element.18, bf16[8,2,192,1024]{3,2,1,0:T(8,128)(2,1)S(1)} %bitcast.112, f32[192,8,2,384]{3,0,2,1:T(8,128)S(1)} %fusion.15), kind=kOutput, calls=%fused_computation.40 | convolution fusion | flops 1212088320 | bytes 9830400 | tf_op jit(solution)/shard_map/dot_general | solution.py:86
  53.8 2.2 %fusion = f32[192,3072]{1,0:T(8,128)S(1)} fusion(bf16[192,1024]{1,0:T(8,128)(2,1)S(1)} %get-tuple-element.12, bf16[1,3072,1024]{2,1,0:T(8,128)(2,1)S(1)} %bitcast.111), kind=kOutput, calls=%fused_computation.1 | convolution fusion | flops 1207959552 | bytes 9043968 | tf_op jit(solution)/shard_map/dot_general | solution.py:100
  56.0 2.2 %fusion.7 = bf16[192,3072]{1,0:T(8,128)(2,1)S(1)} fusion(f32[192,3072]{1,0:T(8,128)S(1)} %fusion, bf16[192,1024]{1,0:T(8,128)(2,1)S(1)} %fusion.39, bf16[1,3072,1024]{2,1,0:T(8,128)(2,1)S(1)} %bitcast.114), kind=kOutput, calls=%fused_computation.6 | convolution fusion | flops 1209139200 | bytes 10223616 | tf_op jit(solution)/shard_map/dot_general | solution.py:98
  58.3 0.1 select_bitcast_fusion.2
  58.4 0.1 collective-permute-start.3
  58.4 2.0 %collective-permute-done.3 = bf16[2,48,3072]{2,1,0:T(8,128)(2,1)S(1)} collective-permute-done((bf16[2,48,3072]{2,1,0:T(8,128)(2,1)S(1)}, bf16[2,48,3072]{2,1,0:T(8,128)(2,1)S(1)}, u32[]{:S(2)}, u32[]{:S(2)}) %collective-permute-start.3) | collective-permute-done | bytes 589856 | tf_op jit(solution)/shard_map/ppermute | solution.py:33
  60.4 0.2 fusion.31
  60.6 0.1 copy.39
  60.7 0.1 bitcast_bitcast_fusion
  60.8 0.9 %copy.31 = bf16[2,8,48,384]{3,2,1,0:T(8,128)(2,1)} copy(bf16[2,8,48,384]{3,1,2,0:T(8,128)(2,1)S(1)} %bitcast_bitcast_fusion) | data formatting | bytes 1179648 | tf_op jit(solution)/shard_map/transpose | solution.py:108
  61.7 5.0 %all-to-all-start.1 = ((bf16[16,48,384]{2,1,0:T(8,128)(2,1)}), bf16[16,48,384]{2,1,0:T(8,128)(2,1)S(1)}, u32[]{:S(2)}, u32[]{:S(2)}) async-start(bf16[16,48,384]{2,1,0:T(8,128)(2,1)} %bitcast.35), calls=%async_computation.1 | async-start | bytes 1179648 | tf_op jit(solution)/shard_map/all_to_all | solution.py:109
  66.7 0.1 eq.46
  66.8 0.1 fusion.44
  66.9 16.4 %all-to-all-done.1 = bf16[16,48,384]{2,1,0:T(8,128)(2,1)S(1)} async-done(((bf16[16,48,384]{2,1,0:T(8,128)(2,1)}), bf16[16,48,384]{2,1,0:T(8,128)(2,1)S(1)}, u32[]{:S(2)}, u32[]{:S(2)}) %all-to-all-start.1) | async-done | bytes 589856 | tf_op jit(solution)/shard_map/all_to_all | solution.py:109
  83.3 0.1 convert_reduce_fusion
  83.4 0.2 convolution_bitcast_fusion.2
  83.6 0.2 fusion.32
  83.8 0.1 slice_select_fusion
  83.9 0.1 collective-permute-start.4
  84.0 1.3 %collective-permute-done.4 = f32[96,192]{1,0:T(8,128)S(1)} collective-permute-done((f32[96,192]{1,0:T(8,128)S(1)}, f32[96,192]{1,0:T(8,128)S(1)}, u32[]{:S(2)}, u32[]{:S(2)}) %collective-permute-start.4) | collective-permute-done | bytes 73760 | tf_op jit(solution)/shard_map/ppermute | solution.py:33
  85.3 0.7 add_convert_fusion
  (27 shorter events, 0.1 us)
Async XLA Ops:
  24.6 14.0 %copy-start = (bf16[8,96,384]{2,1,0:T(8,128)(2,1)}, bf16[8,96,384]{2,1,0:T(8,128)(2,1)S(1)}, u32[]{:S(2)}) copy-start(bf16[8,96,384]{2,1,0:T(8,128)(2,1)S(1)} %all_to_all.10) | copy-start | bytes 1769476
  24.6 14.0 %collective-permute-start.1 = (bf16[8,96,384]{2,1,0:T(8,128)(2,1)S(1)}, bf16[8,96,384]{2,1,0:T(8,128)(2,1)}, u32[]{:S(2)}, u32[]{:S(2)}) collective-permute-start(bf16[8,96,384]{2,1,0:T(8,128)(2,1)S(1)} %all_to_all.10), channel_id=1, source_target_pairs={{0,16},{16,0},{1,17},{17,1},{2,18},{18,2},{3,19},{19,3},{4,20},{20... | collective-permute-start | bytes 1769480 | tf_op jit(solution)/shard_map/ppermute | solution.py:57
  34.8 5.5 %copy-start.1 = (s32[2,96]{1,0:T(2,128)S(1)}, s32[2,96]{1,0:T(2,128)}, u32[]{:S(2)}) copy-start(s32[2,96]{1,0:T(2,128)} %param.13) | copy-start | bytes 2308
  34.8 5.5 %copy-start.2 = (f32[2,96]{1,0:T(2,128)S(1)}, f32[2,96]{1,0:T(2,128)}, u32[]{:S(2)}) copy-start(f32[2,96]{1,0:T(2,128)} %param.14) | copy-start | bytes 2308
  38.6 8.7 %slice-start.2 = ((s8[6291456]{0:T(1024)(128)(4,1)}), s8[2097152]{0:T(1024)(128)(4,1)S(1)}, s32[]{:S(2)}) async-start(s8[6291456]{0:T(1024)(128)(4,1)} %bitcast.113), calls=%async_computation.4 | async-start | bytes 4194304
  40.1 4.6 %collective-permute-start.2 = (bf16[2,8,96,384]{3,2,0,1:T(8,128)(2,1)S(1)}, bf16[2,8,96,384]{3,2,0,1:T(8,128)(2,1)}, u32[]{:S(2)}, u32[]{:S(2)}) collective-permute-start(bf16[2,8,96,384]{3,2,0,1:T(8,128)(2,1)S(1)} %pad_maximum_fusion), channel_id=1, source_target_pairs={{0,1},{1,0},{2,3},{3,2},{4,5},{5,4},{6,7},{7,6},{8,9},{9,8},{10,11... | collective-permute-start | bytes 3538952 | tf_op jit(solution)/shard_map/ppermute | solution.py:33
  40.3 3.6 %collective-permute-start = (f32[2,96]{1,0:T(2,128)S(1)}, f32[2,96]{1,0:T(2,128)S(1)}, u32[]{:S(2)}, u32[]{:S(2)}) collective-permute-start(f32[2,96]{1,0:T(2,128)S(1)} %get-tuple-element.16), channel_id=1, source_target_pairs={{0,16},{16,0},{1,17},{17,1},{2,18},{18,2},{3,19},{19,3},{4,20},{20... | collective-permute-start | bytes 2312 | tf_op jit(solution)/shard_map/ppermute | solution.py:57
  44.7 2.6 %slice-start.3 = ((s8[6291456]{0:T(1024)(128)(4,1)}), s8[4194304]{0:T(1024)(128)(4,1)S(1)}, s32[]{:S(2)}) async-start(s8[6291456]{0:T(1024)(128)(4,1)} %bitcast.113), calls=%async_computation.5 | async-start | bytes 8388608
  44.7 4.1 %slice-start.4 = ((s8[6291456]{0:T(1024)(128)(4,1)}), s8[4194304]{0:T(1024)(128)(4,1)S(1)}, s32[]{:S(2)}) async-start(s8[6291456]{0:T(1024)(128)(4,1)} %bitcast.116), calls=%async_computation.6 | async-start | bytes 8388608
  46.4 3.0 %slice-start.5 = ((s8[6291456]{0:T(1024)(128)(4,1)}), s8[2097152]{0:T(1024)(128)(4,1)S(1)}, s32[]{:S(2)}) async-start(s8[6291456]{0:T(1024)(128)(4,1)} %bitcast.116), calls=%async_computation.7 | async-start | bytes 4194304
  47.3 2.2 %copy-start.3 = (s32[1,192,1024]{2,1,0:T(8,128)S(1)}, s32[1,192,1024]{2,1,0:T(8,128)}, u32[]{:S(2)}) copy-start(s32[1,192,1024]{2,1,0:T(8,128)} %param.15) | copy-start | bytes 2359300
  47.3 4.5 %slice-start = ((s8[6291456]{0:T(1024)(128)(4,1)}), s8[4194304]{0:T(1024)(128)(4,1)S(1)}, s32[]{:S(2)}) async-start(s8[6291456]{0:T(1024)(128)(4,1)} %bitcast.110), calls=%async_computation.2 | async-start | bytes 8388608
  49.5 2.3 %slice-start.1 = ((s8[6291456]{0:T(1024)(128)(4,1)}), s8[2097152]{0:T(1024)(128)(4,1)S(1)}, s32[]{:S(2)}) async-start(s8[6291456]{0:T(1024)(128)(4,1)} %bitcast.110), calls=%async_computation.3 | async-start | bytes 4194304
  58.4 2.1 %collective-permute-start.3 = (bf16[2,48,3072]{2,1,0:T(8,128)(2,1)S(1)}, bf16[2,48,3072]{2,1,0:T(8,128)(2,1)S(1)}, u32[]{:S(2)}, u32[]{:S(2)}) collective-permute-start(bf16[2,48,3072]{2,1,0:T(8,128)(2,1)S(1)} %select_bitcast_fusion.2), channel_id=1, source_target_pairs={{0,1},{1,0},{2,3},{3,2},{4,5},{5,4},{6,7},{7,6},{8,9},{9,8},{10,11... | collective-permute-start | bytes 1769480 | tf_op jit(solution)/shard_map/ppermute | solution.py:33
  61.7 21.6 %all-to-all-start.1 = ((bf16[16,48,384]{2,1,0:T(8,128)(2,1)}), bf16[16,48,384]{2,1,0:T(8,128)(2,1)S(1)}, u32[]{:S(2)}, u32[]{:S(2)}) async-start(bf16[16,48,384]{2,1,0:T(8,128)(2,1)} %bitcast.35), calls=%async_computation.1 | async-start | bytes 1179648 | tf_op jit(solution)/shard_map/all_to_all | solution.py:109
  83.9 1.4 %collective-permute-start.4 = (f32[96,192]{1,0:T(8,128)S(1)}, f32[96,192]{1,0:T(8,128)S(1)}, u32[]{:S(2)}, u32[]{:S(2)}) collective-permute-start(f32[96,192]{1,0:T(8,128)S(1)} %slice_select_fusion), channel_id=1, source_target_pairs={{0,1},{1,0},{2,3},{3,2},{4,5},{5,4},{6,7},{7,6},{8,9},{9,8},{10,11... | collective-permute-start | bytes 221192 | tf_op jit(solution)/shard_map/ppermute | solution.py:33

commit v16 on v15

--- a/solution.py
+++ b/solution.py
@@ -59,15 +59,15 @@
 
     info = jnp.stack([slot_token.astype(jnp.float32), slot_weight], axis=1)
     info_rel = from_groups(info, lambda values, row: values[row])
-    info_abs = info_rel[(group - jnp.arange(expert_count)) % expert_count]
-    mine_tokens = info_abs[:, 0].astype(jnp.int32)
-    mine_weights = info_abs[:, 1].reshape(slot_count, 1, 1, 1)
 
     raw = jnp.concatenate([tokens, cotangent], axis=1)
     outgoing = jnp.broadcast_to(raw[None], (chip_count, group_tokens, 2 * local_width))
     in_plane = lax.all_to_all(outgoing, "chip", split_axis=0, concat_axis=0, tiled=True)
     own = from_groups(in_plane, lambda values, row: values)
-    down_t, own = lax.optimization_barrier((jnp.transpose(down_mat), own))
+    down_t, own, info_rel = lax.optimization_barrier((jnp.transpose(down_mat), own, info_rel))
+    info_abs = info_rel[(group - jnp.arange(expert_count)) % expert_count]
+    mine_tokens = info_abs[:, 0].astype(jnp.int32)
+    mine_weights = info_abs[:, 1].reshape(slot_count, 1, 1, 1)
     other = swap_cores(own)
     full = order_by_core(own, other, axis=2)
     block_rel = (group - jnp.arange(expert_count)) % expert_count

time: 86.5 us -> 85.1 us (0.984)
  waiting for transfers between devices: 25.4 us -> 23.4 us
  other arithmetic: 5.42 us -> 6.76 us
  starting transfers between devices: 8.31 us -> 7.39 us
    ppermute x2, waiting for transfers between devices: 5.69 us -> 1.94 us  [from_groups(): lax.ppermute(moved, 'expert', [(i, (i + shift) % expert_count) for i in r...]
    ppermute x3, waiting for transfers between devices: 3.28 us -> 5.1 us  [swap_cores(): return lax.ppermute(values, 'core', [(0, 1), (1, 0)])]
    ppermute x2, starting transfers between devices: 3.1 us -> 2.03 us  [from_groups(): lax.ppermute(moved, 'expert', [(i, (i + shift) % expert_count) for i in r...]
  transfers between devices with their start and end apart: 6 -> 6, of which waited for: 5 -> 5; matrix products, arithmetic and copies ran while one was open for 11% -> 13% of each run, Pallas kernels for 0% -> 0%
where the time goes in v16:
time: 85.1 us; the launch traced here: 84.6 us
  blocking collectives  23.6 us (28%)
  waiting for transfers between devices  23.4 us (27%)
  local copies, waits for them, and re-layouts  11.6 us (14%)
  matrix products  11.5 us (14%)
  starting transfers between devices  7.39 us (9%)
  other arithmetic  6.76 us (8%)
    all_to_all x1, blocking collectives, body(): lax.all_to_all(outgoing, 'chip', split_axis=0, concat_axis=0, tiled=True)  23.6 us
    all_to_all x1, waiting for transfers between devices, body(): lax.all_to_all(blocks, CROSS, split_axis=0, concat_axis=0, tiled=True)  16.4 us
    unnamed x22, local copies, waits for them, and re-layouts  9.59 us
    ppermute x3, waiting for transfers between devices, swap_cores(): return lax.ppermute(values, 'core', [(0, 1), (1, 0)])  5.1 us
    all_to_all x1, starting transfers between devices, body(): lax.all_to_all(blocks, CROSS, split_axis=0, concat_axis=0, tiled=True)  5 us
    dot_general x1, matrix products, body(): lax.dot_general(part_cot, down_rows, fwd_dims, preferred_element_type=jnp...  2.35 us
    dot_general x1, matrix products, body(): lax.dot_general(grad_gate, gate_mat, back_dims, preferred_element_type=jn...  2.26 us
    dot_general x1, matrix products, body(): lax.dot_general(grad_up, up_mat, back_dims, preferred_element_type=jnp.fl...  2.21 us
  transfers between devices with their start and end apart: 6, of which 5 were waited for; matrix products, arithmetic and copies ran while one was open for 13% of the time, Pallas kernels for 0%

profile of v16, /device:TPU:0, one launch (start us, length us, event | category | flops | bytes accessed | tf_op | source)
XLA Modules:
  0.0 84.6 jit_solution(8037244955201027851)
XLA Ops:
  0.0 0.9 %pad_maximum_fusion.1 = bf16[96,384]{1,0:T(8,128)(2,1)S(1)} fusion(bf16[96,192]{1,0:T(8,128)(2,1)} %param.9, bf16[96,192]{1,0:T(8,128)(2,1)} %param.8), kind=kLoop, calls=%fused_computation.55 | loop fusion | flops 147456 | bytes 147456 | tf_op jit(solution)/shard_map/concatenate | solution.py:63
  0.9 0.1 broadcast_in_dim.2
  1.0 23.6 %all_to_all.10 = bf16[8,96,384]{2,1,0:T(8,128)(2,1)S(1)} all-to-all(bf16[8,96,384]{2,1,0:T(8,128)(2,1)S(1)} %broadcast_in_dim.2), channel_id=1, replica_groups=mesh['expert'=2,'chip'=8,'core'=2] {'chip'}, dimensions={0} | all-to-all | bytes 1179648 | tf_op jit(solution)/shard_map/all_to_all | solution.py:65
  24.6 1.5 %collective-permute-start = (bf16[8,96,384]{2,1,0:T(8,128)(2,1)S(1)}, bf16[8,96,384]{2,1,0:T(8,128)(2,1)S(1)}, u32[]{:S(2)}, u32[]{:S(2)}) collective-permute-start(bf16[8,96,384]{2,1,0:T(8,128)(2,1)S(1)} %all_to_all.10), channel_id=1, source_target_pairs={{0,16},{16,0},{1,17},{17,1},{2,18},{18,2},{3,19},{19,3},{4,20},{20... | collective-permute-start | bytes 1769480 | tf_op jit(solution)/shard_map/ppermute | solution.py:57
  26.1 0.7 convert_element_type.68
  26.8 0.7 fusion.52
  27.5 0.5 collective-permute-start.1
  28.0 8.6 %copy.26 = bf16[1,1024,3072]{1,2,0:T(8,128)(2,1)} copy(bf16[1,1024,3072]{2,1,0:T(8,128)(2,1)} %param.12) | data formatting | bytes 12582912 | tf_op args[4]
  36.6 1.9 %collective-permute-done.1 = f32[2,96]{1,0:T(2,128)S(1)} collective-permute-done((f32[2,96]{1,0:T(2,128)S(1)}, f32[2,96]{1,0:T(2,128)S(1)}, u32[]{:S(2)}, u32[]{:S(2)}) %collective-permute-start.1) | collective-permute-done | bytes 800 | tf_op jit(solution)/shard_map/ppermute | solution.py:57
  38.6 0.0 collective-permute-done
  38.6 0.8 copy-done.1
  39.4 1.5 %pad_maximum_fusion = bf16[2,8,96,384]{3,2,0,1:T(8,128)(2,1)S(1)} fusion(bf16[1,8,96,384]{3,2,0,1:T(8,128)(2,1)} %bitcast.122, bf16[1,8,96,384]{3,2,0,1:T(8,128)(2,1)} %bitcast.121), kind=kLoop, calls=%fused_computation.23 | loop fusion | flops 589824 | bytes 2359296 | tf_op jit(solution)/shard_map/stack | solution.py:58
  40.9 0.1 collective-permute-start.2
  41.0 0.1 add.87
  41.1 0.1 add.88
  41.2 0.6 gather_fusion
  41.8 0.1 convert_element_type.70
  41.9 0.1 mul.77
  42.0 2.0 %collective-permute-done.2 = bf16[2,8,96,384]{3,2,0,1:T(8,128)(2,1)} collective-permute-done((bf16[2,8,96,384]{3,2,0,1:T(8,128)(2,1)S(1)}, bf16[2,8,96,384]{3,2,0,1:T(8,128)(2,1)}, u32[]{:S(2)}, u32[]{:S(2)}) %collective-permute-start.2) | collective-permute-done | bytes 1179680 | tf_op jit(solution)/shard_map/ppermute | solution.py:33
  44.0 1.6 %select_bitcast_fusion.1 = (bf16[2,8,1,96,384]{4,3,0,2,1:T(8,128)(2,1)S(1)}, bf16[2,8,1,96,384]{4,3,0,2,1:T(8,128)(2,1)S(1)}) fusion(bf16[2,8,96,384]{3,2,0,1:T(8,128)(2,1)S(1)} %pad_maximum_fusion, bf16[2,8,96,384]{3,2,0,1:T(8,128)(2,1)} %collective-permute-done.2, pred[]{:T(512)S(6)} %eq.45), kind=kLoop, calls=%fused_computation.28 | loop fusion | flops 1179648 | bytes 4718593 | tf_op jit(solution)/shard_map/stack | solution.py:29
  45.6 0.9 %fusion.15 = f32[192,8,2,384]{3,0,2,1:T(8,128)S(1)} fusion(bf16[2,8,1,96,384]{4,3,0,2,1:T(8,128)(2,1)S(1)} %get-tuple-element.16, bf16[2,8,1,96,384]{4,3,0,2,1:T(8,128)(2,1)S(1)} %get-tuple-element.15, s32[2,96]{1,0:T(2,128)S(1)} %multiply_add_fusion, s32[192]{0:T(256)S(1)} %add.89), kind=kOutput, calls=%fused_computation.14 | convolution fusion | flops 457740288 | bytes 7079424 | tf_op jit(solution)/shard_map/dot_general | solution.py:77
  46.5 0.0 copy-start.3
  46.6 0.0 slice-start
  46.6 1.5 %convolution_bitcast_fusion = f32[192,1024]{1,0:T(8,128)S(1)} fusion(bf16[8,2,192,1024]{3,2,1,0:T(8,128)(2,1)S(1)} %bitcast.115, f32[192,8,2,384]{3,0,2,1:T(8,128)S(1)} %fusion.15), kind=kOutput, calls=%fused_computation.17 | convolution fusion | flops 1207959552 | bytes 8650752 | tf_op jit(solution)/shard_map/dot_general | solution.py:85
  48.1 0.0 slice-start.1
  48.1 2.4 %multiply_convert_fusion = (bf16[192,1024]{1,0:T(8,128)(2,1)S(1)}, f32[192,1024]{1,0:T(8,128)S(1)}) fusion(f32[192,1024]{1,0:T(8,128)S(1)} %convolution_bitcast_fusion, s32[1,192,1024]{2,1,0:T(8,128)S(1)} %copy-done.3, bf16[8,2,192,1024]{3,2,1,0:T(8,128)(2,1)S(1)} %bitcast.118, f32[192,8,2,384]{3,0,2,1:T(8,128)S(1)} %fusion.15, f32[192]{0:T(256)S(1)} %mul.77), kind=kOutput, calls=%fused_computation.41 | convolution fusion | flops 1211695104 | bytes 12190720 | tf_op jit(solution)/shard_map/dot_general | solution.py:87
  50.5 1.9 %fusion.39 = bf16[192,1024]{1,0:T(8,128)(2,1)S(1)} fusion(f32[192,1024]{1,0:T(8,128)S(1)} %convolution_bitcast_fusion, f32[192,1024]{1,0:T(8,128)S(1)} %get-tuple-element.20, bf16[8,2,192,1024]{3,2,1,0:T(8,128)(2,1)S(1)} %bitcast.112, f32[192,8,2,384]{3,0,2,1:T(8,128)S(1)} %fusion.15), kind=kOutput, calls=%fused_computation.40 | convolution fusion | flops 1212088320 | bytes 9830400 | tf_op jit(solution)/shard_map/dot_general | solution.py:86
  52.4 2.2 %fusion = f32[192,3072]{1,0:T(8,128)S(1)} fusion(bf16[192,1024]{1,0:T(8,128)(2,1)S(1)} %get-tuple-element.14, bf16[1,3072,1024]{2,1,0:T(8,128)(2,1)S(1)} %bitcast.111), kind=kOutput, calls=%fused_computation.1 | convolution fusion | flops 1207959552 | bytes 9043968 | tf_op jit(solution)/shard_map/dot_general | solution.py:100
  54.6 2.3 %fusion.7 = bf16[192,3072]{1,0:T(8,128)(2,1)S(1)} fusion(f32[192,3072]{1,0:T(8,128)S(1)} %fusion, bf16[192,1024]{1,0:T(8,128)(2,1)S(1)} %fusion.39, bf16[1,3072,1024]{2,1,0:T(8,128)(2,1)S(1)} %bitcast.114), kind=kOutput, calls=%fused_computation.6 | convolution fusion | flops 1209139200 | bytes 10223616 | tf_op jit(solution)/shard_map/dot_general | solution.py:98
  56.9 0.1 select_bitcast_fusion.2
  57.0 0.2 collective-permute-start.3
  57.2 1.9 %collective-permute-done.3 = bf16[2,48,3072]{2,1,0:T(8,128)(2,1)S(1)} collective-permute-done((bf16[2,48,3072]{2,1,0:T(8,128)(2,1)S(1)}, bf16[2,48,3072]{2,1,0:T(8,128)(2,1)S(1)}, u32[]{:S(2)}, u32[]{:S(2)}) %collective-permute-start.3) | collective-permute-done | bytes 589856 | tf_op jit(solution)/shard_map/ppermute | solution.py:33
  59.1 0.2 fusion.31
  59.3 0.0 copy-start.2
  59.3 0.1 copy.39
  59.4 0.1 bitcast_bitcast_fusion
  59.5 0.9 %copy.31 = bf16[2,8,48,384]{3,2,1,0:T(8,128)(2,1)} copy(bf16[2,8,48,384]{3,1,2,0:T(8,128)(2,1)S(1)} %bitcast_bitcast_fusion) | data formatting | bytes 1179648 | tf_op jit(solution)/shard_map/transpose | solution.py:108
  60.4 5.0 %all-to-all-start.1 = ((bf16[16,48,384]{2,1,0:T(8,128)(2,1)}), bf16[16,48,384]{2,1,0:T(8,128)(2,1)S(1)}, u32[]{:S(2)}, u32[]{:S(2)}) async-start(bf16[16,48,384]{2,1,0:T(8,128)(2,1)} %bitcast.35), calls=%async_computation.1 | async-start | bytes 1179648 | tf_op jit(solution)/shard_map/all_to_all | solution.py:109
  65.4 0.1 eq.46
  65.5 0.1 fusion.44
  65.6 16.4 %all-to-all-done.1 = bf16[16,48,384]{2,1,0:T(8,128)(2,1)S(1)} async-done(((bf16[16,48,384]{2,1,0:T(8,128)(2,1)}), bf16[16,48,384]{2,1,0:T(8,128)(2,1)S(1)}, u32[]{:S(2)}, u32[]{:S(2)}) %all-to-all-start.1) | async-done | bytes 589856 | tf_op jit(solution)/shard_map/all_to_all | solution.py:109
  82.0 0.1 convert_reduce_fusion
  82.0 0.2 convolution_bitcast_fusion.2
  82.2 0.2 fusion.32
  82.4 0.1 slice_select_fusion
  82.5 0.1 collective-permute-start.4
  82.6 1.3 %collective-permute-done.4 = f32[96,192]{1,0:T(8,128)S(1)} collective-permute-done((f32[96,192]{1,0:T(8,128)S(1)}, f32[96,192]{1,0:T(8,128)S(1)}, u32[]{:S(2)}, u32[]{:S(2)}) %collective-permute-start.4) | collective-permute-done | bytes 73760 | tf_op jit(solution)/shard_map/ppermute | solution.py:33
  83.9 0.7 add_convert_fusion
  (27 shorter events, 0.1 us)
Async XLA Ops:
  24.6 12.0 %copy-start = (bf16[8,96,384]{2,1,0:T(8,128)(2,1)}, bf16[8,96,384]{2,1,0:T(8,128)(2,1)S(1)}, u32[]{:S(2)}) copy-start(bf16[8,96,384]{2,1,0:T(8,128)(2,1)S(1)} %all_to_all.10) | copy-start | bytes 1769476
  24.6 14.0 %collective-permute-start = (bf16[8,96,384]{2,1,0:T(8,128)(2,1)S(1)}, bf16[8,96,384]{2,1,0:T(8,128)(2,1)S(1)}, u32[]{:S(2)}, u32[]{:S(2)}) collective-permute-start(bf16[8,96,384]{2,1,0:T(8,128)(2,1)S(1)} %all_to_all.10), channel_id=1, source_target_pairs={{0,16},{16,0},{1,17},{17,1},{2,18},{18,2},{3,19},{19,3},{4,20},{20... | collective-permute-start | bytes 1769480 | tf_op jit(solution)/shard_map/ppermute | solution.py:57
  27.5 11.1 %collective-permute-start.1 = (f32[2,96]{1,0:T(2,128)S(1)}, f32[2,96]{1,0:T(2,128)S(1)}, u32[]{:S(2)}, u32[]{:S(2)}) collective-permute-start(f32[2,96]{1,0:T(2,128)S(1)} %get-tuple-element.18), channel_id=1, source_target_pairs={{0,16},{16,0},{1,17},{17,1},{2,18},{18,2},{3,19},{19,3},{4,20},{20... | collective-permute-start | bytes 2312 | tf_op jit(solution)/shard_map/ppermute | solution.py:57
  38.6 0.8 copy-start.1
  39.4 7.1 %slice-start.2 = ((s8[6291456]{0:T(1024)(128)(4,1)}), s8[2097152]{0:T(1024)(128)(4,1)S(1)}, s32[]{:S(2)}) async-start(s8[6291456]{0:T(1024)(128)(4,1)} %bitcast.113), calls=%async_computation.4 | async-start | bytes 4194304
  40.9 3.0 %collective-permute-start.2 = (bf16[2,8,96,384]{3,2,0,1:T(8,128)(2,1)S(1)}, bf16[2,8,96,384]{3,2,0,1:T(8,128)(2,1)}, u32[]{:S(2)}, u32[]{:S(2)}) collective-permute-start(bf16[2,8,96,384]{3,2,0,1:T(8,128)(2,1)S(1)} %pad_maximum_fusion), channel_id=1, source_target_pairs={{0,1},{1,0},{2,3},{3,2},{4,5},{5,4},{6,7},{7,6},{8,9},{9,8},{10,11... | collective-permute-start | bytes 3538952 | tf_op jit(solution)/shard_map/ppermute | solution.py:33
  42.0 4.5 %slice-start.3 = ((s8[6291456]{0:T(1024)(128)(4,1)}), s8[4194304]{0:T(1024)(128)(4,1)S(1)}, s32[]{:S(2)}) async-start(s8[6291456]{0:T(1024)(128)(4,1)} %bitcast.113), calls=%async_computation.5 | async-start | bytes 8388608
  44.0 4.1 %slice-start.4 = ((s8[6291456]{0:T(1024)(128)(4,1)}), s8[4194304]{0:T(1024)(128)(4,1)S(1)}, s32[]{:S(2)}) async-start(s8[6291456]{0:T(1024)(128)(4,1)} %bitcast.116), calls=%async_computation.6 | async-start | bytes 8388608
  45.6 2.4 %slice-start.5 = ((s8[6291456]{0:T(1024)(128)(4,1)}), s8[2097152]{0:T(1024)(128)(4,1)S(1)}, s32[]{:S(2)}) async-start(s8[6291456]{0:T(1024)(128)(4,1)} %bitcast.116), calls=%async_computation.7 | async-start | bytes 4194304
  46.5 1.5 %copy-start.3 = (s32[1,192,1024]{2,1,0:T(8,128)S(1)}, s32[1,192,1024]{2,1,0:T(8,128)}, u32[]{:S(2)}) copy-start(s32[1,192,1024]{2,1,0:T(8,128)} %param.15) | copy-start | bytes 2359300
  46.6 3.9 %slice-start = ((s8[6291456]{0:T(1024)(128)(4,1)}), s8[4194304]{0:T(1024)(128)(4,1)S(1)}, s32[]{:S(2)}) async-start(s8[6291456]{0:T(1024)(128)(4,1)} %bitcast.110), calls=%async_computation.2 | async-start | bytes 8388608
  48.1 2.4 %slice-start.1 = ((s8[6291456]{0:T(1024)(128)(4,1)}), s8[2097152]{0:T(1024)(128)(4,1)S(1)}, s32[]{:S(2)}) async-start(s8[6291456]{0:T(1024)(128)(4,1)} %bitcast.110), calls=%async_computation.3 | async-start | bytes 4194304
  57.0 2.1 %collective-permute-start.3 = (bf16[2,48,3072]{2,1,0:T(8,128)(2,1)S(1)}, bf16[2,48,3072]{2,1,0:T(8,128)(2,1)S(1)}, u32[]{:S(2)}, u32[]{:S(2)}) collective-permute-start(bf16[2,48,3072]{2,1,0:T(8,128)(2,1)S(1)} %select_bitcast_fusion.2), channel_id=1, source_target_pairs={{0,1},{1,0},{2,3},{3,2},{4,5},{5,4},{6,7},{7,6},{8,9},{9,8},{10,11... | collective-permute-start | bytes 1769480 | tf_op jit(solution)/shard_map/ppermute | solution.py:33
  59.3 6.1 %copy-start.2 = (s32[2,96]{1,0:T(2,128)S(1)}, s32[2,96]{1,0:T(2,128)}, u32[]{:S(2)}) copy-start(s32[2,96]{1,0:T(2,128)} %param.13) | copy-start | bytes 2308
  60.4 21.6 %all-to-all-start.1 = ((bf16[16,48,384]{2,1,0:T(8,128)(2,1)}), bf16[16,48,384]{2,1,0:T(8,128)(2,1)S(1)}, u32[]{:S(2)}, u32[]{:S(2)}) async-start(bf16[16,48,384]{2,1,0:T(8,128)(2,1)} %bitcast.35), calls=%async_computation.1 | async-start | bytes 1179648 | tf_op jit(solution)/shard_map/all_to_all | solution.py:109
  82.5 1.4 %collective-permute-start.4 = (f32[96,192]{1,0:T(8,128)S(1)}, f32[96,192]{1,0:T(8,128)S(1)}, u32[]{:S(2)}, u32[]{:S(2)}) collective-permute-start(f32[96,192]{1,0:T(8,128)S(1)} %slice_select_fusion), channel_id=1, source_target_pairs={{0,1},{1,0},{2,3},{3,2},{4,5},{5,4},{6,7},{7,6},{8,9},{9,8},{10,11... | collective-permute-start | bytes 221192 | tf_op jit(solution)/shard_map/ppermute | solution.py:33

commit v17 on v16

--- a/solution.py
+++ b/solution.py
@@ -63,12 +63,15 @@
     raw = jnp.concatenate([tokens, cotangent], axis=1)
     outgoing = jnp.broadcast_to(raw[None], (chip_count, group_tokens, 2 * local_width))
     in_plane = lax.all_to_all(outgoing, "chip", split_axis=0, concat_axis=0, tiled=True)
+    partner_plane = swap_cores(in_plane)
     own = from_groups(in_plane, lambda values, row: values)
-    down_t, own, info_rel = lax.optimization_barrier((jnp.transpose(down_mat), own, info_rel))
+    down_t, own, info_rel, partner_plane = lax.optimization_barrier(
+        (jnp.transpose(down_mat), own, info_rel, partner_plane)
+    )
     info_abs = info_rel[(group - jnp.arange(expert_count)) % expert_count]
     mine_tokens = info_abs[:, 0].astype(jnp.int32)
     mine_weights = info_abs[:, 1].reshape(slot_count, 1, 1, 1)
-    other = swap_cores(own)
+    other = jnp.concatenate([partner_plane[None], swap_cores(own[1:])], axis=0)
     full = order_by_core(own, other, axis=2)
     block_rel = (group - jnp.arange(expert_count)) % expert_count
     column = (block_rel[:, None] * group_tokens + mine_tokens).reshape(-1)

time: 85.1 us -> 84 us (0.987)
  matrix products: 11.5 us -> 14.8 us
  other arithmetic: 6.76 us -> 4 us
  waiting for transfers between devices: 23.4 us -> 22.5 us
    dot_general x1, matrix products: 1.48 us -> 4.85 us  [body(): lax.dot_general(part_inputs, gate_rows, fwd_dims, preferred_element_type=...]
    another operation x2, other arithmetic: 1.53 us -> 0.14 us  [from_groups(): return jnp.stack(pieces)]
    another operation x1, other arithmetic: 1.64 us -> 0.27 us  [order_by_core(): return jnp.stack([low, high], axis=axis)]
    ppermute x3 -> x4, waiting for transfers between devices: 5.1 us -> 4.14 us  [swap_cores(): return lax.ppermute(values, 'core', [(0, 1), (1, 0)])]
    unnamed x22 -> x18, local copies, waits for them, and re-layouts: 9.59 us -> 8.8 us
  transfers between devices with their start and end apart: 6 -> 7, of which waited for: 5 -> 5; matrix products, arithmetic and copies ran while one was open for 13% -> 14% of each run, Pallas kernels for 0% -> 0%
where the time goes in v17:
time: 84 us; the launch traced here: 83.5 us
  blocking collectives  23.6 us (28%)
  waiting for transfers between devices  22.5 us (27%)
  matrix products  14.8 us (18%)
  local copies, waits for them, and re-layouts  10.9 us (13%)
  starting transfers between devices  7.37 us (9%)
  other arithmetic  4 us (5%)
    all_to_all x1, blocking collectives, body(): lax.all_to_all(outgoing, 'chip', split_axis=0, concat_axis=0, tiled=True)  23.6 us
    all_to_all x1, waiting for transfers between devices, body(): lax.all_to_all(blocks, CROSS, split_axis=0, concat_axis=0, tiled=True)  16.4 us
    unnamed x18, local copies, waits for them, and re-layouts  8.8 us
    all_to_all x1, starting transfers between devices, body(): lax.all_to_all(blocks, CROSS, split_axis=0, concat_axis=0, tiled=True)  5 us
    dot_general x1, matrix products, body(): lax.dot_general(part_inputs, gate_rows, fwd_dims, preferred_element_type=...  4.85 us
    ppermute x4, waiting for transfers between devices, swap_cores(): return lax.ppermute(values, 'core', [(0, 1), (1, 0)])  4.14 us
    dot_general x1, matrix products, body(): lax.dot_general(part_cot, down_rows, fwd_dims, preferred_element_type=jnp...  2.35 us
    dot_general x1, matrix products, body(): lax.dot_general(grad_gate, gate_mat, back_dims, preferred_element_type=jn...  2.22 us
  transfers between devices with their start and end apart: 7, of which 5 were waited for; matrix products, arithmetic and copies ran while one was open for 14% of the time, Pallas kernels for 0%

profile of v17, /device:TPU:0, one launch (start us, length us, event | category | flops | bytes accessed | tf_op | source)
XLA Modules:
  0.0 83.5 jit_solution(13198575670210178099)
XLA Ops:
  0.0 0.9 %pad_maximum_fusion.2 = bf16[96,384]{1,0:T(8,128)(2,1)S(1)} fusion(bf16[96,192]{1,0:T(8,128)(2,1)} %param.9, bf16[96,192]{1,0:T(8,128)(2,1)} %param.8), kind=kLoop, calls=%fused_computation.56 | loop fusion | flops 147456 | bytes 147456 | tf_op jit(solution)/shard_map/concatenate | solution.py:63
  0.9 0.1 broadcast_in_dim.4
  1.0 23.6 %all_to_all.10 = bf16[8,96,384]{2,1,0:T(8,128)(2,1)S(1)} all-to-all(bf16[8,96,384]{2,1,0:T(8,128)(2,1)S(1)} %broadcast_in_dim.4), channel_id=1, replica_groups=mesh['expert'=2,'chip'=8,'core'=2] {'chip'}, dimensions={0} | all-to-all | bytes 1179648 | tf_op jit(solution)/shard_map/all_to_all | solution.py:65
  24.6 1.5 %collective-permute-start = (bf16[8,96,384]{2,1,0:T(8,128)(2,1)S(1)}, bf16[8,96,384]{2,1,0:T(8,128)(2,1)S(1)}, u32[]{:S(2)}, u32[]{:S(2)}) collective-permute-start(bf16[8,96,384]{2,1,0:T(8,128)(2,1)S(1)} %all_to_all.10), channel_id=1, source_target_pairs={{0,16},{16,0},{1,17},{17,1},{2,18},{18,2},{3,19},{19,3},{4,20},{20... | collective-permute-start | bytes 1769480 | tf_op jit(solution)/shard_map/ppermute | solution.py:57
  26.1 0.7 convert_element_type.68
  26.8 0.7 fusion.52
  27.5 0.5 collective-permute-start.1
  28.0 8.7 %copy.28 = bf16[1,1024,3072]{1,2,0:T(8,128)(2,1)} copy(bf16[1,1024,3072]{2,1,0:T(8,128)(2,1)} %param.12) | data formatting | bytes 12582912 | tf_op args[4]
  36.6 1.9 %collective-permute-done.1 = f32[2,96]{1,0:T(2,128)S(1)} collective-permute-done((f32[2,96]{1,0:T(2,128)S(1)}, f32[2,96]{1,0:T(2,128)S(1)}, u32[]{:S(2)}, u32[]{:S(2)}) %collective-permute-start.1) | collective-permute-done | bytes 800 | tf_op jit(solution)/shard_map/ppermute | solution.py:57
  38.6 0.1 pad_maximum_fusion
  38.7 0.1 slice.42
  38.8 0.1 collective-permute-start.3
  38.9 0.1 add.87
  39.0 0.1 add.88
  39.1 0.6 gather_fusion
  39.7 0.1 convert_element_type.70
  39.8 0.1 mul.77
  39.9 1.0 %collective-permute-done.3 = bf16[1,8,96,384]{3,2,0,1:T(8,128)(2,1)S(1)} collective-permute-done((bf16[1,8,96,384]{3,2,0,1:T(8,128)(2,1)S(1)}, bf16[1,8,96,384]{3,2,0,1:T(8,128)(2,1)S(1)}, u32[]{:S(2)}, u32[]{:S(2)}) %collective-permute-start.3) | collective-permute-done | bytes 589856 | tf_op jit(solution)/shard_map/ppermute | solution.py:33
  40.9 0.3 select_bitcast_fusion.1
  41.2 0.9 %fusion.15 = f32[192,8,2,384]{3,0,2,1:T(8,128)S(1)} fusion(bf16[2,8,1,96,384]{4,3,0,2,1:T(8,128)(2,1)S(1)} %get-tuple-element.18, bf16[2,8,1,96,384]{4,3,0,2,1:T(8,128)(2,1)S(1)} %get-tuple-element.17, s32[2,96]{1,0:T(2,128)S(1)} %multiply_add_fusion, s32[192]{0:T(256)S(1)} %add.89), kind=kOutput, calls=%fused_computation.14 | convolution fusion | flops 457740288 | bytes 7079424 | tf_op jit(solution)/shard_map/dot_general | solution.py:80
  42.0 0.0 copy-start.1
  42.1 0.0 slice-start
  42.1 4.8 %convolution_bitcast_fusion = f32[192,1024]{1,0:T(8,128)S(1)} fusion(bf16[8,2,192,1024]{3,2,1,0:T(8,128)(2,1)} %bitcast.116, f32[192,8,2,384]{3,0,2,1:T(8,128)S(1)} %fusion.15), kind=kOutput, calls=%fused_computation.17 | convolution fusion | flops 1207959552 | bytes 8650752 | tf_op jit(solution)/shard_map/dot_general | solution.py:88
  47.0 0.0 slice-start.1
  47.0 0.0 slice-start.2
  47.0 2.4 %multiply_convert_fusion = (bf16[192,1024]{1,0:T(8,128)(2,1)S(1)}, f32[192,1024]{1,0:T(8,128)S(1)}) fusion(f32[192,1024]{1,0:T(8,128)S(1)} %convolution_bitcast_fusion, s32[1,192,1024]{2,1,0:T(8,128)S(1)} %copy-done.1, bf16[8,2,192,1024]{3,2,1,0:T(8,128)(2,1)S(1)} %bitcast.121, f32[192,8,2,384]{3,0,2,1:T(8,128)S(1)} %fusion.15, f32[192]{0:T(256)S(1)} %mul.77), kind=kOutput, calls=%fused_computation.42 | convolution fusion | flops 1211695104 | bytes 12190720 | tf_op jit(solution)/shard_map/dot_general | solution.py:90
  49.4 0.0 slice-start.3
  49.4 1.9 %fusion.39 = bf16[192,1024]{1,0:T(8,128)(2,1)S(1)} fusion(f32[192,1024]{1,0:T(8,128)S(1)} %convolution_bitcast_fusion, f32[192,1024]{1,0:T(8,128)S(1)} %get-tuple-element.22, bf16[8,2,192,1024]{3,2,1,0:T(8,128)(2,1)S(1)} %bitcast.115, f32[192,8,2,384]{3,0,2,1:T(8,128)S(1)} %fusion.15), kind=kOutput, calls=%fused_computation.41 | convolution fusion | flops 1212088320 | bytes 9830400 | tf_op jit(solution)/shard_map/dot_general | solution.py:89
  51.3 2.2 %fusion = f32[192,3072]{1,0:T(8,128)S(1)} fusion(bf16[192,1024]{1,0:T(8,128)(2,1)S(1)} %get-tuple-element.16, bf16[1,3072,1024]{2,1,0:T(8,128)(2,1)S(1)} %bitcast.114), kind=kOutput, calls=%fused_computation.1 | convolution fusion | flops 1207959552 | bytes 9043968 | tf_op jit(solution)/shard_map/dot_general | solution.py:103
  53.6 2.2 %fusion.7 = bf16[192,3072]{1,0:T(8,128)(2,1)S(1)} fusion(f32[192,3072]{1,0:T(8,128)S(1)} %fusion, bf16[192,1024]{1,0:T(8,128)(2,1)S(1)} %fusion.39, bf16[1,3072,1024]{2,1,0:T(8,128)(2,1)S(1)} %bitcast.118), kind=kOutput, calls=%fused_computation.6 | convolution fusion | flops 1209139200 | bytes 10223616 | tf_op jit(solution)/shard_map/dot_general | solution.py:101
  55.8 0.1 select_bitcast_fusion.2
  55.9 0.2 collective-permute-start.4
  56.1 1.9 %collective-permute-done.4 = bf16[2,48,3072]{2,1,0:T(8,128)(2,1)S(1)} collective-permute-done((bf16[2,48,3072]{2,1,0:T(8,128)(2,1)S(1)}, bf16[2,48,3072]{2,1,0:T(8,128)(2,1)S(1)}, u32[]{:S(2)}, u32[]{:S(2)}) %collective-permute-start.4) | collective-permute-done | bytes 589856 | tf_op jit(solution)/shard_map/ppermute | solution.py:33
  57.9 0.2 fusion.31
  58.2 0.1 copy.42
  58.3 0.1 bitcast_bitcast_fusion
  58.3 0.9 %copy.34 = bf16[2,8,48,384]{3,2,1,0:T(8,128)(2,1)} copy(bf16[2,8,48,384]{3,1,2,0:T(8,128)(2,1)S(1)} %bitcast_bitcast_fusion) | data formatting | bytes 1179648 | tf_op jit(solution)/shard_map/transpose | solution.py:111
  59.2 5.0 %all-to-all-start.1 = ((bf16[16,48,384]{2,1,0:T(8,128)(2,1)}), bf16[16,48,384]{2,1,0:T(8,128)(2,1)S(1)}, u32[]{:S(2)}, u32[]{:S(2)}) async-start(bf16[16,48,384]{2,1,0:T(8,128)(2,1)} %bitcast.37), calls=%async_computation.1 | async-start | bytes 1179648 | tf_op jit(solution)/shard_map/all_to_all | solution.py:112
  64.2 0.1 eq.46
  64.3 0.1 fusion.44
  64.4 16.4 %all-to-all-done.1 = bf16[16,48,384]{2,1,0:T(8,128)(2,1)S(1)} async-done(((bf16[16,48,384]{2,1,0:T(8,128)(2,1)}), bf16[16,48,384]{2,1,0:T(8,128)(2,1)S(1)}, u32[]{:S(2)}, u32[]{:S(2)}) %all-to-all-start.1) | async-done | bytes 589856 | tf_op jit(solution)/shard_map/all_to_all | solution.py:112
  80.8 0.1 convert_reduce_fusion
  80.9 0.2 convolution_bitcast_fusion.2
  81.1 0.2 fusion.32
  81.3 0.1 slice_select_fusion
  81.4 0.1 collective-permute-start.5
  81.5 1.3 %collective-permute-done.5 = f32[96,192]{1,0:T(8,128)S(1)} collective-permute-done((f32[96,192]{1,0:T(8,128)S(1)}, f32[96,192]{1,0:T(8,128)S(1)}, u32[]{:S(2)}, u32[]{:S(2)}) %collective-permute-start.5) | collective-permute-done | bytes 73760 | tf_op jit(solution)/shard_map/ppermute | solution.py:33
  82.8 0.7 add_convert_fusion
  (26 shorter events, 0.1 us)
Async XLA Ops:
  24.6 14.0 %collective-permute-start = (bf16[8,96,384]{2,1,0:T(8,128)(2,1)S(1)}, bf16[8,96,384]{2,1,0:T(8,128)(2,1)S(1)}, u32[]{:S(2)}, u32[]{:S(2)}) collective-permute-start(bf16[8,96,384]{2,1,0:T(8,128)(2,1)S(1)} %all_to_all.10), channel_id=1, source_target_pairs={{0,16},{16,0},{1,17},{17,1},{2,18},{18,2},{3,19},{19,3},{4,20},{20... | collective-permute-start | bytes 1769480 | tf_op jit(solution)/shard_map/ppermute | solution.py:57
  26.1 12.6 %collective-permute-start.2 = (bf16[8,96,384]{2,1,0:T(8,128)(2,1)S(1)}, bf16[8,96,384]{2,1,0:T(8,128)(2,1)S(1)}, u32[]{:S(2)}, u32[]{:S(2)}) collective-permute-start(bf16[8,96,384]{2,1,0:T(8,128)(2,1)S(1)} %all_to_all.10), channel_id=1, source_target_pairs={{0,1},{1,0},{2,3},{3,2},{4,5},{5,4},{6,7},{7,6},{8,9},{9,8},{10,11... | collective-permute-start | bytes 1769480 | tf_op jit(solution)/shard_map/ppermute | solution.py:33
  27.5 11.1 %collective-permute-start.1 = (f32[2,96]{1,0:T(2,128)S(1)}, f32[2,96]{1,0:T(2,128)S(1)}, u32[]{:S(2)}, u32[]{:S(2)}) collective-permute-start(f32[2,96]{1,0:T(2,128)S(1)} %get-tuple-element.20), channel_id=1, source_target_pairs={{0,16},{16,0},{1,17},{17,1},{2,18},{18,2},{3,19},{19,3},{4,20},{20... | collective-permute-start | bytes 2312 | tf_op jit(solution)/shard_map/ppermute | solution.py:57
  38.8 2.1 %collective-permute-start.3 = (bf16[1,8,96,384]{3,2,0,1:T(8,128)(2,1)S(1)}, bf16[1,8,96,384]{3,2,0,1:T(8,128)(2,1)S(1)}, u32[]{:S(2)}, u32[]{:S(2)}) collective-permute-start(bf16[1,8,96,384]{3,2,0,1:T(8,128)(2,1)S(1)} %slice.42), channel_id=1, source_target_pairs={{0,1},{1,0},{2,3},{3,2},{4,5},{5,4},{6,7},{7,6},{8,9},{9,8},{10,11... | collective-permute-start | bytes 1769480 | tf_op jit(solution)/shard_map/ppermute | solution.py:33
  40.9 6.1 %slice-start.4 = ((s8[6291456]{0:T(1024)(128)(4,1)}), s8[4194304]{0:T(1024)(128)(4,1)S(1)}, s32[]{:S(2)}) async-start(s8[6291456]{0:T(1024)(128)(4,1)} %bitcast.119), calls=%async_computation.6 | async-start | bytes 8388608
  41.2 5.8 %slice-start.5 = ((s8[6291456]{0:T(1024)(128)(4,1)}), s8[2097152]{0:T(1024)(128)(4,1)S(1)}, s32[]{:S(2)}) async-start(s8[6291456]{0:T(1024)(128)(4,1)} %bitcast.119), calls=%async_computation.7 | async-start | bytes 4194304
  42.0 4.9 %copy-start.1 = (s32[1,192,1024]{2,1,0:T(8,128)S(1)}, s32[1,192,1024]{2,1,0:T(8,128)}, u32[]{:S(2)}) copy-start(s32[1,192,1024]{2,1,0:T(8,128)} %param.15) | copy-start | bytes 2359300
  42.1 7.3 %slice-start = ((s8[6291456]{0:T(1024)(128)(4,1)}), s8[4194304]{0:T(1024)(128)(4,1)S(1)}, s32[]{:S(2)}) async-start(s8[6291456]{0:T(1024)(128)(4,1)} %bitcast.113), calls=%async_computation.2 | async-start | bytes 8388608
  47.0 2.4 %slice-start.1 = ((s8[6291456]{0:T(1024)(128)(4,1)}), s8[2097152]{0:T(1024)(128)(4,1)S(1)}, s32[]{:S(2)}) async-start(s8[6291456]{0:T(1024)(128)(4,1)} %bitcast.113), calls=%async_computation.3 | async-start | bytes 4194304
  47.0 6.6 %slice-start.2 = ((s8[6291456]{0:T(1024)(128)(4,1)}), s8[4194304]{0:T(1024)(128)(4,1)S(1)}, s32[]{:S(2)}) async-start(s8[6291456]{0:T(1024)(128)(4,1)} %bitcast.117), calls=%async_computation.4 | async-start | bytes 8388608
  49.4 4.2 %slice-start.3 = ((s8[6291456]{0:T(1024)(128)(4,1)}), s8[2097152]{0:T(1024)(128)(4,1)S(1)}, s32[]{:S(2)}) async-start(s8[6291456]{0:T(1024)(128)(4,1)} %bitcast.117), calls=%async_computation.5 | async-start | bytes 4194304
  55.9 2.1 %collective-permute-start.4 = (bf16[2,48,3072]{2,1,0:T(8,128)(2,1)S(1)}, bf16[2,48,3072]{2,1,0:T(8,128)(2,1)S(1)}, u32[]{:S(2)}, u32[]{:S(2)}) collective-permute-start(bf16[2,48,3072]{2,1,0:T(8,128)(2,1)S(1)} %select_bitcast_fusion.2), channel_id=1, source_target_pairs={{0,1},{1,0},{2,3},{3,2},{4,5},{5,4},{6,7},{7,6},{8,9},{9,8},{10,11... | collective-permute-start | bytes 1769480 | tf_op jit(solution)/shard_map/ppermute | solution.py:33
  58.2 6.1 %copy-start = (s32[2,96]{1,0:T(2,128)S(1)}, s32[2,96]{1,0:T(2,128)}, u32[]{:S(2)}) copy-start(s32[2,96]{1,0:T(2,128)} %param.13) | copy-start | bytes 2308
  59.2 21.6 %all-to-all-start.1 = ((bf16[16,48,384]{2,1,0:T(8,128)(2,1)}), bf16[16,48,384]{2,1,0:T(8,128)(2,1)S(1)}, u32[]{:S(2)}, u32[]{:S(2)}) async-start(bf16[16,48,384]{2,1,0:T(8,128)(2,1)} %bitcast.37), calls=%async_computation.1 | async-start | bytes 1179648 | tf_op jit(solution)/shard_map/all_to_all | solution.py:112
  81.4 1.4 %collective-permute-start.5 = (f32[96,192]{1,0:T(8,128)S(1)}, f32[96,192]{1,0:T(8,128)S(1)}, u32[]{:S(2)}, u32[]{:S(2)}) collective-permute-start(f32[96,192]{1,0:T(8,128)S(1)} %slice_select_fusion), channel_id=1, source_target_pairs={{0,1},{1,0},{2,3},{3,2},{4,5},{5,4},{6,7},{7,6},{8,9},{9,8},{10,11... | collective-permute-start | bytes 221192 | tf_op jit(solution)/shard_map/ppermute | solution.py:33

commit v18 on v16

--- a/solution.py
+++ b/solution.py
@@ -57,26 +57,35 @@
             pieces.append(lax.ppermute(moved, "expert", [(i, (i + shift) % expert_count) for i in range(expert_count)]))
         return jnp.stack(pieces)
 
-    info = jnp.stack([slot_token.astype(jnp.float32), slot_weight], axis=1)
-    info_rel = from_groups(info, lambda values, row: values[row])
-
     raw = jnp.concatenate([tokens, cotangent], axis=1)
     outgoing = jnp.broadcast_to(raw[None], (chip_count, group_tokens, 2 * local_width))
     in_plane = lax.all_to_all(outgoing, "chip", split_axis=0, concat_axis=0, tiled=True)
-    own = from_groups(in_plane, lambda values, row: values)
-    down_t, own, info_rel = lax.optimization_barrier((jnp.transpose(down_mat), own, info_rel))
-    info_abs = info_rel[(group - jnp.arange(expert_count)) % expert_count]
-    mine_tokens = info_abs[:, 0].astype(jnp.int32)
-    mine_weights = info_abs[:, 1].reshape(slot_count, 1, 1, 1)
-    other = swap_cores(own)
-    full = order_by_core(own, other, axis=2)
+    partner_plane = swap_cores(in_plane)
+    token_ids = jnp.arange(group_tokens, dtype=jnp.int32)
+
+    def rows_for(plane, expert):
+        pick = (slot_token[expert][:, None] == token_ids[None, :]).astype(jnp.bfloat16)
+        picked = lax.dot_general(pick, plane, (((1,), (1,)), ((), ())), preferred_element_type=jnp.float32)
+        scaled = slot_weight[expert].reshape(-1, 1, 1) * picked[..., local_width:]
+        return jnp.concatenate(
+            [picked[..., :local_width].astype(jnp.bfloat16), scaled.astype(jnp.bfloat16)], axis=-1
+        )
+
+    own_rel = [rows_for(in_plane, group)]
+    partner_rel = [rows_for(partner_plane, group)]
+    for shift in shifts:
+        target = (group + shift) % expert_count
+        perm = [(i, (i + shift) % expert_count) for i in range(expert_count)]
+        moved = lax.ppermute(rows_for(in_plane, target), "expert", perm)
+        own_rel.append(moved)
+        partner_rel.append(swap_cores(moved))
     block_rel = (group - jnp.arange(expert_count)) % expert_count
-    column = (block_rel[:, None] * group_tokens + mine_tokens).reshape(-1)
-    pick = (column[:, None] == jnp.arange(expert_count * group_tokens)[None, :]).astype(jnp.bfloat16)
-    pick = pick.reshape(slot_count, expert_count, group_tokens)
-    rows = lax.dot_general(pick, full, (((1, 2), (0, 3)), ((), ())), preferred_element_type=jnp.float32)
-    part_inputs = rows[..., :local_width].astype(jnp.bfloat16)
-    part_cot = (mine_weights * rows[..., local_width:]).astype(jnp.bfloat16)
+    own = jnp.stack(own_rel)[block_rel]
+    other = jnp.stack(partner_rel)[block_rel]
+    down_t, own, other = lax.optimization_barrier((jnp.transpose(down_mat), own, other))
+    full = order_by_core(own, other, axis=3).reshape(slot_count, chip_count, 2, 2 * local_width)
+    part_inputs = full[..., :local_width]
+    part_cot = full[..., local_width:]
 
     gate_rows = gate_mat.reshape(chip_count, 2, local_width, local_ff)
     up_rows = up_mat.reshape(chip_count, 2, local_width, local_ff)

time: 85.1 us -> 93.5 us (1.099)
  blocking collectives: 23.6 us -> 0 us
  waiting for transfers between devices: 23.4 us -> 40.2 us
  starting transfers between devices: 7.39 us -> 14.2 us
  local copies, waits for them, and re-layouts: 11.6 us -> 17.8 us
  other arithmetic: 6.76 us -> 8.53 us
    all_to_all x1 -> x0, blocking collectives: 23.6 us -> none  [body(): lax.all_to_all(outgoing, 'chip', split_axis=0, concat_axis=0, tiled=True)]
    all_to_all x0 -> x1, waiting for transfers between devices: none -> 15.8 us  [body(): lax.all_to_all(outgoing, 'chip', split_axis=0, concat_axis=0, tiled=True)]
    all_to_all x0 -> x1, starting transfers between devices: none -> 7.25 us  [body(): lax.all_to_all(outgoing, 'chip', split_axis=0, concat_axis=0, tiled=True)]
    gather x1 -> x2, local copies, waits for them, and re-layouts: 0.57 us -> 4.07 us  [the longest x1 3.26 us: body(): other = jnp.stack(partner_rel)[block_rel]]
    ppermute x2 -> x1, waiting for transfers between devices: 1.94 us -> 4.83 us  [body(): moved = lax.ppermute(rows_for(in_plane, target), 'expert', perm)]
    ppermute x3 -> x4, waiting for transfers between devices: 5.1 us -> 2.92 us  [swap_cores(): return lax.ppermute(values, 'core', [(0, 1), (1, 0)])]
    select_n x1 -> x2, other arithmetic: 0.01 us -> 1.5 us  [the longest x1 1.49 us: order_by_core(): high = jnp.where(first, other, own)]
    unnamed x22 -> x21, local copies, waits for them, and re-layouts: 9.59 us -> 10.5 us
  transfers between devices with their start and end apart: 6 -> 7, of which waited for: 5 -> 5; matrix products, arithmetic and copies ran while one was open for 13% -> 15% of each run, Pallas kernels for 0% -> 0%
where the time goes in v18:
time: 93.5 us; the launch traced here: 92.8 us
  waiting for transfers between devices  40.2 us (43%)
  local copies, waits for them, and re-layouts  17.8 us (19%)
  starting transfers between devices  14.2 us (15%)
  matrix products  11.8 us (13%)
  other arithmetic  8.53 us (9%)
    all_to_all x1, waiting for transfers between devices, body(): lax.all_to_all(blocks, CROSS, split_axis=0, concat_axis=0, tiled=True)  16.6 us
    all_to_all x1, waiting for transfers between devices, body(): lax.all_to_all(outgoing, 'chip', split_axis=0, concat_axis=0, tiled=True)  15.8 us
    unnamed x21, local copies, waits for them, and re-layouts  10.5 us
    all_to_all x1, starting transfers between devices, body(): lax.all_to_all(outgoing, 'chip', split_axis=0, concat_axis=0, tiled=True)  7.25 us
    ppermute x1, waiting for transfers between devices, body(): moved = lax.ppermute(rows_for(in_plane, target), 'expert', perm)  4.83 us
    all_to_all x1, starting transfers between devices, body(): lax.all_to_all(blocks, CROSS, split_axis=0, concat_axis=0, tiled=True)  4.72 us
    gather x1, local copies, waits for them, and re-layouts, body(): other = jnp.stack(partner_rel)[block_rel]  3.26 us
    ppermute x4, waiting for transfers between devices, swap_cores(): return lax.ppermute(values, 'core', [(0, 1), (1, 0)])  2.92 us
  transfers between devices with their start and end apart: 7, of which 5 were waited for; matrix products, arithmetic and copies ran while one was open for 15% of the time, Pallas kernels for 0%

profile of v18, /device:TPU:0, one launch (start us, length us, event | category | flops | bytes accessed | tf_op | source)
XLA Modules:
  0.0 92.8 jit_solution(10228341713485467490)
XLA Ops:
  0.0 0.9 %pad_maximum_fusion.3 = bf16[96,384]{1,0:T(8,128)(2,1)S(1)} fusion(bf16[96,192]{1,0:T(8,128)(2,1)} %param.9, bf16[96,192]{1,0:T(8,128)(2,1)} %param.8), kind=kLoop, calls=%fused_computation.63 | loop fusion | flops 147456 | bytes 147456 | tf_op jit(solution)/shard_map/concatenate | solution.py:60
  0.9 0.9 broadcast_in_dim.2
  1.8 7.3 %all-to-all-start = ((bf16[8,96,384]{2,1,0:T(8,128)(2,1)}), bf16[8,96,384]{2,1,0:T(8,128)(2,1)S(1)}, u32[]{:S(2)}, u32[]{:S(2)}) async-start(bf16[8,96,384]{2,1,0:T(8,128)(2,1)} %broadcast_in_dim.2), calls=%async_computation | async-start | bytes 1179648 | tf_op jit(solution)/shard_map/all_to_all | solution.py:62
  9.2 15.8 %all-to-all-done = bf16[8,96,384]{2,1,0:T(8,128)(2,1)S(1)} async-done(((bf16[8,96,384]{2,1,0:T(8,128)(2,1)}), bf16[8,96,384]{2,1,0:T(8,128)(2,1)S(1)}, u32[]{:S(2)}, u32[]{:S(2)}) %all-to-all-start) | async-done | bytes 589856 | tf_op jit(solution)/shard_map/all_to_all | solution.py:62
  25.0 0.4 fusion.55
  25.4 0.3 fusion.44
  25.7 0.2 pad_maximum_fusion.2
  25.9 1.6 %collective-permute-start = (bf16[96,8,384]{2,0,1:T(8,128)(2,1)S(1)}, bf16[96,8,384]{2,0,1:T(8,128)(2,1)}, u32[]{:S(2)}, u32[]{:S(2)}) collective-permute-start(bf16[96,8,384]{2,0,1:T(8,128)(2,1)S(1)} %pad_maximum_fusion.2), channel_id=1, source_target_pairs={{0,16},{16,0},{1,17},{17,1},{2,18},{18,2},{3,19},{19,3},{4,20},{20... | collective-permute-start | bytes 1769480 | tf_op jit(solution)/shard_map/ppermute | solution.py:79
  27.5 8.6 %copy.26 = bf16[1,1024,3072]{1,2,0:T(8,128)(2,1)} copy(bf16[1,1024,3072]{2,1,0:T(8,128)(2,1)} %param.12) | data formatting | bytes 12582912 | tf_op args[4]
  36.2 0.3 fusion.52
  36.6 0.4 fusion.50
  37.0 4.8 %collective-permute-done = bf16[96,8,384]{2,0,1:T(8,128)(2,1)} collective-permute-done((bf16[96,8,384]{2,0,1:T(8,128)(2,1)S(1)}, bf16[96,8,384]{2,0,1:T(8,128)(2,1)}, u32[]{:S(2)}, u32[]{:S(2)}) %collective-permute-start) | collective-permute-done | bytes 589856 | tf_op jit(solution)/shard_map/ppermute | solution.py:79
  41.8 0.5 fusion.43
  42.3 0.2 maximum_bitcast_fusion
  42.5 1.2 %pad_maximum_fusion = bf16[2,96,8,384]{3,1,2,0:T(8,128)(2,1)S(1)} fusion(bf16[1,96,8,384]{3,1,2,0:T(8,128)(2,1)} %bitcast.10, bf16[1,96,8,384]{3,1,2,0:T(8,128)(2,1)S(1)} %maximum_bitcast_fusion), kind=kLoop, calls=%fused_computation.20 | loop fusion | flops 589824 | bytes 2359296 | tf_op jit(solution)/shard_map/stack | solution.py:83
  43.7 0.8 gather_fusion
  44.5 0.2 maximum_bitcast_fusion.1
  44.8 2.2 %pad_maximum_fusion.1 = bf16[2,96,8,384]{3,1,2,0:T(8,128)(2,1)} fusion(bf16[1,96,8,384]{3,1,2,0:T(8,128)(2,1)} %bitcast.13, bf16[1,96,8,384]{3,1,2,0:T(8,128)(2,1)S(1)} %maximum_bitcast_fusion.1), kind=kLoop, calls=%fused_computation.21 | loop fusion | flops 589824 | bytes 2359296 | tf_op jit(solution)/shard_map/stack | solution.py:84
  47.0 3.3 %gather_fusion.1 = bf16[2,96,8,384]{3,1,2,0:T(8,128)(2,1)} fusion(bf16[2,96,8,384]{3,1,2,0:T(8,128)(2,1)} %pad_maximum_fusion.1, s32[1024]{0:T(1024)S(1)} %pad_clamp_fusion), kind=kCustom, calls=%fused_computation.1 | custom fusion | bytes 2359304 | tf_op jit(solution)/shard_map/gather | solution.py:84
  50.2 1.5 %broadcast_select_fusion = (bf16[2,96,8,384]{3,1,2,0:T(8,128)(2,1)S(1)}, bf16[2,96,8,384]{3,1,2,0:T(8,128)(2,1)S(1)}) fusion(bf16[2,96,8,384]{3,1,2,0:T(8,128)(2,1)} %gather_fusion.1, bf16[2,96,8,384]{3,1,2,0:T(8,128)(2,1)S(1)} %gather_fusion, pred[]{:T(512)S(6)} %eq.31), kind=kLoop, calls=%fused_computation.27 | loop fusion | flops 1179648 | bytes 4718593 | tf_op jit(solution)/shard_map/jit(_where)/select_n | solution.py:28
  51.8 0.4 copy.27
  52.2 0.2 copy_dynamic-update-slice_fusion.1
  52.3 0.4 copy.28
  52.7 0.3 copy_dynamic-update-slice_fusion
  53.0 0.9 slice-done.3
  53.9 1.5 %fusion.22 = f32[192,1024]{1,0:T(8,128)S(1)} fusion(bf16[8,2,192,1024]{3,2,1,0:T(8,128)(2,1)S(1)} %bitcast.118, bf16[192,8,2,384]{3,0,2,1:T(8,128)(2,1)S(1)} %copy_dynamic-update-slice_fusion), kind=kOutput, calls=%fused_computation.16 | convolution fusion | flops 1207959552 | bytes 8650752 | tf_op jit(solution)/shard_map/dot_general | solution.py:94
  55.4 0.6 slice-done.5
  56.0 0.1 copy-done.2
  56.1 2.4 %multiply_convert_fusion = (bf16[192,1024]{1,0:T(8,128)(2,1)S(1)}, f32[192,1024]{1,0:T(8,128)S(1)}) fusion(f32[192,1024]{1,0:T(8,128)S(1)} %fusion.22, s32[1,192,1024]{2,1,0:T(8,128)S(1)} %copy-done.2, bf16[8,2,192,1024]{3,2,1,0:T(8,128)(2,1)S(1)} %bitcast.121, bf16[192,8,2,384]{3,0,2,1:T(8,128)(2,1)S(1)} %copy_dynamic-update-slice_fusion), kind=kOutput, calls=%fused_computation.50 | convolution fusion | flops 1210515456 | bytes 10616832 | tf_op jit(solution)/shard_map/dot_general | solution.py:96
  58.6 1.9 %fusion.42 = bf16[192,1024]{1,0:T(8,128)(2,1)S(1)} fusion(f32[192,1024]{1,0:T(8,128)S(1)} %fusion.22, f32[192,1024]{1,0:T(8,128)S(1)} %get-tuple-element.24, bf16[8,2,192,1024]{3,2,1,0:T(8,128)(2,1)S(1)} %bitcast.115, bf16[192,8,2,384]{3,0,2,1:T(8,128)(2,1)S(1)} %copy_dynamic-update-slice_fusion), kind=kOutput, calls=%fused_computation.40 | convolution fusion | flops 1212088320 | bytes 9830400 | tf_op jit(solution)/shard_map/dot_general | solution.py:95
  60.5 2.2 %fusion = f32[192,3072]{1,0:T(8,128)S(1)} fusion(bf16[192,1024]{1,0:T(8,128)(2,1)S(1)} %get-tuple-element.14, bf16[1,3072,1024]{2,1,0:T(8,128)(2,1)S(1)} %bitcast.114), kind=kOutput, calls=%fused_computation.2 | convolution fusion | flops 1207959552 | bytes 9043968 | tf_op jit(solution)/shard_map/dot_general | solution.py:109
  62.8 2.3 %fusion.7 = bf16[192,3072]{1,0:T(8,128)(2,1)S(1)} fusion(f32[192,3072]{1,0:T(8,128)S(1)} %fusion, bf16[192,1024]{1,0:T(8,128)(2,1)S(1)} %fusion.42, bf16[1,3072,1024]{2,1,0:T(8,128)(2,1)S(1)} %bitcast.117), kind=kOutput, calls=%fused_computation.7 | convolution fusion | flops 1209139200 | bytes 10223616 | tf_op jit(solution)/shard_map/dot_general | solution.py:107
  65.1 0.6 collective-permute-start.3
  65.7 1.6 %collective-permute-done.3 = bf16[2,48,3072]{2,1,0:T(8,128)(2,1)S(1)} collective-permute-done((bf16[2,48,3072]{2,1,0:T(8,128)(2,1)S(1)}, bf16[2,48,3072]{2,1,0:T(8,128)(2,1)S(1)}, u32[]{:S(2)}, u32[]{:S(2)}) %collective-permute-start.3) | collective-permute-done | bytes 589856 | tf_op jit(solution)/shard_map/ppermute | solution.py:33
  67.3 0.2 fusion.34
  67.5 0.1 copy.39
  67.7 0.9 copy.33
  68.6 4.7 %all-to-all-start.1 = ((bf16[16,48,384]{2,1,0:T(8,128)(2,1)}), bf16[16,48,384]{2,1,0:T(8,128)(2,1)S(1)}, u32[]{:S(2)}, u32[]{:S(2)}) async-start(bf16[16,48,384]{2,1,0:T(8,128)(2,1)} %bitcast.33), calls=%async_computation.1 | async-start | bytes 1179648 | tf_op jit(solution)/shard_map/all_to_all | solution.py:118
  73.3 0.1 eq.32
  73.4 0.1 fusion.48
  73.5 16.6 %all-to-all-done.1 = bf16[16,48,384]{2,1,0:T(8,128)(2,1)S(1)} async-done(((bf16[16,48,384]{2,1,0:T(8,128)(2,1)}), bf16[16,48,384]{2,1,0:T(8,128)(2,1)S(1)}, u32[]{:S(2)}, u32[]{:S(2)}) %all-to-all-start.1) | async-done | bytes 589856 | tf_op jit(solution)/shard_map/all_to_all | solution.py:118
  90.2 0.1 convert_reduce_fusion
  90.2 0.2 convolution_bitcast_fusion
  90.4 0.2 fusion.35
  90.6 0.1 slice_select_fusion
  90.7 0.1 collective-permute-start.4
  90.8 1.3 %collective-permute-done.4 = f32[96,192]{1,0:T(8,128)S(1)} collective-permute-done((f32[96,192]{1,0:T(8,128)S(1)}, f32[96,192]{1,0:T(8,128)S(1)}, u32[]{:S(2)}, u32[]{:S(2)}) %collective-permute-start.4) | collective-permute-done | bytes 73760 | tf_op jit(solution)/shard_map/ppermute | solution.py:33
  92.1 0.7 add_convert_fusion
  (32 shorter events, 0.3 us)
Async XLA Ops:
  0.0 9.1 %copy-start = (s32[2,96]{1,0:T(2,128)S(1)}, s32[2,96]{1,0:T(2,128)}, u32[]{:S(2)}) copy-start(s32[2,96]{1,0:T(2,128)} %param.13) | copy-start | bytes 2308
  0.0 9.1 %copy-start.1 = (f32[2,96]{1,0:T(2,128)S(1)}, f32[2,96]{1,0:T(2,128)}, u32[]{:S(2)}) copy-start(f32[2,96]{1,0:T(2,128)} %param.14) | copy-start | bytes 2308
  1.8 23.1 %all-to-all-start = ((bf16[8,96,384]{2,1,0:T(8,128)(2,1)}), bf16[8,96,384]{2,1,0:T(8,128)(2,1)S(1)}, u32[]{:S(2)}, u32[]{:S(2)}) async-start(bf16[8,96,384]{2,1,0:T(8,128)(2,1)} %broadcast_in_dim.2), calls=%async_computation | async-start | bytes 1179648 | tf_op jit(solution)/shard_map/all_to_all | solution.py:62
  25.0 11.6 %collective-permute-start.1 = (bf16[8,96,384]{2,1,0:T(8,128)(2,1)S(1)}, bf16[8,96,384]{2,1,0:T(8,128)(2,1)S(1)}, u32[]{:S(2)}, u32[]{:S(2)}) collective-permute-start(bf16[8,96,384]{2,1,0:T(8,128)(2,1)S(1)} %all-to-all-done), channel_id=1, source_target_pairs={{0,1},{1,0},{2,3},{3,2},{4,5},{5,4},{6,7},{7,6},{8,9},{9,8},{10,11... | collective-permute-start | bytes 1769480 | tf_op jit(solution)/shard_map/ppermute | solution.py:33
  25.9 15.9 %collective-permute-start = (bf16[96,8,384]{2,0,1:T(8,128)(2,1)S(1)}, bf16[96,8,384]{2,0,1:T(8,128)(2,1)}, u32[]{:S(2)}, u32[]{:S(2)}) collective-permute-start(bf16[96,8,384]{2,0,1:T(8,128)(2,1)S(1)} %pad_maximum_fusion.2), channel_id=1, source_target_pairs={{0,16},{16,0},{1,17},{17,1},{2,18},{18,2},{3,19},{19,3},{4,20},{20... | collective-permute-start | bytes 1769480 | tf_op jit(solution)/shard_map/ppermute | solution.py:79
  41.8 3.0 %collective-permute-start.2 = (bf16[96,8,384]{2,0,1:T(8,128)(2,1)}, bf16[96,8,384]{2,0,1:T(8,128)(2,1)}, u32[]{:S(2)}, u32[]{:S(2)}) collective-permute-start(bf16[96,8,384]{2,0,1:T(8,128)(2,1)} %collective-permute-done), channel_id=1, source_target_pairs={{0,1},{1,0},{2,3},{3,2},{4,5},{5,4},{6,7},{7,6},{8,9},{9,8},{10,11... | collective-permute-start | bytes 1769480 | tf_op jit(solution)/shard_map/ppermute | solution.py:33
  47.0 6.0 %slice-start.2 = ((s8[6291456]{0:T(1024)(128)(4,1)}), s8[2097152]{0:T(1024)(128)(4,1)S(1)}, s32[]{:S(2)}) async-start(s8[6291456]{0:T(1024)(128)(4,1)} %bitcast.116), calls=%async_computation.4 | async-start | bytes 4194304
  51.7 2.2 %slice-start.3 = ((s8[6291456]{0:T(1024)(128)(4,1)}), s8[4194304]{0:T(1024)(128)(4,1)S(1)}, s32[]{:S(2)}) async-start(s8[6291456]{0:T(1024)(128)(4,1)} %bitcast.116), calls=%async_computation.5 | async-start | bytes 8388608
  52.3 3.1 %slice-start.4 = ((s8[6291456]{0:T(1024)(128)(4,1)}), s8[4194304]{0:T(1024)(128)(4,1)S(1)}, s32[]{:S(2)}) async-start(s8[6291456]{0:T(1024)(128)(4,1)} %bitcast.119), calls=%async_computation.6 | async-start | bytes 8388608
  53.9 2.0 %slice-start.5 = ((s8[6291456]{0:T(1024)(128)(4,1)}), s8[2097152]{0:T(1024)(128)(4,1)S(1)}, s32[]{:S(2)}) async-start(s8[6291456]{0:T(1024)(128)(4,1)} %bitcast.119), calls=%async_computation.7 | async-start | bytes 4194304
  53.9 2.2 %copy-start.2 = (s32[1,192,1024]{2,1,0:T(8,128)S(1)}, s32[1,192,1024]{2,1,0:T(8,128)}, u32[]{:S(2)}) copy-start(s32[1,192,1024]{2,1,0:T(8,128)} %param.15) | copy-start | bytes 2359300
  53.9 4.6 %slice-start = ((s8[6291456]{0:T(1024)(128)(4,1)}), s8[4194304]{0:T(1024)(128)(4,1)S(1)}, s32[]{:S(2)}) async-start(s8[6291456]{0:T(1024)(128)(4,1)} %bitcast.113), calls=%async_computation.2 | async-start | bytes 8388608
  56.1 2.5 %slice-start.1 = ((s8[6291456]{0:T(1024)(128)(4,1)}), s8[2097152]{0:T(1024)(128)(4,1)S(1)}, s32[]{:S(2)}) async-start(s8[6291456]{0:T(1024)(128)(4,1)} %bitcast.113), calls=%async_computation.3 | async-start | bytes 4194304
  65.1 2.2 %collective-permute-start.3 = (bf16[2,48,3072]{2,1,0:T(8,128)(2,1)S(1)}, bf16[2,48,3072]{2,1,0:T(8,128)(2,1)S(1)}, u32[]{:S(2)}, u32[]{:S(2)}) collective-permute-start(bf16[2,48,3072]{2,1,0:T(8,128)(2,1)S(1)} %select_bitcast_fusion), channel_id=1, source_target_pairs={{0,1},{1,0},{2,3},{3,2},{4,5},{5,4},{6,7},{7,6},{8,9},{9,8},{10,11... | collective-permute-start | bytes 1769480 | tf_op jit(solution)/shard_map/ppermute | solution.py:33
  68.6 21.6 %all-to-all-start.1 = ((bf16[16,48,384]{2,1,0:T(8,128)(2,1)}), bf16[16,48,384]{2,1,0:T(8,128)(2,1)S(1)}, u32[]{:S(2)}, u32[]{:S(2)}) async-start(bf16[16,48,384]{2,1,0:T(8,128)(2,1)} %bitcast.33), calls=%async_computation.1 | async-start | bytes 1179648 | tf_op jit(solution)/shard_map/all_to_all | solution.py:118
  90.7 1.4 %collective-permute-start.4 = (f32[96,192]{1,0:T(8,128)S(1)}, f32[96,192]{1,0:T(8,128)S(1)}, u32[]{:S(2)}, u32[]{:S(2)}) collective-permute-start(f32[96,192]{1,0:T(8,128)S(1)} %slice_select_fusion), channel_id=1, source_target_pairs={{0,1},{1,0},{2,3},{3,2},{4,5},{5,4},{6,7},{7,6},{8,9},{9,8},{10,11... | collective-permute-start | bytes 221192 | tf_op jit(solution)/shard_map/ppermute | solution.py:33

commit v19 on v17

--- a/solution.py
+++ b/solution.py
@@ -62,12 +62,11 @@
 
     raw = jnp.concatenate([tokens, cotangent], axis=1)
     outgoing = jnp.broadcast_to(raw[None], (chip_count, group_tokens, 2 * local_width))
+    outgoing, info_rel = lax.optimization_barrier((outgoing, info_rel))
     in_plane = lax.all_to_all(outgoing, "chip", split_axis=0, concat_axis=0, tiled=True)
     partner_plane = swap_cores(in_plane)
     own = from_groups(in_plane, lambda values, row: values)
-    down_t, own, info_rel, partner_plane = lax.optimization_barrier(
-        (jnp.transpose(down_mat), own, info_rel, partner_plane)
-    )
+    down_t, own, partner_plane = lax.optimization_barrier((jnp.transpose(down_mat), own, partner_plane))
     info_abs = info_rel[(group - jnp.arange(expert_count)) % expert_count]
     mine_tokens = info_abs[:, 0].astype(jnp.int32)
     mine_weights = info_abs[:, 1].reshape(slot_count, 1, 1, 1)

time: 84 us -> 86.5 us (1.030)
  starting transfers between devices: 7.37 us -> 10.2 us
  blocking collectives: 23.6 us -> 21.5 us
  waiting for transfers between devices: 22.5 us -> 24.3 us
    ppermute x2, starting transfers between devices: 2.03 us -> 4.49 us  [from_groups(): lax.ppermute(moved, 'expert', [(i, (i + shift) % expert_count) for i in r...]
    all_to_all x1, blocking collectives: 23.6 us -> 21.5 us  [body(): lax.all_to_all(outgoing, 'chip', split_axis=0, concat_axis=0, tiled=True)]
    ppermute x2, waiting for transfers between devices: 1.93 us -> 3.72 us  [from_groups(): lax.ppermute(moved, 'expert', [(i, (i + shift) % expert_count) for i in r...]
  transfers between devices with their start and end apart: 7 -> 7, of which waited for: 5 -> 6; matrix products, arithmetic and copies ran while one was open for 14% -> 13% of each run, Pallas kernels for 0% -> 0%
where the time goes in v19:
time: 86.5 us; the launch traced here: 86 us
  waiting for transfers between devices  24.3 us (28%)
  blocking collectives  21.5 us (25%)
  matrix products  14.8 us (17%)
  local copies, waits for them, and re-layouts  10.9 us (13%)
  starting transfers between devices  10.2 us (12%)
  other arithmetic  4 us (5%)
    all_to_all x1, blocking collectives, body(): lax.all_to_all(outgoing, 'chip', split_axis=0, concat_axis=0, tiled=True)  21.5 us
    all_to_all x1, waiting for transfers between devices, body(): lax.all_to_all(blocks, CROSS, split_axis=0, concat_axis=0, tiled=True)  16.4 us
    unnamed x18, local copies, waits for them, and re-layouts  8.8 us
    all_to_all x1, starting transfers between devices, body(): lax.all_to_all(blocks, CROSS, split_axis=0, concat_axis=0, tiled=True)  5.37 us
    dot_general x1, matrix products, body(): lax.dot_general(part_inputs, gate_rows, fwd_dims, preferred_element_type=...  4.84 us
    ppermute x2, starting transfers between devices, from_groups(): lax.ppermute(moved, 'expert', [(i, (i + shift) % expert_count) for i in r...  4.49 us
    ppermute x4, waiting for transfers between devices, swap_cores(): return lax.ppermute(values, 'core', [(0, 1), (1, 0)])  4.14 us
    ppermute x2, waiting for transfers between devices, from_groups(): lax.ppermute(moved, 'expert', [(i, (i + shift) % expert_count) for i in r...  3.72 us
  transfers between devices with their start and end apart: 7, of which 6 were waited for; matrix products, arithmetic and copies ran while one was open for 13% of the time, Pallas kernels for 0%

profile of v19, /device:TPU:0, one launch (start us, length us, event | category | flops | bytes accessed | tf_op | source)
XLA Modules:
  0.0 86.0 jit_solution(10471726796993382922)
XLA Ops:
  0.0 0.7 convert_element_type.68
  0.7 0.7 fusion.52
  1.4 3.0 %collective-permute-start = (f32[2,96]{1,0:T(2,128)S(1)}, f32[2,96]{1,0:T(2,128)S(1)}, u32[]{:S(2)}, u32[]{:S(2)}) collective-permute-start(f32[2,96]{1,0:T(2,128)S(1)} %get-tuple-element.22), channel_id=1, source_target_pairs={{0,16},{16,0},{1,17},{17,1},{2,18},{18,2},{3,19},{19,3},{4,20},{20... | collective-permute-start | bytes 2312 | tf_op jit(solution)/shard_map/ppermute | solution.py:57
  4.3 0.9 %pad_maximum_fusion.2 = bf16[96,384]{1,0:T(8,128)(2,1)S(1)} fusion(bf16[96,192]{1,0:T(8,128)(2,1)} %param.9, bf16[96,192]{1,0:T(8,128)(2,1)} %param.8), kind=kLoop, calls=%fused_computation.56 | loop fusion | flops 147456 | bytes 147456 | tf_op jit(solution)/shard_map/concatenate | solution.py:63
  5.2 0.6 collective-permute-done
  5.9 0.1 broadcast_in_dim.4
  5.9 21.5 %all_to_all.10 = bf16[8,96,384]{2,1,0:T(8,128)(2,1)S(1)} all-to-all(bf16[8,96,384]{2,1,0:T(8,128)(2,1)S(1)} %broadcast_in_dim.4), channel_id=1, replica_groups=mesh['expert'=2,'chip'=8,'core'=2] {'chip'}, dimensions={0} | all-to-all | bytes 1179648 | tf_op jit(solution)/shard_map/all_to_all | solution.py:66
  27.4 1.5 %collective-permute-start.1 = (bf16[8,96,384]{2,1,0:T(8,128)(2,1)S(1)}, bf16[8,96,384]{2,1,0:T(8,128)(2,1)S(1)}, u32[]{:S(2)}, u32[]{:S(2)}) collective-permute-start(bf16[8,96,384]{2,1,0:T(8,128)(2,1)S(1)} %all_to_all.10), channel_id=1, source_target_pairs={{0,16},{16,0},{1,17},{17,1},{2,18},{18,2},{3,19},{19,3},{4,20},{20... | collective-permute-start | bytes 1769480 | tf_op jit(solution)/shard_map/ppermute | solution.py:57
  28.9 8.7 %copy.28 = bf16[1,1024,3072]{1,2,0:T(8,128)(2,1)} copy(bf16[1,1024,3072]{2,1,0:T(8,128)(2,1)} %param.12) | data formatting | bytes 12582912 | tf_op args[4]
  37.6 3.1 %collective-permute-done.1 = bf16[8,96,384]{2,1,0:T(8,128)(2,1)S(1)} collective-permute-done((bf16[8,96,384]{2,1,0:T(8,128)(2,1)S(1)}, bf16[8,96,384]{2,1,0:T(8,128)(2,1)S(1)}, u32[]{:S(2)}, u32[]{:S(2)}) %collective-permute-start.1) | collective-permute-done | bytes 589856 | tf_op jit(solution)/shard_map/ppermute | solution.py:57
  40.7 0.1 pad_maximum_fusion
  40.8 0.1 slice.42
  40.9 0.1 collective-permute-start.3
  41.0 0.1 add.87
  41.1 0.1 add.88
  41.2 0.6 gather_fusion
  41.8 0.1 convert_element_type.70
  41.9 0.1 mul.77
  42.0 1.0 %collective-permute-done.3 = bf16[1,8,96,384]{3,2,0,1:T(8,128)(2,1)S(1)} collective-permute-done((bf16[1,8,96,384]{3,2,0,1:T(8,128)(2,1)S(1)}, bf16[1,8,96,384]{3,2,0,1:T(8,128)(2,1)S(1)}, u32[]{:S(2)}, u32[]{:S(2)}) %collective-permute-start.3) | collective-permute-done | bytes 589856 | tf_op jit(solution)/shard_map/ppermute | solution.py:33
  43.0 0.3 select_bitcast_fusion.1
  43.3 0.9 %fusion.15 = f32[192,8,2,384]{3,0,2,1:T(8,128)S(1)} fusion(bf16[2,8,1,96,384]{4,3,0,2,1:T(8,128)(2,1)S(1)} %get-tuple-element.20, bf16[2,8,1,96,384]{4,3,0,2,1:T(8,128)(2,1)S(1)} %get-tuple-element.19, s32[2,96]{1,0:T(2,128)S(1)} %multiply_add_fusion, s32[192]{0:T(256)S(1)} %add.89), kind=kOutput, calls=%fused_computation.14 | convolution fusion | flops 457740288 | bytes 7079424 | tf_op jit(solution)/shard_map/dot_general | solution.py:79
  44.2 0.0 slice-start
  44.2 4.8 %convolution_bitcast_fusion = f32[192,1024]{1,0:T(8,128)S(1)} fusion(bf16[8,2,192,1024]{3,2,1,0:T(8,128)(2,1)} %bitcast.116, f32[192,8,2,384]{3,0,2,1:T(8,128)S(1)} %fusion.15), kind=kOutput, calls=%fused_computation.17 | convolution fusion | flops 1207959552 | bytes 8650752 | tf_op jit(solution)/shard_map/dot_general | solution.py:87
  49.1 0.0 slice-start.1
  49.1 0.0 slice-start.2
  49.1 2.3 %multiply_convert_fusion = (bf16[192,1024]{1,0:T(8,128)(2,1)S(1)}, f32[192,1024]{1,0:T(8,128)S(1)}) fusion(f32[192,1024]{1,0:T(8,128)S(1)} %convolution_bitcast_fusion, s32[1,192,1024]{2,1,0:T(8,128)S(1)} %copy-done.1, bf16[8,2,192,1024]{3,2,1,0:T(8,128)(2,1)S(1)} %bitcast.121, f32[192,8,2,384]{3,0,2,1:T(8,128)S(1)} %fusion.15, f32[192]{0:T(256)S(1)} %mul.77), kind=kOutput, calls=%fused_computation.42 | convolution fusion | flops 1211695104 | bytes 12190720 | tf_op jit(solution)/shard_map/dot_general | solution.py:89
  51.5 0.0 slice-start.3
  51.5 1.9 %fusion.39 = bf16[192,1024]{1,0:T(8,128)(2,1)S(1)} fusion(f32[192,1024]{1,0:T(8,128)S(1)} %convolution_bitcast_fusion, f32[192,1024]{1,0:T(8,128)S(1)} %get-tuple-element.24, bf16[8,2,192,1024]{3,2,1,0:T(8,128)(2,1)S(1)} %bitcast.115, f32[192,8,2,384]{3,0,2,1:T(8,128)S(1)} %fusion.15), kind=kOutput, calls=%fused_computation.41 | convolution fusion | flops 1212088320 | bytes 9830400 | tf_op jit(solution)/shard_map/dot_general | solution.py:88
  53.4 2.2 %fusion = f32[192,3072]{1,0:T(8,128)S(1)} fusion(bf16[192,1024]{1,0:T(8,128)(2,1)S(1)} %get-tuple-element.18, bf16[1,3072,1024]{2,1,0:T(8,128)(2,1)S(1)} %bitcast.114), kind=kOutput, calls=%fused_computation.1 | convolution fusion | flops 1207959552 | bytes 9043968 | tf_op jit(solution)/shard_map/dot_general | solution.py:102
  55.7 2.2 %fusion.7 = bf16[192,3072]{1,0:T(8,128)(2,1)S(1)} fusion(f32[192,3072]{1,0:T(8,128)S(1)} %fusion, bf16[192,1024]{1,0:T(8,128)(2,1)S(1)} %fusion.39, bf16[1,3072,1024]{2,1,0:T(8,128)(2,1)S(1)} %bitcast.118), kind=kOutput, calls=%fused_computation.6 | convolution fusion | flops 1209139200 | bytes 10223616 | tf_op jit(solution)/shard_map/dot_general | solution.py:100
  57.9 0.1 select_bitcast_fusion.2
  58.0 0.2 collective-permute-start.4
  58.2 1.9 %collective-permute-done.4 = bf16[2,48,3072]{2,1,0:T(8,128)(2,1)S(1)} collective-permute-done((bf16[2,48,3072]{2,1,0:T(8,128)(2,1)S(1)}, bf16[2,48,3072]{2,1,0:T(8,128)(2,1)S(1)}, u32[]{:S(2)}, u32[]{:S(2)}) %collective-permute-start.4) | collective-permute-done | bytes 589856 | tf_op jit(solution)/shard_map/ppermute | solution.py:33
  60.0 0.2 fusion.31
  60.3 0.1 copy.42
  60.4 0.1 bitcast_bitcast_fusion
  60.4 0.9 %copy.34 = bf16[2,8,48,384]{3,2,1,0:T(8,128)(2,1)} copy(bf16[2,8,48,384]{3,1,2,0:T(8,128)(2,1)S(1)} %bitcast_bitcast_fusion) | data formatting | bytes 1179648 | tf_op jit(solution)/shard_map/transpose | solution.py:110
  61.3 5.4 %all-to-all-start.1 = ((bf16[16,48,384]{2,1,0:T(8,128)(2,1)}), bf16[16,48,384]{2,1,0:T(8,128)(2,1)S(1)}, u32[]{:S(2)}, u32[]{:S(2)}) async-start(bf16[16,48,384]{2,1,0:T(8,128)(2,1)} %bitcast.37), calls=%async_computation.1 | async-start | bytes 1179648 | tf_op jit(solution)/shard_map/all_to_all | solution.py:111
  66.7 0.1 eq.46
  66.8 0.1 fusion.44
  66.9 16.4 %all-to-all-done.1 = bf16[16,48,384]{2,1,0:T(8,128)(2,1)S(1)} async-done(((bf16[16,48,384]{2,1,0:T(8,128)(2,1)}), bf16[16,48,384]{2,1,0:T(8,128)(2,1)S(1)}, u32[]{:S(2)}, u32[]{:S(2)}) %all-to-all-start.1) | async-done | bytes 589856 | tf_op jit(solution)/shard_map/all_to_all | solution.py:111
  83.3 0.1 convert_reduce_fusion
  83.4 0.2 convolution_bitcast_fusion.2
  83.6 0.2 fusion.32
  83.8 0.1 slice_select_fusion
  83.9 0.1 collective-permute-start.5
  84.0 1.3 %collective-permute-done.5 = f32[96,192]{1,0:T(8,128)S(1)} collective-permute-done((f32[96,192]{1,0:T(8,128)S(1)}, f32[96,192]{1,0:T(8,128)S(1)}, u32[]{:S(2)}, u32[]{:S(2)}) %collective-permute-start.5) | collective-permute-done | bytes 73760 | tf_op jit(solution)/shard_map/ppermute | solution.py:33
  85.3 0.7 add_convert_fusion
  (26 shorter events, 0.1 us)
Async XLA Ops:
  1.4 4.5 %collective-permute-start = (f32[2,96]{1,0:T(2,128)S(1)}, f32[2,96]{1,0:T(2,128)S(1)}, u32[]{:S(2)}, u32[]{:S(2)}) collective-permute-start(f32[2,96]{1,0:T(2,128)S(1)} %get-tuple-element.22), channel_id=1, source_target_pairs={{0,16},{16,0},{1,17},{17,1},{2,18},{18,2},{3,19},{19,3},{4,20},{20... | collective-permute-start | bytes 2312 | tf_op jit(solution)/shard_map/ppermute | solution.py:57
  27.4 13.3 %collective-permute-start.1 = (bf16[8,96,384]{2,1,0:T(8,128)(2,1)S(1)}, bf16[8,96,384]{2,1,0:T(8,128)(2,1)S(1)}, u32[]{:S(2)}, u32[]{:S(2)}) collective-permute-start(bf16[8,96,384]{2,1,0:T(8,128)(2,1)S(1)} %all_to_all.10), channel_id=1, source_target_pairs={{0,16},{16,0},{1,17},{17,1},{2,18},{18,2},{3,19},{19,3},{4,20},{20... | collective-permute-start | bytes 1769480 | tf_op jit(solution)/shard_map/ppermute | solution.py:57
  28.9 11.9 %collective-permute-start.2 = (bf16[8,96,384]{2,1,0:T(8,128)(2,1)S(1)}, bf16[8,96,384]{2,1,0:T(8,128)(2,1)S(1)}, u32[]{:S(2)}, u32[]{:S(2)}) collective-permute-start(bf16[8,96,384]{2,1,0:T(8,128)(2,1)S(1)} %all_to_all.10), channel_id=1, source_target_pairs={{0,1},{1,0},{2,3},{3,2},{4,5},{5,4},{6,7},{7,6},{8,9},{9,8},{10,11... | collective-permute-start | bytes 1769480 | tf_op jit(solution)/shard_map/ppermute | solution.py:33
  40.9 2.1 %collective-permute-start.3 = (bf16[1,8,96,384]{3,2,0,1:T(8,128)(2,1)S(1)}, bf16[1,8,96,384]{3,2,0,1:T(8,128)(2,1)S(1)}, u32[]{:S(2)}, u32[]{:S(2)}) collective-permute-start(bf16[1,8,96,384]{3,2,0,1:T(8,128)(2,1)S(1)} %slice.42), channel_id=1, source_target_pairs={{0,1},{1,0},{2,3},{3,2},{4,5},{5,4},{6,7},{7,6},{8,9},{9,8},{10,11... | collective-permute-start | bytes 1769480 | tf_op jit(solution)/shard_map/ppermute | solution.py:33
  43.0 6.1 %slice-start.4 = ((s8[6291456]{0:T(1024)(128)(4,1)}), s8[4194304]{0:T(1024)(128)(4,1)S(1)}, s32[]{:S(2)}) async-start(s8[6291456]{0:T(1024)(128)(4,1)} %bitcast.119), calls=%async_computation.6 | async-start | bytes 8388608
  43.2 5.8 %slice-start.5 = ((s8[6291456]{0:T(1024)(128)(4,1)}), s8[2097152]{0:T(1024)(128)(4,1)S(1)}, s32[]{:S(2)}) async-start(s8[6291456]{0:T(1024)(128)(4,1)} %bitcast.119), calls=%async_computation.7 | async-start | bytes 4194304
  44.1 4.9 %copy-start.1 = (s32[1,192,1024]{2,1,0:T(8,128)S(1)}, s32[1,192,1024]{2,1,0:T(8,128)}, u32[]{:S(2)}) copy-start(s32[1,192,1024]{2,1,0:T(8,128)} %param.15) | copy-start | bytes 2359300
  44.2 7.3 %slice-start = ((s8[6291456]{0:T(1024)(128)(4,1)}), s8[4194304]{0:T(1024)(128)(4,1)S(1)}, s32[]{:S(2)}) async-start(s8[6291456]{0:T(1024)(128)(4,1)} %bitcast.113), calls=%async_computation.2 | async-start | bytes 8388608
  49.1 2.4 %slice-start.1 = ((s8[6291456]{0:T(1024)(128)(4,1)}), s8[2097152]{0:T(1024)(128)(4,1)S(1)}, s32[]{:S(2)}) async-start(s8[6291456]{0:T(1024)(128)(4,1)} %bitcast.113), calls=%async_computation.3 | async-start | bytes 4194304
  49.1 6.6 %slice-start.2 = ((s8[6291456]{0:T(1024)(128)(4,1)}), s8[4194304]{0:T(1024)(128)(4,1)S(1)}, s32[]{:S(2)}) async-start(s8[6291456]{0:T(1024)(128)(4,1)} %bitcast.117), calls=%async_computation.4 | async-start | bytes 8388608
  51.5 4.2 %slice-start.3 = ((s8[6291456]{0:T(1024)(128)(4,1)}), s8[2097152]{0:T(1024)(128)(4,1)S(1)}, s32[]{:S(2)}) async-start(s8[6291456]{0:T(1024)(128)(4,1)} %bitcast.117), calls=%async_computation.5 | async-start | bytes 4194304
  58.0 2.1 %collective-permute-start.4 = (bf16[2,48,3072]{2,1,0:T(8,128)(2,1)S(1)}, bf16[2,48,3072]{2,1,0:T(8,128)(2,1)S(1)}, u32[]{:S(2)}, u32[]{:S(2)}) collective-permute-start(bf16[2,48,3072]{2,1,0:T(8,128)(2,1)S(1)} %select_bitcast_fusion.2), channel_id=1, source_target_pairs={{0,1},{1,0},{2,3},{3,2},{4,5},{5,4},{6,7},{7,6},{8,9},{9,8},{10,11... | collective-permute-start | bytes 1769480 | tf_op jit(solution)/shard_map/ppermute | solution.py:33
  60.3 6.5 %copy-start = (s32[2,96]{1,0:T(2,128)S(1)}, s32[2,96]{1,0:T(2,128)}, u32[]{:S(2)}) copy-start(s32[2,96]{1,0:T(2,128)} %param.13) | copy-start | bytes 2308
  61.3 22.0 %all-to-all-start.1 = ((bf16[16,48,384]{2,1,0:T(8,128)(2,1)}), bf16[16,48,384]{2,1,0:T(8,128)(2,1)S(1)}, u32[]{:S(2)}, u32[]{:S(2)}) async-start(bf16[16,48,384]{2,1,0:T(8,128)(2,1)} %bitcast.37), calls=%async_computation.1 | async-start | bytes 1179648 | tf_op jit(solution)/shard_map/all_to_all | solution.py:111
  83.9 1.4 %collective-permute-start.5 = (f32[96,192]{1,0:T(8,128)S(1)}, f32[96,192]{1,0:T(8,128)S(1)}, u32[]{:S(2)}, u32[]{:S(2)}) collective-permute-start(f32[96,192]{1,0:T(8,128)S(1)} %slice_select_fusion), channel_id=1, source_target_pairs={{0,1},{1,0},{2,3},{3,2},{4,5},{5,4},{6,7},{7,6},{8,9},{9,8},{10,11... | collective-permute-start | bytes 221192 | tf_op jit(solution)/shard_map/ppermute | solution.py:33

commit v20 on v17

--- a/solution.py
+++ b/solution.py
@@ -72,7 +72,7 @@
     mine_tokens = info_abs[:, 0].astype(jnp.int32)
     mine_weights = info_abs[:, 1].reshape(slot_count, 1, 1, 1)
     other = jnp.concatenate([partner_plane[None], swap_cores(own[1:])], axis=0)
-    full = order_by_core(own, other, axis=2)
+    full = lax.optimization_barrier(order_by_core(own, other, axis=2))
     block_rel = (group - jnp.arange(expert_count)) % expert_count
     column = (block_rel[:, None] * group_tokens + mine_tokens).reshape(-1)
     pick = (column[:, None] == jnp.arange(expert_count * group_tokens)[None, :]).astype(jnp.bfloat16)

time: 84 us -> 82.9 us (0.987)
  matrix products: 14.8 us -> 11.5 us
  local copies, waits for them, and re-layouts: 10.9 us -> 12.8 us
    dot_general x1, matrix products: 4.85 us -> 1.51 us  [body(): lax.dot_general(part_inputs, gate_rows, fwd_dims, preferred_element_type=...]
    unnamed x18, local copies, waits for them, and re-layouts: 8.8 us -> 10.8 us
where the time goes in v20:
time: 82.9 us; the launch traced here: 82.4 us
  blocking collectives  23.6 us (28%)
  waiting for transfers between devices  22.5 us (27%)
  local copies, waits for them, and re-layouts  12.8 us (15%)
  matrix products  11.5 us (14%)
  starting transfers between devices  7.39 us (9%)
  other arithmetic  4.27 us (5%)
    all_to_all x1, blocking collectives, body(): lax.all_to_all(outgoing, 'chip', split_axis=0, concat_axis=0, tiled=True)  23.6 us
    all_to_all x1, waiting for transfers between devices, body(): lax.all_to_all(blocks, CROSS, split_axis=0, concat_axis=0, tiled=True)  16.4 us
    unnamed x18, local copies, waits for them, and re-layouts  10.8 us
    all_to_all x1, starting transfers between devices, body(): lax.all_to_all(blocks, CROSS, split_axis=0, concat_axis=0, tiled=True)  5 us
    ppermute x4, waiting for transfers between devices, swap_cores(): return lax.ppermute(values, 'core', [(0, 1), (1, 0)])  4.13 us
    dot_general x1, matrix products, body(): lax.dot_general(part_cot, down_rows, fwd_dims, preferred_element_type=jnp...  2.3 us
    dot_general x1, matrix products, body(): lax.dot_general(grad_gate, gate_mat, back_dims, preferred_element_type=jn...  2.22 us
    dot_general x1, matrix products, body(): lax.dot_general(grad_up, up_mat, back_dims, preferred_element_type=jnp.fl...  2.2 us
  transfers between devices with their start and end apart: 7, of which 5 were waited for; matrix products, arithmetic and copies ran while one was open for 14% of the time, Pallas kernels for 0%

profile of v20, /device:TPU:0, one launch (start us, length us, event | category | flops | bytes accessed | tf_op | source)
XLA Modules:
  0.0 82.4 jit_solution(12485162686524481614)
XLA Ops:
  0.0 0.9 %pad_maximum_fusion.3 = bf16[96,384]{1,0:T(8,128)(2,1)S(1)} fusion(bf16[96,192]{1,0:T(8,128)(2,1)} %param.9, bf16[96,192]{1,0:T(8,128)(2,1)} %param.8), kind=kLoop, calls=%fused_computation.53 | loop fusion | flops 147456 | bytes 147456 | tf_op jit(solution)/shard_map/concatenate | solution.py:63
  0.9 0.1 broadcast_in_dim.4
  1.0 23.6 %all_to_all.10 = bf16[8,96,384]{2,1,0:T(8,128)(2,1)S(1)} all-to-all(bf16[8,96,384]{2,1,0:T(8,128)(2,1)S(1)} %broadcast_in_dim.4), channel_id=1, replica_groups=mesh['expert'=2,'chip'=8,'core'=2] {'chip'}, dimensions={0} | all-to-all | bytes 1179648 | tf_op jit(solution)/shard_map/all_to_all | solution.py:65
  24.6 1.5 %collective-permute-start = (bf16[8,96,384]{2,1,0:T(8,128)(2,1)S(1)}, bf16[8,96,384]{2,1,0:T(8,128)(2,1)S(1)}, u32[]{:S(2)}, u32[]{:S(2)}) collective-permute-start(bf16[8,96,384]{2,1,0:T(8,128)(2,1)S(1)} %all_to_all.10), channel_id=1, source_target_pairs={{0,16},{16,0},{1,17},{17,1},{2,18},{18,2},{3,19},{19,3},{4,20},{20... | collective-permute-start | bytes 1769480 | tf_op jit(solution)/shard_map/ppermute | solution.py:57
  26.1 0.7 convert_element_type.68
  26.8 0.7 fusion.45
  27.5 0.5 collective-permute-start.1
  28.0 8.7 %copy.28 = bf16[1,1024,3072]{1,2,0:T(8,128)(2,1)} copy(bf16[1,1024,3072]{2,1,0:T(8,128)(2,1)} %param.12) | data formatting | bytes 12582912 | tf_op args[4]
  36.6 1.9 %collective-permute-done.1 = f32[2,96]{1,0:T(2,128)S(1)} collective-permute-done((f32[2,96]{1,0:T(2,128)S(1)}, f32[2,96]{1,0:T(2,128)S(1)}, u32[]{:S(2)}, u32[]{:S(2)}) %collective-permute-start.1) | collective-permute-done | bytes 800 | tf_op jit(solution)/shard_map/ppermute | solution.py:57
  38.6 0.1 pad_maximum_fusion.1
  38.7 0.1 slice.42
  38.8 0.1 collective-permute-start.3
  38.9 0.1 add.87
  39.0 0.1 add.88
  39.1 0.6 gather_fusion
  39.7 0.1 convert_element_type.70
  39.8 0.1 mul.77
  39.9 1.0 %collective-permute-done.3 = bf16[1,8,96,384]{3,2,0,1:T(8,128)(2,1)S(1)} collective-permute-done((bf16[1,8,96,384]{3,2,0,1:T(8,128)(2,1)S(1)}, bf16[1,8,96,384]{3,2,0,1:T(8,128)(2,1)S(1)}, u32[]{:S(2)}, u32[]{:S(2)}) %collective-permute-start.3) | collective-permute-done | bytes 589856 | tf_op jit(solution)/shard_map/ppermute | solution.py:33
  40.9 0.3 select_bitcast_fusion.1
  41.2 0.3 pad_maximum_fusion
  41.5 0.9 %convolution_bitcast_fusion = f32[192,8,2,384]{3,0,2,1:T(8,128)S(1)} fusion(bf16[2,8,2,96,384]{4,3,0,2,1:T(8,128)(2,1)S(1)} %pad_maximum_fusion, s32[2,96]{1,0:T(2,128)S(1)} %multiply_add_fusion, s32[192]{0:T(256)S(1)} %add.89), kind=kOutput, calls=%fused_computation.11 | convolution fusion | flops 453021696 | bytes 7079424 | tf_op jit(solution)/shard_map/dot_general | solution.py:80
  42.3 0.7 slice-done.2
  43.1 0.7 slice-done.3
  43.8 1.5 %convolution_bitcast_fusion.1 = f32[192,1024]{1,0:T(8,128)S(1)} fusion(bf16[8,2,192,1024]{3,2,1,0:T(8,128)(2,1)S(1)} %bitcast.119, f32[192,8,2,384]{3,0,2,1:T(8,128)S(1)} %convolution_bitcast_fusion), kind=kOutput, calls=%fused_computation.14 | convolution fusion | flops 1207959552 | bytes 8650752 | tf_op jit(solution)/shard_map/dot_general | solution.py:88
  45.3 0.3 slice-done.5
  45.7 0.2 copy-done.1
  45.9 2.3 %multiply_convert_fusion = (bf16[192,1024]{1,0:T(8,128)(2,1)S(1)}, f32[192,1024]{1,0:T(8,128)S(1)}) fusion(f32[192,1024]{1,0:T(8,128)S(1)} %convolution_bitcast_fusion.1, s32[1,192,1024]{2,1,0:T(8,128)S(1)} %copy-done.1, bf16[8,2,192,1024]{3,2,1,0:T(8,128)(2,1)S(1)} %bitcast.122, f32[192,8,2,384]{3,0,2,1:T(8,128)S(1)} %convolution_bitcast_fusion, ...), kind=kOutput, calls=%fused_computation.39 | convolution fusion | flops 1211695104 | bytes 12190720 | tf_op jit(solution)/shard_map/dot_general | solution.py:90
  48.2 2.0 %fusion.32 = bf16[192,1024]{1,0:T(8,128)(2,1)S(1)} fusion(f32[192,1024]{1,0:T(8,128)S(1)} %convolution_bitcast_fusion.1, f32[192,1024]{1,0:T(8,128)S(1)} %get-tuple-element.22, bf16[8,2,192,1024]{3,2,1,0:T(8,128)(2,1)S(1)} %bitcast.116, f32[192,8,2,384]{3,0,2,1:T(8,128)S(1)} %convolution_bitcast_fusion), kind=kOutput, calls=%fused_computation.38 | convolution fusion | flops 1212088320 | bytes 9830400 | tf_op jit(solution)/shard_map/dot_general | solution.py:89
  50.2 2.2 %fusion = f32[192,3072]{1,0:T(8,128)S(1)} fusion(bf16[192,1024]{1,0:T(8,128)(2,1)S(1)} %get-tuple-element.16, bf16[1,3072,1024]{2,1,0:T(8,128)(2,1)S(1)} %bitcast.115), kind=kOutput, calls=%fused_computation.1 | convolution fusion | flops 1207959552 | bytes 9043968 | tf_op jit(solution)/shard_map/dot_general | solution.py:103
  52.4 2.2 %fusion.7 = bf16[192,3072]{1,0:T(8,128)(2,1)S(1)} fusion(f32[192,3072]{1,0:T(8,128)S(1)} %fusion, bf16[192,1024]{1,0:T(8,128)(2,1)S(1)} %fusion.32, bf16[1,3072,1024]{2,1,0:T(8,128)(2,1)S(1)} %bitcast.118), kind=kOutput, calls=%fused_computation.6 | convolution fusion | flops 1209139200 | bytes 10223616 | tf_op jit(solution)/shard_map/dot_general | solution.py:101
  54.7 0.1 select_bitcast_fusion.2
  54.7 0.2 collective-permute-start.4
  54.9 1.9 %collective-permute-done.4 = bf16[2,48,3072]{2,1,0:T(8,128)(2,1)S(1)} collective-permute-done((bf16[2,48,3072]{2,1,0:T(8,128)(2,1)S(1)}, bf16[2,48,3072]{2,1,0:T(8,128)(2,1)S(1)}, u32[]{:S(2)}, u32[]{:S(2)}) %collective-permute-start.4) | collective-permute-done | bytes 589856 | tf_op jit(solution)/shard_map/ppermute | solution.py:33
  56.8 0.2 fusion.24
  57.0 0.1 copy.42
  57.1 0.1 bitcast_bitcast_fusion
  57.2 0.9 %copy.34 = bf16[2,8,48,384]{3,2,1,0:T(8,128)(2,1)} copy(bf16[2,8,48,384]{3,1,2,0:T(8,128)(2,1)S(1)} %bitcast_bitcast_fusion) | data formatting | bytes 1179648 | tf_op jit(solution)/shard_map/transpose | solution.py:111
  58.1 5.0 %all-to-all-start.1 = ((bf16[16,48,384]{2,1,0:T(8,128)(2,1)}), bf16[16,48,384]{2,1,0:T(8,128)(2,1)S(1)}, u32[]{:S(2)}, u32[]{:S(2)}) async-start(bf16[16,48,384]{2,1,0:T(8,128)(2,1)} %bitcast.37), calls=%async_computation.1 | async-start | bytes 1179648 | tf_op jit(solution)/shard_map/all_to_all | solution.py:112
  63.1 0.1 eq.46
  63.2 0.1 fusion.37
  63.3 16.4 %all-to-all-done.1 = bf16[16,48,384]{2,1,0:T(8,128)(2,1)S(1)} async-done(((bf16[16,48,384]{2,1,0:T(8,128)(2,1)}), bf16[16,48,384]{2,1,0:T(8,128)(2,1)S(1)}, u32[]{:S(2)}, u32[]{:S(2)}) %all-to-all-start.1) | async-done | bytes 589856 | tf_op jit(solution)/shard_map/all_to_all | solution.py:112
  79.7 0.1 convert_reduce_fusion
  79.8 0.2 convolution_bitcast_fusion.3
  80.0 0.2 fusion.25
  80.2 0.1 slice_select_fusion
  80.3 0.1 collective-permute-start.5
  80.4 1.3 %collective-permute-done.5 = f32[96,192]{1,0:T(8,128)S(1)} collective-permute-done((f32[96,192]{1,0:T(8,128)S(1)}, f32[96,192]{1,0:T(8,128)S(1)}, u32[]{:S(2)}, u32[]{:S(2)}) %collective-permute-start.5) | collective-permute-done | bytes 73760 | tf_op jit(solution)/shard_map/ppermute | solution.py:33
  81.6 0.7 add_convert_fusion
  (27 shorter events, 0.1 us)
Async XLA Ops:
  24.6 14.0 %collective-permute-start = (bf16[8,96,384]{2,1,0:T(8,128)(2,1)S(1)}, bf16[8,96,384]{2,1,0:T(8,128)(2,1)S(1)}, u32[]{:S(2)}, u32[]{:S(2)}) collective-permute-start(bf16[8,96,384]{2,1,0:T(8,128)(2,1)S(1)} %all_to_all.10), channel_id=1, source_target_pairs={{0,16},{16,0},{1,17},{17,1},{2,18},{18,2},{3,19},{19,3},{4,20},{20... | collective-permute-start | bytes 1769480 | tf_op jit(solution)/shard_map/ppermute | solution.py:57
  26.1 12.6 %collective-permute-start.2 = (bf16[8,96,384]{2,1,0:T(8,128)(2,1)S(1)}, bf16[8,96,384]{2,1,0:T(8,128)(2,1)S(1)}, u32[]{:S(2)}, u32[]{:S(2)}) collective-permute-start(bf16[8,96,384]{2,1,0:T(8,128)(2,1)S(1)} %all_to_all.10), channel_id=1, source_target_pairs={{0,1},{1,0},{2,3},{3,2},{4,5},{5,4},{6,7},{7,6},{8,9},{9,8},{10,11... | collective-permute-start | bytes 1769480 | tf_op jit(solution)/shard_map/ppermute | solution.py:33
  27.5 11.1 %collective-permute-start.1 = (f32[2,96]{1,0:T(2,128)S(1)}, f32[2,96]{1,0:T(2,128)S(1)}, u32[]{:S(2)}, u32[]{:S(2)}) collective-permute-start(f32[2,96]{1,0:T(2,128)S(1)} %get-tuple-element.20), channel_id=1, source_target_pairs={{0,16},{16,0},{1,17},{17,1},{2,18},{18,2},{3,19},{19,3},{4,20},{20... | collective-permute-start | bytes 2312 | tf_op jit(solution)/shard_map/ppermute | solution.py:57
  38.8 2.1 %collective-permute-start.3 = (bf16[1,8,96,384]{3,2,0,1:T(8,128)(2,1)S(1)}, bf16[1,8,96,384]{3,2,0,1:T(8,128)(2,1)S(1)}, u32[]{:S(2)}, u32[]{:S(2)}) collective-permute-start(bf16[1,8,96,384]{3,2,0,1:T(8,128)(2,1)S(1)} %slice.42), channel_id=1, source_target_pairs={{0,1},{1,0},{2,3},{3,2},{4,5},{5,4},{6,7},{7,6},{8,9},{9,8},{10,11... | collective-permute-start | bytes 1769480 | tf_op jit(solution)/shard_map/ppermute | solution.py:33
  40.9 2.2 %slice-start.2 = ((s8[6291456]{0:T(1024)(128)(4,1)}), s8[4194304]{0:T(1024)(128)(4,1)S(1)}, s32[]{:S(2)}) async-start(s8[6291456]{0:T(1024)(128)(4,1)} %bitcast.117), calls=%async_computation.4 | async-start | bytes 8388608
  41.2 2.7 %slice-start.3 = ((s8[6291456]{0:T(1024)(128)(4,1)}), s8[2097152]{0:T(1024)(128)(4,1)S(1)}, s32[]{:S(2)}) async-start(s8[6291456]{0:T(1024)(128)(4,1)} %bitcast.117), calls=%async_computation.5 | async-start | bytes 4194304
  41.2 4.2 %slice-start.4 = ((s8[6291456]{0:T(1024)(128)(4,1)}), s8[4194304]{0:T(1024)(128)(4,1)S(1)}, s32[]{:S(2)}) async-start(s8[6291456]{0:T(1024)(128)(4,1)} %bitcast.120), calls=%async_computation.6 | async-start | bytes 8388608
  41.4 4.2 %slice-start.5 = ((s8[6291456]{0:T(1024)(128)(4,1)}), s8[2097152]{0:T(1024)(128)(4,1)S(1)}, s32[]{:S(2)}) async-start(s8[6291456]{0:T(1024)(128)(4,1)} %bitcast.120), calls=%async_computation.7 | async-start | bytes 4194304
  43.8 2.1 %copy-start.1 = (s32[1,192,1024]{2,1,0:T(8,128)S(1)}, s32[1,192,1024]{2,1,0:T(8,128)}, u32[]{:S(2)}) copy-start(s32[1,192,1024]{2,1,0:T(8,128)} %param.15) | copy-start | bytes 2359300
  43.8 4.4 %slice-start = ((s8[6291456]{0:T(1024)(128)(4,1)}), s8[4194304]{0:T(1024)(128)(4,1)S(1)}, s32[]{:S(2)}) async-start(s8[6291456]{0:T(1024)(128)(4,1)} %bitcast.114), calls=%async_computation.2 | async-start | bytes 8388608
  45.9 2.3 %slice-start.1 = ((s8[6291456]{0:T(1024)(128)(4,1)}), s8[2097152]{0:T(1024)(128)(4,1)S(1)}, s32[]{:S(2)}) async-start(s8[6291456]{0:T(1024)(128)(4,1)} %bitcast.114), calls=%async_computation.3 | async-start | bytes 4194304
  54.7 2.1 %collective-permute-start.4 = (bf16[2,48,3072]{2,1,0:T(8,128)(2,1)S(1)}, bf16[2,48,3072]{2,1,0:T(8,128)(2,1)S(1)}, u32[]{:S(2)}, u32[]{:S(2)}) collective-permute-start(bf16[2,48,3072]{2,1,0:T(8,128)(2,1)S(1)} %select_bitcast_fusion.2), channel_id=1, source_target_pairs={{0,1},{1,0},{2,3},{3,2},{4,5},{5,4},{6,7},{7,6},{8,9},{9,8},{10,11... | collective-permute-start | bytes 1769480 | tf_op jit(solution)/shard_map/ppermute | solution.py:33
  57.0 6.1 %copy-start = (s32[2,96]{1,0:T(2,128)S(1)}, s32[2,96]{1,0:T(2,128)}, u32[]{:S(2)}) copy-start(s32[2,96]{1,0:T(2,128)} %param.13) | copy-start | bytes 2308
  58.1 21.6 %all-to-all-start.1 = ((bf16[16,48,384]{2,1,0:T(8,128)(2,1)}), bf16[16,48,384]{2,1,0:T(8,128)(2,1)S(1)}, u32[]{:S(2)}, u32[]{:S(2)}) async-start(bf16[16,48,384]{2,1,0:T(8,128)(2,1)} %bitcast.37), calls=%async_computation.1 | async-start | bytes 1179648 | tf_op jit(solution)/shard_map/all_to_all | solution.py:112
  80.3 1.4 %collective-permute-start.5 = (f32[96,192]{1,0:T(8,128)S(1)}, f32[96,192]{1,0:T(8,128)S(1)}, u32[]{:S(2)}, u32[]{:S(2)}) collective-permute-start(f32[96,192]{1,0:T(8,128)S(1)} %slice_select_fusion), channel_id=1, source_target_pairs={{0,1},{1,0},{2,3},{3,2},{4,5},{5,4},{6,7},{7,6},{8,9},{9,8},{10,11... | collective-permute-start | bytes 221192 | tf_op jit(solution)/shard_map/ppermute | solution.py:33

commit v21 on v20

--- a/solution.py
+++ b/solution.py
@@ -63,6 +63,7 @@
     raw = jnp.concatenate([tokens, cotangent], axis=1)
     outgoing = jnp.broadcast_to(raw[None], (chip_count, group_tokens, 2 * local_width))
     in_plane = lax.all_to_all(outgoing, "chip", split_axis=0, concat_axis=0, tiled=True)
+    in_plane, info_rel = lax.optimization_barrier((in_plane, info_rel))
     partner_plane = swap_cores(in_plane)
     own = from_groups(in_plane, lambda values, row: values)
     down_t, own, info_rel, partner_plane = lax.optimization_barrier(

time: 82.9 us -> 84.2 us (1.016)
  blocking collectives: 23.6 us -> 0 us
  waiting for transfers between devices: 22.5 us -> 37 us
  starting transfers between devices: 7.39 us -> 17 us
  local copies, waits for them, and re-layouts: 12.8 us -> 13.7 us
    all_to_all x1 -> x0, blocking collectives: 23.6 us -> none  [body(): lax.all_to_all(outgoing, 'chip', split_axis=0, concat_axis=0, tiled=True)]
    all_to_all x0 -> x1, waiting for transfers between devices: none -> 11 us  [body(): lax.all_to_all(outgoing, 'chip', split_axis=0, concat_axis=0, tiled=True)]
    all_to_all x0 -> x1, starting transfers between devices: none -> 7.25 us  [body(): lax.all_to_all(outgoing, 'chip', split_axis=0, concat_axis=0, tiled=True)]
    ppermute x2, waiting for transfers between devices: 1.93 us -> 5.46 us  [from_groups(): lax.ppermute(moved, 'expert', [(i, (i + shift) % expert_count) for i in r...]
    all_to_all x1, starting transfers between devices: 5 us -> 6.36 us  [body(): lax.all_to_all(blocks, CROSS, split_axis=0, concat_axis=0, tiled=True)]
    ppermute x2, starting transfers between devices: 2.03 us -> 3.04 us  [from_groups(): lax.ppermute(moved, 'expert', [(i, (i + shift) % expert_count) for i in r...]
  transfers between devices with their start and end apart: 7 -> 8, of which waited for: 5 -> 7; matrix products, arithmetic and copies ran while one was open for 14% -> 14% of each run, Pallas kernels for 0% -> 0%
where the time goes in v21:
time: 84.2 us; the launch traced here: 83.7 us
  waiting for transfers between devices  37 us (44%)
  starting transfers between devices  17 us (20%)
  local copies, waits for them, and re-layouts  13.7 us (16%)
  matrix products  11.5 us (14%)
  other arithmetic  4.27 us (5%)
    all_to_all x1, waiting for transfers between devices, body(): lax.all_to_all(blocks, CROSS, split_axis=0, concat_axis=0, tiled=True)  16.4 us
    all_to_all x1, waiting for transfers between devices, body(): lax.all_to_all(outgoing, 'chip', split_axis=0, concat_axis=0, tiled=True)  11 us
    unnamed x18, local copies, waits for them, and re-layouts  10.8 us
    all_to_all x1, starting transfers between devices, body(): lax.all_to_all(outgoing, 'chip', split_axis=0, concat_axis=0, tiled=True)  7.25 us
    all_to_all x1, starting transfers between devices, body(): lax.all_to_all(blocks, CROSS, split_axis=0, concat_axis=0, tiled=True)  6.36 us
    ppermute x2, waiting for transfers between devices, from_groups(): lax.ppermute(moved, 'expert', [(i, (i + shift) % expert_count) for i in r...  5.46 us
    ppermute x4, waiting for transfers between devices, swap_cores(): return lax.ppermute(values, 'core', [(0, 1), (1, 0)])  4.14 us
    ppermute x2, starting transfers between devices, from_groups(): lax.ppermute(moved, 'expert', [(i, (i + shift) % expert_count) for i in r...  3.04 us
  transfers between devices with their start and end apart: 8, of which 7 were waited for; matrix products, arithmetic and copies ran while one was open for 14% of the time, Pallas kernels for 0%

profile of v21, /device:TPU:0, one launch (start us, length us, event | category | flops | bytes accessed | tf_op | source)
XLA Modules:
  0.0 83.7 jit_solution(2474733052957637145)
XLA Ops:
  0.0 0.9 %pad_maximum_fusion.3 = bf16[96,384]{1,0:T(8,128)(2,1)S(1)} fusion(bf16[96,192]{1,0:T(8,128)(2,1)} %param.9, bf16[96,192]{1,0:T(8,128)(2,1)} %param.8), kind=kLoop, calls=%fused_computation.53 | loop fusion | flops 147456 | bytes 147456 | tf_op jit(solution)/shard_map/concatenate | solution.py:63
  0.9 0.9 %broadcast_in_dim.4 = bf16[8,96,384]{2,1,0:T(8,128)(2,1)} broadcast(bf16[96,384]{1,0:T(8,128)(2,1)S(1)} %pad_maximum_fusion.3), dimensions={1,2} | broadcast | bytes 663552 | tf_op jit(solution)/shard_map/broadcast_in_dim | solution.py:64
  1.8 7.3 %all-to-all-start = ((bf16[8,96,384]{2,1,0:T(8,128)(2,1)}), bf16[8,96,384]{2,1,0:T(8,128)(2,1)S(1)}, u32[]{:S(2)}, u32[]{:S(2)}) async-start(bf16[8,96,384]{2,1,0:T(8,128)(2,1)} %broadcast_in_dim.4), calls=%async_computation | async-start | bytes 1179648 | tf_op jit(solution)/shard_map/all_to_all | solution.py:65
  9.0 0.7 convert_element_type.68
  9.7 0.7 fusion.45
  10.4 1.5 %collective-permute-start = (f32[2,96]{1,0:T(2,128)S(1)}, f32[2,96]{1,0:T(2,128)S(1)}, u32[]{:S(2)}, u32[]{:S(2)}) collective-permute-start(f32[2,96]{1,0:T(2,128)S(1)} %get-tuple-element.24), channel_id=1, source_target_pairs={{0,16},{16,0},{1,17},{17,1},{2,18},{18,2},{3,19},{19,3},{4,20},{20... | collective-permute-start | bytes 2312 | tf_op jit(solution)/shard_map/ppermute | solution.py:57
  11.9 2.0 %collective-permute-done = f32[2,96]{1,0:T(2,128)S(1)} collective-permute-done((f32[2,96]{1,0:T(2,128)S(1)}, f32[2,96]{1,0:T(2,128)S(1)}, u32[]{:S(2)}, u32[]{:S(2)}) %collective-permute-start) | collective-permute-done | bytes 800 | tf_op jit(solution)/shard_map/ppermute | solution.py:57
  14.0 11.0 %all-to-all-done = bf16[8,96,384]{2,1,0:T(8,128)(2,1)S(1)} async-done(((bf16[8,96,384]{2,1,0:T(8,128)(2,1)}), bf16[8,96,384]{2,1,0:T(8,128)(2,1)S(1)}, u32[]{:S(2)}, u32[]{:S(2)}) %all-to-all-start) | async-done | bytes 589856 | tf_op jit(solution)/shard_map/all_to_all | solution.py:65
  24.9 1.5 %collective-permute-start.1 = (bf16[8,96,384]{2,1,0:T(8,128)(2,1)S(1)}, bf16[8,96,384]{2,1,0:T(8,128)(2,1)S(1)}, u32[]{:S(2)}, u32[]{:S(2)}) collective-permute-start(bf16[8,96,384]{2,1,0:T(8,128)(2,1)S(1)} %all-to-all-done), channel_id=1, source_target_pairs={{0,16},{16,0},{1,17},{17,1},{2,18},{18,2},{3,19},{19,3},{4,20},{20... | collective-permute-start | bytes 1769480 | tf_op jit(solution)/shard_map/ppermute | solution.py:57
  26.5 8.6 %copy.28 = bf16[1,1024,3072]{1,2,0:T(8,128)(2,1)} copy(bf16[1,1024,3072]{2,1,0:T(8,128)(2,1)} %param.12) | data formatting | bytes 12582912 | tf_op args[4]
  35.1 3.4 %collective-permute-done.1 = bf16[8,96,384]{2,1,0:T(8,128)(2,1)S(1)} collective-permute-done((bf16[8,96,384]{2,1,0:T(8,128)(2,1)S(1)}, bf16[8,96,384]{2,1,0:T(8,128)(2,1)S(1)}, u32[]{:S(2)}, u32[]{:S(2)}) %collective-permute-start.1) | collective-permute-done | bytes 589856 | tf_op jit(solution)/shard_map/ppermute | solution.py:57
  38.5 0.1 pad_maximum_fusion.1
  38.7 0.1 collective-permute-start.3
  38.8 0.1 add.87
  38.9 0.1 add.88
  39.0 0.6 gather_fusion
  39.6 0.1 convert_element_type.70
  39.7 0.1 mul.77
  39.8 1.0 %collective-permute-done.3 = bf16[1,8,96,384]{3,2,0,1:T(8,128)(2,1)S(1)} collective-permute-done((bf16[1,8,96,384]{3,2,0,1:T(8,128)(2,1)S(1)}, bf16[1,8,96,384]{3,2,0,1:T(8,128)(2,1)S(1)}, u32[]{:S(2)}, u32[]{:S(2)}) %collective-permute-start.3) | collective-permute-done | bytes 589856 | tf_op jit(solution)/shard_map/ppermute | solution.py:33
  40.8 0.3 select_bitcast_fusion.1
  41.1 0.3 pad_maximum_fusion
  41.4 0.9 %convolution_bitcast_fusion = f32[192,8,2,384]{3,0,2,1:T(8,128)S(1)} fusion(bf16[2,8,2,96,384]{4,3,0,2,1:T(8,128)(2,1)S(1)} %pad_maximum_fusion, s32[2,96]{1,0:T(2,128)S(1)} %multiply_add_fusion, s32[192]{0:T(256)S(1)} %add.89), kind=kOutput, calls=%fused_computation.11 | convolution fusion | flops 453021696 | bytes 7079424 | tf_op jit(solution)/shard_map/dot_general | solution.py:81
  42.3 0.7 slice-done.2
  43.0 0.7 slice-done.3
  43.7 1.5 %convolution_bitcast_fusion.1 = f32[192,1024]{1,0:T(8,128)S(1)} fusion(bf16[8,2,192,1024]{3,2,1,0:T(8,128)(2,1)S(1)} %bitcast.119, f32[192,8,2,384]{3,0,2,1:T(8,128)S(1)} %convolution_bitcast_fusion), kind=kOutput, calls=%fused_computation.14 | convolution fusion | flops 1207959552 | bytes 8650752 | tf_op jit(solution)/shard_map/dot_general | solution.py:89
  45.3 0.3 slice-done.5
  45.6 0.2 copy-done.1
  45.8 2.3 %multiply_convert_fusion = (bf16[192,1024]{1,0:T(8,128)(2,1)S(1)}, f32[192,1024]{1,0:T(8,128)S(1)}) fusion(f32[192,1024]{1,0:T(8,128)S(1)} %convolution_bitcast_fusion.1, s32[1,192,1024]{2,1,0:T(8,128)S(1)} %copy-done.1, bf16[8,2,192,1024]{3,2,1,0:T(8,128)(2,1)S(1)} %bitcast.122, f32[192,8,2,384]{3,0,2,1:T(8,128)S(1)} %convolution_bitcast_fusion, ...), kind=kOutput, calls=%fused_computation.39 | convolution fusion | flops 1211695104 | bytes 12190720 | tf_op jit(solution)/shard_map/dot_general | solution.py:91
  48.2 2.0 %fusion.32 = bf16[192,1024]{1,0:T(8,128)(2,1)S(1)} fusion(f32[192,1024]{1,0:T(8,128)S(1)} %convolution_bitcast_fusion.1, f32[192,1024]{1,0:T(8,128)S(1)} %get-tuple-element.26, bf16[8,2,192,1024]{3,2,1,0:T(8,128)(2,1)S(1)} %bitcast.116, f32[192,8,2,384]{3,0,2,1:T(8,128)S(1)} %convolution_bitcast_fusion), kind=kOutput, calls=%fused_computation.38 | convolution fusion | flops 1212088320 | bytes 9830400 | tf_op jit(solution)/shard_map/dot_general | solution.py:90
  50.2 2.2 %fusion = f32[192,3072]{1,0:T(8,128)S(1)} fusion(bf16[192,1024]{1,0:T(8,128)(2,1)S(1)} %get-tuple-element.20, bf16[1,3072,1024]{2,1,0:T(8,128)(2,1)S(1)} %bitcast.115), kind=kOutput, calls=%fused_computation.1 | convolution fusion | flops 1207959552 | bytes 9043968 | tf_op jit(solution)/shard_map/dot_general | solution.py:104
  52.4 2.2 %fusion.7 = bf16[192,3072]{1,0:T(8,128)(2,1)S(1)} fusion(f32[192,3072]{1,0:T(8,128)S(1)} %fusion, bf16[192,1024]{1,0:T(8,128)(2,1)S(1)} %fusion.32, bf16[1,3072,1024]{2,1,0:T(8,128)(2,1)S(1)} %bitcast.118), kind=kOutput, calls=%fused_computation.6 | convolution fusion | flops 1209139200 | bytes 10223616 | tf_op jit(solution)/shard_map/dot_general | solution.py:102
  54.6 0.1 select_bitcast_fusion.2
  54.7 0.2 collective-permute-start.4
  54.9 1.9 %collective-permute-done.4 = bf16[2,48,3072]{2,1,0:T(8,128)(2,1)S(1)} collective-permute-done((bf16[2,48,3072]{2,1,0:T(8,128)(2,1)S(1)}, bf16[2,48,3072]{2,1,0:T(8,128)(2,1)S(1)}, u32[]{:S(2)}, u32[]{:S(2)}) %collective-permute-start.4) | collective-permute-done | bytes 589856 | tf_op jit(solution)/shard_map/ppermute | solution.py:33
  56.7 0.2 fusion.24
  57.0 0.1 copy.42
  57.1 0.9 %copy.34 = bf16[2,8,48,384]{3,2,1,0:T(8,128)(2,1)} copy(bf16[2,8,48,384]{3,1,2,0:T(8,128)(2,1)S(1)} %bitcast_bitcast_fusion) | data formatting | bytes 1179648 | tf_op jit(solution)/shard_map/transpose | solution.py:112
  58.0 6.4 %all-to-all-start.1 = ((bf16[16,48,384]{2,1,0:T(8,128)(2,1)}), bf16[16,48,384]{2,1,0:T(8,128)(2,1)S(1)}, u32[]{:S(2)}, u32[]{:S(2)}) async-start(bf16[16,48,384]{2,1,0:T(8,128)(2,1)} %bitcast.37), calls=%async_computation.1 | async-start | bytes 1179648 | tf_op jit(solution)/shard_map/all_to_all | solution.py:113
  64.4 0.1 eq.46
  64.5 0.1 fusion.37
  64.6 16.4 %all-to-all-done.1 = bf16[16,48,384]{2,1,0:T(8,128)(2,1)S(1)} async-done(((bf16[16,48,384]{2,1,0:T(8,128)(2,1)}), bf16[16,48,384]{2,1,0:T(8,128)(2,1)S(1)}, u32[]{:S(2)}, u32[]{:S(2)}) %all-to-all-start.1) | async-done | bytes 589856 | tf_op jit(solution)/shard_map/all_to_all | solution.py:113
  81.0 0.1 convert_reduce_fusion
  81.1 0.2 convolution_bitcast_fusion.3
  81.3 0.2 fusion.25
  81.5 0.1 slice_select_fusion
  81.6 0.1 collective-permute-start.5
  81.7 1.3 %collective-permute-done.5 = f32[96,192]{1,0:T(8,128)S(1)} collective-permute-done((f32[96,192]{1,0:T(8,128)S(1)}, f32[96,192]{1,0:T(8,128)S(1)}, u32[]{:S(2)}, u32[]{:S(2)}) %collective-permute-start.5) | collective-permute-done | bytes 73760 | tf_op jit(solution)/shard_map/ppermute | solution.py:33
  82.9 0.7 add_convert_fusion
  (28 shorter events, 0.2 us)
Async XLA Ops:
  1.8 23.1 %all-to-all-start = ((bf16[8,96,384]{2,1,0:T(8,128)(2,1)}), bf16[8,96,384]{2,1,0:T(8,128)(2,1)S(1)}, u32[]{:S(2)}, u32[]{:S(2)}) async-start(bf16[8,96,384]{2,1,0:T(8,128)(2,1)} %broadcast_in_dim.4), calls=%async_computation | async-start | bytes 1179648 | tf_op jit(solution)/shard_map/all_to_all | solution.py:65
  10.4 3.6 %collective-permute-start = (f32[2,96]{1,0:T(2,128)S(1)}, f32[2,96]{1,0:T(2,128)S(1)}, u32[]{:S(2)}, u32[]{:S(2)}) collective-permute-start(f32[2,96]{1,0:T(2,128)S(1)} %get-tuple-element.24), channel_id=1, source_target_pairs={{0,16},{16,0},{1,17},{17,1},{2,18},{18,2},{3,19},{19,3},{4,20},{20... | collective-permute-start | bytes 2312 | tf_op jit(solution)/shard_map/ppermute | solution.py:57
  24.9 13.6 %collective-permute-start.1 = (bf16[8,96,384]{2,1,0:T(8,128)(2,1)S(1)}, bf16[8,96,384]{2,1,0:T(8,128)(2,1)S(1)}, u32[]{:S(2)}, u32[]{:S(2)}) collective-permute-start(bf16[8,96,384]{2,1,0:T(8,128)(2,1)S(1)} %all-to-all-done), channel_id=1, source_target_pairs={{0,16},{16,0},{1,17},{17,1},{2,18},{18,2},{3,19},{19,3},{4,20},{20... | collective-permute-start | bytes 1769480 | tf_op jit(solution)/shard_map/ppermute | solution.py:57
  26.5 12.2 %collective-permute-start.2 = (bf16[8,96,384]{2,1,0:T(8,128)(2,1)S(1)}, bf16[8,96,384]{2,1,0:T(8,128)(2,1)S(1)}, u32[]{:S(2)}, u32[]{:S(2)}) collective-permute-start(bf16[8,96,384]{2,1,0:T(8,128)(2,1)S(1)} %all-to-all-done), channel_id=1, source_target_pairs={{0,1},{1,0},{2,3},{3,2},{4,5},{5,4},{6,7},{7,6},{8,9},{9,8},{10,11... | collective-permute-start | bytes 1769480 | tf_op jit(solution)/shard_map/ppermute | solution.py:33
  38.7 2.1 %collective-permute-start.3 = (bf16[1,8,96,384]{3,2,0,1:T(8,128)(2,1)S(1)}, bf16[1,8,96,384]{3,2,0,1:T(8,128)(2,1)S(1)}, u32[]{:S(2)}, u32[]{:S(2)}) collective-permute-start(bf16[1,8,96,384]{3,2,0,1:T(8,128)(2,1)S(1)} %slice.42), channel_id=1, source_target_pairs={{0,1},{1,0},{2,3},{3,2},{4,5},{5,4},{6,7},{7,6},{8,9},{9,8},{10,11... | collective-permute-start | bytes 1769480 | tf_op jit(solution)/shard_map/ppermute | solution.py:33
  40.8 2.2 %slice-start.2 = ((s8[6291456]{0:T(1024)(128)(4,1)}), s8[4194304]{0:T(1024)(128)(4,1)S(1)}, s32[]{:S(2)}) async-start(s8[6291456]{0:T(1024)(128)(4,1)} %bitcast.117), calls=%async_computation.4 | async-start | bytes 8388608
  41.1 2.7 %slice-start.3 = ((s8[6291456]{0:T(1024)(128)(4,1)}), s8[2097152]{0:T(1024)(128)(4,1)S(1)}, s32[]{:S(2)}) async-start(s8[6291456]{0:T(1024)(128)(4,1)} %bitcast.117), calls=%async_computation.5 | async-start | bytes 4194304
  41.1 4.2 %slice-start.4 = ((s8[6291456]{0:T(1024)(128)(4,1)}), s8[4194304]{0:T(1024)(128)(4,1)S(1)}, s32[]{:S(2)}) async-start(s8[6291456]{0:T(1024)(128)(4,1)} %bitcast.120), calls=%async_computation.6 | async-start | bytes 8388608
  41.4 4.2 %slice-start.5 = ((s8[6291456]{0:T(1024)(128)(4,1)}), s8[2097152]{0:T(1024)(128)(4,1)S(1)}, s32[]{:S(2)}) async-start(s8[6291456]{0:T(1024)(128)(4,1)} %bitcast.120), calls=%async_computation.7 | async-start | bytes 4194304
  43.7 2.1 %copy-start.1 = (s32[1,192,1024]{2,1,0:T(8,128)S(1)}, s32[1,192,1024]{2,1,0:T(8,128)}, u32[]{:S(2)}) copy-start(s32[1,192,1024]{2,1,0:T(8,128)} %param.15) | copy-start | bytes 2359300
  43.7 4.4 %slice-start = ((s8[6291456]{0:T(1024)(128)(4,1)}), s8[4194304]{0:T(1024)(128)(4,1)S(1)}, s32[]{:S(2)}) async-start(s8[6291456]{0:T(1024)(128)(4,1)} %bitcast.114), calls=%async_computation.2 | async-start | bytes 8388608
  45.8 2.3 %slice-start.1 = ((s8[6291456]{0:T(1024)(128)(4,1)}), s8[2097152]{0:T(1024)(128)(4,1)S(1)}, s32[]{:S(2)}) async-start(s8[6291456]{0:T(1024)(128)(4,1)} %bitcast.114), calls=%async_computation.3 | async-start | bytes 4194304
  54.7 2.1 %collective-permute-start.4 = (bf16[2,48,3072]{2,1,0:T(8,128)(2,1)S(1)}, bf16[2,48,3072]{2,1,0:T(8,128)(2,1)S(1)}, u32[]{:S(2)}, u32[]{:S(2)}) collective-permute-start(bf16[2,48,3072]{2,1,0:T(8,128)(2,1)S(1)} %select_bitcast_fusion.2), channel_id=1, source_target_pairs={{0,1},{1,0},{2,3},{3,2},{4,5},{5,4},{6,7},{7,6},{8,9},{9,8},{10,11... | collective-permute-start | bytes 1769480 | tf_op jit(solution)/shard_map/ppermute | solution.py:33
  57.0 7.4 %copy-start = (s32[2,96]{1,0:T(2,128)S(1)}, s32[2,96]{1,0:T(2,128)}, u32[]{:S(2)}) copy-start(s32[2,96]{1,0:T(2,128)} %param.13) | copy-start | bytes 2308
  58.0 23.0 %all-to-all-start.1 = ((bf16[16,48,384]{2,1,0:T(8,128)(2,1)}), bf16[16,48,384]{2,1,0:T(8,128)(2,1)S(1)}, u32[]{:S(2)}, u32[]{:S(2)}) async-start(bf16[16,48,384]{2,1,0:T(8,128)(2,1)} %bitcast.37), calls=%async_computation.1 | async-start | bytes 1179648 | tf_op jit(solution)/shard_map/all_to_all | solution.py:113
  81.6 1.4 %collective-permute-start.5 = (f32[96,192]{1,0:T(8,128)S(1)}, f32[96,192]{1,0:T(8,128)S(1)}, u32[]{:S(2)}, u32[]{:S(2)}) collective-permute-start(f32[96,192]{1,0:T(8,128)S(1)} %slice_select_fusion), channel_id=1, source_target_pairs={{0,1},{1,0},{2,3},{3,2},{4,5},{5,4},{6,7},{7,6},{8,9},{9,8},{10,11... | collective-permute-start | bytes 221192 | tf_op jit(solution)/shard_map/ppermute | solution.py:33

commit v22 on v20

--- a/solution.py
+++ b/solution.py
@@ -102,13 +102,13 @@
         grad_gate, gate_mat, back_dims, preferred_element_type=jnp.float32
     ) + lax.dot_general(grad_up, up_mat, back_dims, preferred_element_type=jnp.float32)
     half = per_source // 2
-    partial = partial.astype(jnp.bfloat16).reshape(expert_count, 2, half, model_width)
+    partial = partial.astype(jnp.bfloat16).reshape(expert_count, 2, half, chip_count, 2 * local_width)
+    partial = partial.transpose(0, 1, 3, 2, 4)
     first = lax.axis_index("core") == 0
     keep_rows = jnp.where(first, partial[:, 0], partial[:, 1])
     send_rows = jnp.where(first, partial[:, 1], partial[:, 0])
     chip_sum = keep_rows.astype(jnp.float32) + swap_cores(send_rows).astype(jnp.float32)
-    blocks = chip_sum.astype(jnp.bfloat16).reshape(expert_count, half, chip_count, 2 * local_width)
-    blocks = blocks.transpose(0, 2, 1, 3).reshape(expert_count * chip_count, half, 2 * local_width)
+    blocks = chip_sum.astype(jnp.bfloat16).reshape(expert_count * chip_count, half, 2 * local_width)
     returned = lax.all_to_all(blocks, CROSS, split_axis=0, concat_axis=0, tiled=True)
     per_expert = returned.reshape(expert_total, chip_count, half, 2 * local_width).astype(jnp.float32).sum(1)
     one_hot = (slot_list[:, None] == jnp.arange(group_tokens, dtype=jnp.int32)[None, :]).astype(jnp.bfloat16)

time: 82.9 us -> 83 us (level)
  other arithmetic: 4.27 us -> 5.11 us
    transpose x2 -> x0, local copies, waits for them, and re-layouts: 0.95 us -> none  [body(): blocks.transpose(0, 2, 1, 3)]
    convert_element_type x1, other arithmetic: 0.22 us -> 1.05 us  [body(): chip_sum.astype(jnp.bfloat16)]
where the time goes in v22:
time: 83 us; the launch traced here: 82.5 us
  blocking collectives  23.6 us (28%)
  waiting for transfers between devices  22.5 us (27%)
  local copies, waits for them, and re-layouts  12.2 us (15%)
  matrix products  11.5 us (14%)
  starting transfers between devices  7.39 us (9%)
  other arithmetic  5.11 us (6%)
    all_to_all x1, blocking collectives, body(): lax.all_to_all(outgoing, 'chip', split_axis=0, concat_axis=0, tiled=True)  23.6 us
    all_to_all x1, waiting for transfers between devices, body(): lax.all_to_all(blocks, CROSS, split_axis=0, concat_axis=0, tiled=True)  16.4 us
    unnamed x18, local copies, waits for them, and re-layouts  10.9 us
    all_to_all x1, starting transfers between devices, body(): lax.all_to_all(blocks, CROSS, split_axis=0, concat_axis=0, tiled=True)  5 us
    ppermute x4, waiting for transfers between devices, swap_cores(): return lax.ppermute(values, 'core', [(0, 1), (1, 0)])  4.13 us
    dot_general x1, matrix products, body(): lax.dot_general(part_cot, down_rows, fwd_dims, preferred_element_type=jnp...  2.3 us
    dot_general x1, matrix products, body(): lax.dot_general(grad_gate, gate_mat, back_dims, preferred_element_type=jn...  2.22 us
    dot_general x1, matrix products, body(): lax.dot_general(grad_up, up_mat, back_dims, preferred_element_type=jnp.fl...  2.2 us
  transfers between devices with their start and end apart: 7, of which 5 were waited for; matrix products, arithmetic and copies ran while one was open for 14% of the time, Pallas kernels for 0%

profile of v22, /device:TPU:0, one launch (start us, length us, event | category | flops | bytes accessed | tf_op | source)
XLA Modules:
  0.0 82.5 jit_solution(10377403371362422658)
XLA Ops:
  0.0 0.9 %pad_maximum_fusion.3 = bf16[96,384]{1,0:T(8,128)(2,1)S(1)} fusion(bf16[96,192]{1,0:T(8,128)(2,1)} %param.9, bf16[96,192]{1,0:T(8,128)(2,1)} %param.8), kind=kLoop, calls=%fused_computation.51 | loop fusion | flops 147456 | bytes 147456 | tf_op jit(solution)/shard_map/concatenate | solution.py:63
  0.9 0.1 broadcast_in_dim.4
  1.0 23.6 %all_to_all.10 = bf16[8,96,384]{2,1,0:T(8,128)(2,1)S(1)} all-to-all(bf16[8,96,384]{2,1,0:T(8,128)(2,1)S(1)} %broadcast_in_dim.4), channel_id=1, replica_groups=mesh['expert'=2,'chip'=8,'core'=2] {'chip'}, dimensions={0} | all-to-all | bytes 1179648 | tf_op jit(solution)/shard_map/all_to_all | solution.py:65
  24.6 1.5 %collective-permute-start = (bf16[8,96,384]{2,1,0:T(8,128)(2,1)S(1)}, bf16[8,96,384]{2,1,0:T(8,128)(2,1)S(1)}, u32[]{:S(2)}, u32[]{:S(2)}) collective-permute-start(bf16[8,96,384]{2,1,0:T(8,128)(2,1)S(1)} %all_to_all.10), channel_id=1, source_target_pairs={{0,16},{16,0},{1,17},{17,1},{2,18},{18,2},{3,19},{19,3},{4,20},{20... | collective-permute-start | bytes 1769480 | tf_op jit(solution)/shard_map/ppermute | solution.py:57
  26.1 0.7 convert_element_type.68
  26.8 0.7 fusion.45
  27.5 0.5 collective-permute-start.1
  28.0 8.7 %copy.19 = bf16[1,1024,3072]{1,2,0:T(8,128)(2,1)} copy(bf16[1,1024,3072]{2,1,0:T(8,128)(2,1)} %param.12) | data formatting | bytes 12582912 | tf_op args[4]
  36.6 1.9 %collective-permute-done.1 = f32[2,96]{1,0:T(2,128)S(1)} collective-permute-done((f32[2,96]{1,0:T(2,128)S(1)}, f32[2,96]{1,0:T(2,128)S(1)}, u32[]{:S(2)}, u32[]{:S(2)}) %collective-permute-start.1) | collective-permute-done | bytes 800 | tf_op jit(solution)/shard_map/ppermute | solution.py:57
  38.6 0.1 pad_maximum_fusion.1
  38.7 0.1 slice.42
  38.8 0.1 collective-permute-start.3
  38.9 0.1 add.87
  39.0 0.1 add.88
  39.1 0.6 gather_fusion
  39.7 0.1 convert_element_type.70
  39.8 0.1 mul.77
  39.9 1.0 %collective-permute-done.3 = bf16[1,8,96,384]{3,2,0,1:T(8,128)(2,1)S(1)} collective-permute-done((bf16[1,8,96,384]{3,2,0,1:T(8,128)(2,1)S(1)}, bf16[1,8,96,384]{3,2,0,1:T(8,128)(2,1)S(1)}, u32[]{:S(2)}, u32[]{:S(2)}) %collective-permute-start.3) | collective-permute-done | bytes 589856 | tf_op jit(solution)/shard_map/ppermute | solution.py:33
  40.9 0.3 select_bitcast_fusion.1
  41.2 0.0 slice-start.3
  41.2 0.3 pad_maximum_fusion
  41.5 0.9 %convolution_bitcast_fusion = f32[192,8,2,384]{3,0,2,1:T(8,128)S(1)} fusion(bf16[2,8,2,96,384]{4,3,0,2,1:T(8,128)(2,1)S(1)} %pad_maximum_fusion, s32[2,96]{1,0:T(2,128)S(1)} %multiply_add_fusion, s32[192]{0:T(256)S(1)} %add.89), kind=kOutput, calls=%fused_computation.11 | convolution fusion | flops 453021696 | bytes 7079424 | tf_op jit(solution)/shard_map/dot_general | solution.py:80
  42.3 0.7 slice-done.2
  43.1 0.7 slice-done.3
  43.8 1.5 %convolution_bitcast_fusion.1 = f32[192,1024]{1,0:T(8,128)S(1)} fusion(bf16[8,2,192,1024]{3,2,1,0:T(8,128)(2,1)S(1)} %bitcast.104, f32[192,8,2,384]{3,0,2,1:T(8,128)S(1)} %convolution_bitcast_fusion), kind=kOutput, calls=%fused_computation.14 | convolution fusion | flops 1207959552 | bytes 8650752 | tf_op jit(solution)/shard_map/dot_general | solution.py:88
  45.3 0.3 slice-done.5
  45.7 0.2 copy-done.1
  45.9 2.3 %multiply_convert_fusion = (bf16[192,1024]{1,0:T(8,128)(2,1)S(1)}, f32[192,1024]{1,0:T(8,128)S(1)}) fusion(f32[192,1024]{1,0:T(8,128)S(1)} %convolution_bitcast_fusion.1, s32[1,192,1024]{2,1,0:T(8,128)S(1)} %copy-done.1, bf16[8,2,192,1024]{3,2,1,0:T(8,128)(2,1)S(1)} %bitcast.107, f32[192,8,2,384]{3,0,2,1:T(8,128)S(1)} %convolution_bitcast_fusion, ...), kind=kOutput, calls=%fused_computation.40 | convolution fusion | flops 1211695104 | bytes 12190720 | tf_op jit(solution)/shard_map/dot_general | solution.py:90
  48.2 2.0 %fusion.32 = bf16[192,1024]{1,0:T(8,128)(2,1)S(1)} fusion(f32[192,1024]{1,0:T(8,128)S(1)} %convolution_bitcast_fusion.1, f32[192,1024]{1,0:T(8,128)S(1)} %get-tuple-element.22, bf16[8,2,192,1024]{3,2,1,0:T(8,128)(2,1)S(1)} %bitcast.101, f32[192,8,2,384]{3,0,2,1:T(8,128)S(1)} %convolution_bitcast_fusion), kind=kOutput, calls=%fused_computation.39 | convolution fusion | flops 1212088320 | bytes 9830400 | tf_op jit(solution)/shard_map/dot_general | solution.py:89
  50.2 2.2 %fusion = f32[192,3072]{1,0:T(8,128)S(1)} fusion(bf16[192,1024]{1,0:T(8,128)(2,1)S(1)} %get-tuple-element.16, bf16[1,3072,1024]{2,1,0:T(8,128)(2,1)S(1)} %bitcast.100), kind=kOutput, calls=%fused_computation.1 | convolution fusion | flops 1207959552 | bytes 9043968 | tf_op jit(solution)/shard_map/dot_general | solution.py:103
  52.4 2.2 %fusion.7 = bf16[192,3072]{1,0:T(8,128)(2,1)S(1)} fusion(f32[192,3072]{1,0:T(8,128)S(1)} %fusion, bf16[192,1024]{1,0:T(8,128)(2,1)S(1)} %fusion.32, bf16[1,3072,1024]{2,1,0:T(8,128)(2,1)S(1)} %bitcast.103), kind=kOutput, calls=%fused_computation.6 | convolution fusion | flops 1209139200 | bytes 10223616 | tf_op jit(solution)/shard_map/dot_general | solution.py:101
  54.6 0.2 copy.29
  54.9 0.2 copy.31
  55.0 0.1 select_bitcast_fusion.2
  55.1 0.2 collective-permute-start.4
  55.3 1.9 %collective-permute-done.4 = bf16[2,8,48,384]{3,2,1,0:T(8,128)(2,1)S(1)} collective-permute-done((bf16[2,8,48,384]{3,2,1,0:T(8,128)(2,1)S(1)}, bf16[2,8,48,384]{3,2,1,0:T(8,128)(2,1)S(1)}, u32[]{:S(2)}, u32[]{:S(2)}) %collective-permute-start.4) | collective-permute-done | bytes 589856 | tf_op jit(solution)/shard_map/ppermute | solution.py:33
  57.2 1.0 %fusion.24 = bf16[2,8,48,384]{3,2,1,0:T(8,128)(2,1)} fusion(bf16[2,8,48,384]{3,2,1,0:T(8,128)(2,1)S(1)} %collective-permute-done.4, pred[]{:T(512)S(6)} %eq.45, bf16[2,2,8,48,384]{4,3,2,0,1:T(8,128)(2,1)S(1)} %bitcast.98), kind=kLoop, calls=%fused_computation.24 | loop fusion | flops 1474560 | bytes 2359297 | tf_op jit(solution)/shard_map/convert_element_type | solution.py:111
  58.2 5.0 %all-to-all-start.1 = ((bf16[16,48,384]{2,1,0:T(8,128)(2,1)}), bf16[16,48,384]{2,1,0:T(8,128)(2,1)S(1)}, u32[]{:S(2)}, u32[]{:S(2)}) async-start(bf16[16,48,384]{2,1,0:T(8,128)(2,1)} %bitcast.36), calls=%async_computation.1 | async-start | bytes 1179648 | tf_op jit(solution)/shard_map/all_to_all | solution.py:112
  63.3 0.1 eq.46
  63.4 0.1 fusion.37
  63.5 16.4 %all-to-all-done.1 = bf16[16,48,384]{2,1,0:T(8,128)(2,1)S(1)} async-done(((bf16[16,48,384]{2,1,0:T(8,128)(2,1)}), bf16[16,48,384]{2,1,0:T(8,128)(2,1)S(1)}, u32[]{:S(2)}, u32[]{:S(2)}) %all-to-all-start.1) | async-done | bytes 589856 | tf_op jit(solution)/shard_map/all_to_all | solution.py:112
  79.9 0.1 convert_reduce_fusion
  79.9 0.2 convolution_bitcast_fusion.3
  80.1 0.2 fusion.25
  80.3 0.1 slice_select_fusion
  80.4 0.1 collective-permute-start.5
  80.5 1.3 %collective-permute-done.5 = f32[96,192]{1,0:T(8,128)S(1)} collective-permute-done((f32[96,192]{1,0:T(8,128)S(1)}, f32[96,192]{1,0:T(8,128)S(1)}, u32[]{:S(2)}, u32[]{:S(2)}) %collective-permute-start.5) | collective-permute-done | bytes 73760 | tf_op jit(solution)/shard_map/ppermute | solution.py:33
  81.8 0.7 add_convert_fusion
  (26 shorter events, 0.1 us)
Async XLA Ops:
  24.6 14.0 %collective-permute-start = (bf16[8,96,384]{2,1,0:T(8,128)(2,1)S(1)}, bf16[8,96,384]{2,1,0:T(8,128)(2,1)S(1)}, u32[]{:S(2)}, u32[]{:S(2)}) collective-permute-start(bf16[8,96,384]{2,1,0:T(8,128)(2,1)S(1)} %all_to_all.10), channel_id=1, source_target_pairs={{0,16},{16,0},{1,17},{17,1},{2,18},{18,2},{3,19},{19,3},{4,20},{20... | collective-permute-start | bytes 1769480 | tf_op jit(solution)/shard_map/ppermute | solution.py:57
  26.1 12.6 %collective-permute-start.2 = (bf16[8,96,384]{2,1,0:T(8,128)(2,1)S(1)}, bf16[8,96,384]{2,1,0:T(8,128)(2,1)S(1)}, u32[]{:S(2)}, u32[]{:S(2)}) collective-permute-start(bf16[8,96,384]{2,1,0:T(8,128)(2,1)S(1)} %all_to_all.10), channel_id=1, source_target_pairs={{0,1},{1,0},{2,3},{3,2},{4,5},{5,4},{6,7},{7,6},{8,9},{9,8},{10,11... | collective-permute-start | bytes 1769480 | tf_op jit(solution)/shard_map/ppermute | solution.py:33
  27.5 11.1 %collective-permute-start.1 = (f32[2,96]{1,0:T(2,128)S(1)}, f32[2,96]{1,0:T(2,128)S(1)}, u32[]{:S(2)}, u32[]{:S(2)}) collective-permute-start(f32[2,96]{1,0:T(2,128)S(1)} %get-tuple-element.20), channel_id=1, source_target_pairs={{0,16},{16,0},{1,17},{17,1},{2,18},{18,2},{3,19},{19,3},{4,20},{20... | collective-permute-start | bytes 2312 | tf_op jit(solution)/shard_map/ppermute | solution.py:57
  38.8 2.1 %collective-permute-start.3 = (bf16[1,8,96,384]{3,2,0,1:T(8,128)(2,1)S(1)}, bf16[1,8,96,384]{3,2,0,1:T(8,128)(2,1)S(1)}, u32[]{:S(2)}, u32[]{:S(2)}) collective-permute-start(bf16[1,8,96,384]{3,2,0,1:T(8,128)(2,1)S(1)} %slice.42), channel_id=1, source_target_pairs={{0,1},{1,0},{2,3},{3,2},{4,5},{5,4},{6,7},{7,6},{8,9},{9,8},{10,11... | collective-permute-start | bytes 1769480 | tf_op jit(solution)/shard_map/ppermute | solution.py:33
  40.9 2.2 %slice-start.2 = ((s8[6291456]{0:T(1024)(128)(4,1)}), s8[4194304]{0:T(1024)(128)(4,1)S(1)}, s32[]{:S(2)}) async-start(s8[6291456]{0:T(1024)(128)(4,1)} %bitcast.102), calls=%async_computation.4 | async-start | bytes 8388608
  41.2 2.7 %slice-start.3 = ((s8[6291456]{0:T(1024)(128)(4,1)}), s8[2097152]{0:T(1024)(128)(4,1)S(1)}, s32[]{:S(2)}) async-start(s8[6291456]{0:T(1024)(128)(4,1)} %bitcast.102), calls=%async_computation.5 | async-start | bytes 4194304
  41.2 4.2 %slice-start.4 = ((s8[6291456]{0:T(1024)(128)(4,1)}), s8[4194304]{0:T(1024)(128)(4,1)S(1)}, s32[]{:S(2)}) async-start(s8[6291456]{0:T(1024)(128)(4,1)} %bitcast.105), calls=%async_computation.6 | async-start | bytes 8388608
  41.4 4.2 %slice-start.5 = ((s8[6291456]{0:T(1024)(128)(4,1)}), s8[2097152]{0:T(1024)(128)(4,1)S(1)}, s32[]{:S(2)}) async-start(s8[6291456]{0:T(1024)(128)(4,1)} %bitcast.105), calls=%async_computation.7 | async-start | bytes 4194304
  43.8 2.1 %copy-start.1 = (s32[1,192,1024]{2,1,0:T(8,128)S(1)}, s32[1,192,1024]{2,1,0:T(8,128)}, u32[]{:S(2)}) copy-start(s32[1,192,1024]{2,1,0:T(8,128)} %param.15) | copy-start | bytes 2359300
  43.8 4.4 %slice-start = ((s8[6291456]{0:T(1024)(128)(4,1)}), s8[4194304]{0:T(1024)(128)(4,1)S(1)}, s32[]{:S(2)}) async-start(s8[6291456]{0:T(1024)(128)(4,1)} %bitcast.99), calls=%async_computation.2 | async-start | bytes 8388608
  45.9 2.3 %slice-start.1 = ((s8[6291456]{0:T(1024)(128)(4,1)}), s8[2097152]{0:T(1024)(128)(4,1)S(1)}, s32[]{:S(2)}) async-start(s8[6291456]{0:T(1024)(128)(4,1)} %bitcast.99), calls=%async_computation.3 | async-start | bytes 4194304
  55.0 8.2 %copy-start = (s32[2,96]{1,0:T(2,128)S(1)}, s32[2,96]{1,0:T(2,128)}, u32[]{:S(2)}) copy-start(s32[2,96]{1,0:T(2,128)} %param.13) | copy-start | bytes 2308
  55.1 2.1 %collective-permute-start.4 = (bf16[2,8,48,384]{3,2,1,0:T(8,128)(2,1)S(1)}, bf16[2,8,48,384]{3,2,1,0:T(8,128)(2,1)S(1)}, u32[]{:S(2)}, u32[]{:S(2)}) collective-permute-start(bf16[2,8,48,384]{3,2,1,0:T(8,128)(2,1)S(1)} %select_bitcast_fusion.2), channel_id=1, source_target_pairs={{0,1},{1,0},{2,3},{3,2},{4,5},{5,4},{6,7},{7,6},{8,9},{9,8},{10,11... | collective-permute-start | bytes 1769480 | tf_op jit(solution)/shard_map/ppermute | solution.py:33
  58.2 21.6 %all-to-all-start.1 = ((bf16[16,48,384]{2,1,0:T(8,128)(2,1)}), bf16[16,48,384]{2,1,0:T(8,128)(2,1)S(1)}, u32[]{:S(2)}, u32[]{:S(2)}) async-start(bf16[16,48,384]{2,1,0:T(8,128)(2,1)} %bitcast.36), calls=%async_computation.1 | async-start | bytes 1179648 | tf_op jit(solution)/shard_map/all_to_all | solution.py:112
  80.4 1.4 %collective-permute-start.5 = (f32[96,192]{1,0:T(8,128)S(1)}, f32[96,192]{1,0:T(8,128)S(1)}, u32[]{:S(2)}, u32[]{:S(2)}) collective-permute-start(f32[96,192]{1,0:T(8,128)S(1)} %slice_select_fusion), channel_id=1, source_target_pairs={{0,1},{1,0},{2,3},{3,2},{4,5},{5,4},{6,7},{7,6},{8,9},{9,8},{10,11... | collective-permute-start | bytes 221192 | tf_op jit(solution)/shard_map/ppermute | solution.py:33

commit v23 on v22

--- a/solution.py
+++ b/solution.py
@@ -77,9 +77,10 @@
     column = (block_rel[:, None] * group_tokens + mine_tokens).reshape(-1)
     pick = (column[:, None] == jnp.arange(expert_count * group_tokens)[None, :]).astype(jnp.bfloat16)
     pick = pick.reshape(slot_count, expert_count, group_tokens)
-    rows = lax.dot_general(pick, full, (((1, 2), (0, 3)), ((), ())), preferred_element_type=jnp.float32)
-    part_inputs = rows[..., :local_width].astype(jnp.bfloat16)
-    part_cot = (mine_weights * rows[..., local_width:]).astype(jnp.bfloat16)
+    pick_dims = (((1, 2), (0, 3)), ((), ()))
+    part_inputs = lax.dot_general(pick, full[..., :local_width], pick_dims, preferred_element_type=jnp.bfloat16)
+    cot_rows = lax.dot_general(pick, full[..., local_width:], pick_dims, preferred_element_type=jnp.float32)
+    part_cot = (mine_weights * cot_rows).astype(jnp.bfloat16)
 
     gate_rows = gate_mat.reshape(chip_count, 2, local_width, local_ff)
     up_rows = up_mat.reshape(chip_count, 2, local_width, local_ff)

time: 83 us -> 97.3 us (1.17)
  matrix products: 11.5 us -> 25.6 us
  other arithmetic: 5.11 us -> 3.79 us
  waiting for transfers between devices: 22.5 us -> 23.8 us
    dot_general x1, matrix products: 2.3 us -> 6.51 us  [body(): lax.dot_general(part_cot, down_rows, fwd_dims, preferred_element_type=jnp...]
    dot_general x1, matrix products: 1.99 us -> 5.46 us  [body(): lax.dot_general(part_inputs, up_rows, fwd_dims, preferred_element_type=jn...]
    dot_general x1, matrix products: 2.22 us -> 5.04 us  [body(): lax.dot_general(grad_gate, gate_mat, back_dims, preferred_element_type=jn...]
    dot_general x1, matrix products: 2.2 us -> 5 us  [body(): lax.dot_general(grad_up, up_mat, back_dims, preferred_element_type=jnp.fl...]
    ppermute x2, waiting for transfers between devices: 1.93 us -> 3.22 us  [from_groups(): lax.ppermute(moved, 'expert', [(i, (i + shift) % expert_count) for i in r...]
    unnamed x18 -> x12, local copies, waits for them, and re-layouts: 10.9 us -> 11.1 us
  transfers between devices with their start and end apart: 7 -> 7, of which waited for: 5 -> 5; matrix products, arithmetic and copies ran while one was open for 14% -> 10% of each run, Pallas kernels for 0% -> 0%
where the time goes in v23:
time: 97.3 us; the launch traced here: 96.8 us
  matrix products  25.6 us (26%)
  waiting for transfers between devices  23.8 us (24%)
  blocking collectives  23.6 us (24%)
  local copies, waits for them, and re-layouts  12.4 us (13%)
  starting transfers between devices  7.44 us (8%)
  other arithmetic  3.79 us (4%)
    all_to_all x1, blocking collectives, body(): lax.all_to_all(outgoing, 'chip', split_axis=0, concat_axis=0, tiled=True)  23.6 us
    all_to_all x1, waiting for transfers between devices, body(): lax.all_to_all(blocks, CROSS, split_axis=0, concat_axis=0, tiled=True)  16.4 us
    unnamed x12, local copies, waits for them, and re-layouts  11.1 us
    dot_general x1, matrix products, body(): lax.dot_general(part_cot, down_rows, fwd_dims, preferred_element_type=jnp...  6.51 us
    dot_general x1, matrix products, body(): lax.dot_general(part_inputs, up_rows, fwd_dims, preferred_element_type=jn...  5.46 us
    dot_general x1, matrix products, body(): lax.dot_general(grad_gate, gate_mat, back_dims, preferred_element_type=jn...  5.04 us
    dot_general x1, matrix products, body(): lax.dot_general(grad_up, up_mat, back_dims, preferred_element_type=jnp.fl...  5 us
    all_to_all x1, starting transfers between devices, body(): lax.all_to_all(blocks, CROSS, split_axis=0, concat_axis=0, tiled=True)  5 us
  transfers between devices with their start and end apart: 7, of which 5 were waited for; matrix products, arithmetic and copies ran while one was open for 10% of the time, Pallas kernels for 0%

profile of v23, /device:TPU:0, one launch (start us, length us, event | category | flops | bytes accessed | tf_op | source)
XLA Modules:
  0.0 96.8 jit_solution(4871918879530812287)
XLA Ops:
  0.0 0.9 pad_maximum_fusion.3
  0.9 0.1 broadcast_in_dim.4
  1.0 23.6 %all_to_all.10 = bf16[8,96,384]{2,1,0:T(8,128)(2,1)S(1)} all-to-all(bf16[8,96,384]{2,1,0:T(8,128)(2,1)S(1)} %broadcast_in_dim.4), channel_id=1, replica_groups=mesh['expert'=2,'chip'=8,'core'=2] {'chip'}, dimensions={0} | all-to-all | bytes 1179648 | tf_op jit(solution)/shard_map/all_to_all | solution.py:65
  24.6 1.5 %collective-permute-start = (bf16[8,96,384]{2,1,0:T(8,128)(2,1)S(1)}, bf16[8,96,384]{2,1,0:T(8,128)(2,1)S(1)}, u32[]{:S(2)}, u32[]{:S(2)}) collective-permute-start(bf16[8,96,384]{2,1,0:T(8,128)(2,1)S(1)} %all_to_all.10), channel_id=1, source_target_pairs={{0,16},{16,0},{1,17},{17,1},{2,18},{18,2},{3,19},{19,3},{4,20},{20... | collective-permute-start | bytes 1769480 | tf_op jit(solution)/shard_map/ppermute | solution.py:57
  26.1 0.0 collective-permute-start.2
  26.1 0.0 copy-done.1
  26.2 0.6 collective-permute-start.1
  26.8 8.6 %copy.19 = bf16[1,1024,3072]{1,2,0:T(8,128)(2,1)} copy(bf16[1,1024,3072]{2,1,0:T(8,128)(2,1)} %param.12) | data formatting | bytes 12582912 | tf_op args[4]
  35.4 3.2 %collective-permute-done.1 = f32[2,96]{1,0:T(2,128)S(1)} collective-permute-done((f32[2,96]{1,0:T(2,128)S(1)}, f32[2,96]{1,0:T(2,128)S(1)}, u32[]{:S(2)}, u32[]{:S(2)}) %collective-permute-start.1) | collective-permute-done | bytes 800 | tf_op jit(solution)/shard_map/ppermute | solution.py:57
  38.6 0.0 collective-permute-done
  38.6 0.1 pad_maximum_fusion.1
  38.8 0.0 collective-permute-done.2
  38.8 0.1 slice.41
  38.8 0.1 collective-permute-start.3
  38.9 0.1 add.87
  39.0 0.1 add.88
  39.1 0.6 gather_fusion
  39.7 0.1 convert_element_type.69
  39.8 0.1 mul.77
  39.9 1.0 %collective-permute-done.3 = bf16[1,8,96,384]{3,2,0,1:T(8,128)(2,1)S(1)} collective-permute-done((bf16[1,8,96,384]{3,2,0,1:T(8,128)(2,1)S(1)}, bf16[1,8,96,384]{3,2,0,1:T(8,128)(2,1)S(1)}, u32[]{:S(2)}, u32[]{:S(2)}) %collective-permute-start.3) | collective-permute-done | bytes 589856 | tf_op jit(solution)/shard_map/ppermute | solution.py:33
  40.9 0.3 select_bitcast_fusion.1
  41.2 0.0 slice-start.1
  41.2 0.3 pad_maximum_fusion
  41.5 0.7 fusion.11
  42.2 0.9 slice-done
  43.1 1.3 %slice-done.1 = s8[2097152]{0:T(1024)(128)(4,1)S(1)} async-done(((s8[6291456]{0:T(1024)(128)(4,1)}), s8[2097152]{0:T(1024)(128)(4,1)S(1)}, s32[]{:S(2)}) %slice-start.1) | async-done | bytes 2097176
  44.4 2.5 %fusion.33 = f32[192,1024]{1,0:T(8,128)} fusion(bf16[8,2,192,1024]{3,2,1,0:T(8,128)(2,1)S(1)} %bitcast.132, bf16[192,8,2,192,1]{3,0,4,2,1:T(8,128)(2,1)S(1)} %fusion.11), kind=kOutput, calls=%fused_computation.22 | convolution fusion | flops 1207959552 | bytes 8257536 | tf_op jit(solution)/shard_map/dot_general | solution.py:89
  46.9 6.5 %multiply_convert_fusion = (bf16[192,1024]{1,0:T(8,128)(2,1)S(1)}, f32[192,1024]{1,0:T(8,128)}) fusion(f32[192,1024]{1,0:T(8,128)} %fusion.33, s32[1,192,1024]{2,1,0:T(8,128)} %param.15, bf16[8,2,192,1024]{3,2,1,0:T(8,128)(2,1)} %bitcast.133, bf16[2,8,2,96,384]{4,3,0,2,1:T(8,128)(2,1)S(1)} %pad_maximum_fusion, f32[192]{0:T(256)S(1)} %mul.77, ...), kind=kOutput, calls=%fused_computation.44 | convolution fusion | flops 1438224384 | bytes 10619904 | tf_op jit(solution)/shard_map/dot_general | solution.py:91
  53.4 5.5 %fusion.47 = bf16[192,1024]{1,0:T(8,128)(2,1)S(1)} fusion(f32[192,1024]{1,0:T(8,128)} %fusion.33, f32[192,1024]{1,0:T(8,128)} %get-tuple-element.22, bf16[8,2,192,1024]{3,2,1,0:T(8,128)(2,1)} %bitcast.129, bf16[192,8,2,192,1]{3,0,4,2,1:T(8,128)(2,1)} %copy-done), kind=kOutput, calls=%fused_computation.43 | convolution fusion | flops 1212088320 | bytes 9437184 | tf_op jit(solution)/shard_map/dot_general | solution.py:90
  58.8 5.0 %fusion = f32[192,3072]{1,0:T(8,128)S(1)} fusion(bf16[192,1024]{1,0:T(8,128)(2,1)S(1)} %get-tuple-element.16, bf16[1,3072,1024]{2,1,0:T(8,128)(2,1)} %param.11), kind=kOutput, calls=%fused_computation.1 | convolution fusion | flops 1207959552 | bytes 9043968 | tf_op jit(solution)/shard_map/dot_general | solution.py:104
  63.9 5.0 %fusion.7 = bf16[192,3072]{1,0:T(8,128)(2,1)S(1)} fusion(f32[192,3072]{1,0:T(8,128)S(1)} %fusion, bf16[192,1024]{1,0:T(8,128)(2,1)S(1)} %fusion.47, bf16[1,3072,1024]{2,1,0:T(8,128)(2,1)} %param.10), kind=kOutput, calls=%fused_computation.6 | convolution fusion | flops 1209139200 | bytes 10223616 | tf_op jit(solution)/shard_map/dot_general | solution.py:102
  68.9 0.2 copy.30
  69.1 0.2 copy.32
  69.3 0.1 select_bitcast_fusion.2
  69.4 0.2 collective-permute-start.4
  69.6 1.9 %collective-permute-done.4 = bf16[2,8,48,384]{3,2,1,0:T(8,128)(2,1)S(1)} collective-permute-done((bf16[2,8,48,384]{3,2,1,0:T(8,128)(2,1)S(1)}, bf16[2,8,48,384]{3,2,1,0:T(8,128)(2,1)S(1)}, u32[]{:S(2)}, u32[]{:S(2)}) %collective-permute-start.4) | collective-permute-done | bytes 589856 | tf_op jit(solution)/shard_map/ppermute | solution.py:33
  71.4 1.1 %fusion.39 = bf16[2,8,48,384]{3,2,1,0:T(8,128)(2,1)} fusion(bf16[2,8,48,384]{3,2,1,0:T(8,128)(2,1)S(1)} %collective-permute-done.4, pred[]{:T(512)S(6)} %eq.45, bf16[2,2,8,48,384]{4,3,2,0,1:T(8,128)(2,1)S(1)} %bitcast.128), kind=kLoop, calls=%fused_computation.28 | loop fusion | flops 1474560 | bytes 2359297 | tf_op jit(solution)/shard_map/convert_element_type | solution.py:112
  72.5 5.0 %all-to-all-start.1 = ((bf16[16,48,384]{2,1,0:T(8,128)(2,1)}), bf16[16,48,384]{2,1,0:T(8,128)(2,1)S(1)}, u32[]{:S(2)}, u32[]{:S(2)}) async-start(bf16[16,48,384]{2,1,0:T(8,128)(2,1)} %bitcast.39), calls=%async_computation.1 | async-start | bytes 1179648 | tf_op jit(solution)/shard_map/all_to_all | solution.py:113
  77.5 0.1 eq.46
  77.6 0.1 fusion.62
  77.7 16.4 %all-to-all-done.1 = bf16[16,48,384]{2,1,0:T(8,128)(2,1)S(1)} async-done(((bf16[16,48,384]{2,1,0:T(8,128)(2,1)}), bf16[16,48,384]{2,1,0:T(8,128)(2,1)S(1)}, u32[]{:S(2)}, u32[]{:S(2)}) %all-to-all-start.1) | async-done | bytes 589856 | tf_op jit(solution)/shard_map/all_to_all | solution.py:113
  94.1 0.1 convert_reduce_fusion
  94.2 0.2 convolution_bitcast_fusion
  94.4 0.2 fusion.40
  94.6 0.1 slice_select_fusion
  94.7 0.1 collective-permute-start.5
  94.8 1.3 %collective-permute-done.5 = f32[96,192]{1,0:T(8,128)S(1)} collective-permute-done((f32[96,192]{1,0:T(8,128)S(1)}, f32[96,192]{1,0:T(8,128)S(1)}, u32[]{:S(2)}, u32[]{:S(2)}) %collective-permute-start.5) | collective-permute-done | bytes 73760 | tf_op jit(solution)/shard_map/ppermute | solution.py:33
  96.0 0.7 add_convert_fusion
  (18 shorter events, 0.1 us)
Async XLA Ops:
  0.0 26.1 %copy-start.1 = (s32[2,96]{1,0:T(2,128)S(1)}, s32[2,96]{1,0:T(2,128)}, u32[]{:S(2)}) copy-start(s32[2,96]{1,0:T(2,128)} %param.13) | copy-start | bytes 2308
  0.0 26.2 %copy-start.2 = (f32[2,96]{1,0:T(2,128)S(1)}, f32[2,96]{1,0:T(2,128)}, u32[]{:S(2)}) copy-start(f32[2,96]{1,0:T(2,128)} %param.14) | copy-start | bytes 2308
  24.6 14.0 %collective-permute-start = (bf16[8,96,384]{2,1,0:T(8,128)(2,1)S(1)}, bf16[8,96,384]{2,1,0:T(8,128)(2,1)S(1)}, u32[]{:S(2)}, u32[]{:S(2)}) collective-permute-start(bf16[8,96,384]{2,1,0:T(8,128)(2,1)S(1)} %all_to_all.10), channel_id=1, source_target_pairs={{0,16},{16,0},{1,17},{17,1},{2,18},{18,2},{3,19},{19,3},{4,20},{20... | collective-permute-start | bytes 1769480 | tf_op jit(solution)/shard_map/ppermute | solution.py:57
  26.1 12.6 %collective-permute-start.2 = (bf16[8,96,384]{2,1,0:T(8,128)(2,1)S(1)}, bf16[8,96,384]{2,1,0:T(8,128)(2,1)S(1)}, u32[]{:S(2)}, u32[]{:S(2)}) collective-permute-start(bf16[8,96,384]{2,1,0:T(8,128)(2,1)S(1)} %all_to_all.10), channel_id=1, source_target_pairs={{0,1},{1,0},{2,3},{3,2},{4,5},{5,4},{6,7},{7,6},{8,9},{9,8},{10,11... | collective-permute-start | bytes 1769480 | tf_op jit(solution)/shard_map/ppermute | solution.py:33
  26.2 12.4 %collective-permute-start.1 = (f32[2,96]{1,0:T(2,128)S(1)}, f32[2,96]{1,0:T(2,128)S(1)}, u32[]{:S(2)}, u32[]{:S(2)}) collective-permute-start(f32[2,96]{1,0:T(2,128)S(1)} %get-tuple-element.20), channel_id=1, source_target_pairs={{0,16},{16,0},{1,17},{17,1},{2,18},{18,2},{3,19},{19,3},{4,20},{20... | collective-permute-start | bytes 2312 | tf_op jit(solution)/shard_map/ppermute | solution.py:57
  38.8 2.1 %collective-permute-start.3 = (bf16[1,8,96,384]{3,2,0,1:T(8,128)(2,1)S(1)}, bf16[1,8,96,384]{3,2,0,1:T(8,128)(2,1)S(1)}, u32[]{:S(2)}, u32[]{:S(2)}) collective-permute-start(bf16[1,8,96,384]{3,2,0,1:T(8,128)(2,1)S(1)} %slice.41), channel_id=1, source_target_pairs={{0,1},{1,0},{2,3},{3,2},{4,5},{5,4},{6,7},{7,6},{8,9},{9,8},{10,11... | collective-permute-start | bytes 1769480 | tf_op jit(solution)/shard_map/ppermute | solution.py:33
  40.9 2.2 %slice-start = ((s8[6291456]{0:T(1024)(128)(4,1)}), s8[4194304]{0:T(1024)(128)(4,1)S(1)}, s32[]{:S(2)}) async-start(s8[6291456]{0:T(1024)(128)(4,1)} %bitcast.130), calls=%async_computation.2 | async-start | bytes 8388608
  41.2 3.2 %slice-start.1 = ((s8[6291456]{0:T(1024)(128)(4,1)}), s8[2097152]{0:T(1024)(128)(4,1)S(1)}, s32[]{:S(2)}) async-start(s8[6291456]{0:T(1024)(128)(4,1)} %bitcast.130), calls=%async_computation.3 | async-start | bytes 4194304
  42.1 4.7 %copy-start = (bf16[192,8,2,192,1]{3,0,4,2,1:T(8,128)(2,1)}, bf16[192,8,2,192,1]{3,0,4,2,1:T(8,128)(2,1)S(1)}, u32[]{:S(2)}) copy-start(bf16[192,8,2,192,1]{3,0,4,2,1:T(8,128)(2,1)S(1)} %fusion.11) | copy-start | bytes 3538948
  69.4 2.1 %collective-permute-start.4 = (bf16[2,8,48,384]{3,2,1,0:T(8,128)(2,1)S(1)}, bf16[2,8,48,384]{3,2,1,0:T(8,128)(2,1)S(1)}, u32[]{:S(2)}, u32[]{:S(2)}) collective-permute-start(bf16[2,8,48,384]{3,2,1,0:T(8,128)(2,1)S(1)} %select_bitcast_fusion.2), channel_id=1, source_target_pairs={{0,1},{1,0},{2,3},{3,2},{4,5},{5,4},{6,7},{7,6},{8,9},{9,8},{10,11... | collective-permute-start | bytes 1769480 | tf_op jit(solution)/shard_map/ppermute | solution.py:33
  72.5 21.6 %all-to-all-start.1 = ((bf16[16,48,384]{2,1,0:T(8,128)(2,1)}), bf16[16,48,384]{2,1,0:T(8,128)(2,1)S(1)}, u32[]{:S(2)}, u32[]{:S(2)}) async-start(bf16[16,48,384]{2,1,0:T(8,128)(2,1)} %bitcast.39), calls=%async_computation.1 | async-start | bytes 1179648 | tf_op jit(solution)/shard_map/all_to_all | solution.py:113
  94.7 1.4 %collective-permute-start.5 = (f32[96,192]{1,0:T(8,128)S(1)}, f32[96,192]{1,0:T(8,128)S(1)}, u32[]{:S(2)}, u32[]{:S(2)}) collective-permute-start(f32[96,192]{1,0:T(8,128)S(1)} %slice_select_fusion), channel_id=1, source_target_pairs={{0,1},{1,0},{2,3},{3,2},{4,5},{5,4},{6,7},{7,6},{8,9},{9,8},{10,11... | collective-permute-start | bytes 221192 | tf_op jit(solution)/shard_map/ppermute | solution.py:33

commit v24 on v22

--- a/solution.py
+++ b/solution.py
@@ -114,10 +114,10 @@
     one_hot = (slot_list[:, None] == jnp.arange(group_tokens, dtype=jnp.int32)[None, :]).astype(jnp.bfloat16)
     row_hot = one_hot.reshape(expert_total, 2, half, group_tokens)
     own_hot = jnp.where(first, row_hot[:, 0], row_hot[:, 1])
-    chip_tokens = fold_slots(own_hot, per_expert)
-    keep_cols = jnp.where(first, chip_tokens[:, :local_width], chip_tokens[:, local_width:])
-    send_cols = jnp.where(first, chip_tokens[:, local_width:], chip_tokens[:, :local_width])
-    token_sum = keep_cols + swap_cores(send_cols)
+    send_vals = jnp.where(first, per_expert[..., local_width:], per_expert[..., :local_width])
+    keep_vals = jnp.where(first, per_expert[..., :local_width], per_expert[..., local_width:])
+    swapped = swap_cores(fold_slots(own_hot, send_vals))
+    token_sum = fold_slots(own_hot, keep_vals) + swapped
     return token_sum.astype(jnp.bfloat16)
 
 

time: 83 us -> 83.1 us (level)
  matrix products: 11.5 us -> 12.5 us
where the time goes in v24:
time: 83.1 us; the launch traced here: 82.6 us
  blocking collectives  23.6 us (28%)
  waiting for transfers between devices  22.2 us (27%)
  matrix products  12.5 us (15%)
  local copies, waits for them, and re-layouts  12.2 us (15%)
  starting transfers between devices  7.39 us (9%)
  other arithmetic  4.4 us (5%)
    all_to_all x1, blocking collectives, body(): lax.all_to_all(outgoing, 'chip', split_axis=0, concat_axis=0, tiled=True)  23.6 us
    all_to_all x1, waiting for transfers between devices, body(): lax.all_to_all(blocks, CROSS, split_axis=0, concat_axis=0, tiled=True)  16.4 us
    unnamed x18, local copies, waits for them, and re-layouts  10.9 us
    all_to_all x1, starting transfers between devices, body(): lax.all_to_all(blocks, CROSS, split_axis=0, concat_axis=0, tiled=True)  5 us
    ppermute x4, waiting for transfers between devices, swap_cores(): return lax.ppermute(values, 'core', [(0, 1), (1, 0)])  3.9 us
    dot_general x1, matrix products, body(): lax.dot_general(part_cot, down_rows, fwd_dims, preferred_element_type=jnp...  2.3 us
    dot_general x1, matrix products, body(): lax.dot_general(grad_gate, gate_mat, back_dims, preferred_element_type=jn...  2.22 us
    dot_general x1, matrix products, body(): lax.dot_general(grad_up, up_mat, back_dims, preferred_element_type=jnp.fl...  2.2 us
  transfers between devices with their start and end apart: 7, of which 5 were waited for; matrix products, arithmetic and copies ran while one was open for 14% of the time, Pallas kernels for 0%

profile of v24, /device:TPU:0, one launch (start us, length us, event | category | flops | bytes accessed | tf_op | source)
XLA Modules:
  0.0 82.6 jit_solution(18179235612141729038)
XLA Ops:
  0.0 0.9 %pad_maximum_fusion.3 = bf16[96,384]{1,0:T(8,128)(2,1)S(1)} fusion(bf16[96,192]{1,0:T(8,128)(2,1)} %param.9, bf16[96,192]{1,0:T(8,128)(2,1)} %param.8), kind=kLoop, calls=%fused_computation.57 | loop fusion | flops 147456 | bytes 147456 | tf_op jit(solution)/shard_map/concatenate | solution.py:63
  0.9 0.1 broadcast_in_dim.4
  1.0 23.6 %all_to_all.10 = bf16[8,96,384]{2,1,0:T(8,128)(2,1)S(1)} all-to-all(bf16[8,96,384]{2,1,0:T(8,128)(2,1)S(1)} %broadcast_in_dim.4), channel_id=1, replica_groups=mesh['expert'=2,'chip'=8,'core'=2] {'chip'}, dimensions={0} | all-to-all | bytes 1179648 | tf_op jit(solution)/shard_map/all_to_all | solution.py:65
  24.6 1.5 %collective-permute-start = (bf16[8,96,384]{2,1,0:T(8,128)(2,1)S(1)}, bf16[8,96,384]{2,1,0:T(8,128)(2,1)S(1)}, u32[]{:S(2)}, u32[]{:S(2)}) collective-permute-start(bf16[8,96,384]{2,1,0:T(8,128)(2,1)S(1)} %all_to_all.10), channel_id=1, source_target_pairs={{0,16},{16,0},{1,17},{17,1},{2,18},{18,2},{3,19},{19,3},{4,20},{20... | collective-permute-start | bytes 1769480 | tf_op jit(solution)/shard_map/ppermute | solution.py:57
  26.1 0.7 convert_element_type.77
  26.8 0.7 fusion.46
  27.5 0.5 collective-permute-start.1
  28.0 8.6 %copy.19 = bf16[1,1024,3072]{1,2,0:T(8,128)(2,1)} copy(bf16[1,1024,3072]{2,1,0:T(8,128)(2,1)} %param.12) | data formatting | bytes 12582912 | tf_op args[4]
  36.6 1.9 %collective-permute-done.1 = f32[2,96]{1,0:T(2,128)S(1)} collective-permute-done((f32[2,96]{1,0:T(2,128)S(1)}, f32[2,96]{1,0:T(2,128)S(1)}, u32[]{:S(2)}, u32[]{:S(2)}) %collective-permute-start.1) | collective-permute-done | bytes 800 | tf_op jit(solution)/shard_map/ppermute | solution.py:57
  38.6 0.1 pad_maximum_fusion.1
  38.7 0.1 slice.42
  38.8 0.1 collective-permute-start.3
  38.9 0.1 add.90
  39.0 0.1 add.91
  39.1 0.6 gather_fusion
  39.7 0.1 convert_element_type.79
  39.8 0.1 mul.77
  39.9 1.0 %collective-permute-done.3 = bf16[1,8,96,384]{3,2,0,1:T(8,128)(2,1)S(1)} collective-permute-done((bf16[1,8,96,384]{3,2,0,1:T(8,128)(2,1)S(1)}, bf16[1,8,96,384]{3,2,0,1:T(8,128)(2,1)S(1)}, u32[]{:S(2)}, u32[]{:S(2)}) %collective-permute-start.3) | collective-permute-done | bytes 589856 | tf_op jit(solution)/shard_map/ppermute | solution.py:33
  40.9 0.3 select_bitcast_fusion.1
  41.2 0.3 pad_maximum_fusion
  41.5 0.9 %convolution_bitcast_fusion = f32[192,8,2,384]{3,0,2,1:T(8,128)S(1)} fusion(bf16[2,8,2,96,384]{4,3,0,2,1:T(8,128)(2,1)S(1)} %pad_maximum_fusion, s32[2,96]{1,0:T(2,128)S(1)} %multiply_add_fusion, s32[192]{0:T(256)S(1)} %add.92), kind=kOutput, calls=%fused_computation.11 | convolution fusion | flops 453021696 | bytes 7079424 | tf_op jit(solution)/shard_map/dot_general | solution.py:80
  42.3 0.7 slice-done.2
  43.1 0.7 slice-done.3
  43.8 1.5 %convolution_bitcast_fusion.1 = f32[192,1024]{1,0:T(8,128)S(1)} fusion(bf16[8,2,192,1024]{3,2,1,0:T(8,128)(2,1)S(1)} %bitcast.118, f32[192,8,2,384]{3,0,2,1:T(8,128)S(1)} %convolution_bitcast_fusion), kind=kOutput, calls=%fused_computation.14 | convolution fusion | flops 1207959552 | bytes 8650752 | tf_op jit(solution)/shard_map/dot_general | solution.py:88
  45.3 0.3 slice-done.5
  45.7 0.2 copy-done.1
  45.9 2.3 %multiply_convert_fusion = (bf16[192,1024]{1,0:T(8,128)(2,1)S(1)}, f32[192,1024]{1,0:T(8,128)S(1)}) fusion(f32[192,1024]{1,0:T(8,128)S(1)} %convolution_bitcast_fusion.1, s32[1,192,1024]{2,1,0:T(8,128)S(1)} %copy-done.1, bf16[8,2,192,1024]{3,2,1,0:T(8,128)(2,1)S(1)} %bitcast.121, f32[192,8,2,384]{3,0,2,1:T(8,128)S(1)} %convolution_bitcast_fusion, ...), kind=kOutput, calls=%fused_computation.45 | convolution fusion | flops 1211695104 | bytes 12190720 | tf_op jit(solution)/shard_map/dot_general | solution.py:90
  48.2 2.0 %fusion.35 = bf16[192,1024]{1,0:T(8,128)(2,1)S(1)} fusion(f32[192,1024]{1,0:T(8,128)S(1)} %convolution_bitcast_fusion.1, f32[192,1024]{1,0:T(8,128)S(1)} %get-tuple-element.24, bf16[8,2,192,1024]{3,2,1,0:T(8,128)(2,1)S(1)} %bitcast.115, f32[192,8,2,384]{3,0,2,1:T(8,128)S(1)} %convolution_bitcast_fusion), kind=kOutput, calls=%fused_computation.44 | convolution fusion | flops 1212088320 | bytes 9830400 | tf_op jit(solution)/shard_map/dot_general | solution.py:89
  50.2 2.2 %fusion = f32[192,3072]{1,0:T(8,128)S(1)} fusion(bf16[192,1024]{1,0:T(8,128)(2,1)S(1)} %get-tuple-element.16, bf16[1,3072,1024]{2,1,0:T(8,128)(2,1)S(1)} %bitcast.114), kind=kOutput, calls=%fused_computation.1 | convolution fusion | flops 1207959552 | bytes 9043968 | tf_op jit(solution)/shard_map/dot_general | solution.py:103
  52.4 2.2 %fusion.7 = bf16[192,3072]{1,0:T(8,128)(2,1)S(1)} fusion(f32[192,3072]{1,0:T(8,128)S(1)} %fusion, bf16[192,1024]{1,0:T(8,128)(2,1)S(1)} %fusion.35, bf16[1,3072,1024]{2,1,0:T(8,128)(2,1)S(1)} %bitcast.117), kind=kOutput, calls=%fused_computation.6 | convolution fusion | flops 1209139200 | bytes 10223616 | tf_op jit(solution)/shard_map/dot_general | solution.py:101
  54.6 0.2 copy.29
  54.9 0.2 copy.31
  55.0 0.1 select_bitcast_fusion.2
  55.1 0.2 collective-permute-start.4
  55.3 1.9 %collective-permute-done.4 = bf16[2,8,48,384]{3,2,1,0:T(8,128)(2,1)S(1)} collective-permute-done((bf16[2,8,48,384]{3,2,1,0:T(8,128)(2,1)S(1)}, bf16[2,8,48,384]{3,2,1,0:T(8,128)(2,1)S(1)}, u32[]{:S(2)}, u32[]{:S(2)}) %collective-permute-start.4) | collective-permute-done | bytes 589856 | tf_op jit(solution)/shard_map/ppermute | solution.py:33
  57.2 1.1 %fusion.24 = bf16[2,8,48,384]{3,2,1,0:T(8,128)(2,1)} fusion(bf16[2,8,48,384]{3,2,1,0:T(8,128)(2,1)S(1)} %collective-permute-done.4, pred[]{:T(512)S(6)} %eq.45, bf16[2,2,8,48,384]{4,3,2,0,1:T(8,128)(2,1)S(1)} %bitcast.112), kind=kLoop, calls=%fused_computation.24 | loop fusion | flops 1474560 | bytes 2359297 | tf_op jit(solution)/shard_map/convert_element_type | solution.py:111
  58.3 5.0 %all-to-all-start.1 = ((bf16[16,48,384]{2,1,0:T(8,128)(2,1)}), bf16[16,48,384]{2,1,0:T(8,128)(2,1)S(1)}, u32[]{:S(2)}, u32[]{:S(2)}) async-start(bf16[16,48,384]{2,1,0:T(8,128)(2,1)} %bitcast.36), calls=%async_computation.1 | async-start | bytes 1179648 | tf_op jit(solution)/shard_map/all_to_all | solution.py:112
  63.3 0.1 eq.46
  63.4 0.1 fusion.40
  63.5 16.4 %all-to-all-done.1 = bf16[16,48,384]{2,1,0:T(8,128)(2,1)S(1)} async-done(((bf16[16,48,384]{2,1,0:T(8,128)(2,1)}), bf16[16,48,384]{2,1,0:T(8,128)(2,1)S(1)}, u32[]{:S(2)}, u32[]{:S(2)}) %all-to-all-start.1) | async-done | bytes 589856 | tf_op jit(solution)/shard_map/all_to_all | solution.py:112
  79.9 0.1 convert_reduce_fusion
  79.9 0.1 fusion.41
  80.0 0.2 convolution_bitcast_fusion.3
  80.3 0.2 fusion.27
  80.5 0.1 collective-permute-start.5
  80.5 0.2 convolution_bitcast_fusion.5
  80.8 1.1 %collective-permute-done.5 = f32[96,192]{1,0:T(8,128)S(1)} collective-permute-done((f32[96,192]{1,0:T(8,128)S(1)}, f32[96,192]{1,0:T(8,128)S(1)}, u32[]{:S(2)}, u32[]{:S(2)}) %collective-permute-start.5) | collective-permute-done | bytes 73760 | tf_op jit(solution)/shard_map/ppermute | solution.py:33
  81.8 0.8 fusion.28
  (28 shorter events, 0.1 us)
Async XLA Ops:
  24.6 14.0 %collective-permute-start = (bf16[8,96,384]{2,1,0:T(8,128)(2,1)S(1)}, bf16[8,96,384]{2,1,0:T(8,128)(2,1)S(1)}, u32[]{:S(2)}, u32[]{:S(2)}) collective-permute-start(bf16[8,96,384]{2,1,0:T(8,128)(2,1)S(1)} %all_to_all.10), channel_id=1, source_target_pairs={{0,16},{16,0},{1,17},{17,1},{2,18},{18,2},{3,19},{19,3},{4,20},{20... | collective-permute-start | bytes 1769480 | tf_op jit(solution)/shard_map/ppermute | solution.py:57
  26.1 12.6 %collective-permute-start.2 = (bf16[8,96,384]{2,1,0:T(8,128)(2,1)S(1)}, bf16[8,96,384]{2,1,0:T(8,128)(2,1)S(1)}, u32[]{:S(2)}, u32[]{:S(2)}) collective-permute-start(bf16[8,96,384]{2,1,0:T(8,128)(2,1)S(1)} %all_to_all.10), channel_id=1, source_target_pairs={{0,1},{1,0},{2,3},{3,2},{4,5},{5,4},{6,7},{7,6},{8,9},{9,8},{10,11... | collective-permute-start | bytes 1769480 | tf_op jit(solution)/shard_map/ppermute | solution.py:33
  27.5 11.1 %collective-permute-start.1 = (f32[2,96]{1,0:T(2,128)S(1)}, f32[2,96]{1,0:T(2,128)S(1)}, u32[]{:S(2)}, u32[]{:S(2)}) collective-permute-start(f32[2,96]{1,0:T(2,128)S(1)} %get-tuple-element.22), channel_id=1, source_target_pairs={{0,16},{16,0},{1,17},{17,1},{2,18},{18,2},{3,19},{19,3},{4,20},{20... | collective-permute-start | bytes 2312 | tf_op jit(solution)/shard_map/ppermute | solution.py:57
  38.8 2.1 %collective-permute-start.3 = (bf16[1,8,96,384]{3,2,0,1:T(8,128)(2,1)S(1)}, bf16[1,8,96,384]{3,2,0,1:T(8,128)(2,1)S(1)}, u32[]{:S(2)}, u32[]{:S(2)}) collective-permute-start(bf16[1,8,96,384]{3,2,0,1:T(8,128)(2,1)S(1)} %slice.42), channel_id=1, source_target_pairs={{0,1},{1,0},{2,3},{3,2},{4,5},{5,4},{6,7},{7,6},{8,9},{9,8},{10,11... | collective-permute-start | bytes 1769480 | tf_op jit(solution)/shard_map/ppermute | solution.py:33
  40.9 2.2 %slice-start.2 = ((s8[6291456]{0:T(1024)(128)(4,1)}), s8[4194304]{0:T(1024)(128)(4,1)S(1)}, s32[]{:S(2)}) async-start(s8[6291456]{0:T(1024)(128)(4,1)} %bitcast.116), calls=%async_computation.4 | async-start | bytes 8388608
  41.2 2.7 %slice-start.3 = ((s8[6291456]{0:T(1024)(128)(4,1)}), s8[2097152]{0:T(1024)(128)(4,1)S(1)}, s32[]{:S(2)}) async-start(s8[6291456]{0:T(1024)(128)(4,1)} %bitcast.116), calls=%async_computation.5 | async-start | bytes 4194304
  41.2 4.2 %slice-start.4 = ((s8[6291456]{0:T(1024)(128)(4,1)}), s8[4194304]{0:T(1024)(128)(4,1)S(1)}, s32[]{:S(2)}) async-start(s8[6291456]{0:T(1024)(128)(4,1)} %bitcast.119), calls=%async_computation.6 | async-start | bytes 8388608
  41.4 4.2 %slice-start.5 = ((s8[6291456]{0:T(1024)(128)(4,1)}), s8[2097152]{0:T(1024)(128)(4,1)S(1)}, s32[]{:S(2)}) async-start(s8[6291456]{0:T(1024)(128)(4,1)} %bitcast.119), calls=%async_computation.7 | async-start | bytes 4194304
  43.8 2.1 %copy-start.1 = (s32[1,192,1024]{2,1,0:T(8,128)S(1)}, s32[1,192,1024]{2,1,0:T(8,128)}, u32[]{:S(2)}) copy-start(s32[1,192,1024]{2,1,0:T(8,128)} %param.15) | copy-start | bytes 2359300
  43.8 4.4 %slice-start = ((s8[6291456]{0:T(1024)(128)(4,1)}), s8[4194304]{0:T(1024)(128)(4,1)S(1)}, s32[]{:S(2)}) async-start(s8[6291456]{0:T(1024)(128)(4,1)} %bitcast.113), calls=%async_computation.2 | async-start | bytes 8388608
  45.9 2.3 %slice-start.1 = ((s8[6291456]{0:T(1024)(128)(4,1)}), s8[2097152]{0:T(1024)(128)(4,1)S(1)}, s32[]{:S(2)}) async-start(s8[6291456]{0:T(1024)(128)(4,1)} %bitcast.113), calls=%async_computation.3 | async-start | bytes 4194304
  55.0 8.2 %copy-start = (s32[2,96]{1,0:T(2,128)S(1)}, s32[2,96]{1,0:T(2,128)}, u32[]{:S(2)}) copy-start(s32[2,96]{1,0:T(2,128)} %param.13) | copy-start | bytes 2308
  55.1 2.1 %collective-permute-start.4 = (bf16[2,8,48,384]{3,2,1,0:T(8,128)(2,1)S(1)}, bf16[2,8,48,384]{3,2,1,0:T(8,128)(2,1)S(1)}, u32[]{:S(2)}, u32[]{:S(2)}) collective-permute-start(bf16[2,8,48,384]{3,2,1,0:T(8,128)(2,1)S(1)} %select_bitcast_fusion.2), channel_id=1, source_target_pairs={{0,1},{1,0},{2,3},{3,2},{4,5},{5,4},{6,7},{7,6},{8,9},{9,8},{10,11... | collective-permute-start | bytes 1769480 | tf_op jit(solution)/shard_map/ppermute | solution.py:33
  58.3 21.6 %all-to-all-start.1 = ((bf16[16,48,384]{2,1,0:T(8,128)(2,1)}), bf16[16,48,384]{2,1,0:T(8,128)(2,1)S(1)}, u32[]{:S(2)}, u32[]{:S(2)}) async-start(bf16[16,48,384]{2,1,0:T(8,128)(2,1)} %bitcast.36), calls=%async_computation.1 | async-start | bytes 1179648 | tf_op jit(solution)/shard_map/all_to_all | solution.py:112
  80.5 1.4 %collective-permute-start.5 = (f32[96,192]{1,0:T(8,128)S(1)}, f32[96,192]{1,0:T(8,128)S(1)}, u32[]{:S(2)}, u32[]{:S(2)}) collective-permute-start(f32[96,192]{1,0:T(8,128)S(1)} %fusion.27), channel_id=1, source_target_pairs={{0,1},{1,0},{2,3},{3,2},{4,5},{5,4},{6,7},{7,6},{8,9},{9,8},{10,11... | collective-permute-start | bytes 221192 | tf_op jit(solution)/shard_map/ppermute | solution.py:33
